TPU v7x, 512 devices: a whole 4x8x8 slice. The times are simulated.
512 devices in a mesh: rows: 32 (over y, x), vocab: 16 (over z, core).
Axes of the slice: x: 4, y: 8, z: 8, core: 2. Of those that a mesh axis runs over, the one named last changes fastest.
Arguments:
- hidden: bfloat16 [12288, 8192], P('rows', 'vocab'), may hold values from -128 to 128
- head: bfloat16 [8192, 8192], P('rows', 'vocab'), may hold values from -4 to 4
- targets: int32 [12288], P('rows'), may hold values from 0 to 128255
- live: int32 [12288], P('rows'), may hold values from 0 to 1, as said below
- prior_lse: float32 [12288], P('rows'), may hold values from 10 to 18
- prior_mean: float32 [12288], P('rows'), may hold values from 2 to 8
- prior_target: float32 [12288], P('rows'), may hold values from -12 to 12
- seq_lengths: int32 [32], replicated, may hold values from 1 to 768, 12288 in all
Outputs:
- logprob: float32 [12288], P(('rows', 'vocab'))
- entropy: float32 [12288], P(('rows', 'vocab'))
- seq_score: float32 [32], replicated
Inputs may be any that keep to these rules, and one draw needn't show every extreme that they name: Within the 384 rows of each index of rows, the live rows come first; every such index has at least 48 live rows and some index has all 384.
All inputs are finite; a program needn't handle non-finite values.
Results may differ from a plain program's by a relative error of at most 0.0003.
Values may be sent and summed in bfloat16 or wider, within the bound.
No kernel may reach another device: no remote copies, remote signals or barrier semaphores. Data moves between devices by JAX's collectives and lax.ppermute only.
A program may use at most 64 MiB of HBM per device.

v0:
```python
import jax
import jax.numpy as jnp
from jax import lax
from jax.sharding import PartitionSpec as P

VOCAB = 128256
SEQS = 32
GSIZE = 8


def finish_rows(block_peak, block_mass, block_moment, block_target, live, prior_lse, prior_mean):
    highest = jnp.maximum(block_peak, prior_lse)
    earlier = jnp.exp(prior_lse - highest)
    scaled = jnp.exp(block_peak - highest)
    total_mass = earlier + block_mass * scaled
    norm_log = highest + jnp.log(total_mass)
    average = (earlier * prior_mean + scaled * block_moment) / total_mass
    keeping = live.astype(jnp.float32)
    return (keeping * (block_target - norm_log), keeping * (norm_log - average))


def local(hidden, head, targets, live, prior_lse, prior_mean, prior_target, seq_lengths):
    rows_here = hidden.shape[0]
    cols_here = head.shape[1]
    spread = lax.axis_size("vocab")
    which = lax.axis_index("vocab")
    block_first = VOCAB - cols_here * spread
    first_col = block_first + which * cols_here
    gathered = lax.all_gather(hidden, "vocab", axis=1, tiled=True)
    logits = jnp.dot(
        gathered,
        lax.all_gather(head, "rows", axis=0, tiled=True),
        preferred_element_type=jnp.float32,
    )
    row_peak = jnp.max(logits, axis=1)
    weights = jnp.exp(logits - row_peak[:, None])
    row_mass = jnp.sum(weights, axis=1)
    moment = jnp.sum(weights * logits, axis=1)
    column = targets - first_col
    columns = lax.broadcasted_iota(jnp.int32, logits.shape, 1)
    picked = jnp.sum(jnp.where(columns == column[:, None], logits, jnp.zeros_like(logits)), axis=1)
    share = rows_here // spread
    begin = which * share

    def own_rows(values):
        return lax.dynamic_slice_in_dim(values, begin, share, 0)

    highest = lax.pmax(row_peak, "vocab")
    factor = jnp.exp(row_peak - highest)
    mass_all, moment_all, picked_all = lax.psum(
        (row_mass * factor, moment * factor, picked), "vocab"
    )
    peak_share = own_rows(highest)
    mass_share = own_rows(mass_all)
    moment_share = own_rows(moment_all)
    picked_share = own_rows(picked_all)
    target_share = own_rows(targets)
    block_target = jnp.where(target_share >= block_first, picked_share, own_rows(prior_target))
    logprob, entropy = finish_rows(
        peak_share,
        mass_share,
        moment_share,
        block_target,
        own_rows(live),
        own_rows(prior_lse),
        own_rows(prior_mean),
    )
    global_rows = lax.axis_index("rows") * rows_here + begin + jnp.arange(share, dtype=jnp.int32)
    endings = jnp.cumsum(seq_lengths)
    member = jnp.sum((global_rows[:, None] >= endings[None, :]).astype(jnp.int32), axis=1)
    onehot = (member[:, None] == jnp.arange(SEQS, dtype=jnp.int32)[None, :]).astype(jnp.float32)
    partial_sums = jnp.sum(onehot * logprob[:, None], axis=0)
    sums = lax.psum(partial_sums, ("rows", "vocab"))
    seq_mean = sums / seq_lengths.astype(jnp.float32)
    grouped = seq_mean.reshape(SEQS // GSIZE, GSIZE)
    seq_score = (grouped - jnp.mean(grouped, axis=1, keepdims=True)).reshape(SEQS)
    return (logprob, entropy, seq_score)


def solution(mesh):
    return jax.shard_map(
        local,
        mesh=mesh,
        in_specs=(
            P("rows", "vocab"),
            P("rows", "vocab"),
            P("rows"),
            P("rows"),
            P("rows"),
            P("rows"),
            P("rows"),
            P(),
        ),
        out_specs=(P(("rows", "vocab")), P(("rows", "vocab")), P()),
        check_vma=False,
    )
```

profile of v0, /device:TPU:1, one launch (start us, length us, event | category | flops | bytes accessed | tf_op | source)
XLA Modules:
  0.0 332.5 jit_solution(5648980550424565232)
XLA Ops:
  7.2 0.0 all-gather.3.cloned.1.call-start
  7.2 0.7 all-gather.3.cloned.1.call-update
  7.9 0.0 all-gather.5.cloned.1.call-start
  7.9 0.7 all-gather.5.cloned.1.call-update
  8.7 0.7 copy.13
  9.4 0.1 reduce-window.8
  9.4 0.1 reduce
  9.6 0.2 convert_reduce_fusion
  9.8 0.7 broadcast_subtract_fusion
  10.4 0.0 copy-start
  10.4 55.1 %all-gather.3.cloned.1.call-done = bf16[384,8192]{1,0:T(8,128)(2,1)} async-done(((bf16[384,512]{1,0:T(8,128)(2,1)}), bf16[384,8192]{1,0:T(8,128)(2,1)}) %all-gather.3.cloned.1.call-update) | async-done | bytes 6291472 | tf_op jit(solution)/shard_map/all_gather | solution.py:29
  65.6 103.9 %all-gather.5.cloned.1.call-done = bf16[8192,512]{1,0:T(8,128)(2,1)} async-done(((bf16[256,512]{1,0:T(8,128)(2,1)}), bf16[8192,512]{1,0:T(8,128)(2,1)}) %all-gather.5.cloned.1.call-update) | async-done | bytes 8388624 | tf_op jit(solution)/shard_map/all_gather | solution.py:32
  169.4 8.0 %fusion.5 = (f32[384]{0:T(512)S(1)}, f32[384,512]{1,0:T(8,128)S(1)}) fusion(bf16[384,8192]{1,0:T(8,128)(2,1)} %all-gather.3.cloned.1.call-done, bf16[8192,512]{1,0:T(8,128)(2,1)} %all-gather.5.cloned.1.call-done), kind=kOutput, calls=%fused_computation.24 | convolution fusion | flops 3221421568 | bytes 15468032 | tf_op jit(solution)/shard_map/dot_general | solution.py:30
  177.4 25.1 %pmax.7 = f32[384]{0:T(512)S(1)} all-reduce(f32[384]{0:T(512)S(1)} %get-tuple-element.13), channel_id=1, replica_groups=mesh['rows'=32,'vocab'=16] {'vocab'}, use_global_device_ids=true, to_apply=%region_3.4 | all-reduce | flops 384 | bytes 3072 | tf_op jit(solution)/shard_map/pmax | solution.py:48
  202.5 0.5 multiply_reduce_fusion
  203.0 25.8 %all-reduce = (f32[384]{0:T(512)S(1)}, f32[384]{0:T(512)S(1)}, f32[384]{0:T(512)S(1)}) all-reduce(f32[384]{0:T(512)S(1)} %get-tuple-element.5, f32[384]{0:T(512)S(1)} %get-tuple-element.12, f32[384]{0:T(512)S(1)} %get-tuple-element.11), channel_id=1, replica_groups=mesh['rows'=32,'vocab'=16] {'vocab'}, use_global_device_ids=true, to_apply=%region_1.0 | all-reduce | flops 1152 | bytes 9216 | tf_op jit(solution)/shard_map/psum | solution.py:50
  228.9 1.4 subtract_multiply_fusion
  230.2 0.0 copy-start.1
  230.2 0.1 select_reduce_fusion.1
  230.3 94.4 %psum.31 = f32[32]{0:T(128)S(1)} all-reduce(f32[32]{0:T(128)S(1)} %select_reduce_fusion.1), channel_id=1, replica_groups=mesh['rows'=32,'vocab'=16] {'rows','vocab'}, use_global_device_ids=true, to_apply=%region_11.12 | all-reduce | flops 32 | bytes 256 | tf_op jit(solution)/shard_map/psum | solution.py:73
  324.7 0.0 copy-done
  324.7 0.1 reshape.49
  324.8 0.1 reduce_sum.59
  325.0 0.1 sub.49
  325.0 0.1 sub.50
  325.1 0.5 sub.51
  325.6 0.0 copy-done.1
  (4 shorter events, 0.0 us)
Async XLA Ops:
  7.2 58.4 %all-gather.3.cloned.1.call-start = ((), (), s32[]{:S(2)}) async-start(), calls=%async_computation | async-start | bytes 6684672 | tf_op jit(solution)/shard_map/all_gather | solution.py:29
  7.9 161.5 %all-gather.5.cloned.1.call-start = ((), (), s32[]{:S(2)}) async-start(), calls=%async_computation.1 | async-start | bytes 8650752 | tf_op jit(solution)/shard_map/all_gather | solution.py:32
  10.4 314.3 %copy-start = (s32[32]{0:T(128)S(1)}, s32[32]{0:T(128)}, u32[]{:S(2)}) copy-start(s32[32]{0:T(128)} %param.15) | copy-start | bytes 388
  230.2 95.4 %copy-start.1 = (f32[24]{0:T(128)}, f32[24]{0:T(128)S(1)}, u32[]{:S(2)}) copy-start(f32[24]{0:T(128)S(1)} %get-tuple-element.10) | copy-start | bytes 292
Sparse Core Ops, SparseCore 0:
  10.1 55.3 all-gather.2
  68.7 100.6 all-gather.4
where the time goes:
time: 333 us; the launch traced here: 332 us
  waiting for transfers between devices  160 us (48%)
  blocking collectives  145 us (44%)
  between operations  14.1 us (4%)
  matrix products  8 us (2%)
  other arithmetic  3.64 us (1%)
    all_gather x1, waiting for transfers between devices, local(): lax.all_gather(head, 'rows', axis=0, tiled=True)  104 us
    psum x1, blocking collectives, local(): sums = lax.psum(partial_sums, ('rows', 'vocab'))  94.4 us
    all_gather x1, waiting for transfers between devices, local(): gathered = lax.all_gather(hidden, 'vocab', axis=1, tiled=True)  55.1 us
    psum x1, blocking collectives, local(): lax.psum((row_mass * factor, moment * factor, picked), 'vocab')  25.8 us
    pmax x1, blocking collectives, local(): highest = lax.pmax(row_peak, 'vocab')  25.1 us
    dot_general x1, matrix products, local(): jnp.dot(gathered, lax.all_gather(head, 'rows', axis=0, tiled=True), prefe...  8 us
  transfers between devices with their start and end apart: 2, of which 2 were waited for; matrix products, arithmetic and copies ran while one was open for 1% of the time, Pallas kernels for 0%

commit v1 on v0

--- a/solution.py
+++ b/solution.py
@@ -39,42 +39,35 @@
     column = targets - first_col
     columns = lax.broadcasted_iota(jnp.int32, logits.shape, 1)
     picked = jnp.sum(jnp.where(columns == column[:, None], logits, jnp.zeros_like(logits)), axis=1)
+
+    stats = jnp.stack([row_peak, row_mass, moment, picked])
+    every = lax.all_gather(stats, "vocab", axis=0, tiled=False)
+    peaks = every[:, 0]
+    highest = jnp.max(peaks, axis=0)
+    factor = jnp.exp(peaks - highest[None, :])
+    mass_all = jnp.sum(every[:, 1] * factor, axis=0)
+    moment_all = jnp.sum(every[:, 2] * factor, axis=0)
+    picked_all = jnp.sum(every[:, 3], axis=0)
+    block_target = jnp.where(targets >= block_first, picked_all, prior_target)
+    logprob, entropy = finish_rows(
+        highest, mass_all, moment_all, block_target, live, prior_lse, prior_mean
+    )
+
     share = rows_here // spread
     begin = which * share
+    logprob_share = lax.dynamic_slice_in_dim(logprob, begin, share, 0)
+    entropy_share = lax.dynamic_slice_in_dim(entropy, begin, share, 0)
 
-    def own_rows(values):
-        return lax.dynamic_slice_in_dim(values, begin, share, 0)
-
-    highest = lax.pmax(row_peak, "vocab")
-    factor = jnp.exp(row_peak - highest)
-    mass_all, moment_all, picked_all = lax.psum(
-        (row_mass * factor, moment * factor, picked), "vocab"
-    )
-    peak_share = own_rows(highest)
-    mass_share = own_rows(mass_all)
-    moment_share = own_rows(moment_all)
-    picked_share = own_rows(picked_all)
-    target_share = own_rows(targets)
-    block_target = jnp.where(target_share >= block_first, picked_share, own_rows(prior_target))
-    logprob, entropy = finish_rows(
-        peak_share,
-        mass_share,
-        moment_share,
-        block_target,
-        own_rows(live),
-        own_rows(prior_lse),
-        own_rows(prior_mean),
-    )
-    global_rows = lax.axis_index("rows") * rows_here + begin + jnp.arange(share, dtype=jnp.int32)
+    global_rows = lax.axis_index("rows") * rows_here + jnp.arange(rows_here, dtype=jnp.int32)
     endings = jnp.cumsum(seq_lengths)
     member = jnp.sum((global_rows[:, None] >= endings[None, :]).astype(jnp.int32), axis=1)
     onehot = (member[:, None] == jnp.arange(SEQS, dtype=jnp.int32)[None, :]).astype(jnp.float32)
     partial_sums = jnp.sum(onehot * logprob[:, None], axis=0)
-    sums = lax.psum(partial_sums, ("rows", "vocab"))
+    sums = jnp.sum(lax.all_gather(partial_sums, "rows", axis=0, tiled=False), axis=0)
     seq_mean = sums / seq_lengths.astype(jnp.float32)
     grouped = seq_mean.reshape(SEQS // GSIZE, GSIZE)
     seq_score = (grouped - jnp.mean(grouped, axis=1, keepdims=True)).reshape(SEQS)
-    return (logprob, entropy, seq_score)
+    return (logprob_share, entropy_share, seq_score)
 
 
 def solution(mesh):

time: 333 us -> 276 us (0.83)
  the two profiles are of different devices: /device:TPU:1 before, /device:TPU:2 now
where the time goes in v1:
time: 276 us
  waiting for transfers between devices  157 us (57%)
  blocking collectives  89.7 us (32%)
  between operations  14.8 us (5%)
  matrix products  8 us (3%)
  local copies, waits for them, and re-layouts  3.78 us (1%)
    all_gather x1, waiting for transfers between devices, local(): lax.all_gather(head, 'rows', axis=0, tiled=True)  103 us
    unnamed x1, blocking collectives  71.4 us
    all_gather x1, waiting for transfers between devices, local(): gathered = lax.all_gather(hidden, 'vocab', axis=1, tiled=True)  52 us
    all_gather x1, blocking collectives, local(): every = lax.all_gather(stats, 'vocab', axis=0, tiled=False)  18.3 us
    dot_general x1, matrix products, local(): jnp.dot(gathered, lax.all_gather(head, 'rows', axis=0, tiled=True), prefe...  8 us
  transfers between devices with their start and end apart: 2, of which 2 were waited for; matrix products, arithmetic and copies ran while one was open for 1% of the time, Pallas kernels for 0%

profile of v1, /device:TPU:2, one launch (start us, length us, event | category | flops | bytes accessed | tf_op | source)
XLA Modules:
  0.0 275.6 jit_solution(6936003982868174059)
XLA Ops:
  7.2 0.0 all-gather.6.cloned.1.call-start
  7.2 0.7 all-gather.6.cloned.1.call-update
  7.9 0.0 all-gather.8.cloned.1.call-start
  7.9 0.7 all-gather.8.cloned.1.call-update
  8.7 0.7 copy.22
  9.4 0.1 reduce-window.8
  9.5 0.1 reduce.2
  9.6 1.3 dynamic-slice
  11.5 0.1 convert_reduce_fusion
  11.6 0.7 broadcast_subtract_fusion
  12.3 0.0 copy-start
  12.3 0.0 copy-start.1
  12.3 0.0 copy-start.2
  12.3 0.0 copy-start.3
  12.3 0.0 copy-start.4
  12.3 0.0 copy-start.5
  12.3 52.0 %all-gather.6.cloned.1.call-done = bf16[384,8192]{1,0:T(8,128)(2,1)} async-done(((bf16[384,512]{1,0:T(8,128)(2,1)}), bf16[384,8192]{1,0:T(8,128)(2,1)}) %all-gather.6.cloned.1.call-update) | async-done | bytes 6291472 | tf_op jit(solution)/shard_map/all_gather | solution.py:29
  64.3 103.5 %all-gather.8.cloned.1.call-done = bf16[8192,512]{1,0:T(8,128)(2,1)} async-done(((bf16[256,512]{1,0:T(8,128)(2,1)}), bf16[8192,512]{1,0:T(8,128)(2,1)}) %all-gather.8.cloned.1.call-update) | async-done | bytes 8388624 | tf_op jit(solution)/shard_map/all_gather | solution.py:32
  167.7 8.0 %fusion.7 = (f32[384]{0:T(512)S(1)}, f32[384,512]{1,0:T(8,128)S(1)}) fusion(bf16[384,8192]{1,0:T(8,128)(2,1)} %all-gather.6.cloned.1.call-done, bf16[8192,512]{1,0:T(8,128)(2,1)} %all-gather.8.cloned.1.call-done), kind=kOutput, calls=%fused_computation.30 | convolution fusion | flops 3221421568 | bytes 15468032 | tf_op jit(solution)/shard_map/dot_general | solution.py:30
  175.8 0.5 fusion
  176.3 18.3 %all-gather.2 = f32[16,4,384]{2,1,0:T(4,128)S(1)} all-gather(f32[1,4,384]{2,1,0:T(4,128)S(1)} %maximum_bitcast_fusion), channel_id=2, replica_groups=mesh['rows'=32,'vocab'=16] {'vocab'}, dimensions={0}, use_global_device_ids=true | all-gather | bytes 104448 | tf_op jit(solution)/shard_map/all_gather | solution.py:44
  194.6 0.1 fusion.6
  194.8 0.0 copy-done
  194.8 0.0 copy-done.1
  194.8 0.0 copy-done.2
  194.8 0.0 copy-done.3
  194.8 0.0 copy-done.4
  194.8 0.6 dynamic_slice.6
  195.4 0.6 dynamic_slice.7
  196.0 0.1 select_reduce_fusion.1
  196.1 0.2 dynamic-update-slice
  196.4 71.4 %all-reduce = f32[1024]{0:T(1024)S(1)} all-reduce(f32[1024]{0:T(1024)S(1)} %dynamic-update-slice), channel_id=3, replica_groups=mesh['rows'=32,'vocab'=16] {'rows'}, use_global_device_ids=true, to_apply=%add | all-reduce | flops 1024 | bytes 8192
  267.8 0.1 reshape.52
  267.9 0.0 copy-done.5
  267.9 0.1 reshape.50
  268.0 0.1 reduce_sum.99
  268.1 0.1 sub.55
  268.2 0.1 sub.56
  268.2 0.5 sub.57
  (12 shorter events, 0.1 us)
Async XLA Ops:
  7.2 57.1 %all-gather.6.cloned.1.call-start = ((), (), s32[]{:S(2)}) async-start(), calls=%async_computation | async-start | bytes 6684672 | tf_op jit(solution)/shard_map/all_gather | solution.py:29
  7.9 159.8 %all-gather.8.cloned.1.call-start = ((), (), s32[]{:S(2)}) async-start(), calls=%async_computation.1 | async-start | bytes 8650752 | tf_op jit(solution)/shard_map/all_gather | solution.py:32
  12.3 182.5 %copy-start = (s32[384]{0:T(512)S(1)}, s32[384]{0:T(512)}, u32[]{:S(2)}) copy-start(s32[384]{0:T(512)} %param.10) | copy-start | bytes 4612
  12.3 182.5 %copy-start.1 = (f32[384]{0:T(512)S(1)}, f32[384]{0:T(512)}, u32[]{:S(2)}) copy-start(f32[384]{0:T(512)} %param.13) | copy-start | bytes 4612
  12.3 182.5 %copy-start.2 = (s32[384]{0:T(512)S(1)}, s32[384]{0:T(512)}, u32[]{:S(2)}) copy-start(s32[384]{0:T(512)} %param.11) | copy-start | bytes 4612
  12.3 182.5 %copy-start.3 = (f32[384]{0:T(512)S(1)}, f32[384]{0:T(512)}, u32[]{:S(2)}) copy-start(f32[384]{0:T(512)} %param.12) | copy-start | bytes 4612
  12.3 182.5 %copy-start.4 = (f32[384]{0:T(512)S(1)}, f32[384]{0:T(512)}, u32[]{:S(2)}) copy-start(f32[384]{0:T(512)} %param.14) | copy-start | bytes 4612
  12.3 255.5 %copy-start.5 = (s32[32]{0:T(128)S(1)}, s32[32]{0:T(128)}, u32[]{:S(2)}) copy-start(s32[32]{0:T(128)} %param.15) | copy-start | bytes 388
Sparse Core Ops, SparseCore 0:
  10.1 54.0 all-gather.5
  67.4 100.2 all-gather.7

commit v2 on v1

--- a/solution.py
+++ b/solution.py
@@ -6,6 +6,8 @@
 VOCAB = 128256
 SEQS = 32
 GSIZE = 8
+ROW_AXES = ("y", "x")
+VOCAB_AXES = ("z", "c")
 
 
 def finish_rows(block_peak, block_mass, block_moment, block_target, live, prior_lse, prior_mean):
@@ -22,14 +24,14 @@
 def local(hidden, head, targets, live, prior_lse, prior_mean, prior_target, seq_lengths):
     rows_here = hidden.shape[0]
     cols_here = head.shape[1]
-    spread = lax.axis_size("vocab")
-    which = lax.axis_index("vocab")
+    spread = lax.axis_size(VOCAB_AXES)
+    which = lax.axis_index(VOCAB_AXES)
     block_first = VOCAB - cols_here * spread
     first_col = block_first + which * cols_here
-    gathered = lax.all_gather(hidden, "vocab", axis=1, tiled=True)
+    gathered = lax.all_gather(hidden, VOCAB_AXES, axis=1, tiled=True)
     logits = jnp.dot(
         gathered,
-        lax.all_gather(head, "rows", axis=0, tiled=True),
+        lax.all_gather(head, ROW_AXES, axis=0, tiled=True),
         preferred_element_type=jnp.float32,
     )
     row_peak = jnp.max(logits, axis=1)
@@ -41,7 +43,7 @@
     picked = jnp.sum(jnp.where(columns == column[:, None], logits, jnp.zeros_like(logits)), axis=1)
 
     stats = jnp.stack([row_peak, row_mass, moment, picked])
-    every = lax.all_gather(stats, "vocab", axis=0, tiled=False)
+    every = lax.all_gather(stats, VOCAB_AXES, axis=0, tiled=False)
     peaks = every[:, 0]
     highest = jnp.max(peaks, axis=0)
     factor = jnp.exp(peaks - highest[None, :])
@@ -58,12 +60,12 @@
     logprob_share = lax.dynamic_slice_in_dim(logprob, begin, share, 0)
     entropy_share = lax.dynamic_slice_in_dim(entropy, begin, share, 0)
 
-    global_rows = lax.axis_index("rows") * rows_here + jnp.arange(rows_here, dtype=jnp.int32)
+    global_rows = lax.axis_index(ROW_AXES) * rows_here + jnp.arange(rows_here, dtype=jnp.int32)
     endings = jnp.cumsum(seq_lengths)
     member = jnp.sum((global_rows[:, None] >= endings[None, :]).astype(jnp.int32), axis=1)
     onehot = (member[:, None] == jnp.arange(SEQS, dtype=jnp.int32)[None, :]).astype(jnp.float32)
     partial_sums = jnp.sum(onehot * logprob[:, None], axis=0)
-    sums = jnp.sum(lax.all_gather(partial_sums, "rows", axis=0, tiled=False), axis=0)
+    sums = lax.psum(lax.psum(partial_sums, "x"), "y")
     seq_mean = sums / seq_lengths.astype(jnp.float32)
     grouped = seq_mean.reshape(SEQS // GSIZE, GSIZE)
     seq_score = (grouped - jnp.mean(grouped, axis=1, keepdims=True)).reshape(SEQS)
@@ -71,19 +73,26 @@
 
 
 def solution(mesh):
+    rows_y = 8 if mesh.shape["rows"] % 8 == 0 else 1
+    vocab_c = 2 if mesh.shape["vocab"] % 2 == 0 else 1
+    devices = mesh.devices.reshape(
+        rows_y, mesh.shape["rows"] // rows_y, mesh.shape["vocab"] // vocab_c, vocab_c
+    )
+    fine = jax.sharding.Mesh(devices, ("y", "x", "z", "c"))
+    rows, vocab = ROW_AXES, VOCAB_AXES
     return jax.shard_map(
         local,
-        mesh=mesh,
+        mesh=fine,
         in_specs=(
-            P("rows", "vocab"),
-            P("rows", "vocab"),
-            P("rows"),
-            P("rows"),
-            P("rows"),
-            P("rows"),
-            P("rows"),
+            P(rows, vocab),
+            P(rows, vocab),
+            P(rows),
+            P(rows),
+            P(rows),
+            P(rows),
+            P(rows),
             P(),
         ),
-        out_specs=(P(("rows", "vocab")), P(("rows", "vocab")), P()),
+        out_specs=(P(rows + vocab), P(rows + vocab), P()),
         check_vma=False,
     )

time: 276 us -> 229 us (0.83)
  the two profiles are of different devices: /device:TPU:2 before, /device:TPU:1 now
where the time goes in v2:
time: 229 us; the launch traced here: 225 us
  waiting for transfers between devices  160 us (70%)
  blocking collectives  37.6 us (16%)
  between operations  14.2 us (6%)
  matrix products  8 us (3%)
  other arithmetic  2.36 us (1%)
    all_gather x1, waiting for transfers between devices, local(): lax.all_gather(head, ROW_AXES, axis=0, tiled=True)  104 us
    all_gather x1, waiting for transfers between devices, local(): gathered = lax.all_gather(hidden, VOCAB_AXES, axis=1, tiled=True)  55.2 us
    all_gather x1, blocking collectives, local(): every = lax.all_gather(stats, VOCAB_AXES, axis=0, tiled=False)  19.3 us
    psum x2, blocking collectives, local(): sums = lax.psum(lax.psum(partial_sums, 'x'), 'y')  18.4 us
    dot_general x1, matrix products, local(): jnp.dot(gathered, lax.all_gather(head, ROW_AXES, axis=0, tiled=True), pre...  8 us
  transfers between devices with their start and end apart: 2, of which 2 were waited for; matrix products, arithmetic and copies ran while one was open for 1% of the time, Pallas kernels for 0%

profile of v2, /device:TPU:1, one launch (start us, length us, event | category | flops | bytes accessed | tf_op | source)
XLA Modules:
  0.0 224.8 jit_solution(4650545966353559341)
XLA Ops:
  7.2 0.0 all-gather.5.cloned.1.call-start
  7.2 0.7 all-gather.5.cloned.1.call-update
  7.9 0.0 all-gather.7.cloned.1.call-start
  7.9 0.7 all-gather.7.cloned.1.call-update
  8.7 0.7 copy.22
  9.4 0.1 reduce-window.8
  9.5 0.1 reduce.2
  9.6 0.1 convert_reduce_fusion
  9.7 0.7 broadcast_subtract_fusion
  10.4 0.0 copy-start
  10.4 0.0 copy-start.1
  10.4 0.0 copy-start.2
  10.4 0.0 copy-start.3
  10.4 0.0 copy-start.4
  10.4 0.0 copy-start.5
  10.4 55.2 %all-gather.5.cloned.1.call-done = bf16[384,8192]{1,0:T(8,128)(2,1)} async-done(((bf16[384,512]{1,0:T(8,128)(2,1)}), bf16[384,8192]{1,0:T(8,128)(2,1)}) %all-gather.5.cloned.1.call-update) | async-done | bytes 6291472 | tf_op jit(solution)/shard_map/all_gather | solution.py:31
  65.6 103.9 %all-gather.7.cloned.1.call-done = bf16[8192,512]{1,0:T(8,128)(2,1)} async-done(((bf16[256,512]{1,0:T(8,128)(2,1)}), bf16[8192,512]{1,0:T(8,128)(2,1)}) %all-gather.7.cloned.1.call-update) | async-done | bytes 8388624 | tf_op jit(solution)/shard_map/all_gather | solution.py:34
  169.4 8.0 %fusion.7 = (f32[384]{0:T(512)S(1)}, f32[384,512]{1,0:T(8,128)S(1)}) fusion(bf16[384,8192]{1,0:T(8,128)(2,1)} %all-gather.5.cloned.1.call-done, bf16[8192,512]{1,0:T(8,128)(2,1)} %all-gather.7.cloned.1.call-done), kind=kOutput, calls=%fused_computation.30 | convolution fusion | flops 3221421568 | bytes 15468032 | tf_op jit(solution)/shard_map/dot_general | solution.py:32
  177.4 0.5 fusion
  178.0 19.3 %all-gather.1 = f32[16,4,384]{2,1,0:T(4,128)S(1)} all-gather(f32[1,4,384]{2,1,0:T(4,128)S(1)} %maximum_bitcast_fusion), channel_id=2, replica_groups=mesh['y'=8,'x'=4,'z'=8,'c'=2] {'z','c'}, dimensions={0}, use_global_device_ids=true | all-gather | bytes 104448 | tf_op jit(solution)/shard_map/all_gather | solution.py:46
  197.2 0.1 fusion.6
  197.3 0.0 copy-done
  197.4 0.0 copy-done.1
  197.4 0.0 copy-done.2
  197.4 0.0 copy-done.3
  197.4 0.0 copy-done.4
  197.4 0.6 dynamic_slice.6
  198.0 0.6 dynamic_slice.7
  198.6 0.1 select_reduce_fusion.1
  198.7 6.6 %psum.14 = f32[32]{0:T(128)S(1)} all-reduce(f32[32]{0:T(128)S(1)} %select_reduce_fusion.1), channel_id=1, replica_groups=mesh['y'=8,'x'=4,'z'=8,'c'=2] {'x'}, use_global_device_ids=true, to_apply=%region_11.12 | all-reduce | flops 32 | bytes 256 | tf_op jit(solution)/shard_map/psum | solution.py:68
  205.3 11.8 %psum.15 = f32[32]{0:T(128)S(1)} all-reduce(f32[32]{0:T(128)S(1)} %psum.14), channel_id=1, replica_groups=mesh['y'=8,'x'=4,'z'=8,'c'=2] {'y'}, use_global_device_ids=true, to_apply=%region_12.13 | all-reduce | flops 32 | bytes 256 | tf_op jit(solution)/shard_map/psum | solution.py:68
  217.1 0.0 copy-done.5
  217.1 0.1 reshape.50
  217.2 0.1 reduce_sum.89
  217.3 0.1 sub.55
  217.4 0.1 sub.56
  217.5 0.5 sub.57
  (10 shorter events, 0.1 us)
Async XLA Ops:
  7.2 58.4 %all-gather.5.cloned.1.call-start = ((), (), s32[]{:S(2)}) async-start(), calls=%async_computation | async-start | bytes 6684672 | tf_op jit(solution)/shard_map/all_gather | solution.py:31
  7.9 161.5 %all-gather.7.cloned.1.call-start = ((), (), s32[]{:S(2)}) async-start(), calls=%async_computation.1 | async-start | bytes 8650752 | tf_op jit(solution)/shard_map/all_gather | solution.py:34
  10.4 187.0 %copy-start = (s32[384]{0:T(512)S(1)}, s32[384]{0:T(512)}, u32[]{:S(2)}) copy-start(s32[384]{0:T(512)} %param.10) | copy-start | bytes 4612
  10.4 187.0 %copy-start.1 = (f32[384]{0:T(512)S(1)}, f32[384]{0:T(512)}, u32[]{:S(2)}) copy-start(f32[384]{0:T(512)} %param.13) | copy-start | bytes 4612
  10.4 187.0 %copy-start.2 = (s32[384]{0:T(512)S(1)}, s32[384]{0:T(512)}, u32[]{:S(2)}) copy-start(s32[384]{0:T(512)} %param.11) | copy-start | bytes 4612
  10.4 187.0 %copy-start.3 = (f32[384]{0:T(512)S(1)}, f32[384]{0:T(512)}, u32[]{:S(2)}) copy-start(f32[384]{0:T(512)} %param.12) | copy-start | bytes 4612
  10.4 187.0 %copy-start.4 = (f32[384]{0:T(512)S(1)}, f32[384]{0:T(512)}, u32[]{:S(2)}) copy-start(f32[384]{0:T(512)} %param.14) | copy-start | bytes 4612
  10.4 206.7 %copy-start.5 = (s32[32]{0:T(128)S(1)}, s32[32]{0:T(128)}, u32[]{:S(2)}) copy-start(s32[32]{0:T(128)} %param.15) | copy-start | bytes 388
Sparse Core Ops, SparseCore 0:
  10.1 55.3 all-gather.4
  68.7 100.6 all-gather.6

commit v3 on v2

--- a/solution.py
+++ b/solution.py
@@ -21,6 +21,41 @@
     return (keeping * (block_target - norm_log), keeping * (norm_log - average))
 
 
+def gather_hidden(hidden):
+    nz = lax.axis_size("z")
+    z = lax.axis_index("z")
+    c = lax.axis_index("c")
+    nc = lax.axis_size("c")
+    width = hidden.shape[1]
+    ahead = [(i, (i + 1) % nz) for i in range(nz)]
+    behind = [(i, (i - 1) % nz) for i in range(nz)]
+    across = [(i, (i + 1) % nc) for i in range(nc)]
+    full = jnp.zeros((hidden.shape[0], width * nz * nc), hidden.dtype)
+
+    def place(buf, piece, chip, core):
+        slot = (chip * nc + core) * width
+        return lax.dynamic_update_slice(buf, piece, (0, slot))
+
+    def share(buf, piece, chip):
+        buf = place(buf, piece, chip, c)
+        if nc > 1:
+            other = lax.ppermute(piece, "c", across)
+            buf = place(buf, other, chip, (c + 1) % nc)
+        return buf
+
+    full = share(full, hidden, z)
+    fwd = hidden
+    bwd = hidden
+    for step in range(1, nz // 2 + 1):
+        fwd = lax.ppermute(fwd, "z", ahead)
+        if step <= (nz - 1) // 2:
+            bwd = lax.ppermute(bwd, "z", behind)
+        full = share(full, fwd, (z - step) % nz)
+        if step <= (nz - 1) // 2:
+            full = share(full, bwd, (z + step) % nz)
+    return full
+
+
 def local(hidden, head, targets, live, prior_lse, prior_mean, prior_target, seq_lengths):
     rows_here = hidden.shape[0]
     cols_here = head.shape[1]
@@ -28,7 +63,7 @@
     which = lax.axis_index(VOCAB_AXES)
     block_first = VOCAB - cols_here * spread
     first_col = block_first + which * cols_here
-    gathered = lax.all_gather(hidden, VOCAB_AXES, axis=1, tiled=True)
+    gathered = gather_hidden(hidden)
     logits = jnp.dot(
         gathered,
         lax.all_gather(head, ROW_AXES, axis=0, tiled=True),

time: 229 us -> 180 us (0.79)
  the two profiles are of different devices: /device:TPU:1 before, /device:TPU:2 now
where the time goes in v3:
time: 180 us; the launch traced here: 179 us
  waiting for transfers between devices  46.9 us (26%)
  starting transfers between devices  45.2 us (25%)
  blocking collectives  43.4 us (24%)
  local copies, waits for them, and re-layouts  18.7 us (10%)
  between operations  14.6 us (8%)
  matrix products  8 us (4%)
  other arithmetic  2.36 us (1%)
    all_gather x1, waiting for transfers between devices, local(): lax.all_gather(head, ROW_AXES, axis=0, tiled=True)  33.5 us
    psum x2, blocking collectives, local(): sums = lax.psum(lax.psum(partial_sums, 'x'), 'y')  25.1 us
    ppermute x3, starting transfers between devices, gather_hidden(): bwd = lax.ppermute(bwd, 'z', behind)  18.9 us
    all_gather x1, blocking collectives, local(): every = lax.all_gather(stats, VOCAB_AXES, axis=0, tiled=False)  18.3 us
    ppermute x8, starting transfers between devices, share(): other = lax.ppermute(piece, 'c', across)  16.3 us
    dynamic_update_slice x16, local copies, waits for them, and re-layouts, place(): return lax.dynamic_update_slice(buf, piece, (0, slot))  13.1 us
    ppermute x4, waiting for transfers between devices, gather_hidden(): fwd = lax.ppermute(fwd, 'z', ahead)  12.6 us
    ppermute x4, starting transfers between devices, gather_hidden(): fwd = lax.ppermute(fwd, 'z', ahead)  10 us
  transfers between devices with their start and end apart: 16, of which 5 were waited for; matrix products, arithmetic and copies ran while one was open for 10% of the time, Pallas kernels for 0%

profile of v3, /device:TPU:2, one launch (start us, length us, event | category | flops | bytes accessed | tf_op | source)
XLA Modules:
  0.0 179.1 jit_solution(7350973113880770912)
XLA Ops:
  7.2 0.7 all-gather.4.cloned.1.call-update
  7.9 4.3 %collective-permute-start.1 = (bf16[384,512]{1,0:T(8,128)(2,1)}, bf16[384,512]{1,0:T(8,128)(2,1)S(1)}, u32[]{:S(2)}, u32[]{:S(2)}) collective-permute-start(bf16[384,512]{1,0:T(8,128)(2,1)} %param.8), channel_id=1, source_target_pairs={{0,2},{2,4},{4,6},{6,8},{8,10},{10,12},{12,14},{14,0},{1,3},{3,5},... | collective-permute-start | bytes 1179656 | tf_op jit(solution)/shard_map/ppermute | solution.py:50
  12.2 8.6 %collective-permute-start.3 = (bf16[384,512]{1,0:T(8,128)(2,1)}, bf16[384,512]{1,0:T(8,128)(2,1)S(1)}, u32[]{:S(2)}, u32[]{:S(2)}) collective-permute-start(bf16[384,512]{1,0:T(8,128)(2,1)} %param.8), channel_id=1, source_target_pairs={{0,14},{2,0},{4,2},{6,4},{8,6},{10,8},{12,10},{14,12},{1,15},{3,1}... | collective-permute-start | bytes 1179656 | tf_op jit(solution)/shard_map/ppermute | solution.py:52
  20.8 1.9 %collective-permute-start = (bf16[384,512]{1,0:T(8,128)(2,1)}, bf16[384,512]{1,0:T(8,128)(2,1)S(1)}, u32[]{:S(2)}, u32[]{:S(2)}) collective-permute-start(bf16[384,512]{1,0:T(8,128)(2,1)} %param.8), channel_id=1, source_target_pairs={{0,1},{1,0},{2,3},{3,2},{4,5},{5,4},{6,7},{7,6},{8,9},{9,8},{10,11... | collective-permute-start | bytes 1179656 | tf_op jit(solution)/shard_map/ppermute | solution.py:42
  22.7 0.7 broadcast_subtract_fusion
  23.4 0.7 copy.22
  24.3 3.8 %collective-permute-done.1 = bf16[384,512]{1,0:T(8,128)(2,1)S(1)} collective-permute-done((bf16[384,512]{1,0:T(8,128)(2,1)}, bf16[384,512]{1,0:T(8,128)(2,1)S(1)}, u32[]{:S(2)}, u32[]{:S(2)}) %collective-permute-start.1) | collective-permute-done | bytes 393248 | tf_op jit(solution)/shard_map/ppermute | solution.py:50
  28.2 1.9 %collective-permute-start.2 = (bf16[384,512]{1,0:T(8,128)(2,1)S(1)}, bf16[384,512]{1,0:T(8,128)(2,1)S(1)}, u32[]{:S(2)}, u32[]{:S(2)}) collective-permute-start(bf16[384,512]{1,0:T(8,128)(2,1)S(1)} %collective-permute-done.1), channel_id=1, source_target_pairs={{0,1},{1,0},{2,3},{3,2},{4,5},{5,4},{6,7},{7,6},{8,9},{9,8},{10,11... | collective-permute-start | bytes 1179656 | tf_op jit(solution)/shard_map/ppermute | solution.py:42
  30.1 1.9 %collective-permute-start.5 = (bf16[384,512]{1,0:T(8,128)(2,1)S(1)}, bf16[384,512]{1,0:T(8,128)(2,1)S(1)}, u32[]{:S(2)}, u32[]{:S(2)}) collective-permute-start(bf16[384,512]{1,0:T(8,128)(2,1)S(1)} %collective-permute-done.1), channel_id=1, source_target_pairs={{0,2},{2,4},{4,6},{6,8},{8,10},{10,12},{12,14},{14,0},{1,3},{3,5},... | collective-permute-start | bytes 1179656 | tf_op jit(solution)/shard_map/ppermute | solution.py:50
  32.0 5.1 %collective-permute-start.7 = (bf16[384,512]{1,0:T(8,128)(2,1)S(1)}, bf16[384,512]{1,0:T(8,128)(2,1)S(1)}, u32[]{:S(2)}, u32[]{:S(2)}) collective-permute-start(bf16[384,512]{1,0:T(8,128)(2,1)S(1)} %collective-permute-done.3), channel_id=1, source_target_pairs={{0,14},{2,0},{4,2},{6,4},{8,6},{10,8},{12,10},{14,12},{1,15},{3,1}... | collective-permute-start | bytes 1179656 | tf_op jit(solution)/shard_map/ppermute | solution.py:52
  37.5 3.5 %broadcast_in_dim.4 = bf16[384,8192]{1,0:T(8,128)(2,1)} broadcast(bf16[]{:T(256)} %constant.94.clone.1), dimensions={} | broadcast | bytes 6291458 | tf_op jit(solution)/shard_map/broadcast_in_dim | solution.py:33
  40.9 0.9 constant_dynamic-update-slice_fusion.15
  41.8 1.9 %collective-permute-start.4 = (bf16[384,512]{1,0:T(8,128)(2,1)S(1)}, bf16[384,512]{1,0:T(8,128)(2,1)S(1)}, u32[]{:S(2)}, u32[]{:S(2)}) collective-permute-start(bf16[384,512]{1,0:T(8,128)(2,1)S(1)} %collective-permute-done.3), channel_id=1, source_target_pairs={{0,1},{1,0},{2,3},{3,2},{4,5},{5,4},{6,7},{7,6},{8,9},{9,8},{10,11... | collective-permute-start | bytes 1179656 | tf_op jit(solution)/shard_map/ppermute | solution.py:42
  43.7 0.9 constant_dynamic-update-slice_fusion.14
  44.6 0.8 constant_dynamic-update-slice_fusion.13
  45.4 2.4 %collective-permute-start.6 = (bf16[384,512]{1,0:T(8,128)(2,1)S(1)}, bf16[384,512]{1,0:T(8,128)(2,1)S(1)}, u32[]{:S(2)}, u32[]{:S(2)}) collective-permute-start(bf16[384,512]{1,0:T(8,128)(2,1)S(1)} %collective-permute-done.5), channel_id=1, source_target_pairs={{0,1},{1,0},{2,3},{3,2},{4,5},{5,4},{6,7},{7,6},{8,9},{9,8},{10,11... | collective-permute-start | bytes 1179656 | tf_op jit(solution)/shard_map/ppermute | solution.py:42
  47.8 1.9 %collective-permute-start.9 = (bf16[384,512]{1,0:T(8,128)(2,1)S(1)}, bf16[384,512]{1,0:T(8,128)(2,1)S(1)}, u32[]{:S(2)}, u32[]{:S(2)}) collective-permute-start(bf16[384,512]{1,0:T(8,128)(2,1)S(1)} %collective-permute-done.5), channel_id=1, source_target_pairs={{0,2},{2,4},{4,6},{6,8},{8,10},{10,12},{12,14},{14,0},{1,3},{3,5},... | collective-permute-start | bytes 1179656 | tf_op jit(solution)/shard_map/ppermute | solution.py:50
  49.7 1.9 %collective-permute-start.8 = (bf16[384,512]{1,0:T(8,128)(2,1)S(1)}, bf16[384,512]{1,0:T(8,128)(2,1)S(1)}, u32[]{:S(2)}, u32[]{:S(2)}) collective-permute-start(bf16[384,512]{1,0:T(8,128)(2,1)S(1)} %collective-permute-done.7), channel_id=1, source_target_pairs={{0,1},{1,0},{2,3},{3,2},{4,5},{5,4},{6,7},{7,6},{8,9},{9,8},{10,11... | collective-permute-start | bytes 1179656 | tf_op jit(solution)/shard_map/ppermute | solution.py:42
  51.7 5.1 %collective-permute-start.11 = (bf16[384,512]{1,0:T(8,128)(2,1)S(1)}, bf16[384,512]{1,0:T(8,128)(2,1)S(1)}, u32[]{:S(2)}, u32[]{:S(2)}) collective-permute-start(bf16[384,512]{1,0:T(8,128)(2,1)S(1)} %collective-permute-done.7), channel_id=1, source_target_pairs={{0,14},{2,0},{4,2},{6,4},{8,6},{10,8},{12,10},{14,12},{1,15},{3,1}... | collective-permute-start | bytes 1179656 | tf_op jit(solution)/shard_map/ppermute | solution.py:52
  56.8 0.8 constant_dynamic-update-slice_fusion.12
  57.6 0.8 constant_dynamic-update-slice_fusion.11
  58.5 0.8 constant_dynamic-update-slice_fusion.10
  59.3 0.8 constant_dynamic-update-slice_fusion.9
  60.1 1.8 %collective-permute-done.9 = bf16[384,512]{1,0:T(8,128)(2,1)S(1)} collective-permute-done((bf16[384,512]{1,0:T(8,128)(2,1)S(1)}, bf16[384,512]{1,0:T(8,128)(2,1)S(1)}, u32[]{:S(2)}, u32[]{:S(2)}) %collective-permute-start.9) | collective-permute-done | bytes 393248 | tf_op jit(solution)/shard_map/ppermute | solution.py:50
  61.9 1.9 %collective-permute-start.10 = (bf16[384,512]{1,0:T(8,128)(2,1)S(1)}, bf16[384,512]{1,0:T(8,128)(2,1)S(1)}, u32[]{:S(2)}, u32[]{:S(2)}) collective-permute-start(bf16[384,512]{1,0:T(8,128)(2,1)S(1)} %collective-permute-done.9), channel_id=1, source_target_pairs={{0,1},{1,0},{2,3},{3,2},{4,5},{5,4},{6,7},{7,6},{8,9},{9,8},{10,11... | collective-permute-start | bytes 1179656 | tf_op jit(solution)/shard_map/ppermute | solution.py:42
  63.8 1.9 %collective-permute-start.13 = (bf16[384,512]{1,0:T(8,128)(2,1)S(1)}, bf16[384,512]{1,0:T(8,128)(2,1)S(1)}, u32[]{:S(2)}, u32[]{:S(2)}) collective-permute-start(bf16[384,512]{1,0:T(8,128)(2,1)S(1)} %collective-permute-done.9), channel_id=1, source_target_pairs={{0,2},{2,4},{4,6},{6,8},{8,10},{10,12},{12,14},{14,0},{1,3},{3,5},... | collective-permute-start | bytes 1179656 | tf_op jit(solution)/shard_map/ppermute | solution.py:50
  65.8 2.4 %collective-permute-start.12 = (bf16[384,512]{1,0:T(8,128)(2,1)S(1)}, bf16[384,512]{1,0:T(8,128)(2,1)S(1)}, u32[]{:S(2)}, u32[]{:S(2)}) collective-permute-start(bf16[384,512]{1,0:T(8,128)(2,1)S(1)} %collective-permute-done.11), channel_id=1, source_target_pairs={{0,1},{1,0},{2,3},{3,2},{4,5},{5,4},{6,7},{7,6},{8,9},{9,8},{10,11... | collective-permute-start | bytes 1179656 | tf_op jit(solution)/shard_map/ppermute | solution.py:42
  68.2 0.8 constant_dynamic-update-slice_fusion.8
  69.0 0.8 constant_dynamic-update-slice_fusion.7
  69.8 0.8 constant_dynamic-update-slice_fusion.6
  70.7 0.8 constant_dynamic-update-slice_fusion.5
  71.5 7.0 %collective-permute-done.13 = bf16[384,512]{1,0:T(8,128)(2,1)S(1)} collective-permute-done((bf16[384,512]{1,0:T(8,128)(2,1)S(1)}, bf16[384,512]{1,0:T(8,128)(2,1)S(1)}, u32[]{:S(2)}, u32[]{:S(2)}) %collective-permute-start.13) | collective-permute-done | bytes 393248 | tf_op jit(solution)/shard_map/ppermute | solution.py:50
  78.5 1.9 %collective-permute-start.14 = (bf16[384,512]{1,0:T(8,128)(2,1)S(1)}, bf16[384,512]{1,0:T(8,128)(2,1)S(1)}, u32[]{:S(2)}, u32[]{:S(2)}) collective-permute-start(bf16[384,512]{1,0:T(8,128)(2,1)S(1)} %collective-permute-done.13), channel_id=1, source_target_pairs={{0,1},{1,0},{2,3},{3,2},{4,5},{5,4},{6,7},{7,6},{8,9},{9,8},{10,11... | collective-permute-start | bytes 1179656 | tf_op jit(solution)/shard_map/ppermute | solution.py:42
  80.4 0.8 constant_dynamic-update-slice_fusion.4
  81.2 0.8 constant_dynamic-update-slice_fusion.3
  82.0 0.8 constant_dynamic-update-slice_fusion.2
  82.8 0.8 constant_dynamic-update-slice_fusion.1
  83.6 0.8 constant_dynamic-update-slice_fusion
  84.4 33.5 %all-gather.4.cloned.1.call-done = bf16[8192,512]{1,0:T(8,128)(2,1)} async-done(((bf16[256,512]{1,0:T(8,128)(2,1)}), bf16[8192,512]{1,0:T(8,128)(2,1)}) %all-gather.4.cloned.1.call-update) | async-done | bytes 8388624 | tf_op jit(solution)/shard_map/all_gather | solution.py:69
  117.9 8.0 %fusion.7 = (f32[384]{0:T(512)S(1)}, f32[384,512]{1,0:T(8,128)S(1)}) fusion(bf16[384,8192]{1,0:T(8,128)(2,1)} %constant_dynamic-update-slice_fusion, bf16[8192,512]{1,0:T(8,128)(2,1)} %all-gather.4.cloned.1.call-done), kind=kOutput, calls=%fused_computation.46 | convolution fusion | flops 3221421568 | bytes 15468032 | tf_op jit(solution)/shard_map/dot_general | solution.py:67
  125.9 0.5 fusion
  126.5 18.3 %all-gather.1 = f32[16,4,384]{2,1,0:T(4,128)S(1)} all-gather(f32[1,4,384]{2,1,0:T(4,128)S(1)} %maximum_bitcast_fusion), channel_id=2, replica_groups=mesh['y'=8,'x'=4,'z'=8,'c'=2] {'z','c'}, dimensions={0}, use_global_device_ids=true | all-gather | bytes 104448 | tf_op jit(solution)/shard_map/all_gather | solution.py:81
  145.1 9.5 %psum.14 = f32[32]{0:T(128)S(1)} all-reduce(f32[32]{0:T(128)S(1)} %select_reduce_fusion.1), channel_id=1, replica_groups=mesh['y'=8,'x'=4,'z'=8,'c'=2] {'x'}, use_global_device_ids=true, to_apply=%region_11.12 | all-reduce | flops 32 | bytes 256 | tf_op jit(solution)/shard_map/psum | solution.py:103
  154.7 15.6 %psum.15 = f32[32]{0:T(128)S(1)} all-reduce(f32[32]{0:T(128)S(1)} %psum.14), channel_id=1, replica_groups=mesh['y'=8,'x'=4,'z'=8,'c'=2] {'y'}, use_global_device_ids=true, to_apply=%region_12.13 | all-reduce | flops 32 | bytes 256 | tf_op jit(solution)/shard_map/psum | solution.py:103
  170.3 0.1 reduce_sum.89
  170.6 0.5 sub.73
  171.1 0.6 dynamic_slice.6
  171.7 0.6 dynamic_slice.7
  (45 shorter events, 0.9 us)
Async XLA Ops:
  7.2 33.8 %copy-start = (bf16[384,512]{1,0:T(8,128)(2,1)S(1)}, bf16[384,512]{1,0:T(8,128)(2,1)}, u32[]{:S(2)}) copy-start(bf16[384,512]{1,0:T(8,128)(2,1)} %param.8) | copy-start | bytes 1179652
  7.2 110.8 %all-gather.4.cloned.1.call-start = ((), (), s32[]{:S(2)}) async-start(), calls=%async_computation | async-start | bytes 8650752 | tf_op jit(solution)/shard_map/all_gather | solution.py:69
  7.9 20.3 %collective-permute-start.1 = (bf16[384,512]{1,0:T(8,128)(2,1)}, bf16[384,512]{1,0:T(8,128)(2,1)S(1)}, u32[]{:S(2)}, u32[]{:S(2)}) collective-permute-start(bf16[384,512]{1,0:T(8,128)(2,1)} %param.8), channel_id=1, source_target_pairs={{0,2},{2,4},{4,6},{6,8},{8,10},{10,12},{12,14},{14,0},{1,3},{3,5},... | collective-permute-start | bytes 1179656 | tf_op jit(solution)/shard_map/ppermute | solution.py:50
  12.2 19.8 %collective-permute-start.3 = (bf16[384,512]{1,0:T(8,128)(2,1)}, bf16[384,512]{1,0:T(8,128)(2,1)S(1)}, u32[]{:S(2)}, u32[]{:S(2)}) collective-permute-start(bf16[384,512]{1,0:T(8,128)(2,1)} %param.8), channel_id=1, source_target_pairs={{0,14},{2,0},{4,2},{6,4},{8,6},{10,8},{12,10},{14,12},{1,15},{3,1}... | collective-permute-start | bytes 1179656 | tf_op jit(solution)/shard_map/ppermute | solution.py:52
  20.8 22.9 %collective-permute-start = (bf16[384,512]{1,0:T(8,128)(2,1)}, bf16[384,512]{1,0:T(8,128)(2,1)S(1)}, u32[]{:S(2)}, u32[]{:S(2)}) collective-permute-start(bf16[384,512]{1,0:T(8,128)(2,1)} %param.8), channel_id=1, source_target_pairs={{0,1},{1,0},{2,3},{3,2},{4,5},{5,4},{6,7},{7,6},{8,9},{9,8},{10,11... | collective-permute-start | bytes 1179656 | tf_op jit(solution)/shard_map/ppermute | solution.py:42
  28.2 23.5 %collective-permute-start.2 = (bf16[384,512]{1,0:T(8,128)(2,1)S(1)}, bf16[384,512]{1,0:T(8,128)(2,1)S(1)}, u32[]{:S(2)}, u32[]{:S(2)}) collective-permute-start(bf16[384,512]{1,0:T(8,128)(2,1)S(1)} %collective-permute-done.1), channel_id=1, source_target_pairs={{0,1},{1,0},{2,3},{3,2},{4,5},{5,4},{6,7},{7,6},{8,9},{9,8},{10,11... | collective-permute-start | bytes 1179656 | tf_op jit(solution)/shard_map/ppermute | solution.py:42
  30.1 15.3 %collective-permute-start.5 = (bf16[384,512]{1,0:T(8,128)(2,1)S(1)}, bf16[384,512]{1,0:T(8,128)(2,1)S(1)}, u32[]{:S(2)}, u32[]{:S(2)}) collective-permute-start(bf16[384,512]{1,0:T(8,128)(2,1)S(1)} %collective-permute-done.1), channel_id=1, source_target_pairs={{0,2},{2,4},{4,6},{6,8},{8,10},{10,12},{12,14},{14,0},{1,3},{3,5},... | collective-permute-start | bytes 1179656 | tf_op jit(solution)/shard_map/ppermute | solution.py:50
  32.0 17.7 %collective-permute-start.7 = (bf16[384,512]{1,0:T(8,128)(2,1)S(1)}, bf16[384,512]{1,0:T(8,128)(2,1)S(1)}, u32[]{:S(2)}, u32[]{:S(2)}) collective-permute-start(bf16[384,512]{1,0:T(8,128)(2,1)S(1)} %collective-permute-done.3), channel_id=1, source_target_pairs={{0,14},{2,0},{4,2},{6,4},{8,6},{10,8},{12,10},{14,12},{1,15},{3,1}... | collective-permute-start | bytes 1179656 | tf_op jit(solution)/shard_map/ppermute | solution.py:52
  41.8 16.7 %collective-permute-start.4 = (bf16[384,512]{1,0:T(8,128)(2,1)S(1)}, bf16[384,512]{1,0:T(8,128)(2,1)S(1)}, u32[]{:S(2)}, u32[]{:S(2)}) collective-permute-start(bf16[384,512]{1,0:T(8,128)(2,1)S(1)} %collective-permute-done.3), channel_id=1, source_target_pairs={{0,1},{1,0},{2,3},{3,2},{4,5},{5,4},{6,7},{7,6},{8,9},{9,8},{10,11... | collective-permute-start | bytes 1179656 | tf_op jit(solution)/shard_map/ppermute | solution.py:42
  45.4 22.8 %collective-permute-start.6 = (bf16[384,512]{1,0:T(8,128)(2,1)S(1)}, bf16[384,512]{1,0:T(8,128)(2,1)S(1)}, u32[]{:S(2)}, u32[]{:S(2)}) collective-permute-start(bf16[384,512]{1,0:T(8,128)(2,1)S(1)} %collective-permute-done.5), channel_id=1, source_target_pairs={{0,1},{1,0},{2,3},{3,2},{4,5},{5,4},{6,7},{7,6},{8,9},{9,8},{10,11... | collective-permute-start | bytes 1179656 | tf_op jit(solution)/shard_map/ppermute | solution.py:42
  47.8 14.1 %collective-permute-start.9 = (bf16[384,512]{1,0:T(8,128)(2,1)S(1)}, bf16[384,512]{1,0:T(8,128)(2,1)S(1)}, u32[]{:S(2)}, u32[]{:S(2)}) collective-permute-start(bf16[384,512]{1,0:T(8,128)(2,1)S(1)} %collective-permute-done.5), channel_id=1, source_target_pairs={{0,2},{2,4},{4,6},{6,8},{8,10},{10,12},{12,14},{14,0},{1,3},{3,5},... | collective-permute-start | bytes 1179656 | tf_op jit(solution)/shard_map/ppermute | solution.py:50
  49.7 20.1 %collective-permute-start.8 = (bf16[384,512]{1,0:T(8,128)(2,1)S(1)}, bf16[384,512]{1,0:T(8,128)(2,1)S(1)}, u32[]{:S(2)}, u32[]{:S(2)}) collective-permute-start(bf16[384,512]{1,0:T(8,128)(2,1)S(1)} %collective-permute-done.7), channel_id=1, source_target_pairs={{0,1},{1,0},{2,3},{3,2},{4,5},{5,4},{6,7},{7,6},{8,9},{9,8},{10,11... | collective-permute-start | bytes 1179656 | tf_op jit(solution)/shard_map/ppermute | solution.py:42
  51.7 14.2 %collective-permute-start.11 = (bf16[384,512]{1,0:T(8,128)(2,1)S(1)}, bf16[384,512]{1,0:T(8,128)(2,1)S(1)}, u32[]{:S(2)}, u32[]{:S(2)}) collective-permute-start(bf16[384,512]{1,0:T(8,128)(2,1)S(1)} %collective-permute-done.7), channel_id=1, source_target_pairs={{0,14},{2,0},{4,2},{6,4},{8,6},{10,8},{12,10},{14,12},{1,15},{3,1}... | collective-permute-start | bytes 1179656 | tf_op jit(solution)/shard_map/ppermute | solution.py:52
  61.9 18.5 %collective-permute-start.10 = (bf16[384,512]{1,0:T(8,128)(2,1)S(1)}, bf16[384,512]{1,0:T(8,128)(2,1)S(1)}, u32[]{:S(2)}, u32[]{:S(2)}) collective-permute-start(bf16[384,512]{1,0:T(8,128)(2,1)S(1)} %collective-permute-done.9), channel_id=1, source_target_pairs={{0,1},{1,0},{2,3},{3,2},{4,5},{5,4},{6,7},{7,6},{8,9},{9,8},{10,11... | collective-permute-start | bytes 1179656 | tf_op jit(solution)/shard_map/ppermute | solution.py:42
  63.8 14.6 %collective-permute-start.13 = (bf16[384,512]{1,0:T(8,128)(2,1)S(1)}, bf16[384,512]{1,0:T(8,128)(2,1)S(1)}, u32[]{:S(2)}, u32[]{:S(2)}) collective-permute-start(bf16[384,512]{1,0:T(8,128)(2,1)S(1)} %collective-permute-done.9), channel_id=1, source_target_pairs={{0,2},{2,4},{4,6},{6,8},{8,10},{10,12},{12,14},{14,0},{1,3},{3,5},... | collective-permute-start | bytes 1179656 | tf_op jit(solution)/shard_map/ppermute | solution.py:50
  65.8 16.2 %collective-permute-start.12 = (bf16[384,512]{1,0:T(8,128)(2,1)S(1)}, bf16[384,512]{1,0:T(8,128)(2,1)S(1)}, u32[]{:S(2)}, u32[]{:S(2)}) collective-permute-start(bf16[384,512]{1,0:T(8,128)(2,1)S(1)} %collective-permute-done.11), channel_id=1, source_target_pairs={{0,1},{1,0},{2,3},{3,2},{4,5},{5,4},{6,7},{7,6},{8,9},{9,8},{10,11... | collective-permute-start | bytes 1179656 | tf_op jit(solution)/shard_map/ppermute | solution.py:42
  78.5 5.1 %collective-permute-start.14 = (bf16[384,512]{1,0:T(8,128)(2,1)S(1)}, bf16[384,512]{1,0:T(8,128)(2,1)S(1)}, u32[]{:S(2)}, u32[]{:S(2)}) collective-permute-start(bf16[384,512]{1,0:T(8,128)(2,1)S(1)} %collective-permute-done.13), channel_id=1, source_target_pairs={{0,1},{1,0},{2,3},{3,2},{4,5},{5,4},{6,7},{7,6},{8,9},{9,8},{10,11... | collective-permute-start | bytes 1179656 | tf_op jit(solution)/shard_map/ppermute | solution.py:42
  84.4 60.5 %copy-start.1 = (s32[384]{0:T(512)S(1)}, s32[384]{0:T(512)}, u32[]{:S(2)}) copy-start(s32[384]{0:T(512)} %param.10) | copy-start | bytes 4612
  84.4 60.5 %copy-start.2 = (f32[384]{0:T(512)S(1)}, f32[384]{0:T(512)}, u32[]{:S(2)}) copy-start(f32[384]{0:T(512)} %param.13) | copy-start | bytes 4612
  84.4 60.6 %copy-start.3 = (s32[384]{0:T(512)S(1)}, s32[384]{0:T(512)}, u32[]{:S(2)}) copy-start(s32[384]{0:T(512)} %param.11) | copy-start | bytes 4612
  84.4 60.6 %copy-start.4 = (f32[384]{0:T(512)S(1)}, f32[384]{0:T(512)}, u32[]{:S(2)}) copy-start(f32[384]{0:T(512)} %param.12) | copy-start | bytes 4612
  84.4 60.6 %copy-start.5 = (f32[384]{0:T(512)S(1)}, f32[384]{0:T(512)}, u32[]{:S(2)}) copy-start(f32[384]{0:T(512)} %param.14) | copy-start | bytes 4612
  84.4 85.8 %copy-start.6 = (s32[32]{0:T(128)S(1)}, s32[32]{0:T(128)}, u32[]{:S(2)}) copy-start(s32[32]{0:T(128)} %param.15) | copy-start | bytes 388
Sparse Core Ops, SparseCore 0:
  11.2 106.7 all-gather.3

commit v4 on v3

--- a/solution.py
+++ b/solution.py
@@ -56,6 +56,40 @@
     return full
 
 
+def ring_gather(block, axis, place, buf):
+    n = lax.axis_size(axis)
+    me = lax.axis_index(axis)
+    ahead = [(i, (i + 1) % n) for i in range(n)]
+    behind = [(i, (i - 1) % n) for i in range(n)]
+    buf = place(buf, block, me)
+    fwd = block
+    bwd = block
+    for step in range(1, n // 2 + 1):
+        fwd = lax.ppermute(fwd, axis, ahead)
+        if step <= (n - 1) // 2:
+            bwd = lax.ppermute(bwd, axis, behind)
+        buf = place(buf, fwd, (me - step) % n)
+        if step <= (n - 1) // 2:
+            buf = place(buf, bwd, (me + step) % n)
+    return buf
+
+
+def gather_head_part(part):
+    depth = part.shape[0]
+    nx = lax.axis_size("x")
+    ny = lax.axis_size("y")
+
+    def put_x(buf, piece, index):
+        return lax.dynamic_update_slice(buf, piece, (index * depth, 0))
+
+    strip = ring_gather(part, "x", put_x, jnp.zeros((depth * nx, part.shape[1]), part.dtype))
+
+    def put_y(buf, piece, index):
+        return lax.dynamic_update_slice(buf, piece, (index * depth * nx, 0))
+
+    return ring_gather(strip, "y", put_y, jnp.zeros((depth * nx * ny, part.shape[1]), part.dtype))
+
+
 def local(hidden, head, targets, live, prior_lse, prior_mean, prior_target, seq_lengths):
     rows_here = hidden.shape[0]
     cols_here = head.shape[1]
@@ -64,10 +98,15 @@
     block_first = VOCAB - cols_here * spread
     first_col = block_first + which * cols_here
     gathered = gather_hidden(hidden)
-    logits = jnp.dot(
-        gathered,
-        lax.all_gather(head, ROW_AXES, axis=0, tiled=True),
-        preferred_element_type=jnp.float32,
+    split = (cols_here // 2) // 128 * 128
+    head_sc = lax.all_gather(head[:, :split], ROW_AXES, axis=0, tiled=True)
+    head_ring = gather_head_part(head[:, split:])
+    logits = jnp.concatenate(
+        [
+            jnp.dot(gathered, head_sc, preferred_element_type=jnp.float32),
+            jnp.dot(gathered, head_ring, preferred_element_type=jnp.float32),
+        ],
+        axis=1,
     )
     row_peak = jnp.max(logits, axis=1)
     weights = jnp.exp(logits - row_peak[:, None])

time: 180 us -> 198 us (1.10)
  the two profiles are of different devices: /device:TPU:2 before, /device:TPU:8 now
where the time goes in v4:
time: 198 us; the launch traced here: 197 us
  starting transfers between devices  77 us (39%)
  blocking collectives  42.8 us (22%)
  waiting for transfers between devices  28.2 us (14%)
  local copies, waits for them, and re-layouts  20.6 us (10%)
  between operations  15 us (8%)
  matrix products  11.7 us (6%)
  other arithmetic  2.15 us (1%)
    psum x2, blocking collectives, local(): sums = lax.psum(lax.psum(partial_sums, 'x'), 'y')  26.5 us
    ppermute x6, starting transfers between devices, ring_gather(): fwd = lax.ppermute(fwd, axis, ahead)  22.1 us
    ppermute x3, starting transfers between devices, gather_hidden(): bwd = lax.ppermute(bwd, 'z', behind)  18.5 us
    ppermute x8, starting transfers between devices, share(): other = lax.ppermute(piece, 'c', across)  16.4 us
    all_gather x1, blocking collectives, local(): every = lax.all_gather(stats, VOCAB_AXES, axis=0, tiled=False)  16.3 us
    ppermute x4, waiting for transfers between devices, ring_gather(): bwd = lax.ppermute(bwd, axis, behind)  15.1 us
    dynamic_update_slice x16, local copies, waits for them, and re-layouts, place(): return lax.dynamic_update_slice(buf, piece, (0, slot))  13.3 us
    ppermute x6, waiting for transfers between devices, ring_gather(): fwd = lax.ppermute(fwd, axis, ahead)  13 us
  transfers between devices with their start and end apart: 26, of which 4 were waited for; matrix products, arithmetic and copies ran while one was open for 12% of the time, Pallas kernels for 0%

profile of v4, /device:TPU:8, one launch (start us, length us, event | category | flops | bytes accessed | tf_op | source)
XLA Modules:
  0.0 197.3 jit_solution(12449575186856411913)
XLA Ops:
  7.3 1.7 fusion.6
  9.0 1.9 collective-permute-start
  10.9 4.3 %collective-permute-start.1 = (bf16[384,512]{1,0:T(8,128)(2,1)}, bf16[384,512]{1,0:T(8,128)(2,1)S(1)}, u32[]{:S(2)}, u32[]{:S(2)}) collective-permute-start(bf16[384,512]{1,0:T(8,128)(2,1)} %param.8), channel_id=1, source_target_pairs={{0,2},{2,4},{4,6},{6,8},{8,10},{10,12},{12,14},{14,0},{1,3},{3,5},... | collective-permute-start | bytes 1179656 | tf_op jit(solution)/shard_map/ppermute | solution.py:50
  15.2 8.6 %collective-permute-start.3 = (bf16[384,512]{1,0:T(8,128)(2,1)}, bf16[384,512]{1,0:T(8,128)(2,1)S(1)}, u32[]{:S(2)}, u32[]{:S(2)}) collective-permute-start(bf16[384,512]{1,0:T(8,128)(2,1)} %param.8), channel_id=1, source_target_pairs={{0,14},{2,0},{4,2},{6,4},{8,6},{10,8},{12,10},{14,12},{1,15},{3,1}... | collective-permute-start | bytes 1179656 | tf_op jit(solution)/shard_map/ppermute | solution.py:52
  23.8 3.4 %collective-permute-start.15 = (bf16[256,256]{1,0:T(8,128)(2,1)S(1)}, bf16[256,256]{1,0:T(8,128)(2,1)S(1)}, u32[]{:S(2)}, u32[]{:S(2)}) collective-permute-start(bf16[256,256]{1,0:T(8,128)(2,1)S(1)} %get-tuple-element.12), channel_id=1, source_target_pairs={{0,16},{16,32},{32,48},{48,0},{1,17},{17,33},{33,49},{49,1},{2,18}... | collective-permute-start | bytes 393224 | tf_op jit(solution)/shard_map/ppermute | solution.py:68
  27.2 3.7 %collective-permute-start.16 = (bf16[256,256]{1,0:T(8,128)(2,1)S(1)}, bf16[256,256]{1,0:T(8,128)(2,1)S(1)}, u32[]{:S(2)}, u32[]{:S(2)}) collective-permute-start(bf16[256,256]{1,0:T(8,128)(2,1)S(1)} %get-tuple-element.12), channel_id=1, source_target_pairs={{0,48},{16,0},{32,16},{48,32},{1,49},{17,1},{33,17},{49,33},{2,50}... | collective-permute-start | bytes 393224 | tf_op jit(solution)/shard_map/ppermute | solution.py:70
  31.5 3.4 %broadcast_in_dim.8 = bf16[384,8192]{1,0:T(8,128)(2,1)} broadcast(bf16[]{:T(256)} %constant.155.clone.1), dimensions={} | broadcast | bytes 6291458 | tf_op jit(solution)/shard_map/broadcast_in_dim | solution.py:33
  35.0 0.8 constant_dynamic-update-slice_fusion.27
  35.8 2.2 %collective-permute-start.17 = (bf16[256,256]{1,0:T(8,128)(2,1)S(1)}, bf16[256,256]{1,0:T(8,128)(2,1)S(1)}, u32[]{:S(2)}, u32[]{:S(2)}) collective-permute-start(bf16[256,256]{1,0:T(8,128)(2,1)S(1)} %collective-permute-done.15), channel_id=1, source_target_pairs={{0,16},{16,32},{32,48},{48,0},{1,17},{17,33},{33,49},{49,1},{2,18}... | collective-permute-start | bytes 393224 | tf_op jit(solution)/shard_map/ppermute | solution.py:68
  38.0 6.1 %collective-permute-done.17 = bf16[256,256]{1,0:T(8,128)(2,1)S(1)} collective-permute-done((bf16[256,256]{1,0:T(8,128)(2,1)S(1)}, bf16[256,256]{1,0:T(8,128)(2,1)S(1)}, u32[]{:S(2)}, u32[]{:S(2)}) %collective-permute-start.17) | collective-permute-done | bytes 131104 | tf_op jit(solution)/shard_map/ppermute | solution.py:68
  44.2 3.7 %collective-permute-start.18 = (bf16[1024,256]{1,0:T(8,128)(2,1)S(1)}, bf16[1024,256]{1,0:T(8,128)(2,1)S(1)}, u32[]{:S(2)}, u32[]{:S(2)}) collective-permute-start(bf16[1024,256]{1,0:T(8,128)(2,1)S(1)} %constant_dynamic-update-slice_fusion.8), channel_id=1, source_target_pairs={{0,64},{64,128},{128,192},{192,256},{256,320},{320,384},{384,448},... | collective-permute-start | bytes 1572872 | tf_op jit(solution)/shard_map/ppermute | solution.py:68
  48.2 2.1 %collective-permute-start.19 = (bf16[1024,256]{1,0:T(8,128)(2,1)S(1)}, bf16[1024,256]{1,0:T(8,128)(2,1)S(1)}, u32[]{:S(2)}, u32[]{:S(2)}) collective-permute-start(bf16[1024,256]{1,0:T(8,128)(2,1)S(1)} %constant_dynamic-update-slice_fusion.8), channel_id=1, source_target_pairs={{0,448},{64,0},{128,64},{192,128},{256,192},{320,256},{384,320},{4... | collective-permute-start | bytes 1572872 | tf_op jit(solution)/shard_map/ppermute | solution.py:70
  50.8 1.9 collective-permute-start.5
  53.0 1.9 collective-permute-start.2
  55.0 5.1 %collective-permute-start.7 = (bf16[384,512]{1,0:T(8,128)(2,1)S(1)}, bf16[384,512]{1,0:T(8,128)(2,1)S(1)}, u32[]{:S(2)}, u32[]{:S(2)}) collective-permute-start(bf16[384,512]{1,0:T(8,128)(2,1)S(1)} %collective-permute-done.3), channel_id=1, source_target_pairs={{0,14},{2,0},{4,2},{6,4},{8,6},{10,8},{12,10},{14,12},{1,15},{3,1}... | collective-permute-start | bytes 1179656 | tf_op jit(solution)/shard_map/ppermute | solution.py:52
  60.1 0.9 constant_dynamic-update-slice_fusion.26
  61.0 0.8 constant_dynamic-update-slice_fusion.25
  61.8 2.1 %collective-permute-start.4 = (bf16[384,512]{1,0:T(8,128)(2,1)S(1)}, bf16[384,512]{1,0:T(8,128)(2,1)S(1)}, u32[]{:S(2)}, u32[]{:S(2)}) collective-permute-start(bf16[384,512]{1,0:T(8,128)(2,1)S(1)} %collective-permute-done.3), channel_id=1, source_target_pairs={{0,1},{1,0},{2,3},{3,2},{4,5},{5,4},{6,7},{7,6},{8,9},{9,8},{10,11... | collective-permute-start | bytes 1179656 | tf_op jit(solution)/shard_map/ppermute | solution.py:42
  63.9 3.9 %collective-permute-start.20 = (bf16[1024,256]{1,0:T(8,128)(2,1)S(1)}, bf16[1024,256]{1,0:T(8,128)(2,1)S(1)}, u32[]{:S(2)}, u32[]{:S(2)}) collective-permute-start(bf16[1024,256]{1,0:T(8,128)(2,1)S(1)} %collective-permute-done.18), channel_id=1, source_target_pairs={{0,64},{64,128},{128,192},{192,256},{256,320},{320,384},{384,448},... | collective-permute-start | bytes 1572872 | tf_op jit(solution)/shard_map/ppermute | solution.py:68
  67.8 1.9 collective-permute-start.6
  69.8 1.9 collective-permute-start.9
  71.7 2.4 %collective-permute-start.8 = (bf16[384,512]{1,0:T(8,128)(2,1)S(1)}, bf16[384,512]{1,0:T(8,128)(2,1)S(1)}, u32[]{:S(2)}, u32[]{:S(2)}) collective-permute-start(bf16[384,512]{1,0:T(8,128)(2,1)S(1)} %collective-permute-done.7), channel_id=1, source_target_pairs={{0,1},{1,0},{2,3},{3,2},{4,5},{5,4},{6,7},{7,6},{8,9},{9,8},{10,11... | collective-permute-start | bytes 1179656 | tf_op jit(solution)/shard_map/ppermute | solution.py:42
  75.0 0.9 constant_dynamic-update-slice_fusion.23
  75.8 4.8 %collective-permute-start.11 = (bf16[384,512]{1,0:T(8,128)(2,1)S(1)}, bf16[384,512]{1,0:T(8,128)(2,1)S(1)}, u32[]{:S(2)}, u32[]{:S(2)}) collective-permute-start(bf16[384,512]{1,0:T(8,128)(2,1)S(1)} %collective-permute-done.7), channel_id=1, source_target_pairs={{0,14},{2,0},{4,2},{6,4},{8,6},{10,8},{12,10},{14,12},{1,15},{3,1}... | collective-permute-start | bytes 1179656 | tf_op jit(solution)/shard_map/ppermute | solution.py:52
  80.7 0.9 constant_dynamic-update-slice_fusion.22
  81.5 2.1 %collective-permute-start.21 = (bf16[1024,256]{1,0:T(8,128)(2,1)S(1)}, bf16[1024,256]{1,0:T(8,128)(2,1)S(1)}, u32[]{:S(2)}, u32[]{:S(2)}) collective-permute-start(bf16[1024,256]{1,0:T(8,128)(2,1)S(1)} %collective-permute-done.19), channel_id=1, source_target_pairs={{0,448},{64,0},{128,64},{192,128},{256,192},{320,256},{384,320},{4... | collective-permute-start | bytes 1572872 | tf_op jit(solution)/shard_map/ppermute | solution.py:70
  84.5 1.9 collective-permute-start.10
  86.4 0.8 constant_dynamic-update-slice_fusion.20
  87.2 0.9 constant_dynamic-update-slice_fusion.19
  88.1 1.9 collective-permute-start.13
  90.0 2.4 %collective-permute-start.12 = (bf16[384,512]{1,0:T(8,128)(2,1)S(1)}, bf16[384,512]{1,0:T(8,128)(2,1)S(1)}, u32[]{:S(2)}, u32[]{:S(2)}) collective-permute-start(bf16[384,512]{1,0:T(8,128)(2,1)S(1)} %collective-permute-done.11), channel_id=1, source_target_pairs={{0,1},{1,0},{2,3},{3,2},{4,5},{5,4},{6,7},{7,6},{8,9},{9,8},{10,11... | collective-permute-start | bytes 1179656 | tf_op jit(solution)/shard_map/ppermute | solution.py:42
  92.4 0.8 constant_dynamic-update-slice_fusion.18
  93.2 4.5 %collective-permute-start.22 = (bf16[1024,256]{1,0:T(8,128)(2,1)S(1)}, bf16[1024,256]{1,0:T(8,128)(2,1)S(1)}, u32[]{:S(2)}, u32[]{:S(2)}) collective-permute-start(bf16[1024,256]{1,0:T(8,128)(2,1)S(1)} %collective-permute-done.20), channel_id=1, source_target_pairs={{0,64},{64,128},{128,192},{192,256},{256,320},{320,384},{384,448},... | collective-permute-start | bytes 1572872 | tf_op jit(solution)/shard_map/ppermute | solution.py:68
  98.6 11.0 %collective-permute-done.21 = bf16[1024,256]{1,0:T(8,128)(2,1)S(1)} collective-permute-done((bf16[1024,256]{1,0:T(8,128)(2,1)S(1)}, bf16[1024,256]{1,0:T(8,128)(2,1)S(1)}, u32[]{:S(2)}, u32[]{:S(2)}) %collective-permute-start.21) | collective-permute-done | bytes 524320 | tf_op jit(solution)/shard_map/ppermute | solution.py:70
  109.6 1.9 collective-permute-start.23
  111.6 1.9 collective-permute-start.14
  113.5 0.8 constant_dynamic-update-slice_fusion.16
  114.3 0.8 constant_dynamic-update-slice_fusion.15
  115.2 4.4 %collective-permute-start.24 = (bf16[1024,256]{1,0:T(8,128)(2,1)S(1)}, bf16[1024,256]{1,0:T(8,128)(2,1)S(1)}, u32[]{:S(2)}, u32[]{:S(2)}) collective-permute-start(bf16[1024,256]{1,0:T(8,128)(2,1)S(1)} %collective-permute-done.22), channel_id=1, source_target_pairs={{0,64},{64,128},{128,192},{192,256},{256,320},{320,384},{384,448},... | collective-permute-start | bytes 1572872 | tf_op jit(solution)/shard_map/ppermute | solution.py:68
  119.6 0.9 constant_dynamic-update-slice_fusion.14
  120.5 0.8 constant_dynamic-update-slice_fusion.13
  121.4 4.1 %collective-permute-done.23 = bf16[1024,256]{1,0:T(8,128)(2,1)S(1)} collective-permute-done((bf16[1024,256]{1,0:T(8,128)(2,1)S(1)}, bf16[1024,256]{1,0:T(8,128)(2,1)S(1)}, u32[]{:S(2)}, u32[]{:S(2)}) %collective-permute-start.23) | collective-permute-done | bytes 524320 | tf_op jit(solution)/shard_map/ppermute | solution.py:70
  126.3 6.9 %collective-permute-done.24 = bf16[1024,256]{1,0:T(8,128)(2,1)S(1)} collective-permute-done((bf16[1024,256]{1,0:T(8,128)(2,1)S(1)}, bf16[1024,256]{1,0:T(8,128)(2,1)S(1)}, u32[]{:S(2)}, u32[]{:S(2)}) %collective-permute-start.24) | collective-permute-done | bytes 524320 | tf_op jit(solution)/shard_map/ppermute | solution.py:68
  133.2 5.3 %fusion.9 = (f32[384]{0:T(512)S(1)}, f32[384,256]{0,1:T(8,128)S(1)}) fusion(bf16[384,8192]{1,0:T(8,128)(2,1)} %constant_dynamic-update-slice_fusion.12, bf16[8192,256]{1,0:T(8,128)(2,1)S(1)} %constant_dynamic-update-slice_fusion), kind=kOutput, calls=%fused_computation.61 | convolution fusion | flops 1610710656 | bytes 10880512 | tf_op jit(solution)/shard_map/dot_general | solution.py:107
  138.6 6.4 %fusion.8 = (f32[384]{0:T(512)S(1)}, f32[384,256]{0,1:T(8,128)S(1)}) fusion(bf16[384,8192]{1,0:T(8,128)(2,1)} %constant_dynamic-update-slice_fusion.12, bf16[8192,256]{1,0:T(8,128)(2,1)} %all-gather.4.cloned.1.call-done), kind=kOutput, calls=%fused_computation.60 | convolution fusion | flops 1610710656 | bytes 10880512 | tf_op jit(solution)/shard_map/dot_general | solution.py:106
  145.3 16.3 %all-gather.1 = f32[16,4,384]{2,1,0:T(4,128)S(1)} all-gather(f32[1,4,384]{2,1,0:T(4,128)S(1)} %maximum_bitcast_fusion), channel_id=2, replica_groups=mesh['y'=8,'x'=4,'z'=8,'c'=2] {'z','c'}, dimensions={0}, use_global_device_ids=true | all-gather | bytes 104448 | tf_op jit(solution)/shard_map/all_gather | solution.py:120
  163.1 9.4 %psum.14 = f32[32]{0:T(128)S(1)} all-reduce(f32[32]{0:T(128)S(1)} %select_reduce_fusion.1), channel_id=1, replica_groups=mesh['y'=8,'x'=4,'z'=8,'c'=2] {'x'}, use_global_device_ids=true, to_apply=%region_12.13 | all-reduce | flops 32 | bytes 256 | tf_op jit(solution)/shard_map/psum | solution.py:142
  172.5 17.1 %psum.15 = f32[32]{0:T(128)S(1)} all-reduce(f32[32]{0:T(128)S(1)} %psum.14), channel_id=1, replica_groups=mesh['y'=8,'x'=4,'z'=8,'c'=2] {'y'}, use_global_device_ids=true, to_apply=%region_13.14 | all-reduce | flops 32 | bytes 256 | tf_op jit(solution)/shard_map/psum | solution.py:142
  (81 shorter events, 7.7 us)
Async XLA Ops:
  7.2 27.8 %copy-start = (bf16[384,512]{1,0:T(8,128)(2,1)S(1)}, bf16[384,512]{1,0:T(8,128)(2,1)}, u32[]{:S(2)}) copy-start(bf16[384,512]{1,0:T(8,128)(2,1)} %param.8) | copy-start | bytes 1179652
  7.2 40.8 %copy-start.6 = (s32[32]{0:T(128)S(1)}, s32[32]{0:T(128)}, u32[]{:S(2)}) copy-start(s32[32]{0:T(128)} %param.15) | copy-start | bytes 388
  7.2 131.4 %all-gather.4.cloned.1.call-start = ((), (), s32[]{:S(2)}) async-start(), calls=%async_computation | async-start | bytes 4325376 | tf_op jit(solution)/shard_map/all_gather | solution.py:102
  9.0 44.1 %collective-permute-start = (bf16[384,512]{1,0:T(8,128)(2,1)}, bf16[384,512]{1,0:T(8,128)(2,1)S(1)}, u32[]{:S(2)}, u32[]{:S(2)}) collective-permute-start(bf16[384,512]{1,0:T(8,128)(2,1)} %param.8), channel_id=1, source_target_pairs={{0,1},{1,0},{2,3},{3,2},{4,5},{5,4},{6,7},{7,6},{8,9},{9,8},{10,11... | collective-permute-start | bytes 1179656 | tf_op jit(solution)/shard_map/ppermute | solution.py:42
  10.9 39.9 %collective-permute-start.1 = (bf16[384,512]{1,0:T(8,128)(2,1)}, bf16[384,512]{1,0:T(8,128)(2,1)S(1)}, u32[]{:S(2)}, u32[]{:S(2)}) collective-permute-start(bf16[384,512]{1,0:T(8,128)(2,1)} %param.8), channel_id=1, source_target_pairs={{0,2},{2,4},{4,6},{6,8},{8,10},{10,12},{12,14},{14,0},{1,3},{3,5},... | collective-permute-start | bytes 1179656 | tf_op jit(solution)/shard_map/ppermute | solution.py:50
  15.2 39.8 %collective-permute-start.3 = (bf16[384,512]{1,0:T(8,128)(2,1)}, bf16[384,512]{1,0:T(8,128)(2,1)S(1)}, u32[]{:S(2)}, u32[]{:S(2)}) collective-permute-start(bf16[384,512]{1,0:T(8,128)(2,1)} %param.8), channel_id=1, source_target_pairs={{0,14},{2,0},{4,2},{6,4},{8,6},{10,8},{12,10},{14,12},{1,15},{3,1}... | collective-permute-start | bytes 1179656 | tf_op jit(solution)/shard_map/ppermute | solution.py:52
  23.8 12.0 %collective-permute-start.15 = (bf16[256,256]{1,0:T(8,128)(2,1)S(1)}, bf16[256,256]{1,0:T(8,128)(2,1)S(1)}, u32[]{:S(2)}, u32[]{:S(2)}) collective-permute-start(bf16[256,256]{1,0:T(8,128)(2,1)S(1)} %get-tuple-element.12), channel_id=1, source_target_pairs={{0,16},{16,32},{32,48},{48,0},{1,17},{17,33},{33,49},{49,1},{2,18}... | collective-permute-start | bytes 393224 | tf_op jit(solution)/shard_map/ppermute | solution.py:68
  27.2 10.8 %collective-permute-start.16 = (bf16[256,256]{1,0:T(8,128)(2,1)S(1)}, bf16[256,256]{1,0:T(8,128)(2,1)S(1)}, u32[]{:S(2)}, u32[]{:S(2)}) collective-permute-start(bf16[256,256]{1,0:T(8,128)(2,1)S(1)} %get-tuple-element.12), channel_id=1, source_target_pairs={{0,48},{16,0},{32,16},{48,32},{1,49},{17,1},{33,17},{49,33},{2,50}... | collective-permute-start | bytes 393224 | tf_op jit(solution)/shard_map/ppermute | solution.py:70
  35.8 8.4 %collective-permute-start.17 = (bf16[256,256]{1,0:T(8,128)(2,1)S(1)}, bf16[256,256]{1,0:T(8,128)(2,1)S(1)}, u32[]{:S(2)}, u32[]{:S(2)}) collective-permute-start(bf16[256,256]{1,0:T(8,128)(2,1)S(1)} %collective-permute-done.15), channel_id=1, source_target_pairs={{0,16},{16,32},{32,48},{48,0},{1,17},{17,33},{33,49},{49,1},{2,18}... | collective-permute-start | bytes 393224 | tf_op jit(solution)/shard_map/ppermute | solution.py:68
  44.2 17.6 %collective-permute-start.18 = (bf16[1024,256]{1,0:T(8,128)(2,1)S(1)}, bf16[1024,256]{1,0:T(8,128)(2,1)S(1)}, u32[]{:S(2)}, u32[]{:S(2)}) collective-permute-start(bf16[1024,256]{1,0:T(8,128)(2,1)S(1)} %constant_dynamic-update-slice_fusion.8), channel_id=1, source_target_pairs={{0,64},{64,128},{128,192},{192,256},{256,320},{320,384},{384,448},... | collective-permute-start | bytes 1572872 | tf_op jit(solution)/shard_map/ppermute | solution.py:68
  48.2 15.7 %collective-permute-start.19 = (bf16[1024,256]{1,0:T(8,128)(2,1)S(1)}, bf16[1024,256]{1,0:T(8,128)(2,1)S(1)}, u32[]{:S(2)}, u32[]{:S(2)}) collective-permute-start(bf16[1024,256]{1,0:T(8,128)(2,1)S(1)} %constant_dynamic-update-slice_fusion.8), channel_id=1, source_target_pairs={{0,448},{64,0},{128,64},{192,128},{256,192},{320,256},{384,320},{4... | collective-permute-start | bytes 1572872 | tf_op jit(solution)/shard_map/ppermute | solution.py:70
  50.8 17.1 %collective-permute-start.5 = (bf16[384,512]{1,0:T(8,128)(2,1)S(1)}, bf16[384,512]{1,0:T(8,128)(2,1)S(1)}, u32[]{:S(2)}, u32[]{:S(2)}) collective-permute-start(bf16[384,512]{1,0:T(8,128)(2,1)S(1)} %collective-permute-done.1), channel_id=1, source_target_pairs={{0,2},{2,4},{4,6},{6,8},{8,10},{10,12},{12,14},{14,0},{1,3},{3,5},... | collective-permute-start | bytes 1179656 | tf_op jit(solution)/shard_map/ppermute | solution.py:50
  53.0 16.8 %collective-permute-start.2 = (bf16[384,512]{1,0:T(8,128)(2,1)S(1)}, bf16[384,512]{1,0:T(8,128)(2,1)S(1)}, u32[]{:S(2)}, u32[]{:S(2)}) collective-permute-start(bf16[384,512]{1,0:T(8,128)(2,1)S(1)} %collective-permute-done.1), channel_id=1, source_target_pairs={{0,1},{1,0},{2,3},{3,2},{4,5},{5,4},{6,7},{7,6},{8,9},{9,8},{10,11... | collective-permute-start | bytes 1179656 | tf_op jit(solution)/shard_map/ppermute | solution.py:42
  55.0 16.8 %collective-permute-start.7 = (bf16[384,512]{1,0:T(8,128)(2,1)S(1)}, bf16[384,512]{1,0:T(8,128)(2,1)S(1)}, u32[]{:S(2)}, u32[]{:S(2)}) collective-permute-start(bf16[384,512]{1,0:T(8,128)(2,1)S(1)} %collective-permute-done.3), channel_id=1, source_target_pairs={{0,14},{2,0},{4,2},{6,4},{8,6},{10,8},{12,10},{14,12},{1,15},{3,1}... | collective-permute-start | bytes 1179656 | tf_op jit(solution)/shard_map/ppermute | solution.py:52
  61.8 14.1 %collective-permute-start.4 = (bf16[384,512]{1,0:T(8,128)(2,1)S(1)}, bf16[384,512]{1,0:T(8,128)(2,1)S(1)}, u32[]{:S(2)}, u32[]{:S(2)}) collective-permute-start(bf16[384,512]{1,0:T(8,128)(2,1)S(1)} %collective-permute-done.3), channel_id=1, source_target_pairs={{0,1},{1,0},{2,3},{3,2},{4,5},{5,4},{6,7},{7,6},{8,9},{9,8},{10,11... | collective-permute-start | bytes 1179656 | tf_op jit(solution)/shard_map/ppermute | solution.py:42
  63.9 29.3 %collective-permute-start.20 = (bf16[1024,256]{1,0:T(8,128)(2,1)S(1)}, bf16[1024,256]{1,0:T(8,128)(2,1)S(1)}, u32[]{:S(2)}, u32[]{:S(2)}) collective-permute-start(bf16[1024,256]{1,0:T(8,128)(2,1)S(1)} %collective-permute-done.18), channel_id=1, source_target_pairs={{0,64},{64,128},{128,192},{192,256},{256,320},{320,384},{384,448},... | collective-permute-start | bytes 1572872 | tf_op jit(solution)/shard_map/ppermute | solution.py:68
  67.8 13.7 %collective-permute-start.6 = (bf16[384,512]{1,0:T(8,128)(2,1)S(1)}, bf16[384,512]{1,0:T(8,128)(2,1)S(1)}, u32[]{:S(2)}, u32[]{:S(2)}) collective-permute-start(bf16[384,512]{1,0:T(8,128)(2,1)S(1)} %collective-permute-done.5), channel_id=1, source_target_pairs={{0,1},{1,0},{2,3},{3,2},{4,5},{5,4},{6,7},{7,6},{8,9},{9,8},{10,11... | collective-permute-start | bytes 1179656 | tf_op jit(solution)/shard_map/ppermute | solution.py:42
  69.8 14.7 %collective-permute-start.9 = (bf16[384,512]{1,0:T(8,128)(2,1)S(1)}, bf16[384,512]{1,0:T(8,128)(2,1)S(1)}, u32[]{:S(2)}, u32[]{:S(2)}) collective-permute-start(bf16[384,512]{1,0:T(8,128)(2,1)S(1)} %collective-permute-done.5), channel_id=1, source_target_pairs={{0,2},{2,4},{4,6},{6,8},{8,10},{10,12},{12,14},{14,0},{1,3},{3,5},... | collective-permute-start | bytes 1179656 | tf_op jit(solution)/shard_map/ppermute | solution.py:50
  71.7 16.4 %collective-permute-start.8 = (bf16[384,512]{1,0:T(8,128)(2,1)S(1)}, bf16[384,512]{1,0:T(8,128)(2,1)S(1)}, u32[]{:S(2)}, u32[]{:S(2)}) collective-permute-start(bf16[384,512]{1,0:T(8,128)(2,1)S(1)} %collective-permute-done.7), channel_id=1, source_target_pairs={{0,1},{1,0},{2,3},{3,2},{4,5},{5,4},{6,7},{7,6},{8,9},{9,8},{10,11... | collective-permute-start | bytes 1179656 | tf_op jit(solution)/shard_map/ppermute | solution.py:42
  75.8 14.2 %collective-permute-start.11 = (bf16[384,512]{1,0:T(8,128)(2,1)S(1)}, bf16[384,512]{1,0:T(8,128)(2,1)S(1)}, u32[]{:S(2)}, u32[]{:S(2)}) collective-permute-start(bf16[384,512]{1,0:T(8,128)(2,1)S(1)} %collective-permute-done.7), channel_id=1, source_target_pairs={{0,14},{2,0},{4,2},{6,4},{8,6},{10,8},{12,10},{14,12},{1,15},{3,1}... | collective-permute-start | bytes 1179656 | tf_op jit(solution)/shard_map/ppermute | solution.py:52
  81.5 28.0 %collective-permute-start.21 = (bf16[1024,256]{1,0:T(8,128)(2,1)S(1)}, bf16[1024,256]{1,0:T(8,128)(2,1)S(1)}, u32[]{:S(2)}, u32[]{:S(2)}) collective-permute-start(bf16[1024,256]{1,0:T(8,128)(2,1)S(1)} %collective-permute-done.19), channel_id=1, source_target_pairs={{0,448},{64,0},{128,64},{192,128},{256,192},{320,256},{384,320},{4... | collective-permute-start | bytes 1572872 | tf_op jit(solution)/shard_map/ppermute | solution.py:70
  84.5 29.0 %collective-permute-start.10 = (bf16[384,512]{1,0:T(8,128)(2,1)S(1)}, bf16[384,512]{1,0:T(8,128)(2,1)S(1)}, u32[]{:S(2)}, u32[]{:S(2)}) collective-permute-start(bf16[384,512]{1,0:T(8,128)(2,1)S(1)} %collective-permute-done.9), channel_id=1, source_target_pairs={{0,1},{1,0},{2,3},{3,2},{4,5},{5,4},{6,7},{7,6},{8,9},{9,8},{10,11... | collective-permute-start | bytes 1179656 | tf_op jit(solution)/shard_map/ppermute | solution.py:42
  88.1 23.5 %collective-permute-start.13 = (bf16[384,512]{1,0:T(8,128)(2,1)S(1)}, bf16[384,512]{1,0:T(8,128)(2,1)S(1)}, u32[]{:S(2)}, u32[]{:S(2)}) collective-permute-start(bf16[384,512]{1,0:T(8,128)(2,1)S(1)} %collective-permute-done.9), channel_id=1, source_target_pairs={{0,2},{2,4},{4,6},{6,8},{8,10},{10,12},{12,14},{14,0},{1,3},{3,5},... | collective-permute-start | bytes 1179656 | tf_op jit(solution)/shard_map/ppermute | solution.py:50
  90.0 29.6 %collective-permute-start.12 = (bf16[384,512]{1,0:T(8,128)(2,1)S(1)}, bf16[384,512]{1,0:T(8,128)(2,1)S(1)}, u32[]{:S(2)}, u32[]{:S(2)}) collective-permute-start(bf16[384,512]{1,0:T(8,128)(2,1)S(1)} %collective-permute-done.11), channel_id=1, source_target_pairs={{0,1},{1,0},{2,3},{3,2},{4,5},{5,4},{6,7},{7,6},{8,9},{9,8},{10,11... | collective-permute-start | bytes 1179656 | tf_op jit(solution)/shard_map/ppermute | solution.py:42
  93.2 21.9 %collective-permute-start.22 = (bf16[1024,256]{1,0:T(8,128)(2,1)S(1)}, bf16[1024,256]{1,0:T(8,128)(2,1)S(1)}, u32[]{:S(2)}, u32[]{:S(2)}) collective-permute-start(bf16[1024,256]{1,0:T(8,128)(2,1)S(1)} %collective-permute-done.20), channel_id=1, source_target_pairs={{0,64},{64,128},{128,192},{192,256},{256,320},{320,384},{384,448},... | collective-permute-start | bytes 1572872 | tf_op jit(solution)/shard_map/ppermute | solution.py:68
  109.6 15.9 %collective-permute-start.23 = (bf16[1024,256]{1,0:T(8,128)(2,1)S(1)}, bf16[1024,256]{1,0:T(8,128)(2,1)S(1)}, u32[]{:S(2)}, u32[]{:S(2)}) collective-permute-start(bf16[1024,256]{1,0:T(8,128)(2,1)S(1)} %collective-permute-done.21), channel_id=1, source_target_pairs={{0,448},{64,0},{128,64},{192,128},{256,192},{320,256},{384,320},{4... | collective-permute-start | bytes 1572872 | tf_op jit(solution)/shard_map/ppermute | solution.py:70
  111.6 13.9 %collective-permute-start.14 = (bf16[384,512]{1,0:T(8,128)(2,1)S(1)}, bf16[384,512]{1,0:T(8,128)(2,1)S(1)}, u32[]{:S(2)}, u32[]{:S(2)}) collective-permute-start(bf16[384,512]{1,0:T(8,128)(2,1)S(1)} %collective-permute-done.13), channel_id=1, source_target_pairs={{0,1},{1,0},{2,3},{3,2},{4,5},{5,4},{6,7},{7,6},{8,9},{9,8},{10,11... | collective-permute-start | bytes 1179656 | tf_op jit(solution)/shard_map/ppermute | solution.py:42
  115.2 18.0 %collective-permute-start.24 = (bf16[1024,256]{1,0:T(8,128)(2,1)S(1)}, bf16[1024,256]{1,0:T(8,128)(2,1)S(1)}, u32[]{:S(2)}, u32[]{:S(2)}) collective-permute-start(bf16[1024,256]{1,0:T(8,128)(2,1)S(1)} %collective-permute-done.22), channel_id=1, source_target_pairs={{0,64},{64,128},{128,192},{192,256},{256,320},{320,384},{384,448},... | collective-permute-start | bytes 1572872 | tf_op jit(solution)/shard_map/ppermute | solution.py:68
  138.5 23.2 %copy-start.1 = (s32[384]{0:T(512)S(1)}, s32[384]{0:T(512)}, u32[]{:S(2)}) copy-start(s32[384]{0:T(512)} %param.10) | copy-start | bytes 4612
  138.5 23.2 %copy-start.2 = (f32[384]{0:T(512)S(1)}, f32[384]{0:T(512)}, u32[]{:S(2)}) copy-start(f32[384]{0:T(512)} %param.13) | copy-start | bytes 4612
  138.5 23.2 %copy-start.3 = (s32[384]{0:T(512)S(1)}, s32[384]{0:T(512)}, u32[]{:S(2)}) copy-start(s32[384]{0:T(512)} %param.11) | copy-start | bytes 4612
  138.5 23.2 %copy-start.4 = (f32[384]{0:T(512)S(1)}, f32[384]{0:T(512)}, u32[]{:S(2)}) copy-start(f32[384]{0:T(512)} %param.12) | copy-start | bytes 4612
  138.5 23.2 %copy-start.5 = (f32[384]{0:T(512)S(1)}, f32[384]{0:T(512)}, u32[]{:S(2)}) copy-start(f32[384]{0:T(512)} %param.14) | copy-start | bytes 4612
Sparse Core Ops, SparseCore 0:
  11.2 99.5 all-gather.3

commit v5 on v4

--- a/solution.py
+++ b/solution.py
@@ -74,20 +74,34 @@
     return buf
 
 
-def gather_head_part(part):
-    depth = part.shape[0]
+def gather_head(head):
+    depth, cols = head.shape
     nx = lax.axis_size("x")
     ny = lax.axis_size("y")
+    half = (cols // 2) // 128 * 128
 
     def put_x(buf, piece, index):
         return lax.dynamic_update_slice(buf, piece, (index * depth, 0))
 
-    strip = ring_gather(part, "x", put_x, jnp.zeros((depth * nx, part.shape[1]), part.dtype))
-
     def put_y(buf, piece, index):
         return lax.dynamic_update_slice(buf, piece, (index * depth * nx, 0))
 
-    return ring_gather(strip, "y", put_y, jnp.zeros((depth * nx * ny, part.shape[1]), part.dtype))
+    first = head[:, :half]
+    strip = ring_gather(first, "x", put_x, jnp.zeros((depth * nx, half), head.dtype))
+    first_full = ring_gather(strip, "y", put_y, jnp.zeros((depth * nx * ny, half), head.dtype))
+
+    second = head[:, half:]
+    width = cols - half
+
+    def put_col(buf, piece, index):
+        return lax.dynamic_update_slice(buf, piece[:, None], (0, index, 0, 0))
+
+    def put_row(buf, piece, index):
+        return lax.dynamic_update_slice(buf, piece[None], (index, 0, 0))
+
+    column = ring_gather(second, "y", put_row, jnp.zeros((ny, depth, width), head.dtype))
+    second_full = ring_gather(column, "x", put_col, jnp.zeros((ny, nx, depth, width), head.dtype))
+    return first_full, second_full.reshape(ny * nx * depth, width)
 
 
 def local(hidden, head, targets, live, prior_lse, prior_mean, prior_target, seq_lengths):
@@ -97,14 +111,12 @@
     which = lax.axis_index(VOCAB_AXES)
     block_first = VOCAB - cols_here * spread
     first_col = block_first + which * cols_here
-    gathered = gather_hidden(hidden)
-    split = (cols_here // 2) // 128 * 128
-    head_sc = lax.all_gather(head[:, :split], ROW_AXES, axis=0, tiled=True)
-    head_ring = gather_head_part(head[:, split:])
+    gathered = lax.all_gather(hidden, VOCAB_AXES, axis=1, tiled=True)
+    head_first, head_second = gather_head(head)
     logits = jnp.concatenate(
         [
-            jnp.dot(gathered, head_sc, preferred_element_type=jnp.float32),
-            jnp.dot(gathered, head_ring, preferred_element_type=jnp.float32),
+            jnp.dot(gathered, head_first, preferred_element_type=jnp.float32),
+            jnp.dot(gathered, head_second, preferred_element_type=jnp.float32),
         ],
         axis=1,
     )

time: 198 us -> 189 us (0.955)
  the two profiles are of different devices: /device:TPU:8 before, /device:TPU:26 now
where the time goes in v5:
time: 189 us; the launch traced here: 188 us
  starting transfers between devices  71.9 us (38%)
  blocking collectives  49.3 us (26%)
  local copies, waits for them, and re-layouts  21.3 us (11%)
  waiting for transfers between devices  18.4 us (10%)
  between operations  14.9 us (8%)
  matrix products  11.2 us (6%)
    ppermute x12, starting transfers between devices, ring_gather(): fwd = lax.ppermute(fwd, axis, ahead)  54.5 us
    psum x2, blocking collectives, local(): sums = lax.psum(lax.psum(partial_sums, 'x'), 'y')  26.5 us
    all_gather x1, blocking collectives, local(): every = lax.all_gather(stats, VOCAB_AXES, axis=0, tiled=False)  22.8 us
    ppermute x12, waiting for transfers between devices, ring_gather(): fwd = lax.ppermute(fwd, axis, ahead)  17.7 us
    ppermute x8, starting transfers between devices, ring_gather(): bwd = lax.ppermute(bwd, axis, behind)  17.3 us
    dynamic_update_slice x8, local copies, waits for them, and re-layouts, put_y(): return lax.dynamic_update_slice(buf, piece, (index * depth * nx, 0))  7.81 us
    dot_general x1, matrix products, local(): jnp.dot(gathered, head_second, preferred_element_type=jnp.float32)  6.59 us
    dot_general x1, matrix products, local(): jnp.dot(gathered, head_first, preferred_element_type=jnp.float32)  4.65 us
  transfers between devices with their start and end apart: 21, of which 5 were waited for; matrix products, arithmetic and copies ran while one was open for 11% of the time, Pallas kernels for 0%

profile of v5, /device:TPU:26, one launch (start us, length us, event | category | flops | bytes accessed | tf_op | source)
XLA Modules:
  0.0 188.5 jit_solution(10105410834359374988)
XLA Ops:
  7.2 0.7 all-gather.4.cloned.1.call-update
  8.0 1.0 fusion.6
  9.0 4.7 %collective-permute-start.10 = (bf16[256,256]{1,0:T(8,128)(2,1)S(1)}, bf16[256,256]{1,0:T(8,128)(2,1)S(1)}, u32[]{:S(2)}, u32[]{:S(2)}) collective-permute-start(bf16[256,256]{1,0:T(8,128)(2,1)S(1)} %get-tuple-element.12), channel_id=1, source_target_pairs={{0,64},{64,128},{128,192},{192,256},{256,320},{320,384},{384,448},... | collective-permute-start | bytes 393224 | tf_op jit(solution)/shard_map/ppermute | solution.py:68
  13.7 1.9 %collective-permute-start.11 = (bf16[256,256]{1,0:T(8,128)(2,1)S(1)}, bf16[256,256]{1,0:T(8,128)(2,1)S(1)}, u32[]{:S(2)}, u32[]{:S(2)}) collective-permute-start(bf16[256,256]{1,0:T(8,128)(2,1)S(1)} %get-tuple-element.12), channel_id=1, source_target_pairs={{0,448},{64,0},{128,64},{192,128},{256,192},{320,256},{384,320},{4... | collective-permute-start | bytes 393224 | tf_op jit(solution)/shard_map/ppermute | solution.py:70
  15.6 3.4 %collective-permute-start = (bf16[256,256]{1,0:T(8,128)(2,1)S(1)}, bf16[256,256]{1,0:T(8,128)(2,1)S(1)}, u32[]{:S(2)}, u32[]{:S(2)}) collective-permute-start(bf16[256,256]{1,0:T(8,128)(2,1)S(1)} %get-tuple-element.10), channel_id=1, source_target_pairs={{0,16},{16,32},{32,48},{48,0},{1,17},{17,33},{33,49},{49,1},{2,18}... | collective-permute-start | bytes 393224 | tf_op jit(solution)/shard_map/ppermute | solution.py:68
  19.0 2.4 %collective-permute-start.1 = (bf16[256,256]{1,0:T(8,128)(2,1)S(1)}, bf16[256,256]{1,0:T(8,128)(2,1)S(1)}, u32[]{:S(2)}, u32[]{:S(2)}) collective-permute-start(bf16[256,256]{1,0:T(8,128)(2,1)S(1)} %get-tuple-element.10), channel_id=1, source_target_pairs={{0,48},{16,0},{32,16},{48,32},{1,49},{17,1},{33,17},{49,33},{2,50}... | collective-permute-start | bytes 393224 | tf_op jit(solution)/shard_map/ppermute | solution.py:70
  21.5 0.9 bitcast_dynamic-update-slice_fusion.11
  22.6 0.7 copy.31
  23.6 5.1 %collective-permute-start.12 = (bf16[256,256]{1,0:T(8,128)(2,1)S(1)}, bf16[256,256]{1,0:T(8,128)(2,1)S(1)}, u32[]{:S(2)}, u32[]{:S(2)}) collective-permute-start(bf16[256,256]{1,0:T(8,128)(2,1)S(1)} %collective-permute-done.10), channel_id=1, source_target_pairs={{0,64},{64,128},{128,192},{192,256},{256,320},{320,384},{384,448},... | collective-permute-start | bytes 393224 | tf_op jit(solution)/shard_map/ppermute | solution.py:68
  28.8 1.9 %collective-permute-start.13 = (bf16[256,256]{1,0:T(8,128)(2,1)S(1)}, bf16[256,256]{1,0:T(8,128)(2,1)S(1)}, u32[]{:S(2)}, u32[]{:S(2)}) collective-permute-start(bf16[256,256]{1,0:T(8,128)(2,1)S(1)} %collective-permute-done.11), channel_id=1, source_target_pairs={{0,448},{64,0},{128,64},{192,128},{256,192},{320,256},{384,320},{4... | collective-permute-start | bytes 393224 | tf_op jit(solution)/shard_map/ppermute | solution.py:70
  30.7 3.4 %collective-permute-start.2 = (bf16[256,256]{1,0:T(8,128)(2,1)S(1)}, bf16[256,256]{1,0:T(8,128)(2,1)S(1)}, u32[]{:S(2)}, u32[]{:S(2)}) collective-permute-start(bf16[256,256]{1,0:T(8,128)(2,1)S(1)} %collective-permute-done), channel_id=1, source_target_pairs={{0,16},{16,32},{32,48},{48,0},{1,17},{17,33},{33,49},{49,1},{2,18}... | collective-permute-start | bytes 393224 | tf_op jit(solution)/shard_map/ppermute | solution.py:68
  34.2 3.3 %collective-permute-done.2 = bf16[256,256]{1,0:T(8,128)(2,1)S(1)} collective-permute-done((bf16[256,256]{1,0:T(8,128)(2,1)S(1)}, bf16[256,256]{1,0:T(8,128)(2,1)S(1)}, u32[]{:S(2)}, u32[]{:S(2)}) %collective-permute-start.2) | collective-permute-done | bytes 131104 | tf_op jit(solution)/shard_map/ppermute | solution.py:68
  37.6 5.1 %collective-permute-start.3 = (bf16[1024,256]{1,0:T(8,128)(2,1)S(1)}, bf16[1024,256]{1,0:T(8,128)(2,1)}, u32[]{:S(2)}, u32[]{:S(2)}) collective-permute-start(bf16[1024,256]{1,0:T(8,128)(2,1)S(1)} %constant_dynamic-update-slice_fusion.8), channel_id=1, source_target_pairs={{0,64},{64,128},{128,192},{192,256},{256,320},{320,384},{384,448},... | collective-permute-start | bytes 1572872 | tf_op jit(solution)/shard_map/ppermute | solution.py:68
  42.7 1.9 %collective-permute-start.4 = (bf16[1024,256]{1,0:T(8,128)(2,1)S(1)}, bf16[1024,256]{1,0:T(8,128)(2,1)S(1)}, u32[]{:S(2)}, u32[]{:S(2)}) collective-permute-start(bf16[1024,256]{1,0:T(8,128)(2,1)S(1)} %constant_dynamic-update-slice_fusion.8), channel_id=1, source_target_pairs={{0,448},{64,0},{128,64},{192,128},{256,192},{320,256},{384,320},{4... | collective-permute-start | bytes 1572872 | tf_op jit(solution)/shard_map/ppermute | solution.py:70
  44.7 5.1 %collective-permute-start.14 = (bf16[256,256]{1,0:T(8,128)(2,1)S(1)}, bf16[256,256]{1,0:T(8,128)(2,1)S(1)}, u32[]{:S(2)}, u32[]{:S(2)}) collective-permute-start(bf16[256,256]{1,0:T(8,128)(2,1)S(1)} %collective-permute-done.12), channel_id=1, source_target_pairs={{0,64},{64,128},{128,192},{192,256},{256,320},{320,384},{384,448},... | collective-permute-start | bytes 393224 | tf_op jit(solution)/shard_map/ppermute | solution.py:68
  49.8 1.9 %collective-permute-start.15 = (bf16[256,256]{1,0:T(8,128)(2,1)S(1)}, bf16[256,256]{1,0:T(8,128)(2,1)S(1)}, u32[]{:S(2)}, u32[]{:S(2)}) collective-permute-start(bf16[256,256]{1,0:T(8,128)(2,1)S(1)} %collective-permute-done.13), channel_id=1, source_target_pairs={{0,448},{64,0},{128,64},{192,128},{256,192},{320,256},{384,320},{4... | collective-permute-start | bytes 393224 | tf_op jit(solution)/shard_map/ppermute | solution.py:70
  51.8 2.5 %collective-permute-done.14 = bf16[256,256]{1,0:T(8,128)(2,1)S(1)} collective-permute-done((bf16[256,256]{1,0:T(8,128)(2,1)S(1)}, bf16[256,256]{1,0:T(8,128)(2,1)S(1)}, u32[]{:S(2)}, u32[]{:S(2)}) %collective-permute-start.14) | collective-permute-done | bytes 131104 | tf_op jit(solution)/shard_map/ppermute | solution.py:68
  54.3 5.6 %collective-permute-start.16 = (bf16[256,256]{1,0:T(8,128)(2,1)S(1)}, bf16[256,256]{1,0:T(8,128)(2,1)S(1)}, u32[]{:S(2)}, u32[]{:S(2)}) collective-permute-start(bf16[256,256]{1,0:T(8,128)(2,1)S(1)} %collective-permute-done.14), channel_id=1, source_target_pairs={{0,64},{64,128},{128,192},{192,256},{256,320},{320,384},{384,448},... | collective-permute-start | bytes 393224 | tf_op jit(solution)/shard_map/ppermute | solution.py:68
  59.9 2.4 %collective-permute-done.16 = bf16[256,256]{1,0:T(8,128)(2,1)S(1)} collective-permute-done((bf16[256,256]{1,0:T(8,128)(2,1)S(1)}, bf16[256,256]{1,0:T(8,128)(2,1)S(1)}, u32[]{:S(2)}, u32[]{:S(2)}) %collective-permute-start.16) | collective-permute-done | bytes 131104 | tf_op jit(solution)/shard_map/ppermute | solution.py:68
  62.4 3.4 %collective-permute-start.17 = (bf16[8,256,256]{2,1,0:T(8,128)(2,1)S(1)}, bf16[8,256,256]{2,1,0:T(8,128)(2,1)S(1)}, u32[]{:S(2)}, u32[]{:S(2)}) collective-permute-start(bf16[8,256,256]{2,1,0:T(8,128)(2,1)S(1)} %bitcast_dynamic-update-slice_fusion.4), channel_id=1, source_target_pairs={{0,16},{16,32},{32,48},{48,0},{1,17},{17,33},{33,49},{49,1},{2,18}... | collective-permute-start | bytes 3145736 | tf_op jit(solution)/shard_map/ppermute | solution.py:68
  66.0 2.4 %broadcast_in_dim.60 = bf16[8192,256]{1,0:T(8,128)(2,1)} broadcast(bf16[]{:T(256)} %constant.123.clone.1), dimensions={} | broadcast | bytes 4194306 | tf_op jit(solution)/shard_map/broadcast_in_dim | solution.py:91
  68.3 0.8 constant_dynamic-update-slice_fusion.7
  69.2 3.4 %collective-permute-start.18 = (bf16[8,256,256]{2,1,0:T(8,128)(2,1)S(1)}, bf16[8,256,256]{2,1,0:T(8,128)(2,1)S(1)}, u32[]{:S(2)}, u32[]{:S(2)}) collective-permute-start(bf16[8,256,256]{2,1,0:T(8,128)(2,1)S(1)} %bitcast_dynamic-update-slice_fusion.4), channel_id=1, source_target_pairs={{0,48},{16,0},{32,16},{48,32},{1,49},{17,1},{33,17},{49,33},{2,50}... | collective-permute-start | bytes 3145736 | tf_op jit(solution)/shard_map/ppermute | solution.py:70
  72.6 5.6 %collective-permute-start.5 = (bf16[1024,256]{1,0:T(8,128)(2,1)}, bf16[1024,256]{1,0:T(8,128)(2,1)S(1)}, u32[]{:S(2)}, u32[]{:S(2)}) collective-permute-start(bf16[1024,256]{1,0:T(8,128)(2,1)} %collective-permute-done.3), channel_id=1, source_target_pairs={{0,64},{64,128},{128,192},{192,256},{256,320},{320,384},{384,448},... | collective-permute-start | bytes 1572872 | tf_op jit(solution)/shard_map/ppermute | solution.py:68
  78.2 1.9 %collective-permute-start.6 = (bf16[1024,256]{1,0:T(8,128)(2,1)S(1)}, bf16[1024,256]{1,0:T(8,128)(2,1)S(1)}, u32[]{:S(2)}, u32[]{:S(2)}) collective-permute-start(bf16[1024,256]{1,0:T(8,128)(2,1)S(1)} %collective-permute-done.4), channel_id=1, source_target_pairs={{0,448},{64,0},{128,64},{192,128},{256,192},{320,256},{384,320},{4... | collective-permute-start | bytes 1572872 | tf_op jit(solution)/shard_map/ppermute | solution.py:70
  80.1 2.5 %broadcast_in_dim.62 = bf16[8,4,256,256]{3,2,1,0:T(8,128)(2,1)} broadcast(bf16[]{:T(256)} %constant.123.clone.1), dimensions={} | broadcast | bytes 4194306 | tf_op jit(solution)/shard_map/broadcast_in_dim | solution.py:103
  82.6 1.1 bitcast_dynamic-update-slice_fusion.2
  83.7 1.9 constant_dynamic-update-slice_fusion.6
  85.5 0.9 constant_dynamic-update-slice_fusion.5
  86.4 5.2 %collective-permute-start.7 = (bf16[1024,256]{1,0:T(8,128)(2,1)S(1)}, bf16[1024,256]{1,0:T(8,128)(2,1)S(1)}, u32[]{:S(2)}, u32[]{:S(2)}) collective-permute-start(bf16[1024,256]{1,0:T(8,128)(2,1)S(1)} %collective-permute-done.5), channel_id=1, source_target_pairs={{0,64},{64,128},{128,192},{192,256},{256,320},{320,384},{384,448},... | collective-permute-start | bytes 1572872 | tf_op jit(solution)/shard_map/ppermute | solution.py:68
  91.6 1.9 %collective-permute-start.8 = (bf16[1024,256]{1,0:T(8,128)(2,1)S(1)}, bf16[1024,256]{1,0:T(8,128)(2,1)S(1)}, u32[]{:S(2)}, u32[]{:S(2)}) collective-permute-start(bf16[1024,256]{1,0:T(8,128)(2,1)S(1)} %collective-permute-done.6), channel_id=1, source_target_pairs={{0,448},{64,0},{128,64},{192,128},{256,192},{320,256},{384,320},{4... | collective-permute-start | bytes 1572872 | tf_op jit(solution)/shard_map/ppermute | solution.py:70
  93.5 0.9 constant_dynamic-update-slice_fusion.4
  94.3 2.4 %collective-permute-start.19 = (bf16[8,256,256]{2,1,0:T(8,128)(2,1)S(1)}, bf16[8,256,256]{2,1,0:T(8,128)(2,1)S(1)}, u32[]{:S(2)}, u32[]{:S(2)}) collective-permute-start(bf16[8,256,256]{2,1,0:T(8,128)(2,1)S(1)} %collective-permute-done.17), channel_id=1, source_target_pairs={{0,16},{16,32},{32,48},{48,0},{1,17},{17,33},{33,49},{49,1},{2,18}... | collective-permute-start | bytes 3145736 | tf_op jit(solution)/shard_map/ppermute | solution.py:68
  96.8 0.9 constant_dynamic-update-slice_fusion.3
  97.7 1.0 bitcast_dynamic-update-slice_fusion.1
  98.7 5.5 %collective-permute-start.9 = (bf16[1024,256]{1,0:T(8,128)(2,1)S(1)}, bf16[1024,256]{1,0:T(8,128)(2,1)S(1)}, u32[]{:S(2)}, u32[]{:S(2)}) collective-permute-start(bf16[1024,256]{1,0:T(8,128)(2,1)S(1)} %collective-permute-done.7), channel_id=1, source_target_pairs={{0,64},{64,128},{128,192},{192,256},{256,320},{320,384},{384,448},... | collective-permute-start | bytes 1572872 | tf_op jit(solution)/shard_map/ppermute | solution.py:68
  104.2 1.0 bitcast_dynamic-update-slice_fusion
  105.3 0.9 constant_dynamic-update-slice_fusion.2
  106.1 0.8 constant_dynamic-update-slice_fusion.1
  106.9 5.1 %collective-permute-done.9 = bf16[1024,256]{1,0:T(8,128)(2,1)S(1)} collective-permute-done((bf16[1024,256]{1,0:T(8,128)(2,1)S(1)}, bf16[1024,256]{1,0:T(8,128)(2,1)S(1)}, u32[]{:S(2)}, u32[]{:S(2)}) %collective-permute-start.9) | collective-permute-done | bytes 524320 | tf_op jit(solution)/shard_map/ppermute | solution.py:68
  112.1 0.8 constant_dynamic-update-slice_fusion
  112.9 4.3 %collective-permute-done.19 = bf16[8,256,256]{2,1,0:T(8,128)(2,1)S(1)} collective-permute-done((bf16[8,256,256]{2,1,0:T(8,128)(2,1)S(1)}, bf16[8,256,256]{2,1,0:T(8,128)(2,1)S(1)}, u32[]{:S(2)}, u32[]{:S(2)}) %collective-permute-start.19) | collective-permute-done | bytes 1048608 | tf_op jit(solution)/shard_map/ppermute | solution.py:68
  117.2 1.1 bitcast_dynamic-update-slice_fusion.3
  118.3 6.6 %fusion.9 = (f32[384]{0:T(512)S(1)}, f32[256,384]{1,0:T(8,128)S(1)}) fusion(bf16[8192,256]{1,0:T(8,128)(2,1)} %bitcast.15, bf16[384,8192]{1,0:T(8,128)(2,1)} %all-gather.4.cloned.1.call-done), kind=kOutput, calls=%fused_computation.57 | convolution fusion | flops 1610710656 | bytes 10880512 | tf_op jit(solution)/shard_map/dot_general | solution.py:119
  125.0 4.6 %fusion.8 = (f32[384]{0:T(512)S(1)}, f32[256,384]{1,0:T(8,128)S(1)}) fusion(bf16[8192,256]{1,0:T(8,128)(2,1)} %constant_dynamic-update-slice_fusion, bf16[384,8192]{1,0:T(8,128)(2,1)S(1)} %copy-done.6), kind=kOutput, calls=%fused_computation.56 | convolution fusion | flops 1610710656 | bytes 10880512 | tf_op jit(solution)/shard_map/dot_general | solution.py:118
  130.0 22.8 %all-gather.1 = f32[16,4,384]{2,1,0:T(4,128)S(1)} all-gather(f32[1,4,384]{2,1,0:T(4,128)S(1)} %maximum_bitcast_fusion), channel_id=2, replica_groups=mesh['y'=8,'x'=4,'z'=8,'c'=2] {'z','c'}, dimensions={0}, use_global_device_ids=true | all-gather | bytes 104448 | tf_op jit(solution)/shard_map/all_gather | solution.py:132
  154.3 10.6 %psum.14 = f32[32]{0:T(128)S(1)} all-reduce(f32[32]{0:T(128)S(1)} %select_reduce_fusion.1), channel_id=1, replica_groups=mesh['y'=8,'x'=4,'z'=8,'c'=2] {'x'}, use_global_device_ids=true, to_apply=%region_12.13 | all-reduce | flops 32 | bytes 256 | tf_op jit(solution)/shard_map/psum | solution.py:154
  164.9 15.9 %psum.15 = f32[32]{0:T(128)S(1)} all-reduce(f32[32]{0:T(128)S(1)} %psum.14), channel_id=1, replica_groups=mesh['y'=8,'x'=4,'z'=8,'c'=2] {'y'}, use_global_device_ids=true, to_apply=%region_13.14 | all-reduce | flops 32 | bytes 256 | tf_op jit(solution)/shard_map/psum | solution.py:154
  (68 shorter events, 3.3 us)
Async XLA Ops:
  7.2 58.8 %copy-start = (s32[384]{0:T(512)S(1)}, s32[384]{0:T(512)}, u32[]{:S(2)}) copy-start(s32[384]{0:T(512)} %param.10) | copy-start | bytes 4612
  7.2 111.1 %all-gather.4.cloned.1.call-start = ((), (), s32[]{:S(2)}) async-start(), calls=%async_computation | async-start | bytes 6684672 | tf_op jit(solution)/shard_map/all_gather | solution.py:114
  9.0 14.6 %collective-permute-start.10 = (bf16[256,256]{1,0:T(8,128)(2,1)S(1)}, bf16[256,256]{1,0:T(8,128)(2,1)S(1)}, u32[]{:S(2)}, u32[]{:S(2)}) collective-permute-start(bf16[256,256]{1,0:T(8,128)(2,1)S(1)} %get-tuple-element.12), channel_id=1, source_target_pairs={{0,64},{64,128},{128,192},{192,256},{256,320},{320,384},{384,448},... | collective-permute-start | bytes 393224 | tf_op jit(solution)/shard_map/ppermute | solution.py:68
  13.7 15.1 %collective-permute-start.11 = (bf16[256,256]{1,0:T(8,128)(2,1)S(1)}, bf16[256,256]{1,0:T(8,128)(2,1)S(1)}, u32[]{:S(2)}, u32[]{:S(2)}) collective-permute-start(bf16[256,256]{1,0:T(8,128)(2,1)S(1)} %get-tuple-element.12), channel_id=1, source_target_pairs={{0,448},{64,0},{128,64},{192,128},{256,192},{320,256},{384,320},{4... | collective-permute-start | bytes 393224 | tf_op jit(solution)/shard_map/ppermute | solution.py:70
  15.6 15.1 %collective-permute-start = (bf16[256,256]{1,0:T(8,128)(2,1)S(1)}, bf16[256,256]{1,0:T(8,128)(2,1)S(1)}, u32[]{:S(2)}, u32[]{:S(2)}) collective-permute-start(bf16[256,256]{1,0:T(8,128)(2,1)S(1)} %get-tuple-element.10), channel_id=1, source_target_pairs={{0,16},{16,32},{32,48},{48,0},{1,17},{17,33},{33,49},{49,1},{2,18}... | collective-permute-start | bytes 393224 | tf_op jit(solution)/shard_map/ppermute | solution.py:68
  19.0 15.2 %collective-permute-start.1 = (bf16[256,256]{1,0:T(8,128)(2,1)S(1)}, bf16[256,256]{1,0:T(8,128)(2,1)S(1)}, u32[]{:S(2)}, u32[]{:S(2)}) collective-permute-start(bf16[256,256]{1,0:T(8,128)(2,1)S(1)} %get-tuple-element.10), channel_id=1, source_target_pairs={{0,48},{16,0},{32,16},{48,32},{1,49},{17,1},{33,17},{49,33},{2,50}... | collective-permute-start | bytes 393224 | tf_op jit(solution)/shard_map/ppermute | solution.py:70
  23.6 21.0 %collective-permute-start.12 = (bf16[256,256]{1,0:T(8,128)(2,1)S(1)}, bf16[256,256]{1,0:T(8,128)(2,1)S(1)}, u32[]{:S(2)}, u32[]{:S(2)}) collective-permute-start(bf16[256,256]{1,0:T(8,128)(2,1)S(1)} %collective-permute-done.10), channel_id=1, source_target_pairs={{0,64},{64,128},{128,192},{192,256},{256,320},{320,384},{384,448},... | collective-permute-start | bytes 393224 | tf_op jit(solution)/shard_map/ppermute | solution.py:68
  28.8 21.0 %collective-permute-start.13 = (bf16[256,256]{1,0:T(8,128)(2,1)S(1)}, bf16[256,256]{1,0:T(8,128)(2,1)S(1)}, u32[]{:S(2)}, u32[]{:S(2)}) collective-permute-start(bf16[256,256]{1,0:T(8,128)(2,1)S(1)} %collective-permute-done.11), channel_id=1, source_target_pairs={{0,448},{64,0},{128,64},{192,128},{256,192},{320,256},{384,320},{4... | collective-permute-start | bytes 393224 | tf_op jit(solution)/shard_map/ppermute | solution.py:70
  30.7 6.9 %collective-permute-start.2 = (bf16[256,256]{1,0:T(8,128)(2,1)S(1)}, bf16[256,256]{1,0:T(8,128)(2,1)S(1)}, u32[]{:S(2)}, u32[]{:S(2)}) collective-permute-start(bf16[256,256]{1,0:T(8,128)(2,1)S(1)} %collective-permute-done), channel_id=1, source_target_pairs={{0,16},{16,32},{32,48},{48,0},{1,17},{17,33},{33,49},{49,1},{2,18}... | collective-permute-start | bytes 393224 | tf_op jit(solution)/shard_map/ppermute | solution.py:68
  37.6 35.0 %collective-permute-start.3 = (bf16[1024,256]{1,0:T(8,128)(2,1)S(1)}, bf16[1024,256]{1,0:T(8,128)(2,1)}, u32[]{:S(2)}, u32[]{:S(2)}) collective-permute-start(bf16[1024,256]{1,0:T(8,128)(2,1)S(1)} %constant_dynamic-update-slice_fusion.8), channel_id=1, source_target_pairs={{0,64},{64,128},{128,192},{192,256},{256,320},{320,384},{384,448},... | collective-permute-start | bytes 1572872 | tf_op jit(solution)/shard_map/ppermute | solution.py:68
  42.7 35.4 %collective-permute-start.4 = (bf16[1024,256]{1,0:T(8,128)(2,1)S(1)}, bf16[1024,256]{1,0:T(8,128)(2,1)S(1)}, u32[]{:S(2)}, u32[]{:S(2)}) collective-permute-start(bf16[1024,256]{1,0:T(8,128)(2,1)S(1)} %constant_dynamic-update-slice_fusion.8), channel_id=1, source_target_pairs={{0,448},{64,0},{128,64},{192,128},{256,192},{320,256},{384,320},{4... | collective-permute-start | bytes 1572872 | tf_op jit(solution)/shard_map/ppermute | solution.py:70
  44.7 9.6 %collective-permute-start.14 = (bf16[256,256]{1,0:T(8,128)(2,1)S(1)}, bf16[256,256]{1,0:T(8,128)(2,1)S(1)}, u32[]{:S(2)}, u32[]{:S(2)}) collective-permute-start(bf16[256,256]{1,0:T(8,128)(2,1)S(1)} %collective-permute-done.12), channel_id=1, source_target_pairs={{0,64},{64,128},{128,192},{192,256},{256,320},{320,384},{384,448},... | collective-permute-start | bytes 393224 | tf_op jit(solution)/shard_map/ppermute | solution.py:68
  49.8 10.1 %collective-permute-start.15 = (bf16[256,256]{1,0:T(8,128)(2,1)S(1)}, bf16[256,256]{1,0:T(8,128)(2,1)S(1)}, u32[]{:S(2)}, u32[]{:S(2)}) collective-permute-start(bf16[256,256]{1,0:T(8,128)(2,1)S(1)} %collective-permute-done.13), channel_id=1, source_target_pairs={{0,448},{64,0},{128,64},{192,128},{256,192},{320,256},{384,320},{4... | collective-permute-start | bytes 393224 | tf_op jit(solution)/shard_map/ppermute | solution.py:70
  54.3 8.1 %collective-permute-start.16 = (bf16[256,256]{1,0:T(8,128)(2,1)S(1)}, bf16[256,256]{1,0:T(8,128)(2,1)S(1)}, u32[]{:S(2)}, u32[]{:S(2)}) collective-permute-start(bf16[256,256]{1,0:T(8,128)(2,1)S(1)} %collective-permute-done.14), channel_id=1, source_target_pairs={{0,64},{64,128},{128,192},{192,256},{256,320},{320,384},{384,448},... | collective-permute-start | bytes 393224 | tf_op jit(solution)/shard_map/ppermute | solution.py:68
  62.4 32.0 %collective-permute-start.17 = (bf16[8,256,256]{2,1,0:T(8,128)(2,1)S(1)}, bf16[8,256,256]{2,1,0:T(8,128)(2,1)S(1)}, u32[]{:S(2)}, u32[]{:S(2)}) collective-permute-start(bf16[8,256,256]{2,1,0:T(8,128)(2,1)S(1)} %bitcast_dynamic-update-slice_fusion.4), channel_id=1, source_target_pairs={{0,16},{16,32},{32,48},{48,0},{1,17},{17,33},{33,49},{49,1},{2,18}... | collective-permute-start | bytes 3145736 | tf_op jit(solution)/shard_map/ppermute | solution.py:68
  69.2 35.0 %collective-permute-start.18 = (bf16[8,256,256]{2,1,0:T(8,128)(2,1)S(1)}, bf16[8,256,256]{2,1,0:T(8,128)(2,1)S(1)}, u32[]{:S(2)}, u32[]{:S(2)}) collective-permute-start(bf16[8,256,256]{2,1,0:T(8,128)(2,1)S(1)} %bitcast_dynamic-update-slice_fusion.4), channel_id=1, source_target_pairs={{0,48},{16,0},{32,16},{48,32},{1,49},{17,1},{33,17},{49,33},{2,50}... | collective-permute-start | bytes 3145736 | tf_op jit(solution)/shard_map/ppermute | solution.py:70
  72.6 13.8 %collective-permute-start.5 = (bf16[1024,256]{1,0:T(8,128)(2,1)}, bf16[1024,256]{1,0:T(8,128)(2,1)S(1)}, u32[]{:S(2)}, u32[]{:S(2)}) collective-permute-start(bf16[1024,256]{1,0:T(8,128)(2,1)} %collective-permute-done.3), channel_id=1, source_target_pairs={{0,64},{64,128},{128,192},{192,256},{256,320},{320,384},{384,448},... | collective-permute-start | bytes 1572872 | tf_op jit(solution)/shard_map/ppermute | solution.py:68
  78.2 13.4 %collective-permute-start.6 = (bf16[1024,256]{1,0:T(8,128)(2,1)S(1)}, bf16[1024,256]{1,0:T(8,128)(2,1)S(1)}, u32[]{:S(2)}, u32[]{:S(2)}) collective-permute-start(bf16[1024,256]{1,0:T(8,128)(2,1)S(1)} %collective-permute-done.4), channel_id=1, source_target_pairs={{0,448},{64,0},{128,64},{192,128},{256,192},{320,256},{384,320},{4... | collective-permute-start | bytes 1572872 | tf_op jit(solution)/shard_map/ppermute | solution.py:70
  86.4 12.3 %collective-permute-start.7 = (bf16[1024,256]{1,0:T(8,128)(2,1)S(1)}, bf16[1024,256]{1,0:T(8,128)(2,1)S(1)}, u32[]{:S(2)}, u32[]{:S(2)}) collective-permute-start(bf16[1024,256]{1,0:T(8,128)(2,1)S(1)} %collective-permute-done.5), channel_id=1, source_target_pairs={{0,64},{64,128},{128,192},{192,256},{256,320},{320,384},{384,448},... | collective-permute-start | bytes 1572872 | tf_op jit(solution)/shard_map/ppermute | solution.py:68
  91.6 14.6 %collective-permute-start.8 = (bf16[1024,256]{1,0:T(8,128)(2,1)S(1)}, bf16[1024,256]{1,0:T(8,128)(2,1)S(1)}, u32[]{:S(2)}, u32[]{:S(2)}) collective-permute-start(bf16[1024,256]{1,0:T(8,128)(2,1)S(1)} %collective-permute-done.6), channel_id=1, source_target_pairs={{0,448},{64,0},{128,64},{192,128},{256,192},{320,256},{384,320},{4... | collective-permute-start | bytes 1572872 | tf_op jit(solution)/shard_map/ppermute | solution.py:70
  94.3 22.9 %collective-permute-start.19 = (bf16[8,256,256]{2,1,0:T(8,128)(2,1)S(1)}, bf16[8,256,256]{2,1,0:T(8,128)(2,1)S(1)}, u32[]{:S(2)}, u32[]{:S(2)}) collective-permute-start(bf16[8,256,256]{2,1,0:T(8,128)(2,1)S(1)} %collective-permute-done.17), channel_id=1, source_target_pairs={{0,16},{16,32},{32,48},{48,0},{1,17},{17,33},{33,49},{49,1},{2,18}... | collective-permute-start | bytes 3145736 | tf_op jit(solution)/shard_map/ppermute | solution.py:68
  98.7 13.3 %collective-permute-start.9 = (bf16[1024,256]{1,0:T(8,128)(2,1)S(1)}, bf16[1024,256]{1,0:T(8,128)(2,1)S(1)}, u32[]{:S(2)}, u32[]{:S(2)}) collective-permute-start(bf16[1024,256]{1,0:T(8,128)(2,1)S(1)} %collective-permute-done.7), channel_id=1, source_target_pairs={{0,64},{64,128},{128,192},{192,256},{256,320},{320,384},{384,448},... | collective-permute-start | bytes 1572872 | tf_op jit(solution)/shard_map/ppermute | solution.py:68
  118.3 6.6 %copy-start.6 = (bf16[384,8192]{1,0:T(8,128)(2,1)S(1)}, bf16[384,8192]{1,0:T(8,128)(2,1)}, u32[]{:S(2)}) copy-start(bf16[384,8192]{1,0:T(8,128)(2,1)} %all-gather.4.cloned.1.call-done) | copy-start | bytes 18874372
  124.9 28.0 %copy-start.1 = (f32[384]{0:T(512)S(1)}, f32[384]{0:T(512)}, u32[]{:S(2)}) copy-start(f32[384]{0:T(512)} %param.13) | copy-start | bytes 4612
  124.9 28.0 %copy-start.2 = (s32[384]{0:T(512)S(1)}, s32[384]{0:T(512)}, u32[]{:S(2)}) copy-start(s32[384]{0:T(512)} %param.11) | copy-start | bytes 4612
  124.9 28.0 %copy-start.3 = (f32[384]{0:T(512)S(1)}, f32[384]{0:T(512)}, u32[]{:S(2)}) copy-start(f32[384]{0:T(512)} %param.12) | copy-start | bytes 4612
  124.9 28.0 %copy-start.4 = (f32[384]{0:T(512)S(1)}, f32[384]{0:T(512)}, u32[]{:S(2)}) copy-start(f32[384]{0:T(512)} %param.14) | copy-start | bytes 4612
  124.9 55.8 %copy-start.5 = (s32[32]{0:T(128)S(1)}, s32[32]{0:T(128)}, u32[]{:S(2)}) copy-start(s32[32]{0:T(128)} %param.15) | copy-start | bytes 388
Sparse Core Ops, SparseCore 0:
  10.2 53.8 all-gather.3

commit v6 on v3

--- a/solution.py
+++ b/solution.py
@@ -66,7 +66,7 @@
     gathered = gather_hidden(hidden)
     logits = jnp.dot(
         gathered,
-        lax.all_gather(head, ROW_AXES, axis=0, tiled=True),
+        lax.all_gather(lax.all_gather(head, "x", axis=0, tiled=True), "y", axis=0, tiled=True),
         preferred_element_type=jnp.float32,
     )
     row_peak = jnp.max(logits, axis=1)

time: 180 us -> 205 us (1.14)
  the two profiles are of different devices: /device:TPU:2 before, /device:TPU:1 now
where the time goes in v6:
time: 205 us; the launch traced here: 201 us
  waiting for transfers between devices  72.9 us (36%)
  starting transfers between devices  45.1 us (22%)
  blocking collectives  39.1 us (19%)
  local copies, waits for them, and re-layouts  18.7 us (9%)
  between operations  14.6 us (7%)
  matrix products  7.99 us (4%)
  other arithmetic  2.36 us (1%)
    all_gather x1, waiting for transfers between devices, local(): lax.all_gather(head, 'x', axis=0, tiled=True)  36.1 us
    all_gather x1, waiting for transfers between devices, local(): lax.all_gather(lax.all_gather(head, 'x', axis=0, tiled=True), 'y', axis=0...  27.7 us
    ppermute x8, starting transfers between devices, share(): other = lax.ppermute(piece, 'c', across)  22.3 us
    psum x2, blocking collectives, local(): sums = lax.psum(lax.psum(partial_sums, 'x'), 'y')  20.2 us
    all_gather x1, blocking collectives, local(): every = lax.all_gather(stats, VOCAB_AXES, axis=0, tiled=False)  18.8 us
    ppermute x3, starting transfers between devices, gather_hidden(): bwd = lax.ppermute(bwd, 'z', behind)  13.7 us
    dynamic_update_slice x16, local copies, waits for them, and re-layouts, place(): return lax.dynamic_update_slice(buf, piece, (0, slot))  13.1 us
    ppermute x4, starting transfers between devices, gather_hidden(): fwd = lax.ppermute(fwd, 'z', ahead)  9.03 us
  transfers between devices with their start and end apart: 17, of which 5 were waited for; matrix products, arithmetic and copies ran while one was open for 9% of the time, Pallas kernels for 0%

profile of v6, /device:TPU:1, one launch (start us, length us, event | category | flops | bytes accessed | tf_op | source)
XLA Modules:
  0.0 200.7 jit_solution(7501806929328468304)
XLA Ops:
  7.2 0.7 all-gather.5.cloned.1.call-update
  8.0 36.1 %all-gather.5.cloned.1.call-done = bf16[1024,512]{1,0:T(8,128)(2,1)} async-done(((bf16[256,512]{1,0:T(8,128)(2,1)}), bf16[1024,512]{1,0:T(8,128)(2,1)}) %all-gather.5.cloned.1.call-update) | async-done | bytes 1048592 | tf_op jit(solution)/shard_map/all_gather | solution.py:69
  44.0 3.3 %collective-permute-start.1 = (bf16[384,512]{1,0:T(8,128)(2,1)}, bf16[384,512]{1,0:T(8,128)(2,1)S(1)}, u32[]{:S(2)}, u32[]{:S(2)}) collective-permute-start(bf16[384,512]{1,0:T(8,128)(2,1)} %param.8), channel_id=1, source_target_pairs={{0,2},{2,4},{4,6},{6,8},{8,10},{10,12},{12,14},{14,0},{1,3},{3,5},... | collective-permute-start | bytes 1179656 | tf_op jit(solution)/shard_map/ppermute | solution.py:50
  47.3 4.2 %collective-permute-start.3 = (bf16[384,512]{1,0:T(8,128)(2,1)}, bf16[384,512]{1,0:T(8,128)(2,1)S(1)}, u32[]{:S(2)}, u32[]{:S(2)}) collective-permute-start(bf16[384,512]{1,0:T(8,128)(2,1)} %param.8), channel_id=1, source_target_pairs={{0,14},{2,0},{4,2},{6,4},{8,6},{10,8},{12,10},{14,12},{1,15},{3,1}... | collective-permute-start | bytes 1179656 | tf_op jit(solution)/shard_map/ppermute | solution.py:52
  51.6 3.8 %collective-permute-start = (bf16[384,512]{1,0:T(8,128)(2,1)}, bf16[384,512]{1,0:T(8,128)(2,1)S(1)}, u32[]{:S(2)}, u32[]{:S(2)}) collective-permute-start(bf16[384,512]{1,0:T(8,128)(2,1)} %param.8), channel_id=1, source_target_pairs={{0,1},{1,0},{2,3},{3,2},{4,5},{5,4},{6,7},{7,6},{8,9},{9,8},{10,11... | collective-permute-start | bytes 1179656 | tf_op jit(solution)/shard_map/ppermute | solution.py:42
  55.3 0.7 broadcast_subtract_fusion
  56.0 0.7 copy.22
  57.0 0.7 collective-permute-done.1
  57.7 4.1 %collective-permute-start.2 = (bf16[384,512]{1,0:T(8,128)(2,1)S(1)}, bf16[384,512]{1,0:T(8,128)(2,1)S(1)}, u32[]{:S(2)}, u32[]{:S(2)}) collective-permute-start(bf16[384,512]{1,0:T(8,128)(2,1)S(1)} %collective-permute-done.1), channel_id=1, source_target_pairs={{0,1},{1,0},{2,3},{3,2},{4,5},{5,4},{6,7},{7,6},{8,9},{9,8},{10,11... | collective-permute-start | bytes 1179656 | tf_op jit(solution)/shard_map/ppermute | solution.py:42
  61.8 1.9 collective-permute-start.5
  63.7 4.6 %collective-permute-start.7 = (bf16[384,512]{1,0:T(8,128)(2,1)S(1)}, bf16[384,512]{1,0:T(8,128)(2,1)S(1)}, u32[]{:S(2)}, u32[]{:S(2)}) collective-permute-start(bf16[384,512]{1,0:T(8,128)(2,1)S(1)} %collective-permute-done.3), channel_id=1, source_target_pairs={{0,14},{2,0},{4,2},{6,4},{8,6},{10,8},{12,10},{14,12},{1,15},{3,1}... | collective-permute-start | bytes 1179656 | tf_op jit(solution)/shard_map/ppermute | solution.py:52
  68.6 3.5 %broadcast_in_dim.4 = bf16[384,8192]{1,0:T(8,128)(2,1)} broadcast(bf16[]{:T(256)} %constant.94.clone.1), dimensions={} | broadcast | bytes 6291458 | tf_op jit(solution)/shard_map/broadcast_in_dim | solution.py:33
  72.1 0.9 constant_dynamic-update-slice_fusion.15
  72.9 2.5 %collective-permute-start.4 = (bf16[384,512]{1,0:T(8,128)(2,1)S(1)}, bf16[384,512]{1,0:T(8,128)(2,1)S(1)}, u32[]{:S(2)}, u32[]{:S(2)}) collective-permute-start(bf16[384,512]{1,0:T(8,128)(2,1)S(1)} %collective-permute-done.3), channel_id=1, source_target_pairs={{0,1},{1,0},{2,3},{3,2},{4,5},{5,4},{6,7},{7,6},{8,9},{9,8},{10,11... | collective-permute-start | bytes 1179656 | tf_op jit(solution)/shard_map/ppermute | solution.py:42
  75.4 0.9 constant_dynamic-update-slice_fusion.14
  76.3 0.8 constant_dynamic-update-slice_fusion.13
  77.1 1.9 collective-permute-start.6
  79.0 1.9 collective-permute-start.9
  80.9 2.4 %collective-permute-start.8 = (bf16[384,512]{1,0:T(8,128)(2,1)S(1)}, bf16[384,512]{1,0:T(8,128)(2,1)S(1)}, u32[]{:S(2)}, u32[]{:S(2)}) collective-permute-start(bf16[384,512]{1,0:T(8,128)(2,1)S(1)} %collective-permute-done.7), channel_id=1, source_target_pairs={{0,1},{1,0},{2,3},{3,2},{4,5},{5,4},{6,7},{7,6},{8,9},{9,8},{10,11... | collective-permute-start | bytes 1179656 | tf_op jit(solution)/shard_map/ppermute | solution.py:42
  83.4 4.9 %collective-permute-start.11 = (bf16[384,512]{1,0:T(8,128)(2,1)S(1)}, bf16[384,512]{1,0:T(8,128)(2,1)S(1)}, u32[]{:S(2)}, u32[]{:S(2)}) collective-permute-start(bf16[384,512]{1,0:T(8,128)(2,1)S(1)} %collective-permute-done.7), channel_id=1, source_target_pairs={{0,14},{2,0},{4,2},{6,4},{8,6},{10,8},{12,10},{14,12},{1,15},{3,1}... | collective-permute-start | bytes 1179656 | tf_op jit(solution)/shard_map/ppermute | solution.py:52
  88.2 0.8 constant_dynamic-update-slice_fusion.12
  89.0 0.8 constant_dynamic-update-slice_fusion.11
  89.9 0.8 constant_dynamic-update-slice_fusion.10
  90.7 0.8 constant_dynamic-update-slice_fusion.9
  91.5 0.9 collective-permute-done.9
  92.4 3.1 %collective-permute-start.10 = (bf16[384,512]{1,0:T(8,128)(2,1)S(1)}, bf16[384,512]{1,0:T(8,128)(2,1)S(1)}, u32[]{:S(2)}, u32[]{:S(2)}) collective-permute-start(bf16[384,512]{1,0:T(8,128)(2,1)S(1)} %collective-permute-done.9), channel_id=1, source_target_pairs={{0,1},{1,0},{2,3},{3,2},{4,5},{5,4},{6,7},{7,6},{8,9},{9,8},{10,11... | collective-permute-start | bytes 1179656 | tf_op jit(solution)/shard_map/ppermute | solution.py:42
  95.5 1.9 collective-permute-start.13
  97.5 1.9 collective-permute-start.12
  99.5 0.8 constant_dynamic-update-slice_fusion.8
  100.3 0.8 constant_dynamic-update-slice_fusion.7
  101.1 0.8 constant_dynamic-update-slice_fusion.6
  101.9 0.8 constant_dynamic-update-slice_fusion.5
  102.7 6.8 %collective-permute-done.13 = bf16[384,512]{1,0:T(8,128)(2,1)S(1)} collective-permute-done((bf16[384,512]{1,0:T(8,128)(2,1)S(1)}, bf16[384,512]{1,0:T(8,128)(2,1)S(1)}, u32[]{:S(2)}, u32[]{:S(2)}) %collective-permute-start.13) | collective-permute-done | bytes 393248 | tf_op jit(solution)/shard_map/ppermute | solution.py:50
  109.5 2.6 %collective-permute-start.14 = (bf16[384,512]{1,0:T(8,128)(2,1)S(1)}, bf16[384,512]{1,0:T(8,128)(2,1)S(1)}, u32[]{:S(2)}, u32[]{:S(2)}) collective-permute-start(bf16[384,512]{1,0:T(8,128)(2,1)S(1)} %collective-permute-done.13), channel_id=1, source_target_pairs={{0,1},{1,0},{2,3},{3,2},{4,5},{5,4},{6,7},{7,6},{8,9},{9,8},{10,11... | collective-permute-start | bytes 1179656 | tf_op jit(solution)/shard_map/ppermute | solution.py:42
  112.1 0.8 constant_dynamic-update-slice_fusion.4
  112.9 0.8 constant_dynamic-update-slice_fusion.3
  113.7 0.8 constant_dynamic-update-slice_fusion.2
  114.5 0.8 constant_dynamic-update-slice_fusion.1
  115.3 0.8 constant_dynamic-update-slice_fusion
  116.2 27.7 %all-gather.7.cloned.1.call-done = bf16[8192,512]{1,0:T(8,128)(2,1)} async-done(((bf16[1024,512]{1,0:T(8,128)(2,1)}), bf16[8192,512]{1,0:T(8,128)(2,1)}) %all-gather.7.cloned.1.call-update) | async-done | bytes 8388624 | tf_op jit(solution)/shard_map/all_gather | solution.py:69
  143.9 8.0 %fusion.7 = (f32[384]{0:T(512)S(1)}, f32[384,512]{1,0:T(8,128)S(1)}) fusion(bf16[384,8192]{1,0:T(8,128)(2,1)} %constant_dynamic-update-slice_fusion, bf16[8192,512]{1,0:T(8,128)(2,1)} %all-gather.7.cloned.1.call-done), kind=kOutput, calls=%fused_computation.46 | convolution fusion | flops 3221421568 | bytes 15468032 | tf_op jit(solution)/shard_map/dot_general | solution.py:67
  151.9 0.5 fusion
  152.4 18.8 %all-gather.1 = f32[16,4,384]{2,1,0:T(4,128)S(1)} all-gather(f32[1,4,384]{2,1,0:T(4,128)S(1)} %maximum_bitcast_fusion), channel_id=2, replica_groups=mesh['y'=8,'x'=4,'z'=8,'c'=2] {'z','c'}, dimensions={0}, use_global_device_ids=true | all-gather | bytes 104448 | tf_op jit(solution)/shard_map/all_gather | solution.py:81
  171.6 8.4 %psum.14 = f32[32]{0:T(128)S(1)} all-reduce(f32[32]{0:T(128)S(1)} %select_reduce_fusion.1), channel_id=1, replica_groups=mesh['y'=8,'x'=4,'z'=8,'c'=2] {'x'}, use_global_device_ids=true, to_apply=%region_11.12 | all-reduce | flops 32 | bytes 256 | tf_op jit(solution)/shard_map/psum | solution.py:103
  180.0 11.8 %psum.15 = f32[32]{0:T(128)S(1)} all-reduce(f32[32]{0:T(128)S(1)} %psum.14), channel_id=1, replica_groups=mesh['y'=8,'x'=4,'z'=8,'c'=2] {'y'}, use_global_device_ids=true, to_apply=%region_12.13 | all-reduce | flops 32 | bytes 256 | tf_op jit(solution)/shard_map/psum | solution.py:103
  192.2 0.5 sub.73
  192.7 0.6 dynamic_slice.6
  193.3 0.6 dynamic_slice.7
  (48 shorter events, 1.1 us)
Async XLA Ops:
  7.2 64.9 %copy-start = (bf16[384,512]{1,0:T(8,128)(2,1)S(1)}, bf16[384,512]{1,0:T(8,128)(2,1)}, u32[]{:S(2)}) copy-start(bf16[384,512]{1,0:T(8,128)(2,1)} %param.8) | copy-start | bytes 1179652
  7.2 36.8 %all-gather.5.cloned.1.call-start = ((), (), s32[]{:S(2)}) async-start(), calls=%async_computation | async-start | bytes 1310720 | tf_op jit(solution)/shard_map/all_gather | solution.py:69
  7.9 136.0 %all-gather.7.cloned.1.call-start = ((), (), s32[]{:S(2)}) async-start(), calls=%async_computation.1 | async-start | bytes 9437184 | tf_op jit(solution)/shard_map/all_gather | solution.py:69
  44.0 13.6 %collective-permute-start.1 = (bf16[384,512]{1,0:T(8,128)(2,1)}, bf16[384,512]{1,0:T(8,128)(2,1)S(1)}, u32[]{:S(2)}, u32[]{:S(2)}) collective-permute-start(bf16[384,512]{1,0:T(8,128)(2,1)} %param.8), channel_id=1, source_target_pairs={{0,2},{2,4},{4,6},{6,8},{8,10},{10,12},{12,14},{14,0},{1,3},{3,5},... | collective-permute-start | bytes 1179656 | tf_op jit(solution)/shard_map/ppermute | solution.py:50
  47.3 16.4 %collective-permute-start.3 = (bf16[384,512]{1,0:T(8,128)(2,1)}, bf16[384,512]{1,0:T(8,128)(2,1)S(1)}, u32[]{:S(2)}, u32[]{:S(2)}) collective-permute-start(bf16[384,512]{1,0:T(8,128)(2,1)} %param.8), channel_id=1, source_target_pairs={{0,14},{2,0},{4,2},{6,4},{8,6},{10,8},{12,10},{14,12},{1,15},{3,1}... | collective-permute-start | bytes 1179656 | tf_op jit(solution)/shard_map/ppermute | solution.py:52
  51.6 23.8 %collective-permute-start = (bf16[384,512]{1,0:T(8,128)(2,1)}, bf16[384,512]{1,0:T(8,128)(2,1)S(1)}, u32[]{:S(2)}, u32[]{:S(2)}) collective-permute-start(bf16[384,512]{1,0:T(8,128)(2,1)} %param.8), channel_id=1, source_target_pairs={{0,1},{1,0},{2,3},{3,2},{4,5},{5,4},{6,7},{7,6},{8,9},{9,8},{10,11... | collective-permute-start | bytes 1179656 | tf_op jit(solution)/shard_map/ppermute | solution.py:42
  57.7 25.7 %collective-permute-start.2 = (bf16[384,512]{1,0:T(8,128)(2,1)S(1)}, bf16[384,512]{1,0:T(8,128)(2,1)S(1)}, u32[]{:S(2)}, u32[]{:S(2)}) collective-permute-start(bf16[384,512]{1,0:T(8,128)(2,1)S(1)} %collective-permute-done.1), channel_id=1, source_target_pairs={{0,1},{1,0},{2,3},{3,2},{4,5},{5,4},{6,7},{7,6},{8,9},{9,8},{10,11... | collective-permute-start | bytes 1179656 | tf_op jit(solution)/shard_map/ppermute | solution.py:42
  61.8 15.3 %collective-permute-start.5 = (bf16[384,512]{1,0:T(8,128)(2,1)S(1)}, bf16[384,512]{1,0:T(8,128)(2,1)S(1)}, u32[]{:S(2)}, u32[]{:S(2)}) collective-permute-start(bf16[384,512]{1,0:T(8,128)(2,1)S(1)} %collective-permute-done.1), channel_id=1, source_target_pairs={{0,2},{2,4},{4,6},{6,8},{8,10},{10,12},{12,14},{14,0},{1,3},{3,5},... | collective-permute-start | bytes 1179656 | tf_op jit(solution)/shard_map/ppermute | solution.py:50
  63.7 17.2 %collective-permute-start.7 = (bf16[384,512]{1,0:T(8,128)(2,1)S(1)}, bf16[384,512]{1,0:T(8,128)(2,1)S(1)}, u32[]{:S(2)}, u32[]{:S(2)}) collective-permute-start(bf16[384,512]{1,0:T(8,128)(2,1)S(1)} %collective-permute-done.3), channel_id=1, source_target_pairs={{0,14},{2,0},{4,2},{6,4},{8,6},{10,8},{12,10},{14,12},{1,15},{3,1}... | collective-permute-start | bytes 1179656 | tf_op jit(solution)/shard_map/ppermute | solution.py:52
  72.9 16.9 %collective-permute-start.4 = (bf16[384,512]{1,0:T(8,128)(2,1)S(1)}, bf16[384,512]{1,0:T(8,128)(2,1)S(1)}, u32[]{:S(2)}, u32[]{:S(2)}) collective-permute-start(bf16[384,512]{1,0:T(8,128)(2,1)S(1)} %collective-permute-done.3), channel_id=1, source_target_pairs={{0,1},{1,0},{2,3},{3,2},{4,5},{5,4},{6,7},{7,6},{8,9},{9,8},{10,11... | collective-permute-start | bytes 1179656 | tf_op jit(solution)/shard_map/ppermute | solution.py:42
  77.1 22.4 %collective-permute-start.6 = (bf16[384,512]{1,0:T(8,128)(2,1)S(1)}, bf16[384,512]{1,0:T(8,128)(2,1)S(1)}, u32[]{:S(2)}, u32[]{:S(2)}) collective-permute-start(bf16[384,512]{1,0:T(8,128)(2,1)S(1)} %collective-permute-done.5), channel_id=1, source_target_pairs={{0,1},{1,0},{2,3},{3,2},{4,5},{5,4},{6,7},{7,6},{8,9},{9,8},{10,11... | collective-permute-start | bytes 1179656 | tf_op jit(solution)/shard_map/ppermute | solution.py:42
  79.0 13.4 %collective-permute-start.9 = (bf16[384,512]{1,0:T(8,128)(2,1)S(1)}, bf16[384,512]{1,0:T(8,128)(2,1)S(1)}, u32[]{:S(2)}, u32[]{:S(2)}) collective-permute-start(bf16[384,512]{1,0:T(8,128)(2,1)S(1)} %collective-permute-done.5), channel_id=1, source_target_pairs={{0,2},{2,4},{4,6},{6,8},{8,10},{10,12},{12,14},{14,0},{1,3},{3,5},... | collective-permute-start | bytes 1179656 | tf_op jit(solution)/shard_map/ppermute | solution.py:50
  80.9 20.1 %collective-permute-start.8 = (bf16[384,512]{1,0:T(8,128)(2,1)S(1)}, bf16[384,512]{1,0:T(8,128)(2,1)S(1)}, u32[]{:S(2)}, u32[]{:S(2)}) collective-permute-start(bf16[384,512]{1,0:T(8,128)(2,1)S(1)} %collective-permute-done.7), channel_id=1, source_target_pairs={{0,1},{1,0},{2,3},{3,2},{4,5},{5,4},{6,7},{7,6},{8,9},{9,8},{10,11... | collective-permute-start | bytes 1179656 | tf_op jit(solution)/shard_map/ppermute | solution.py:42
  83.4 14.1 %collective-permute-start.11 = (bf16[384,512]{1,0:T(8,128)(2,1)S(1)}, bf16[384,512]{1,0:T(8,128)(2,1)S(1)}, u32[]{:S(2)}, u32[]{:S(2)}) collective-permute-start(bf16[384,512]{1,0:T(8,128)(2,1)S(1)} %collective-permute-done.7), channel_id=1, source_target_pairs={{0,14},{2,0},{4,2},{6,4},{8,6},{10,8},{12,10},{14,12},{1,15},{3,1}... | collective-permute-start | bytes 1179656 | tf_op jit(solution)/shard_map/ppermute | solution.py:52
  92.4 19.7 %collective-permute-start.10 = (bf16[384,512]{1,0:T(8,128)(2,1)S(1)}, bf16[384,512]{1,0:T(8,128)(2,1)S(1)}, u32[]{:S(2)}, u32[]{:S(2)}) collective-permute-start(bf16[384,512]{1,0:T(8,128)(2,1)S(1)} %collective-permute-done.9), channel_id=1, source_target_pairs={{0,1},{1,0},{2,3},{3,2},{4,5},{5,4},{6,7},{7,6},{8,9},{9,8},{10,11... | collective-permute-start | bytes 1179656 | tf_op jit(solution)/shard_map/ppermute | solution.py:42
  95.5 13.9 %collective-permute-start.13 = (bf16[384,512]{1,0:T(8,128)(2,1)S(1)}, bf16[384,512]{1,0:T(8,128)(2,1)S(1)}, u32[]{:S(2)}, u32[]{:S(2)}) collective-permute-start(bf16[384,512]{1,0:T(8,128)(2,1)S(1)} %collective-permute-done.9), channel_id=1, source_target_pairs={{0,2},{2,4},{4,6},{6,8},{8,10},{10,12},{12,14},{14,0},{1,3},{3,5},... | collective-permute-start | bytes 1179656 | tf_op jit(solution)/shard_map/ppermute | solution.py:50
  97.5 16.2 %collective-permute-start.12 = (bf16[384,512]{1,0:T(8,128)(2,1)S(1)}, bf16[384,512]{1,0:T(8,128)(2,1)S(1)}, u32[]{:S(2)}, u32[]{:S(2)}) collective-permute-start(bf16[384,512]{1,0:T(8,128)(2,1)S(1)} %collective-permute-done.11), channel_id=1, source_target_pairs={{0,1},{1,0},{2,3},{3,2},{4,5},{5,4},{6,7},{7,6},{8,9},{9,8},{10,11... | collective-permute-start | bytes 1179656 | tf_op jit(solution)/shard_map/ppermute | solution.py:42
  109.5 5.9 %collective-permute-start.14 = (bf16[384,512]{1,0:T(8,128)(2,1)S(1)}, bf16[384,512]{1,0:T(8,128)(2,1)S(1)}, u32[]{:S(2)}, u32[]{:S(2)}) collective-permute-start(bf16[384,512]{1,0:T(8,128)(2,1)S(1)} %collective-permute-done.13), channel_id=1, source_target_pairs={{0,1},{1,0},{2,3},{3,2},{4,5},{5,4},{6,7},{7,6},{8,9},{9,8},{10,11... | collective-permute-start | bytes 1179656 | tf_op jit(solution)/shard_map/ppermute | solution.py:42
  116.1 55.2 %copy-start.1 = (s32[384]{0:T(512)S(1)}, s32[384]{0:T(512)}, u32[]{:S(2)}) copy-start(s32[384]{0:T(512)} %param.10) | copy-start | bytes 4612
  116.1 55.3 %copy-start.2 = (f32[384]{0:T(512)S(1)}, f32[384]{0:T(512)}, u32[]{:S(2)}) copy-start(f32[384]{0:T(512)} %param.13) | copy-start | bytes 4612
  116.1 55.3 %copy-start.3 = (s32[384]{0:T(512)S(1)}, s32[384]{0:T(512)}, u32[]{:S(2)}) copy-start(s32[384]{0:T(512)} %param.11) | copy-start | bytes 4612
  116.1 55.3 %copy-start.4 = (f32[384]{0:T(512)S(1)}, f32[384]{0:T(512)}, u32[]{:S(2)}) copy-start(f32[384]{0:T(512)} %param.12) | copy-start | bytes 4612
  116.1 55.3 %copy-start.5 = (f32[384]{0:T(512)S(1)}, f32[384]{0:T(512)}, u32[]{:S(2)}) copy-start(f32[384]{0:T(512)} %param.14) | copy-start | bytes 4612
  116.2 75.6 %copy-start.6 = (s32[32]{0:T(128)S(1)}, s32[32]{0:T(128)}, u32[]{:S(2)}) copy-start(s32[32]{0:T(128)} %param.15) | copy-start | bytes 388
Sparse Core Ops, SparseCore 0:
  10.1 33.8 all-gather.4
  46.1 97.7 all-gather.6

commit v7 on v3

--- a/solution.py
+++ b/solution.py
@@ -56,6 +56,15 @@
     return full
 
 
+def butterfly_sum(value, axis):
+    n = lax.axis_size(axis)
+    step = 1
+    while step < n:
+        value = value + lax.ppermute(value, axis, [(i, i ^ step) for i in range(n)])
+        step *= 2
+    return value
+
+
 def local(hidden, head, targets, live, prior_lse, prior_mean, prior_target, seq_lengths):
     rows_here = hidden.shape[0]
     cols_here = head.shape[1]
@@ -78,7 +87,9 @@
     picked = jnp.sum(jnp.where(columns == column[:, None], logits, jnp.zeros_like(logits)), axis=1)
 
     stats = jnp.stack([row_peak, row_mass, moment, picked])
-    every = lax.all_gather(stats, VOCAB_AXES, axis=0, tiled=False)
+    slots = jnp.zeros((spread,) + stats.shape, stats.dtype)
+    every = lax.dynamic_update_slice(slots, stats[None], (which, 0, 0))
+    every = butterfly_sum(butterfly_sum(every, "c"), "z")
     peaks = every[:, 0]
     highest = jnp.max(peaks, axis=0)
     factor = jnp.exp(peaks - highest[None, :])
@@ -100,7 +111,7 @@
     member = jnp.sum((global_rows[:, None] >= endings[None, :]).astype(jnp.int32), axis=1)
     onehot = (member[:, None] == jnp.arange(SEQS, dtype=jnp.int32)[None, :]).astype(jnp.float32)
     partial_sums = jnp.sum(onehot * logprob[:, None], axis=0)
-    sums = lax.psum(lax.psum(partial_sums, "x"), "y")
+    sums = butterfly_sum(butterfly_sum(partial_sums, "x"), "y")
     seq_mean = sums / seq_lengths.astype(jnp.float32)
     grouped = seq_mean.reshape(SEQS // GSIZE, GSIZE)
     seq_score = (grouped - jnp.mean(grouped, axis=1, keepdims=True)).reshape(SEQS)

time: 180 us -> 200 us (1.11)
  the two profiles are of different devices: /device:TPU:2 before, /device:TPU:24 now
where the time goes in v7:
time: 200 us
  waiting for transfers between devices  80.6 us (40%)
  starting transfers between devices  75.9 us (38%)
  local copies, waits for them, and re-layouts  18.2 us (9%)
  between operations  14.5 us (7%)
  matrix products  8 us (4%)
  other arithmetic  2.36 us (1%)
    all_gather x1, waiting for transfers between devices, local(): lax.all_gather(head, ROW_AXES, axis=0, tiled=True)  33.9 us
    ppermute x9, waiting for transfers between devices, butterfly_sum(): value = value + lax.ppermute(value, axis, [(i, i ^ step) for i in range(n)])  31.6 us
    ppermute x9, starting transfers between devices, butterfly_sum(): value = value + lax.ppermute(value, axis, [(i, i ^ step) for i in range(n)])  30.7 us
    ppermute x3, starting transfers between devices, gather_hidden(): bwd = lax.ppermute(bwd, 'z', behind)  18.9 us
    ppermute x8, starting transfers between devices, share(): other = lax.ppermute(piece, 'c', across)  16.2 us
    ppermute x4, waiting for transfers between devices, gather_hidden(): fwd = lax.ppermute(fwd, 'z', ahead)  14.3 us
    dynamic_update_slice x16, local copies, waits for them, and re-layouts, place(): return lax.dynamic_update_slice(buf, piece, (0, slot))  13.1 us
    ppermute x4, starting transfers between devices, gather_hidden(): fwd = lax.ppermute(fwd, 'z', ahead)  10 us
  transfers between devices with their start and end apart: 25, of which 14 were waited for; matrix products, arithmetic and copies ran while one was open for 9% of the time, Pallas kernels for 0%

profile of v7, /device:TPU:24, one launch (start us, length us, event | category | flops | bytes accessed | tf_op | source)
XLA Modules:
  0.0 199.5 jit_solution(202787692359542829)
XLA Ops:
  7.9 4.3 %collective-permute-start.1 = (bf16[384,512]{1,0:T(8,128)(2,1)}, bf16[384,512]{1,0:T(8,128)(2,1)S(1)}, u32[]{:S(2)}, u32[]{:S(2)}) collective-permute-start(bf16[384,512]{1,0:T(8,128)(2,1)} %param.8), channel_id=1, source_target_pairs={{0,2},{2,4},{4,6},{6,8},{8,10},{10,12},{12,14},{14,0},{1,3},{3,5},... | collective-permute-start | bytes 1179656 | tf_op jit(solution)/shard_map/ppermute | solution.py:50
  12.2 8.6 %collective-permute-start.3 = (bf16[384,512]{1,0:T(8,128)(2,1)}, bf16[384,512]{1,0:T(8,128)(2,1)S(1)}, u32[]{:S(2)}, u32[]{:S(2)}) collective-permute-start(bf16[384,512]{1,0:T(8,128)(2,1)} %param.8), channel_id=1, source_target_pairs={{0,14},{2,0},{4,2},{6,4},{8,6},{10,8},{12,10},{14,12},{1,15},{3,1}... | collective-permute-start | bytes 1179656 | tf_op jit(solution)/shard_map/ppermute | solution.py:52
  20.8 1.9 collective-permute-start
  22.7 5.4 %collective-permute-done.1 = bf16[384,512]{1,0:T(8,128)(2,1)S(1)} collective-permute-done((bf16[384,512]{1,0:T(8,128)(2,1)}, bf16[384,512]{1,0:T(8,128)(2,1)S(1)}, u32[]{:S(2)}, u32[]{:S(2)}) %collective-permute-start.1) | collective-permute-done | bytes 393248 | tf_op jit(solution)/shard_map/ppermute | solution.py:50
  28.2 1.9 collective-permute-start.2
  30.1 1.9 collective-permute-start.5
  32.0 5.1 %collective-permute-start.7 = (bf16[384,512]{1,0:T(8,128)(2,1)S(1)}, bf16[384,512]{1,0:T(8,128)(2,1)S(1)}, u32[]{:S(2)}, u32[]{:S(2)}) collective-permute-start(bf16[384,512]{1,0:T(8,128)(2,1)S(1)} %collective-permute-done.3), channel_id=1, source_target_pairs={{0,14},{2,0},{4,2},{6,4},{8,6},{10,8},{12,10},{14,12},{1,15},{3,1}... | collective-permute-start | bytes 1179656 | tf_op jit(solution)/shard_map/ppermute | solution.py:52
  37.9 3.5 %broadcast_in_dim.9 = bf16[384,8192]{1,0:T(8,128)(2,1)} broadcast(bf16[]{:T(256)} %constant.97.clone.1), dimensions={} | broadcast | bytes 6291458 | tf_op jit(solution)/shard_map/broadcast_in_dim | solution.py:33
  41.3 0.8 constant_dynamic-update-slice_fusion.15
  42.2 1.9 collective-permute-start.4
  44.1 0.9 constant_dynamic-update-slice_fusion.14
  44.9 0.9 constant_dynamic-update-slice_fusion.13
  45.8 2.4 %collective-permute-start.6 = (bf16[384,512]{1,0:T(8,128)(2,1)S(1)}, bf16[384,512]{1,0:T(8,128)(2,1)S(1)}, u32[]{:S(2)}, u32[]{:S(2)}) collective-permute-start(bf16[384,512]{1,0:T(8,128)(2,1)S(1)} %collective-permute-done.5), channel_id=1, source_target_pairs={{0,1},{1,0},{2,3},{3,2},{4,5},{5,4},{6,7},{7,6},{8,9},{9,8},{10,11... | collective-permute-start | bytes 1179656 | tf_op jit(solution)/shard_map/ppermute | solution.py:42
  48.2 1.9 collective-permute-start.9
  50.1 1.9 collective-permute-start.8
  52.1 5.1 %collective-permute-start.11 = (bf16[384,512]{1,0:T(8,128)(2,1)S(1)}, bf16[384,512]{1,0:T(8,128)(2,1)S(1)}, u32[]{:S(2)}, u32[]{:S(2)}) collective-permute-start(bf16[384,512]{1,0:T(8,128)(2,1)S(1)} %collective-permute-done.7), channel_id=1, source_target_pairs={{0,14},{2,0},{4,2},{6,4},{8,6},{10,8},{12,10},{14,12},{1,15},{3,1}... | collective-permute-start | bytes 1179656 | tf_op jit(solution)/shard_map/ppermute | solution.py:52
  57.2 0.9 constant_dynamic-update-slice_fusion.12
  58.1 0.8 constant_dynamic-update-slice_fusion.11
  58.9 0.8 constant_dynamic-update-slice_fusion.10
  60.5 1.8 collective-permute-done.9
  62.3 1.9 collective-permute-start.10
  64.3 1.9 collective-permute-start.13
  66.2 2.4 %collective-permute-start.12 = (bf16[384,512]{1,0:T(8,128)(2,1)S(1)}, bf16[384,512]{1,0:T(8,128)(2,1)S(1)}, u32[]{:S(2)}, u32[]{:S(2)}) collective-permute-start(bf16[384,512]{1,0:T(8,128)(2,1)S(1)} %collective-permute-done.11), channel_id=1, source_target_pairs={{0,1},{1,0},{2,3},{3,2},{4,5},{5,4},{6,7},{7,6},{8,9},{9,8},{10,11... | collective-permute-start | bytes 1179656 | tf_op jit(solution)/shard_map/ppermute | solution.py:42
  68.6 0.8 constant_dynamic-update-slice_fusion.8
  70.2 0.8 constant_dynamic-update-slice_fusion.6
  71.9 7.0 %collective-permute-done.13 = bf16[384,512]{1,0:T(8,128)(2,1)S(1)} collective-permute-done((bf16[384,512]{1,0:T(8,128)(2,1)S(1)}, bf16[384,512]{1,0:T(8,128)(2,1)S(1)}, u32[]{:S(2)}, u32[]{:S(2)}) %collective-permute-start.13) | collective-permute-done | bytes 393248 | tf_op jit(solution)/shard_map/ppermute | solution.py:50
  78.9 1.9 collective-permute-start.14
  82.4 0.8 constant_dynamic-update-slice_fusion.2
  84.9 33.9 %all-gather.2.cloned.1.call-done = bf16[8192,512]{1,0:T(8,128)(2,1)} async-done(((bf16[256,512]{1,0:T(8,128)(2,1)}), bf16[8192,512]{1,0:T(8,128)(2,1)}) %all-gather.2.cloned.1.call-update) | async-done | bytes 8388624 | tf_op jit(solution)/shard_map/all_gather | solution.py:78
  118.8 8.0 %fusion.6 = (f32[384]{0:T(512)S(1)}, f32[384,512]{1,0:T(8,128)S(1)}) fusion(bf16[384,8192]{1,0:T(8,128)(2,1)} %constant_dynamic-update-slice_fusion, bf16[8192,512]{1,0:T(8,128)(2,1)} %all-gather.2.cloned.1.call-done), kind=kOutput, calls=%fused_computation.46 | convolution fusion | flops 3221421568 | bytes 15468032 | tf_op jit(solution)/shard_map/dot_general | solution.py:76
  127.4 1.9 collective-permute-start.15
  129.4 1.3 collective-permute-done.15
  130.7 3.6 %collective-permute-start.16 = (f32[16,4,384]{2,0,1:T(8,128)S(1)}, f32[16,4,384]{2,0,1:T(8,128)S(1)}, u32[]{:S(2)}, u32[]{:S(2)}) collective-permute-start(f32[16,4,384]{2,0,1:T(8,128)S(1)} %add.258), channel_id=1, source_target_pairs={{0,2},{2,0},{4,6},{6,4},{8,10},{10,8},{12,14},{14,12},{1,3},{3,1},... | collective-permute-start | bytes 294920 | tf_op jit(solution)/shard_map/ppermute | solution.py:63
  134.6 2.9 %collective-permute-done.16 = f32[16,4,384]{2,0,1:T(8,128)S(1)} collective-permute-done((f32[16,4,384]{2,0,1:T(8,128)S(1)}, f32[16,4,384]{2,0,1:T(8,128)S(1)}, u32[]{:S(2)}, u32[]{:S(2)}) %collective-permute-start.16) | collective-permute-done | bytes 98336 | tf_op jit(solution)/shard_map/ppermute | solution.py:63
  137.5 4.6 %collective-permute-start.17 = (f32[16,4,384]{2,0,1:T(8,128)S(1)}, f32[16,4,384]{2,0,1:T(8,128)S(1)}, u32[]{:S(2)}, u32[]{:S(2)}) collective-permute-start(f32[16,4,384]{2,0,1:T(8,128)S(1)} %add.259), channel_id=1, source_target_pairs={{0,4},{2,6},{4,0},{6,2},{8,12},{10,14},{12,8},{14,10},{1,5},{3,7},... | collective-permute-start | bytes 294920 | tf_op jit(solution)/shard_map/ppermute | solution.py:63
  142.1 4.4 %collective-permute-done.17 = f32[16,4,384]{2,0,1:T(8,128)S(1)} collective-permute-done((f32[16,4,384]{2,0,1:T(8,128)S(1)}, f32[16,4,384]{2,0,1:T(8,128)S(1)}, u32[]{:S(2)}, u32[]{:S(2)}) %collective-permute-start.17) | collective-permute-done | bytes 98336 | tf_op jit(solution)/shard_map/ppermute | solution.py:63
  146.6 7.9 %collective-permute-start.18 = (f32[16,4,384]{2,0,1:T(8,128)S(1)}, f32[16,4,384]{2,0,1:T(8,128)S(1)}, u32[]{:S(2)}, u32[]{:S(2)}) collective-permute-start(f32[16,4,384]{2,0,1:T(8,128)S(1)} %add.260), channel_id=1, source_target_pairs={{0,8},{2,10},{4,12},{6,14},{8,0},{10,2},{12,4},{14,6},{1,9},{3,11}... | collective-permute-start | bytes 294920 | tf_op jit(solution)/shard_map/ppermute | solution.py:63
  154.5 3.5 %collective-permute-done.18 = f32[16,4,384]{2,0,1:T(8,128)S(1)} collective-permute-done((f32[16,4,384]{2,0,1:T(8,128)S(1)}, f32[16,4,384]{2,0,1:T(8,128)S(1)}, u32[]{:S(2)}, u32[]{:S(2)}) %collective-permute-start.18) | collective-permute-done | bytes 98336 | tf_op jit(solution)/shard_map/ppermute | solution.py:63
  158.3 2.1 %collective-permute-start.19 = (f32[32]{0:T(128)S(1)}, f32[32]{0:T(128)S(1)}, u32[]{:S(2)}, u32[]{:S(2)}) collective-permute-start(f32[32]{0:T(128)S(1)} %select_reduce_fusion.1), channel_id=1, source_target_pairs={{0,16},{16,0},{32,48},{48,32},{1,17},{17,1},{33,49},{49,33},{2,18}... | collective-permute-start | bytes 392 | tf_op jit(solution)/shard_map/ppermute | solution.py:63
  160.5 3.3 %collective-permute-done.19 = f32[32]{0:T(128)S(1)} collective-permute-done((f32[32]{0:T(128)S(1)}, f32[32]{0:T(128)S(1)}, u32[]{:S(2)}, u32[]{:S(2)}) %collective-permute-start.19) | collective-permute-done | bytes 160 | tf_op jit(solution)/shard_map/ppermute | solution.py:63
  163.8 3.3 %collective-permute-start.20 = (f32[32]{0:T(128)S(1)}, f32[32]{0:T(128)S(1)}, u32[]{:S(2)}, u32[]{:S(2)}) collective-permute-start(f32[32]{0:T(128)S(1)} %add.269), channel_id=1, source_target_pairs={{0,32},{16,48},{32,0},{48,16},{1,33},{17,49},{33,1},{49,17},{2,34}... | collective-permute-start | bytes 392 | tf_op jit(solution)/shard_map/ppermute | solution.py:63
  167.1 3.6 %collective-permute-done.20 = f32[32]{0:T(128)S(1)} collective-permute-done((f32[32]{0:T(128)S(1)}, f32[32]{0:T(128)S(1)}, u32[]{:S(2)}, u32[]{:S(2)}) %collective-permute-start.20) | collective-permute-done | bytes 160 | tf_op jit(solution)/shard_map/ppermute | solution.py:63
  170.7 1.9 collective-permute-start.21
  172.6 3.5 %collective-permute-done.21 = f32[32]{0:T(128)S(1)} collective-permute-done((f32[32]{0:T(128)S(1)}, f32[32]{0:T(128)S(1)}, u32[]{:S(2)}, u32[]{:S(2)}) %collective-permute-start.21) | collective-permute-done | bytes 160 | tf_op jit(solution)/shard_map/ppermute | solution.py:63
  176.1 1.9 collective-permute-start.22
  178.6 3.8 %collective-permute-done.22 = f32[32]{0:T(128)S(1)} collective-permute-done((f32[32]{0:T(128)S(1)}, f32[32]{0:T(128)S(1)}, u32[]{:S(2)}, u32[]{:S(2)}) %collective-permute-start.22) | collective-permute-done | bytes 160 | tf_op jit(solution)/shard_map/ppermute | solution.py:63
  182.5 3.4 %collective-permute-start.23 = (f32[32]{0:T(128)S(1)}, f32[32]{0:T(128)S(1)}, u32[]{:S(2)}, u32[]{:S(2)}) collective-permute-start(f32[32]{0:T(128)S(1)} %add.272), channel_id=1, source_target_pairs={{0,256},{64,320},{128,384},{192,448},{256,0},{320,64},{384,128},{4... | collective-permute-start | bytes 392 | tf_op jit(solution)/shard_map/ppermute | solution.py:63
  186.5 5.3 %collective-permute-done.23 = f32[32]{0:T(128)S(1)} collective-permute-done((f32[32]{0:T(128)S(1)}, f32[32]{0:T(128)S(1)}, u32[]{:S(2)}, u32[]{:S(2)}) %collective-permute-start.23) | collective-permute-done | bytes 160 | tf_op jit(solution)/shard_map/ppermute | solution.py:63
  (72 shorter events, 10.4 us)
Async XLA Ops:
  7.2 34.1 %copy-start = (bf16[384,512]{1,0:T(8,128)(2,1)S(1)}, bf16[384,512]{1,0:T(8,128)(2,1)}, u32[]{:S(2)}) copy-start(bf16[384,512]{1,0:T(8,128)(2,1)} %param.8) | copy-start | bytes 1179652
  7.2 111.6 %all-gather.2.cloned.1.call-start = ((), (), s32[]{:S(2)}) async-start(), calls=%async_computation | async-start | bytes 8650752 | tf_op jit(solution)/shard_map/all_gather | solution.py:78
  7.9 20.3 %collective-permute-start.1 = (bf16[384,512]{1,0:T(8,128)(2,1)}, bf16[384,512]{1,0:T(8,128)(2,1)S(1)}, u32[]{:S(2)}, u32[]{:S(2)}) collective-permute-start(bf16[384,512]{1,0:T(8,128)(2,1)} %param.8), channel_id=1, source_target_pairs={{0,2},{2,4},{4,6},{6,8},{8,10},{10,12},{12,14},{14,0},{1,3},{3,5},... | collective-permute-start | bytes 1179656 | tf_op jit(solution)/shard_map/ppermute | solution.py:50
  12.2 19.8 %collective-permute-start.3 = (bf16[384,512]{1,0:T(8,128)(2,1)}, bf16[384,512]{1,0:T(8,128)(2,1)S(1)}, u32[]{:S(2)}, u32[]{:S(2)}) collective-permute-start(bf16[384,512]{1,0:T(8,128)(2,1)} %param.8), channel_id=1, source_target_pairs={{0,14},{2,0},{4,2},{6,4},{8,6},{10,8},{12,10},{14,12},{1,15},{3,1}... | collective-permute-start | bytes 1179656 | tf_op jit(solution)/shard_map/ppermute | solution.py:52
  20.8 23.3 %collective-permute-start = (bf16[384,512]{1,0:T(8,128)(2,1)}, bf16[384,512]{1,0:T(8,128)(2,1)S(1)}, u32[]{:S(2)}, u32[]{:S(2)}) collective-permute-start(bf16[384,512]{1,0:T(8,128)(2,1)} %param.8), channel_id=1, source_target_pairs={{0,1},{1,0},{2,3},{3,2},{4,5},{5,4},{6,7},{7,6},{8,9},{9,8},{10,11... | collective-permute-start | bytes 1179656 | tf_op jit(solution)/shard_map/ppermute | solution.py:42
  28.2 23.9 %collective-permute-start.2 = (bf16[384,512]{1,0:T(8,128)(2,1)S(1)}, bf16[384,512]{1,0:T(8,128)(2,1)S(1)}, u32[]{:S(2)}, u32[]{:S(2)}) collective-permute-start(bf16[384,512]{1,0:T(8,128)(2,1)S(1)} %collective-permute-done.1), channel_id=1, source_target_pairs={{0,1},{1,0},{2,3},{3,2},{4,5},{5,4},{6,7},{7,6},{8,9},{9,8},{10,11... | collective-permute-start | bytes 1179656 | tf_op jit(solution)/shard_map/ppermute | solution.py:42
  30.1 15.7 %collective-permute-start.5 = (bf16[384,512]{1,0:T(8,128)(2,1)S(1)}, bf16[384,512]{1,0:T(8,128)(2,1)S(1)}, u32[]{:S(2)}, u32[]{:S(2)}) collective-permute-start(bf16[384,512]{1,0:T(8,128)(2,1)S(1)} %collective-permute-done.1), channel_id=1, source_target_pairs={{0,2},{2,4},{4,6},{6,8},{8,10},{10,12},{12,14},{14,0},{1,3},{3,5},... | collective-permute-start | bytes 1179656 | tf_op jit(solution)/shard_map/ppermute | solution.py:50
  32.0 18.1 %collective-permute-start.7 = (bf16[384,512]{1,0:T(8,128)(2,1)S(1)}, bf16[384,512]{1,0:T(8,128)(2,1)S(1)}, u32[]{:S(2)}, u32[]{:S(2)}) collective-permute-start(bf16[384,512]{1,0:T(8,128)(2,1)S(1)} %collective-permute-done.3), channel_id=1, source_target_pairs={{0,14},{2,0},{4,2},{6,4},{8,6},{10,8},{12,10},{14,12},{1,15},{3,1}... | collective-permute-start | bytes 1179656 | tf_op jit(solution)/shard_map/ppermute | solution.py:52
  42.2 16.8 %collective-permute-start.4 = (bf16[384,512]{1,0:T(8,128)(2,1)S(1)}, bf16[384,512]{1,0:T(8,128)(2,1)S(1)}, u32[]{:S(2)}, u32[]{:S(2)}) collective-permute-start(bf16[384,512]{1,0:T(8,128)(2,1)S(1)} %collective-permute-done.3), channel_id=1, source_target_pairs={{0,1},{1,0},{2,3},{3,2},{4,5},{5,4},{6,7},{7,6},{8,9},{9,8},{10,11... | collective-permute-start | bytes 1179656 | tf_op jit(solution)/shard_map/ppermute | solution.py:42
  45.8 22.8 %collective-permute-start.6 = (bf16[384,512]{1,0:T(8,128)(2,1)S(1)}, bf16[384,512]{1,0:T(8,128)(2,1)S(1)}, u32[]{:S(2)}, u32[]{:S(2)}) collective-permute-start(bf16[384,512]{1,0:T(8,128)(2,1)S(1)} %collective-permute-done.5), channel_id=1, source_target_pairs={{0,1},{1,0},{2,3},{3,2},{4,5},{5,4},{6,7},{7,6},{8,9},{9,8},{10,11... | collective-permute-start | bytes 1179656 | tf_op jit(solution)/shard_map/ppermute | solution.py:42
  48.2 14.1 %collective-permute-start.9 = (bf16[384,512]{1,0:T(8,128)(2,1)S(1)}, bf16[384,512]{1,0:T(8,128)(2,1)S(1)}, u32[]{:S(2)}, u32[]{:S(2)}) collective-permute-start(bf16[384,512]{1,0:T(8,128)(2,1)S(1)} %collective-permute-done.5), channel_id=1, source_target_pairs={{0,2},{2,4},{4,6},{6,8},{8,10},{10,12},{12,14},{14,0},{1,3},{3,5},... | collective-permute-start | bytes 1179656 | tf_op jit(solution)/shard_map/ppermute | solution.py:50
  50.1 20.1 %collective-permute-start.8 = (bf16[384,512]{1,0:T(8,128)(2,1)S(1)}, bf16[384,512]{1,0:T(8,128)(2,1)S(1)}, u32[]{:S(2)}, u32[]{:S(2)}) collective-permute-start(bf16[384,512]{1,0:T(8,128)(2,1)S(1)} %collective-permute-done.7), channel_id=1, source_target_pairs={{0,1},{1,0},{2,3},{3,2},{4,5},{5,4},{6,7},{7,6},{8,9},{9,8},{10,11... | collective-permute-start | bytes 1179656 | tf_op jit(solution)/shard_map/ppermute | solution.py:42
  52.1 14.2 %collective-permute-start.11 = (bf16[384,512]{1,0:T(8,128)(2,1)S(1)}, bf16[384,512]{1,0:T(8,128)(2,1)S(1)}, u32[]{:S(2)}, u32[]{:S(2)}) collective-permute-start(bf16[384,512]{1,0:T(8,128)(2,1)S(1)} %collective-permute-done.7), channel_id=1, source_target_pairs={{0,14},{2,0},{4,2},{6,4},{8,6},{10,8},{12,10},{14,12},{1,15},{3,1}... | collective-permute-start | bytes 1179656 | tf_op jit(solution)/shard_map/ppermute | solution.py:52
  62.3 18.5 %collective-permute-start.10 = (bf16[384,512]{1,0:T(8,128)(2,1)S(1)}, bf16[384,512]{1,0:T(8,128)(2,1)S(1)}, u32[]{:S(2)}, u32[]{:S(2)}) collective-permute-start(bf16[384,512]{1,0:T(8,128)(2,1)S(1)} %collective-permute-done.9), channel_id=1, source_target_pairs={{0,1},{1,0},{2,3},{3,2},{4,5},{5,4},{6,7},{7,6},{8,9},{9,8},{10,11... | collective-permute-start | bytes 1179656 | tf_op jit(solution)/shard_map/ppermute | solution.py:42
  64.3 14.6 %collective-permute-start.13 = (bf16[384,512]{1,0:T(8,128)(2,1)S(1)}, bf16[384,512]{1,0:T(8,128)(2,1)S(1)}, u32[]{:S(2)}, u32[]{:S(2)}) collective-permute-start(bf16[384,512]{1,0:T(8,128)(2,1)S(1)} %collective-permute-done.9), channel_id=1, source_target_pairs={{0,2},{2,4},{4,6},{6,8},{8,10},{10,12},{12,14},{14,0},{1,3},{3,5},... | collective-permute-start | bytes 1179656 | tf_op jit(solution)/shard_map/ppermute | solution.py:50
  66.2 16.2 %collective-permute-start.12 = (bf16[384,512]{1,0:T(8,128)(2,1)S(1)}, bf16[384,512]{1,0:T(8,128)(2,1)S(1)}, u32[]{:S(2)}, u32[]{:S(2)}) collective-permute-start(bf16[384,512]{1,0:T(8,128)(2,1)S(1)} %collective-permute-done.11), channel_id=1, source_target_pairs={{0,1},{1,0},{2,3},{3,2},{4,5},{5,4},{6,7},{7,6},{8,9},{9,8},{10,11... | collective-permute-start | bytes 1179656 | tf_op jit(solution)/shard_map/ppermute | solution.py:42
  78.9 5.2 %collective-permute-start.14 = (bf16[384,512]{1,0:T(8,128)(2,1)S(1)}, bf16[384,512]{1,0:T(8,128)(2,1)S(1)}, u32[]{:S(2)}, u32[]{:S(2)}) collective-permute-start(bf16[384,512]{1,0:T(8,128)(2,1)S(1)} %collective-permute-done.13), channel_id=1, source_target_pairs={{0,1},{1,0},{2,3},{3,2},{4,5},{5,4},{6,7},{7,6},{8,9},{9,8},{10,11... | collective-permute-start | bytes 1179656 | tf_op jit(solution)/shard_map/ppermute | solution.py:42
  84.8 49.5 %copy-start.2 = (s32[32]{0:T(128)S(1)}, s32[32]{0:T(128)}, u32[]{:S(2)}) copy-start(s32[32]{0:T(128)} %param.15) | copy-start | bytes 388
  84.8 73.3 %copy-start.1 = (s32[384]{0:T(512)S(1)}, s32[384]{0:T(512)}, u32[]{:S(2)}) copy-start(s32[384]{0:T(512)} %param.10) | copy-start | bytes 4612
  84.8 73.3 %copy-start.3 = (f32[384]{0:T(512)S(1)}, f32[384]{0:T(512)}, u32[]{:S(2)}) copy-start(f32[384]{0:T(512)} %param.13) | copy-start | bytes 4612
  84.8 73.3 %copy-start.4 = (s32[384]{0:T(512)S(1)}, s32[384]{0:T(512)}, u32[]{:S(2)}) copy-start(s32[384]{0:T(512)} %param.11) | copy-start | bytes 4612
  84.8 73.4 %copy-start.5 = (f32[384]{0:T(512)S(1)}, f32[384]{0:T(512)}, u32[]{:S(2)}) copy-start(f32[384]{0:T(512)} %param.12) | copy-start | bytes 4612
  84.8 73.3 %copy-start.6 = (f32[384]{0:T(512)S(1)}, f32[384]{0:T(512)}, u32[]{:S(2)}) copy-start(f32[384]{0:T(512)} %param.14) | copy-start | bytes 4612
  127.4 3.2 %collective-permute-start.15 = (f32[16,4,384]{2,0,1:T(8,128)S(1)}, f32[16,4,384]{2,0,1:T(8,128)S(1)}, u32[]{:S(2)}, u32[]{:S(2)}) collective-permute-start(f32[16,4,384]{2,0,1:T(8,128)S(1)} %dynamic_update_slice.69), channel_id=1, source_target_pairs={{0,1},{1,0},{2,3},{3,2},{4,5},{5,4},{6,7},{7,6},{8,9},{9,8},{10,11... | collective-permute-start | bytes 294920 | tf_op jit(solution)/shard_map/ppermute | solution.py:63
  130.7 6.7 %collective-permute-start.16 = (f32[16,4,384]{2,0,1:T(8,128)S(1)}, f32[16,4,384]{2,0,1:T(8,128)S(1)}, u32[]{:S(2)}, u32[]{:S(2)}) collective-permute-start(f32[16,4,384]{2,0,1:T(8,128)S(1)} %add.258), channel_id=1, source_target_pairs={{0,2},{2,0},{4,6},{6,4},{8,10},{10,8},{12,14},{14,12},{1,3},{3,1},... | collective-permute-start | bytes 294920 | tf_op jit(solution)/shard_map/ppermute | solution.py:63
  137.5 9.0 %collective-permute-start.17 = (f32[16,4,384]{2,0,1:T(8,128)S(1)}, f32[16,4,384]{2,0,1:T(8,128)S(1)}, u32[]{:S(2)}, u32[]{:S(2)}) collective-permute-start(f32[16,4,384]{2,0,1:T(8,128)S(1)} %add.259), channel_id=1, source_target_pairs={{0,4},{2,6},{4,0},{6,2},{8,12},{10,14},{12,8},{14,10},{1,5},{3,7},... | collective-permute-start | bytes 294920 | tf_op jit(solution)/shard_map/ppermute | solution.py:63
  146.6 11.5 %collective-permute-start.18 = (f32[16,4,384]{2,0,1:T(8,128)S(1)}, f32[16,4,384]{2,0,1:T(8,128)S(1)}, u32[]{:S(2)}, u32[]{:S(2)}) collective-permute-start(f32[16,4,384]{2,0,1:T(8,128)S(1)} %add.260), channel_id=1, source_target_pairs={{0,8},{2,10},{4,12},{6,14},{8,0},{10,2},{12,4},{14,6},{1,9},{3,11}... | collective-permute-start | bytes 294920 | tf_op jit(solution)/shard_map/ppermute | solution.py:63
  158.3 5.4 %collective-permute-start.19 = (f32[32]{0:T(128)S(1)}, f32[32]{0:T(128)S(1)}, u32[]{:S(2)}, u32[]{:S(2)}) collective-permute-start(f32[32]{0:T(128)S(1)} %select_reduce_fusion.1), channel_id=1, source_target_pairs={{0,16},{16,0},{32,48},{48,32},{1,17},{17,1},{33,49},{49,33},{2,18}... | collective-permute-start | bytes 392 | tf_op jit(solution)/shard_map/ppermute | solution.py:63
  163.8 6.9 %collective-permute-start.20 = (f32[32]{0:T(128)S(1)}, f32[32]{0:T(128)S(1)}, u32[]{:S(2)}, u32[]{:S(2)}) collective-permute-start(f32[32]{0:T(128)S(1)} %add.269), channel_id=1, source_target_pairs={{0,32},{16,48},{32,0},{48,16},{1,33},{17,49},{33,1},{49,17},{2,34}... | collective-permute-start | bytes 392 | tf_op jit(solution)/shard_map/ppermute | solution.py:63
  170.7 5.4 %collective-permute-start.21 = (f32[32]{0:T(128)S(1)}, f32[32]{0:T(128)S(1)}, u32[]{:S(2)}, u32[]{:S(2)}) collective-permute-start(f32[32]{0:T(128)S(1)} %add.270), channel_id=1, source_target_pairs={{0,64},{64,0},{128,192},{192,128},{256,320},{320,256},{384,448},{4... | collective-permute-start | bytes 392 | tf_op jit(solution)/shard_map/ppermute | solution.py:63
  176.1 6.3 %collective-permute-start.22 = (f32[32]{0:T(128)S(1)}, f32[32]{0:T(128)S(1)}, u32[]{:S(2)}, u32[]{:S(2)}) collective-permute-start(f32[32]{0:T(128)S(1)} %add.271), channel_id=1, source_target_pairs={{0,128},{64,192},{128,0},{192,64},{256,384},{320,448},{384,256},{4... | collective-permute-start | bytes 392 | tf_op jit(solution)/shard_map/ppermute | solution.py:63
  182.5 9.3 %collective-permute-start.23 = (f32[32]{0:T(128)S(1)}, f32[32]{0:T(128)S(1)}, u32[]{:S(2)}, u32[]{:S(2)}) collective-permute-start(f32[32]{0:T(128)S(1)} %add.272), channel_id=1, source_target_pairs={{0,256},{64,320},{128,384},{192,448},{256,0},{320,64},{384,128},{4... | collective-permute-start | bytes 392 | tf_op jit(solution)/shard_map/ppermute | solution.py:63
Sparse Core Ops, SparseCore 0:
  11.2 107.5 all-gather.1

commit v8 on v3

--- a/solution.py
+++ b/solution.py
@@ -78,7 +78,8 @@
     picked = jnp.sum(jnp.where(columns == column[:, None], logits, jnp.zeros_like(logits)), axis=1)
 
     stats = jnp.stack([row_peak, row_mass, moment, picked])
-    every = lax.all_gather(stats, VOCAB_AXES, axis=0, tiled=False)
+    copies = jnp.broadcast_to(stats[None], (spread,) + stats.shape)
+    every = lax.all_to_all(copies, VOCAB_AXES, 0, 0, tiled=True)
     peaks = every[:, 0]
     highest = jnp.max(peaks, axis=0)
     factor = jnp.exp(peaks - highest[None, :])
@@ -100,7 +101,9 @@
     member = jnp.sum((global_rows[:, None] >= endings[None, :]).astype(jnp.int32), axis=1)
     onehot = (member[:, None] == jnp.arange(SEQS, dtype=jnp.int32)[None, :]).astype(jnp.float32)
     partial_sums = jnp.sum(onehot * logprob[:, None], axis=0)
-    sums = lax.psum(lax.psum(partial_sums, "x"), "y")
+    peers = lax.axis_size(ROW_AXES)
+    spread_sums = jnp.broadcast_to(partial_sums[None], (peers, SEQS))
+    sums = jnp.sum(lax.all_to_all(spread_sums, ROW_AXES, 0, 0, tiled=True), axis=0)
     seq_mean = sums / seq_lengths.astype(jnp.float32)
     grouped = seq_mean.reshape(SEQS // GSIZE, GSIZE)
     seq_score = (grouped - jnp.mean(grouped, axis=1, keepdims=True)).reshape(SEQS)

time: 180 us -> 169 us (0.939)
  the two profiles are of different devices: /device:TPU:2 before, /device:TPU:1 now
where the time goes in v8:
time: 169 us
  starting transfers between devices  63.2 us (37%)
  waiting for transfers between devices  60.7 us (36%)
  local copies, waits for them, and re-layouts  20 us (12%)
  between operations  14.5 us (9%)
  matrix products  8 us (5%)
  other arithmetic  2.39 us (1%)
    all_gather x1, waiting for transfers between devices, local(): lax.all_gather(head, ROW_AXES, axis=0, tiled=True)  32.4 us
    ppermute x8, starting transfers between devices, share(): other = lax.ppermute(piece, 'c', across)  20.6 us
    ppermute x3, starting transfers between devices, gather_hidden(): bwd = lax.ppermute(bwd, 'z', behind)  18 us
    dynamic_update_slice x16, local copies, waits for them, and re-layouts, place(): return lax.dynamic_update_slice(buf, piece, (0, slot))  13.1 us
    ppermute x4, waiting for transfers between devices, gather_hidden(): fwd = lax.ppermute(fwd, 'z', ahead)  11.8 us
    ppermute x4, starting transfers between devices, gather_hidden(): fwd = lax.ppermute(fwd, 'z', ahead)  10.6 us
    all_to_all x1, starting transfers between devices, local(): every = lax.all_to_all(copies, VOCAB_AXES, 0, 0, tiled=True)  8.48 us
    all_to_all x1, waiting for transfers between devices, local(): every = lax.all_to_all(copies, VOCAB_AXES, 0, 0, tiled=True)  8.39 us
  transfers between devices with their start and end apart: 18, of which 6 were waited for; matrix products, arithmetic and copies ran while one was open for 12% of the time, Pallas kernels for 0%

profile of v8, /device:TPU:1, one launch (start us, length us, event | category | flops | bytes accessed | tf_op | source)
XLA Modules:
  0.0 168.7 jit_solution(15446300404419286020)
XLA Ops:
  7.2 0.7 all-gather.2.cloned.1.call-update
  7.9 4.8 %collective-permute-start.1 = (bf16[384,512]{1,0:T(8,128)(2,1)}, bf16[384,512]{1,0:T(8,128)(2,1)S(1)}, u32[]{:S(2)}, u32[]{:S(2)}) collective-permute-start(bf16[384,512]{1,0:T(8,128)(2,1)} %param.8), channel_id=1, source_target_pairs={{0,2},{2,4},{4,6},{6,8},{8,10},{10,12},{12,14},{14,0},{1,3},{3,5},... | collective-permute-start | bytes 1179656 | tf_op jit(solution)/shard_map/ppermute | solution.py:50
  12.7 8.6 %collective-permute-start.3 = (bf16[384,512]{1,0:T(8,128)(2,1)}, bf16[384,512]{1,0:T(8,128)(2,1)S(1)}, u32[]{:S(2)}, u32[]{:S(2)}) collective-permute-start(bf16[384,512]{1,0:T(8,128)(2,1)} %param.8), channel_id=1, source_target_pairs={{0,14},{2,0},{4,2},{6,4},{8,6},{10,8},{12,10},{14,12},{1,15},{3,1}... | collective-permute-start | bytes 1179656 | tf_op jit(solution)/shard_map/ppermute | solution.py:52
  21.3 2.9 %collective-permute-start = (bf16[384,512]{1,0:T(8,128)(2,1)}, bf16[384,512]{1,0:T(8,128)(2,1)S(1)}, u32[]{:S(2)}, u32[]{:S(2)}) collective-permute-start(bf16[384,512]{1,0:T(8,128)(2,1)} %param.8), channel_id=1, source_target_pairs={{0,1},{1,0},{2,3},{3,2},{4,5},{5,4},{6,7},{7,6},{8,9},{9,8},{10,11... | collective-permute-start | bytes 1179656 | tf_op jit(solution)/shard_map/ppermute | solution.py:42
  24.2 4.2 %collective-permute-done.1 = bf16[384,512]{1,0:T(8,128)(2,1)S(1)} collective-permute-done((bf16[384,512]{1,0:T(8,128)(2,1)}, bf16[384,512]{1,0:T(8,128)(2,1)S(1)}, u32[]{:S(2)}, u32[]{:S(2)}) %collective-permute-start.1) | collective-permute-done | bytes 393248 | tf_op jit(solution)/shard_map/ppermute | solution.py:50
  28.4 3.1 %collective-permute-start.2 = (bf16[384,512]{1,0:T(8,128)(2,1)S(1)}, bf16[384,512]{1,0:T(8,128)(2,1)S(1)}, u32[]{:S(2)}, u32[]{:S(2)}) collective-permute-start(bf16[384,512]{1,0:T(8,128)(2,1)S(1)} %collective-permute-done.1), channel_id=1, source_target_pairs={{0,1},{1,0},{2,3},{3,2},{4,5},{5,4},{6,7},{7,6},{8,9},{9,8},{10,11... | collective-permute-start | bytes 1179656 | tf_op jit(solution)/shard_map/ppermute | solution.py:42
  31.6 1.9 %collective-permute-start.5 = (bf16[384,512]{1,0:T(8,128)(2,1)S(1)}, bf16[384,512]{1,0:T(8,128)(2,1)S(1)}, u32[]{:S(2)}, u32[]{:S(2)}) collective-permute-start(bf16[384,512]{1,0:T(8,128)(2,1)S(1)} %collective-permute-done.1), channel_id=1, source_target_pairs={{0,2},{2,4},{4,6},{6,8},{8,10},{10,12},{12,14},{14,0},{1,3},{3,5},... | collective-permute-start | bytes 1179656 | tf_op jit(solution)/shard_map/ppermute | solution.py:50
  33.5 4.6 %collective-permute-start.7 = (bf16[384,512]{1,0:T(8,128)(2,1)S(1)}, bf16[384,512]{1,0:T(8,128)(2,1)S(1)}, u32[]{:S(2)}, u32[]{:S(2)}) collective-permute-start(bf16[384,512]{1,0:T(8,128)(2,1)S(1)} %collective-permute-done.3), channel_id=1, source_target_pairs={{0,14},{2,0},{4,2},{6,4},{8,6},{10,8},{12,10},{14,12},{1,15},{3,1}... | collective-permute-start | bytes 1179656 | tf_op jit(solution)/shard_map/ppermute | solution.py:52
  38.1 0.7 broadcast_subtract_fusion
  38.8 0.7 copy.21
  39.8 3.5 %broadcast_in_dim.8 = bf16[384,8192]{1,0:T(8,128)(2,1)} broadcast(bf16[]{:T(256)} %constant.94.clone.1), dimensions={} | broadcast | bytes 6291458 | tf_op jit(solution)/shard_map/broadcast_in_dim | solution.py:33
  43.2 0.9 constant_dynamic-update-slice_fusion.15
  44.1 2.5 %collective-permute-start.4 = (bf16[384,512]{1,0:T(8,128)(2,1)S(1)}, bf16[384,512]{1,0:T(8,128)(2,1)S(1)}, u32[]{:S(2)}, u32[]{:S(2)}) collective-permute-start(bf16[384,512]{1,0:T(8,128)(2,1)S(1)} %collective-permute-done.3), channel_id=1, source_target_pairs={{0,1},{1,0},{2,3},{3,2},{4,5},{5,4},{6,7},{7,6},{8,9},{9,8},{10,11... | collective-permute-start | bytes 1179656 | tf_op jit(solution)/shard_map/ppermute | solution.py:42
  46.6 0.9 constant_dynamic-update-slice_fusion.14
  47.5 0.8 constant_dynamic-update-slice_fusion.13
  48.3 1.9 %collective-permute-start.6 = (bf16[384,512]{1,0:T(8,128)(2,1)S(1)}, bf16[384,512]{1,0:T(8,128)(2,1)S(1)}, u32[]{:S(2)}, u32[]{:S(2)}) collective-permute-start(bf16[384,512]{1,0:T(8,128)(2,1)S(1)} %collective-permute-done.5), channel_id=1, source_target_pairs={{0,1},{1,0},{2,3},{3,2},{4,5},{5,4},{6,7},{7,6},{8,9},{9,8},{10,11... | collective-permute-start | bytes 1179656 | tf_op jit(solution)/shard_map/ppermute | solution.py:42
  50.2 1.9 %collective-permute-start.9 = (bf16[384,512]{1,0:T(8,128)(2,1)S(1)}, bf16[384,512]{1,0:T(8,128)(2,1)S(1)}, u32[]{:S(2)}, u32[]{:S(2)}) collective-permute-start(bf16[384,512]{1,0:T(8,128)(2,1)S(1)} %collective-permute-done.5), channel_id=1, source_target_pairs={{0,2},{2,4},{4,6},{6,8},{8,10},{10,12},{12,14},{14,0},{1,3},{3,5},... | collective-permute-start | bytes 1179656 | tf_op jit(solution)/shard_map/ppermute | solution.py:50
  52.1 2.4 %collective-permute-start.8 = (bf16[384,512]{1,0:T(8,128)(2,1)S(1)}, bf16[384,512]{1,0:T(8,128)(2,1)S(1)}, u32[]{:S(2)}, u32[]{:S(2)}) collective-permute-start(bf16[384,512]{1,0:T(8,128)(2,1)S(1)} %collective-permute-done.7), channel_id=1, source_target_pairs={{0,1},{1,0},{2,3},{3,2},{4,5},{5,4},{6,7},{7,6},{8,9},{9,8},{10,11... | collective-permute-start | bytes 1179656 | tf_op jit(solution)/shard_map/ppermute | solution.py:42
  54.6 4.9 %collective-permute-start.11 = (bf16[384,512]{1,0:T(8,128)(2,1)S(1)}, bf16[384,512]{1,0:T(8,128)(2,1)S(1)}, u32[]{:S(2)}, u32[]{:S(2)}) collective-permute-start(bf16[384,512]{1,0:T(8,128)(2,1)S(1)} %collective-permute-done.7), channel_id=1, source_target_pairs={{0,14},{2,0},{4,2},{6,4},{8,6},{10,8},{12,10},{14,12},{1,15},{3,1}... | collective-permute-start | bytes 1179656 | tf_op jit(solution)/shard_map/ppermute | solution.py:52
  59.4 0.8 constant_dynamic-update-slice_fusion.12
  60.2 0.8 constant_dynamic-update-slice_fusion.11
  61.1 0.8 constant_dynamic-update-slice_fusion.10
  61.9 0.8 constant_dynamic-update-slice_fusion.9
  62.7 0.8 collective-permute-done.9
  63.5 3.2 %collective-permute-start.10 = (bf16[384,512]{1,0:T(8,128)(2,1)S(1)}, bf16[384,512]{1,0:T(8,128)(2,1)S(1)}, u32[]{:S(2)}, u32[]{:S(2)}) collective-permute-start(bf16[384,512]{1,0:T(8,128)(2,1)S(1)} %collective-permute-done.9), channel_id=1, source_target_pairs={{0,1},{1,0},{2,3},{3,2},{4,5},{5,4},{6,7},{7,6},{8,9},{9,8},{10,11... | collective-permute-start | bytes 1179656 | tf_op jit(solution)/shard_map/ppermute | solution.py:42
  66.7 1.9 %collective-permute-start.13 = (bf16[384,512]{1,0:T(8,128)(2,1)S(1)}, bf16[384,512]{1,0:T(8,128)(2,1)S(1)}, u32[]{:S(2)}, u32[]{:S(2)}) collective-permute-start(bf16[384,512]{1,0:T(8,128)(2,1)S(1)} %collective-permute-done.9), channel_id=1, source_target_pairs={{0,2},{2,4},{4,6},{6,8},{8,10},{10,12},{12,14},{14,0},{1,3},{3,5},... | collective-permute-start | bytes 1179656 | tf_op jit(solution)/shard_map/ppermute | solution.py:50
  68.7 1.9 %collective-permute-start.12 = (bf16[384,512]{1,0:T(8,128)(2,1)S(1)}, bf16[384,512]{1,0:T(8,128)(2,1)S(1)}, u32[]{:S(2)}, u32[]{:S(2)}) collective-permute-start(bf16[384,512]{1,0:T(8,128)(2,1)S(1)} %collective-permute-done.11), channel_id=1, source_target_pairs={{0,1},{1,0},{2,3},{3,2},{4,5},{5,4},{6,7},{7,6},{8,9},{9,8},{10,11... | collective-permute-start | bytes 1179656 | tf_op jit(solution)/shard_map/ppermute | solution.py:42
  70.6 0.8 constant_dynamic-update-slice_fusion.8
  71.4 0.8 constant_dynamic-update-slice_fusion.7
  72.3 0.8 constant_dynamic-update-slice_fusion.6
  73.1 0.8 constant_dynamic-update-slice_fusion.5
  73.9 6.8 %collective-permute-done.13 = bf16[384,512]{1,0:T(8,128)(2,1)S(1)} collective-permute-done((bf16[384,512]{1,0:T(8,128)(2,1)S(1)}, bf16[384,512]{1,0:T(8,128)(2,1)S(1)}, u32[]{:S(2)}, u32[]{:S(2)}) %collective-permute-start.13) | collective-permute-done | bytes 393248 | tf_op jit(solution)/shard_map/ppermute | solution.py:50
  80.7 2.6 %collective-permute-start.14 = (bf16[384,512]{1,0:T(8,128)(2,1)S(1)}, bf16[384,512]{1,0:T(8,128)(2,1)S(1)}, u32[]{:S(2)}, u32[]{:S(2)}) collective-permute-start(bf16[384,512]{1,0:T(8,128)(2,1)S(1)} %collective-permute-done.13), channel_id=1, source_target_pairs={{0,1},{1,0},{2,3},{3,2},{4,5},{5,4},{6,7},{7,6},{8,9},{9,8},{10,11... | collective-permute-start | bytes 1179656 | tf_op jit(solution)/shard_map/ppermute | solution.py:42
  83.3 0.8 constant_dynamic-update-slice_fusion.4
  84.1 0.8 constant_dynamic-update-slice_fusion.3
  84.9 0.8 constant_dynamic-update-slice_fusion.2
  85.7 0.8 constant_dynamic-update-slice_fusion.1
  86.5 0.8 constant_dynamic-update-slice_fusion
  87.4 32.4 %all-gather.2.cloned.1.call-done = bf16[8192,512]{1,0:T(8,128)(2,1)} async-done(((bf16[256,512]{1,0:T(8,128)(2,1)}), bf16[8192,512]{1,0:T(8,128)(2,1)}) %all-gather.2.cloned.1.call-update) | async-done | bytes 8388624 | tf_op jit(solution)/shard_map/all_gather | solution.py:69
  119.7 8.0 %fusion.7 = (f32[384]{0:T(512)S(1)}, f32[384,512]{1,0:T(8,128)S(1)}) fusion(bf16[384,8192]{1,0:T(8,128)(2,1)} %constant_dynamic-update-slice_fusion, bf16[8192,512]{1,0:T(8,128)(2,1)} %all-gather.2.cloned.1.call-done), kind=kOutput, calls=%fused_computation.46 | convolution fusion | flops 3221421568 | bytes 15468032 | tf_op jit(solution)/shard_map/dot_general | solution.py:67
  128.3 0.6 broadcast_in_dim.10
  128.9 8.5 %all-to-all-start = ((f32[16,4,384]{2,1,0:T(4,128)}), f32[16,4,384]{2,1,0:T(4,128)S(1)}, u32[]{:S(2)}, u32[]{:S(2)}) async-start(f32[16,4,384]{2,1,0:T(4,128)} %broadcast_in_dim.10), calls=%async_computation | async-start | bytes 196608 | tf_op jit(solution)/shard_map/all_to_all | solution.py:82
  137.5 8.4 %all-to-all-done = f32[16,4,384]{2,1,0:T(4,128)S(1)} async-done(((f32[16,4,384]{2,1,0:T(4,128)}), f32[16,4,384]{2,1,0:T(4,128)S(1)}, u32[]{:S(2)}, u32[]{:S(2)}) %all-to-all-start) | async-done | bytes 98336 | tf_op jit(solution)/shard_map/all_to_all | solution.py:82
  146.2 0.6 broadcast_in_dim.11
  146.8 5.5 %all-to-all-start.1 = ((f32[32,1,32]{2,1,0:T(1,128)}), f32[32,1,32]{2,1,0:T(1,128)S(1)}, u32[]{:S(2)}, u32[]{:S(2)}) async-start(f32[32,1,32]{2,1,0:T(1,128)} %broadcast_in_dim.11), calls=%async_computation.1 | async-start | bytes 32768 | tf_op jit(solution)/shard_map/all_to_all | solution.py:106
  152.3 0.6 dynamic_slice.6
  152.9 0.6 dynamic_slice.7
  153.5 7.4 %all-to-all-done.1 = f32[32,1,32]{2,1,0:T(1,128)S(1)} async-done(((f32[32,1,32]{2,1,0:T(1,128)}), f32[32,1,32]{2,1,0:T(1,128)S(1)}, u32[]{:S(2)}, u32[]{:S(2)}) %all-to-all-start.1) | async-done | bytes 4128 | tf_op jit(solution)/shard_map/all_to_all | solution.py:106
  (49 shorter events, 2.1 us)
Async XLA Ops:
  7.2 36.1 %copy-start = (bf16[384,512]{1,0:T(8,128)(2,1)S(1)}, bf16[384,512]{1,0:T(8,128)(2,1)}, u32[]{:S(2)}) copy-start(bf16[384,512]{1,0:T(8,128)(2,1)} %param.8) | copy-start | bytes 1179652
  7.2 112.5 %all-gather.2.cloned.1.call-start = ((), (), s32[]{:S(2)}) async-start(), calls=%async_computation.2 | async-start | bytes 8650752 | tf_op jit(solution)/shard_map/all_gather | solution.py:69
  7.9 20.5 %collective-permute-start.1 = (bf16[384,512]{1,0:T(8,128)(2,1)}, bf16[384,512]{1,0:T(8,128)(2,1)S(1)}, u32[]{:S(2)}, u32[]{:S(2)}) collective-permute-start(bf16[384,512]{1,0:T(8,128)(2,1)} %param.8), channel_id=1, source_target_pairs={{0,2},{2,4},{4,6},{6,8},{8,10},{10,12},{12,14},{14,0},{1,3},{3,5},... | collective-permute-start | bytes 1179656 | tf_op jit(solution)/shard_map/ppermute | solution.py:50
  12.7 20.8 %collective-permute-start.3 = (bf16[384,512]{1,0:T(8,128)(2,1)}, bf16[384,512]{1,0:T(8,128)(2,1)S(1)}, u32[]{:S(2)}, u32[]{:S(2)}) collective-permute-start(bf16[384,512]{1,0:T(8,128)(2,1)} %param.8), channel_id=1, source_target_pairs={{0,14},{2,0},{4,2},{6,4},{8,6},{10,8},{12,10},{14,12},{1,15},{3,1}... | collective-permute-start | bytes 1179656 | tf_op jit(solution)/shard_map/ppermute | solution.py:52
  21.3 25.2 %collective-permute-start = (bf16[384,512]{1,0:T(8,128)(2,1)}, bf16[384,512]{1,0:T(8,128)(2,1)S(1)}, u32[]{:S(2)}, u32[]{:S(2)}) collective-permute-start(bf16[384,512]{1,0:T(8,128)(2,1)} %param.8), channel_id=1, source_target_pairs={{0,1},{1,0},{2,3},{3,2},{4,5},{5,4},{6,7},{7,6},{8,9},{9,8},{10,11... | collective-permute-start | bytes 1179656 | tf_op jit(solution)/shard_map/ppermute | solution.py:42
  28.4 26.1 %collective-permute-start.2 = (bf16[384,512]{1,0:T(8,128)(2,1)S(1)}, bf16[384,512]{1,0:T(8,128)(2,1)S(1)}, u32[]{:S(2)}, u32[]{:S(2)}) collective-permute-start(bf16[384,512]{1,0:T(8,128)(2,1)S(1)} %collective-permute-done.1), channel_id=1, source_target_pairs={{0,1},{1,0},{2,3},{3,2},{4,5},{5,4},{6,7},{7,6},{8,9},{9,8},{10,11... | collective-permute-start | bytes 1179656 | tf_op jit(solution)/shard_map/ppermute | solution.py:42
  31.6 16.7 %collective-permute-start.5 = (bf16[384,512]{1,0:T(8,128)(2,1)S(1)}, bf16[384,512]{1,0:T(8,128)(2,1)S(1)}, u32[]{:S(2)}, u32[]{:S(2)}) collective-permute-start(bf16[384,512]{1,0:T(8,128)(2,1)S(1)} %collective-permute-done.1), channel_id=1, source_target_pairs={{0,2},{2,4},{4,6},{6,8},{8,10},{10,12},{12,14},{14,0},{1,3},{3,5},... | collective-permute-start | bytes 1179656 | tf_op jit(solution)/shard_map/ppermute | solution.py:50
  33.5 18.6 %collective-permute-start.7 = (bf16[384,512]{1,0:T(8,128)(2,1)S(1)}, bf16[384,512]{1,0:T(8,128)(2,1)S(1)}, u32[]{:S(2)}, u32[]{:S(2)}) collective-permute-start(bf16[384,512]{1,0:T(8,128)(2,1)S(1)} %collective-permute-done.3), channel_id=1, source_target_pairs={{0,14},{2,0},{4,2},{6,4},{8,6},{10,8},{12,10},{14,12},{1,15},{3,1}... | collective-permute-start | bytes 1179656 | tf_op jit(solution)/shard_map/ppermute | solution.py:52
  44.1 16.9 %collective-permute-start.4 = (bf16[384,512]{1,0:T(8,128)(2,1)S(1)}, bf16[384,512]{1,0:T(8,128)(2,1)S(1)}, u32[]{:S(2)}, u32[]{:S(2)}) collective-permute-start(bf16[384,512]{1,0:T(8,128)(2,1)S(1)} %collective-permute-done.3), channel_id=1, source_target_pairs={{0,1},{1,0},{2,3},{3,2},{4,5},{5,4},{6,7},{7,6},{8,9},{9,8},{10,11... | collective-permute-start | bytes 1179656 | tf_op jit(solution)/shard_map/ppermute | solution.py:42
  48.3 22.4 %collective-permute-start.6 = (bf16[384,512]{1,0:T(8,128)(2,1)S(1)}, bf16[384,512]{1,0:T(8,128)(2,1)S(1)}, u32[]{:S(2)}, u32[]{:S(2)}) collective-permute-start(bf16[384,512]{1,0:T(8,128)(2,1)S(1)} %collective-permute-done.5), channel_id=1, source_target_pairs={{0,1},{1,0},{2,3},{3,2},{4,5},{5,4},{6,7},{7,6},{8,9},{9,8},{10,11... | collective-permute-start | bytes 1179656 | tf_op jit(solution)/shard_map/ppermute | solution.py:42
  50.2 13.3 %collective-permute-start.9 = (bf16[384,512]{1,0:T(8,128)(2,1)S(1)}, bf16[384,512]{1,0:T(8,128)(2,1)S(1)}, u32[]{:S(2)}, u32[]{:S(2)}) collective-permute-start(bf16[384,512]{1,0:T(8,128)(2,1)S(1)} %collective-permute-done.5), channel_id=1, source_target_pairs={{0,2},{2,4},{4,6},{6,8},{8,10},{10,12},{12,14},{14,0},{1,3},{3,5},... | collective-permute-start | bytes 1179656 | tf_op jit(solution)/shard_map/ppermute | solution.py:50
  52.1 20.1 %collective-permute-start.8 = (bf16[384,512]{1,0:T(8,128)(2,1)S(1)}, bf16[384,512]{1,0:T(8,128)(2,1)S(1)}, u32[]{:S(2)}, u32[]{:S(2)}) collective-permute-start(bf16[384,512]{1,0:T(8,128)(2,1)S(1)} %collective-permute-done.7), channel_id=1, source_target_pairs={{0,1},{1,0},{2,3},{3,2},{4,5},{5,4},{6,7},{7,6},{8,9},{9,8},{10,11... | collective-permute-start | bytes 1179656 | tf_op jit(solution)/shard_map/ppermute | solution.py:42
  54.6 14.1 %collective-permute-start.11 = (bf16[384,512]{1,0:T(8,128)(2,1)S(1)}, bf16[384,512]{1,0:T(8,128)(2,1)S(1)}, u32[]{:S(2)}, u32[]{:S(2)}) collective-permute-start(bf16[384,512]{1,0:T(8,128)(2,1)S(1)} %collective-permute-done.7), channel_id=1, source_target_pairs={{0,14},{2,0},{4,2},{6,4},{8,6},{10,8},{12,10},{14,12},{1,15},{3,1}... | collective-permute-start | bytes 1179656 | tf_op jit(solution)/shard_map/ppermute | solution.py:52
  63.5 19.8 %collective-permute-start.10 = (bf16[384,512]{1,0:T(8,128)(2,1)S(1)}, bf16[384,512]{1,0:T(8,128)(2,1)S(1)}, u32[]{:S(2)}, u32[]{:S(2)}) collective-permute-start(bf16[384,512]{1,0:T(8,128)(2,1)S(1)} %collective-permute-done.9), channel_id=1, source_target_pairs={{0,1},{1,0},{2,3},{3,2},{4,5},{5,4},{6,7},{7,6},{8,9},{9,8},{10,11... | collective-permute-start | bytes 1179656 | tf_op jit(solution)/shard_map/ppermute | solution.py:42
  66.7 13.9 %collective-permute-start.13 = (bf16[384,512]{1,0:T(8,128)(2,1)S(1)}, bf16[384,512]{1,0:T(8,128)(2,1)S(1)}, u32[]{:S(2)}, u32[]{:S(2)}) collective-permute-start(bf16[384,512]{1,0:T(8,128)(2,1)S(1)} %collective-permute-done.9), channel_id=1, source_target_pairs={{0,2},{2,4},{4,6},{6,8},{8,10},{10,12},{12,14},{14,0},{1,3},{3,5},... | collective-permute-start | bytes 1179656 | tf_op jit(solution)/shard_map/ppermute | solution.py:50
  68.7 16.2 %collective-permute-start.12 = (bf16[384,512]{1,0:T(8,128)(2,1)S(1)}, bf16[384,512]{1,0:T(8,128)(2,1)S(1)}, u32[]{:S(2)}, u32[]{:S(2)}) collective-permute-start(bf16[384,512]{1,0:T(8,128)(2,1)S(1)} %collective-permute-done.11), channel_id=1, source_target_pairs={{0,1},{1,0},{2,3},{3,2},{4,5},{5,4},{6,7},{7,6},{8,9},{9,8},{10,11... | collective-permute-start | bytes 1179656 | tf_op jit(solution)/shard_map/ppermute | solution.py:42
  80.7 5.9 %collective-permute-start.14 = (bf16[384,512]{1,0:T(8,128)(2,1)S(1)}, bf16[384,512]{1,0:T(8,128)(2,1)S(1)}, u32[]{:S(2)}, u32[]{:S(2)}) collective-permute-start(bf16[384,512]{1,0:T(8,128)(2,1)S(1)} %collective-permute-done.13), channel_id=1, source_target_pairs={{0,1},{1,0},{2,3},{3,2},{4,5},{5,4},{6,7},{7,6},{8,9},{9,8},{10,11... | collective-permute-start | bytes 1179656 | tf_op jit(solution)/shard_map/ppermute | solution.py:42
  87.3 58.7 %copy-start.1 = (s32[384]{0:T(512)S(1)}, s32[384]{0:T(512)}, u32[]{:S(2)}) copy-start(s32[384]{0:T(512)} %param.10) | copy-start | bytes 4612
  87.3 58.7 %copy-start.2 = (f32[384]{0:T(512)S(1)}, f32[384]{0:T(512)}, u32[]{:S(2)}) copy-start(f32[384]{0:T(512)} %param.13) | copy-start | bytes 4612
  87.3 58.7 %copy-start.3 = (s32[384]{0:T(512)S(1)}, s32[384]{0:T(512)}, u32[]{:S(2)}) copy-start(s32[384]{0:T(512)} %param.11) | copy-start | bytes 4612
  87.3 58.7 %copy-start.4 = (f32[384]{0:T(512)S(1)}, f32[384]{0:T(512)}, u32[]{:S(2)}) copy-start(f32[384]{0:T(512)} %param.12) | copy-start | bytes 4612
  87.3 58.7 %copy-start.5 = (f32[384]{0:T(512)S(1)}, f32[384]{0:T(512)}, u32[]{:S(2)}) copy-start(f32[384]{0:T(512)} %param.14) | copy-start | bytes 4612
  87.3 73.6 %copy-start.6 = (s32[32]{0:T(128)S(1)}, s32[32]{0:T(128)}, u32[]{:S(2)}) copy-start(s32[32]{0:T(128)} %param.15) | copy-start | bytes 388
  128.9 17.0 %all-to-all-start = ((f32[16,4,384]{2,1,0:T(4,128)}), f32[16,4,384]{2,1,0:T(4,128)S(1)}, u32[]{:S(2)}, u32[]{:S(2)}) async-start(f32[16,4,384]{2,1,0:T(4,128)} %broadcast_in_dim.10), calls=%async_computation | async-start | bytes 196608 | tf_op jit(solution)/shard_map/all_to_all | solution.py:82
  146.8 14.1 %all-to-all-start.1 = ((f32[32,1,32]{2,1,0:T(1,128)}), f32[32,1,32]{2,1,0:T(1,128)S(1)}, u32[]{:S(2)}, u32[]{:S(2)}) async-start(f32[32,1,32]{2,1,0:T(1,128)} %broadcast_in_dim.11), calls=%async_computation.1 | async-start | bytes 32768 | tf_op jit(solution)/shard_map/all_to_all | solution.py:106
Sparse Core Ops, SparseCore 0:
  11.2 108.4 all-gather.1

commit v9 on v3

--- a/solution.py
+++ b/solution.py
@@ -77,30 +77,55 @@
     columns = lax.broadcasted_iota(jnp.int32, logits.shape, 1)
     picked = jnp.sum(jnp.where(columns == column[:, None], logits, jnp.zeros_like(logits)), axis=1)
 
-    stats = jnp.stack([row_peak, row_mass, moment, picked])
-    every = lax.all_gather(stats, VOCAB_AXES, axis=0, tiled=False)
-    peaks = every[:, 0]
-    highest = jnp.max(peaks, axis=0)
-    factor = jnp.exp(peaks - highest[None, :])
-    mass_all = jnp.sum(every[:, 1] * factor, axis=0)
-    moment_all = jnp.sum(every[:, 2] * factor, axis=0)
-    picked_all = jnp.sum(every[:, 3], axis=0)
-    block_target = jnp.where(targets >= block_first, picked_all, prior_target)
-    logprob, entropy = finish_rows(
-        highest, mass_all, moment_all, block_target, live, prior_lse, prior_mean
-    )
-
     share = rows_here // spread
     begin = which * share
-    logprob_share = lax.dynamic_slice_in_dim(logprob, begin, share, 0)
-    entropy_share = lax.dynamic_slice_in_dim(entropy, begin, share, 0)
+    inputs = jnp.stack(
+        [
+            prior_lse,
+            prior_mean,
+            prior_target,
+            live.astype(jnp.float32),
+            (targets >= block_first).astype(jnp.float32),
+        ]
+    )
+    mine = lax.dynamic_slice_in_dim(inputs, begin, share, 1)
+    stats = jnp.stack([row_peak, row_mass, moment, picked])
+    payload = jnp.concatenate([stats.reshape(-1), mine.reshape(-1)])
+    groups = lax.axis_size(ROW_AXES)
+    everyone = groups * spread
+    got = lax.all_to_all(
+        jnp.broadcast_to(payload[None], (everyone, payload.shape[0])),
+        ROW_AXES + VOCAB_AXES,
+        0,
+        0,
+        tiled=True,
+    ).reshape(groups, spread, payload.shape[0])
+    every = got[:, :, : stats.size].reshape(groups, spread, 4, rows_here)
+    rows_in = (
+        got[:, :, stats.size :]
+        .reshape(groups, spread, 5, share)
+        .transpose(0, 2, 1, 3)
+        .reshape(groups, 5, rows_here)
+    )
+    peaks = every[:, :, 0]
+    highest = jnp.max(peaks, axis=1)
+    factor = jnp.exp(peaks - highest[:, None, :])
+    mass_all = jnp.sum(every[:, :, 1] * factor, axis=1)
+    moment_all = jnp.sum(every[:, :, 2] * factor, axis=1)
+    picked_all = jnp.sum(every[:, :, 3], axis=1)
+    block_target = jnp.where(rows_in[:, 4] > 0.5, picked_all, rows_in[:, 2])
+    logprob, entropy = finish_rows(
+        highest, mass_all, moment_all, block_target, rows_in[:, 3], rows_in[:, 0], rows_in[:, 1]
+    )
+    group = lax.axis_index(ROW_AXES)
+    logprob_share = lax.dynamic_slice(logprob, (group, begin), (1, share)).reshape(share)
+    entropy_share = lax.dynamic_slice(entropy, (group, begin), (1, share)).reshape(share)
 
-    global_rows = lax.axis_index(ROW_AXES) * rows_here + jnp.arange(rows_here, dtype=jnp.int32)
+    all_rows = jnp.arange(groups * rows_here, dtype=jnp.int32)
     endings = jnp.cumsum(seq_lengths)
-    member = jnp.sum((global_rows[:, None] >= endings[None, :]).astype(jnp.int32), axis=1)
+    member = jnp.sum((all_rows[:, None] >= endings[None, :]).astype(jnp.int32), axis=1)
     onehot = (member[:, None] == jnp.arange(SEQS, dtype=jnp.int32)[None, :]).astype(jnp.float32)
-    partial_sums = jnp.sum(onehot * logprob[:, None], axis=0)
-    sums = lax.psum(lax.psum(partial_sums, "x"), "y")
+    sums = jnp.sum(onehot * logprob.reshape(-1)[:, None], axis=0)
     seq_mean = sums / seq_lengths.astype(jnp.float32)
     grouped = seq_mean.reshape(SEQS // GSIZE, GSIZE)
     seq_score = (grouped - jnp.mean(grouped, axis=1, keepdims=True)).reshape(SEQS)

time: 180 us -> 258 us (1.43)
  the two profiles are of different devices: /device:TPU:2 before, /device:TPU:1 now
where the time goes in v9:
time: 258 us; the launch traced here: 257 us
  waiting for transfers between devices  125 us (48%)
  starting transfers between devices  62.9 us (24%)
  local copies, waits for them, and re-layouts  32.3 us (13%)
  other arithmetic  14.6 us (6%)
  between operations  14.6 us (6%)
  matrix products  8 us (3%)
    all_to_all x1, waiting for transfers between devices, local(): lax.all_to_all(jnp.broadcast_to(payload[None], (everyone, payload.shape[0...  82 us
    all_gather x1, waiting for transfers between devices, local(): lax.all_gather(head, ROW_AXES, axis=0, tiled=True)  31.1 us
    ppermute x8, starting transfers between devices, share(): other = lax.ppermute(piece, 'c', across)  25.8 us
    ppermute x3, starting transfers between devices, gather_hidden(): bwd = lax.ppermute(bwd, 'z', behind)  14.7 us
    all_to_all x1, starting transfers between devices, local(): lax.all_to_all(jnp.broadcast_to(payload[None], (everyone, payload.shape[0...  14.6 us
    dynamic_update_slice x16, local copies, waits for them, and re-layouts, place(): return lax.dynamic_update_slice(buf, piece, (0, slot))  13.1 us
    ppermute x4, waiting for transfers between devices, gather_hidden(): fwd = lax.ppermute(fwd, 'z', ahead)  11.2 us
    slice x1, other arithmetic, local(): mass_all = jnp.sum(every[:, :, 1] * factor, axis=1)  8.79 us
  transfers between devices with their start and end apart: 17, of which 5 were waited for; matrix products, arithmetic and copies ran while one was open for 8% of the time, Pallas kernels for 0%

profile of v9, /device:TPU:1, one launch (start us, length us, event | category | flops | bytes accessed | tf_op | source)
XLA Modules:
  0.0 257.3 jit_solution(2077367380879198741)
XLA Ops:
  7.9 8.8 %collective-permute-start = (bf16[384,512]{1,0:T(8,128)(2,1)}, bf16[384,512]{1,0:T(8,128)(2,1)S(1)}, u32[]{:S(2)}, u32[]{:S(2)}) collective-permute-start(bf16[384,512]{1,0:T(8,128)(2,1)} %param.8), channel_id=1, source_target_pairs={{0,1},{1,0},{2,3},{3,2},{4,5},{5,4},{6,7},{7,6},{8,9},{9,8},{10,11... | collective-permute-start | bytes 1179656 | tf_op jit(solution)/shard_map/ppermute | solution.py:42
  16.7 1.9 collective-permute-start.1
  18.6 5.3 %collective-permute-start.3 = (bf16[384,512]{1,0:T(8,128)(2,1)}, bf16[384,512]{1,0:T(8,128)(2,1)S(1)}, u32[]{:S(2)}, u32[]{:S(2)}) collective-permute-start(bf16[384,512]{1,0:T(8,128)(2,1)} %param.8), channel_id=1, source_target_pairs={{0,14},{2,0},{4,2},{6,4},{8,6},{10,8},{12,10},{14,12},{1,15},{3,1}... | collective-permute-start | bytes 1179656 | tf_op jit(solution)/shard_map/ppermute | solution.py:52
  23.9 0.7 compare_convert_fusion
  28.1 3.6 %collective-permute-done.1 = bf16[384,512]{1,0:T(8,128)(2,1)S(1)} collective-permute-done((bf16[384,512]{1,0:T(8,128)(2,1)}, bf16[384,512]{1,0:T(8,128)(2,1)S(1)}, u32[]{:S(2)}, u32[]{:S(2)}) %collective-permute-start.1) | collective-permute-done | bytes 393248 | tf_op jit(solution)/shard_map/ppermute | solution.py:50
  31.7 2.5 collective-permute-start.2
  34.2 1.9 collective-permute-start.5
  36.1 4.6 %collective-permute-start.7 = (bf16[384,512]{1,0:T(8,128)(2,1)S(1)}, bf16[384,512]{1,0:T(8,128)(2,1)S(1)}, u32[]{:S(2)}, u32[]{:S(2)}) collective-permute-start(bf16[384,512]{1,0:T(8,128)(2,1)S(1)} %collective-permute-done.3), channel_id=1, source_target_pairs={{0,14},{2,0},{4,2},{6,4},{8,6},{10,8},{12,10},{14,12},{1,15},{3,1}... | collective-permute-start | bytes 1179656 | tf_op jit(solution)/shard_map/ppermute | solution.py:52
  41.0 3.5 %broadcast_in_dim.6 = bf16[384,8192]{1,0:T(8,128)(2,1)} broadcast(bf16[]{:T(256)} %constant.95.clone.1), dimensions={} | broadcast | bytes 6291458 | tf_op jit(solution)/shard_map/broadcast_in_dim | solution.py:33
  44.4 0.9 constant_dynamic-update-slice_fusion.15
  45.3 2.5 collective-permute-start.4
  47.8 0.9 constant_dynamic-update-slice_fusion.14
  48.7 0.8 constant_dynamic-update-slice_fusion.13
  49.5 1.9 collective-permute-start.6
  51.4 1.9 collective-permute-start.9
  53.3 2.4 collective-permute-start.8
  55.8 4.9 %collective-permute-start.11 = (bf16[384,512]{1,0:T(8,128)(2,1)S(1)}, bf16[384,512]{1,0:T(8,128)(2,1)S(1)}, u32[]{:S(2)}, u32[]{:S(2)}) collective-permute-start(bf16[384,512]{1,0:T(8,128)(2,1)S(1)} %collective-permute-done.7), channel_id=1, source_target_pairs={{0,14},{2,0},{4,2},{6,4},{8,6},{10,8},{12,10},{14,12},{1,15},{3,1}... | collective-permute-start | bytes 1179656 | tf_op jit(solution)/shard_map/ppermute | solution.py:52
  60.6 0.8 constant_dynamic-update-slice_fusion.12
  61.4 0.8 constant_dynamic-update-slice_fusion.11
  62.3 0.8 constant_dynamic-update-slice_fusion.10
  63.1 0.8 constant_dynamic-update-slice_fusion.9
  63.9 0.8 collective-permute-done.9
  64.7 3.2 %collective-permute-start.10 = (bf16[384,512]{1,0:T(8,128)(2,1)S(1)}, bf16[384,512]{1,0:T(8,128)(2,1)S(1)}, u32[]{:S(2)}, u32[]{:S(2)}) collective-permute-start(bf16[384,512]{1,0:T(8,128)(2,1)S(1)} %collective-permute-done.9), channel_id=1, source_target_pairs={{0,1},{1,0},{2,3},{3,2},{4,5},{5,4},{6,7},{7,6},{8,9},{9,8},{10,11... | collective-permute-start | bytes 1179656 | tf_op jit(solution)/shard_map/ppermute | solution.py:42
  67.9 1.9 collective-permute-start.13
  69.9 1.9 collective-permute-start.12
  71.8 0.8 constant_dynamic-update-slice_fusion.8
  72.6 0.8 constant_dynamic-update-slice_fusion.7
  73.5 0.8 constant_dynamic-update-slice_fusion.6
  74.3 0.8 constant_dynamic-update-slice_fusion.5
  75.1 6.8 %collective-permute-done.13 = bf16[384,512]{1,0:T(8,128)(2,1)S(1)} collective-permute-done((bf16[384,512]{1,0:T(8,128)(2,1)S(1)}, bf16[384,512]{1,0:T(8,128)(2,1)S(1)}, u32[]{:S(2)}, u32[]{:S(2)}) %collective-permute-start.13) | collective-permute-done | bytes 393248 | tf_op jit(solution)/shard_map/ppermute | solution.py:50
  81.9 2.6 %collective-permute-start.14 = (bf16[384,512]{1,0:T(8,128)(2,1)S(1)}, bf16[384,512]{1,0:T(8,128)(2,1)S(1)}, u32[]{:S(2)}, u32[]{:S(2)}) collective-permute-start(bf16[384,512]{1,0:T(8,128)(2,1)S(1)} %collective-permute-done.13), channel_id=1, source_target_pairs={{0,1},{1,0},{2,3},{3,2},{4,5},{5,4},{6,7},{7,6},{8,9},{9,8},{10,11... | collective-permute-start | bytes 1179656 | tf_op jit(solution)/shard_map/ppermute | solution.py:42
  84.5 0.8 constant_dynamic-update-slice_fusion.4
  85.3 0.8 constant_dynamic-update-slice_fusion.3
  86.1 0.8 constant_dynamic-update-slice_fusion.2
  86.9 0.8 constant_dynamic-update-slice_fusion.1
  87.7 0.8 constant_dynamic-update-slice_fusion
  88.5 31.1 %all-gather.2.cloned.1.call-done = bf16[8192,512]{1,0:T(8,128)(2,1)} async-done(((bf16[256,512]{1,0:T(8,128)(2,1)}), bf16[8192,512]{1,0:T(8,128)(2,1)}) %all-gather.2.cloned.1.call-update) | async-done | bytes 8388624 | tf_op jit(solution)/shard_map/all_gather | solution.py:69
  119.6 8.0 %fusion.15 = (f32[384]{0:T(512)S(1)}, f32[384,512]{1,0:T(8,128)S(1)}) fusion(bf16[384,8192]{1,0:T(8,128)(2,1)} %constant_dynamic-update-slice_fusion, bf16[8192,512]{1,0:T(8,128)(2,1)} %all-gather.2.cloned.1.call-done), kind=kOutput, calls=%fused_computation.66 | convolution fusion | flops 3221421568 | bytes 15468032 | tf_op jit(solution)/shard_map/dot_general | solution.py:67
  128.2 3.5 %broadcast_in_dim.8 = f32[512,1,1656]{2,1,0:T(1,128)} broadcast(f32[1656]{0:T(1024)S(1)} %pad_maximum_fusion), dimensions={2} | broadcast | bytes 3398112 | tf_op jit(solution)/shard_map/broadcast_in_dim | solution.py:97
  131.7 14.6 %all-to-all-start = ((f32[512,1,1656]{2,1,0:T(1,128)}), f32[512,1,1656]{2,1,0:T(1,128)S(1)}, u32[]{:S(2)}, u32[]{:S(2)}) async-start(f32[512,1,1656]{2,1,0:T(1,128)} %broadcast_in_dim.8), calls=%async_computation | async-start | bytes 6815744 | tf_op jit(solution)/shard_map/all_to_all | solution.py:96
  146.9 82.0 %all-to-all-done = f32[512,1,1656]{2,1,0:T(1,128)S(1)} async-done(((f32[512,1,1656]{2,1,0:T(1,128)}), f32[512,1,1656]{2,1,0:T(1,128)S(1)}, u32[]{:S(2)}, u32[]{:S(2)}) %all-to-all-start) | async-done | bytes 3391520 | tf_op jit(solution)/shard_map/all_to_all | solution.py:96
  229.6 1.3 copy.24
  230.9 2.8 %copy.25 = f32[32,5,16,24]{3,2,0,1:T(8,128)} copy(f32[32,5,16,24]{0,3,1,2:T(8,128)} %bitcast.66) | data formatting | bytes 491520 | tf_op jit(solution)/shard_map/transpose | solution.py:107
  233.7 1.9 reshape.129
  235.6 0.7 fusion.14
  236.3 2.3 reshape.130
  238.5 8.8 %fusion.13 = (f32[32,16,1,384]{3,2,1,0:T(1,128)S(1)}, f32[32,16,1,384]{3,2,1,0:T(1,128)S(1)}, f32[32,16,1,384]{3,2,1,0:T(1,128)S(1)}, f32[32,384]{1,0:T(8,128)S(1)}, f32[32,384]{1,0:T(8,128)S(1)}) fusion(f32[32,16,4,384]{3,2,1,0:T(4,128)} %reshape.130), kind=kLoop, calls=%fused_computation.64 | loop fusion | flops 368640 | bytes 5603328 | tf_op jit(solution)/shard_map/slice | solution.py:113
  249.1 1.3 multiply_bitcast_fusion
  (67 shorter events, 7.8 us)
Async XLA Ops:
  7.2 37.3 %copy-start = (bf16[384,512]{1,0:T(8,128)(2,1)S(1)}, bf16[384,512]{1,0:T(8,128)(2,1)}, u32[]{:S(2)}) copy-start(bf16[384,512]{1,0:T(8,128)(2,1)} %param.8) | copy-start | bytes 1179652
  7.2 112.4 %all-gather.2.cloned.1.call-start = ((), (), s32[]{:S(2)}) async-start(), calls=%async_computation.1 | async-start | bytes 8650752 | tf_op jit(solution)/shard_map/all_gather | solution.py:69
  7.9 39.9 %collective-permute-start = (bf16[384,512]{1,0:T(8,128)(2,1)}, bf16[384,512]{1,0:T(8,128)(2,1)S(1)}, u32[]{:S(2)}, u32[]{:S(2)}) collective-permute-start(bf16[384,512]{1,0:T(8,128)(2,1)} %param.8), channel_id=1, source_target_pairs={{0,1},{1,0},{2,3},{3,2},{4,5},{5,4},{6,7},{7,6},{8,9},{9,8},{10,11... | collective-permute-start | bytes 1179656 | tf_op jit(solution)/shard_map/ppermute | solution.py:42
  16.7 15.0 %collective-permute-start.1 = (bf16[384,512]{1,0:T(8,128)(2,1)}, bf16[384,512]{1,0:T(8,128)(2,1)S(1)}, u32[]{:S(2)}, u32[]{:S(2)}) collective-permute-start(bf16[384,512]{1,0:T(8,128)(2,1)} %param.8), channel_id=1, source_target_pairs={{0,2},{2,4},{4,6},{6,8},{8,10},{10,12},{12,14},{14,0},{1,3},{3,5},... | collective-permute-start | bytes 1179656 | tf_op jit(solution)/shard_map/ppermute | solution.py:50
  18.6 17.5 %collective-permute-start.3 = (bf16[384,512]{1,0:T(8,128)(2,1)}, bf16[384,512]{1,0:T(8,128)(2,1)S(1)}, u32[]{:S(2)}, u32[]{:S(2)}) collective-permute-start(bf16[384,512]{1,0:T(8,128)(2,1)} %param.8), channel_id=1, source_target_pairs={{0,14},{2,0},{4,2},{6,4},{8,6},{10,8},{12,10},{14,12},{1,15},{3,1}... | collective-permute-start | bytes 1179656 | tf_op jit(solution)/shard_map/ppermute | solution.py:52
  31.7 24.1 %collective-permute-start.2 = (bf16[384,512]{1,0:T(8,128)(2,1)S(1)}, bf16[384,512]{1,0:T(8,128)(2,1)S(1)}, u32[]{:S(2)}, u32[]{:S(2)}) collective-permute-start(bf16[384,512]{1,0:T(8,128)(2,1)S(1)} %collective-permute-done.1), channel_id=1, source_target_pairs={{0,1},{1,0},{2,3},{3,2},{4,5},{5,4},{6,7},{7,6},{8,9},{9,8},{10,11... | collective-permute-start | bytes 1179656 | tf_op jit(solution)/shard_map/ppermute | solution.py:42
  34.2 15.3 %collective-permute-start.5 = (bf16[384,512]{1,0:T(8,128)(2,1)S(1)}, bf16[384,512]{1,0:T(8,128)(2,1)S(1)}, u32[]{:S(2)}, u32[]{:S(2)}) collective-permute-start(bf16[384,512]{1,0:T(8,128)(2,1)S(1)} %collective-permute-done.1), channel_id=1, source_target_pairs={{0,2},{2,4},{4,6},{6,8},{8,10},{10,12},{12,14},{14,0},{1,3},{3,5},... | collective-permute-start | bytes 1179656 | tf_op jit(solution)/shard_map/ppermute | solution.py:50
  36.1 17.2 %collective-permute-start.7 = (bf16[384,512]{1,0:T(8,128)(2,1)S(1)}, bf16[384,512]{1,0:T(8,128)(2,1)S(1)}, u32[]{:S(2)}, u32[]{:S(2)}) collective-permute-start(bf16[384,512]{1,0:T(8,128)(2,1)S(1)} %collective-permute-done.3), channel_id=1, source_target_pairs={{0,14},{2,0},{4,2},{6,4},{8,6},{10,8},{12,10},{14,12},{1,15},{3,1}... | collective-permute-start | bytes 1179656 | tf_op jit(solution)/shard_map/ppermute | solution.py:52
  45.3 16.9 %collective-permute-start.4 = (bf16[384,512]{1,0:T(8,128)(2,1)S(1)}, bf16[384,512]{1,0:T(8,128)(2,1)S(1)}, u32[]{:S(2)}, u32[]{:S(2)}) collective-permute-start(bf16[384,512]{1,0:T(8,128)(2,1)S(1)} %collective-permute-done.3), channel_id=1, source_target_pairs={{0,1},{1,0},{2,3},{3,2},{4,5},{5,4},{6,7},{7,6},{8,9},{9,8},{10,11... | collective-permute-start | bytes 1179656 | tf_op jit(solution)/shard_map/ppermute | solution.py:42
  49.5 22.4 %collective-permute-start.6 = (bf16[384,512]{1,0:T(8,128)(2,1)S(1)}, bf16[384,512]{1,0:T(8,128)(2,1)S(1)}, u32[]{:S(2)}, u32[]{:S(2)}) collective-permute-start(bf16[384,512]{1,0:T(8,128)(2,1)S(1)} %collective-permute-done.5), channel_id=1, source_target_pairs={{0,1},{1,0},{2,3},{3,2},{4,5},{5,4},{6,7},{7,6},{8,9},{9,8},{10,11... | collective-permute-start | bytes 1179656 | tf_op jit(solution)/shard_map/ppermute | solution.py:42
  51.4 13.3 %collective-permute-start.9 = (bf16[384,512]{1,0:T(8,128)(2,1)S(1)}, bf16[384,512]{1,0:T(8,128)(2,1)S(1)}, u32[]{:S(2)}, u32[]{:S(2)}) collective-permute-start(bf16[384,512]{1,0:T(8,128)(2,1)S(1)} %collective-permute-done.5), channel_id=1, source_target_pairs={{0,2},{2,4},{4,6},{6,8},{8,10},{10,12},{12,14},{14,0},{1,3},{3,5},... | collective-permute-start | bytes 1179656 | tf_op jit(solution)/shard_map/ppermute | solution.py:50
  53.3 20.1 %collective-permute-start.8 = (bf16[384,512]{1,0:T(8,128)(2,1)S(1)}, bf16[384,512]{1,0:T(8,128)(2,1)S(1)}, u32[]{:S(2)}, u32[]{:S(2)}) collective-permute-start(bf16[384,512]{1,0:T(8,128)(2,1)S(1)} %collective-permute-done.7), channel_id=1, source_target_pairs={{0,1},{1,0},{2,3},{3,2},{4,5},{5,4},{6,7},{7,6},{8,9},{9,8},{10,11... | collective-permute-start | bytes 1179656 | tf_op jit(solution)/shard_map/ppermute | solution.py:42
  55.8 14.1 %collective-permute-start.11 = (bf16[384,512]{1,0:T(8,128)(2,1)S(1)}, bf16[384,512]{1,0:T(8,128)(2,1)S(1)}, u32[]{:S(2)}, u32[]{:S(2)}) collective-permute-start(bf16[384,512]{1,0:T(8,128)(2,1)S(1)} %collective-permute-done.7), channel_id=1, source_target_pairs={{0,14},{2,0},{4,2},{6,4},{8,6},{10,8},{12,10},{14,12},{1,15},{3,1}... | collective-permute-start | bytes 1179656 | tf_op jit(solution)/shard_map/ppermute | solution.py:52
  64.7 19.8 %collective-permute-start.10 = (bf16[384,512]{1,0:T(8,128)(2,1)S(1)}, bf16[384,512]{1,0:T(8,128)(2,1)S(1)}, u32[]{:S(2)}, u32[]{:S(2)}) collective-permute-start(bf16[384,512]{1,0:T(8,128)(2,1)S(1)} %collective-permute-done.9), channel_id=1, source_target_pairs={{0,1},{1,0},{2,3},{3,2},{4,5},{5,4},{6,7},{7,6},{8,9},{9,8},{10,11... | collective-permute-start | bytes 1179656 | tf_op jit(solution)/shard_map/ppermute | solution.py:42
  67.9 13.9 %collective-permute-start.13 = (bf16[384,512]{1,0:T(8,128)(2,1)S(1)}, bf16[384,512]{1,0:T(8,128)(2,1)S(1)}, u32[]{:S(2)}, u32[]{:S(2)}) collective-permute-start(bf16[384,512]{1,0:T(8,128)(2,1)S(1)} %collective-permute-done.9), channel_id=1, source_target_pairs={{0,2},{2,4},{4,6},{6,8},{8,10},{10,12},{12,14},{14,0},{1,3},{3,5},... | collective-permute-start | bytes 1179656 | tf_op jit(solution)/shard_map/ppermute | solution.py:50
  69.9 16.2 %collective-permute-start.12 = (bf16[384,512]{1,0:T(8,128)(2,1)S(1)}, bf16[384,512]{1,0:T(8,128)(2,1)S(1)}, u32[]{:S(2)}, u32[]{:S(2)}) collective-permute-start(bf16[384,512]{1,0:T(8,128)(2,1)S(1)} %collective-permute-done.11), channel_id=1, source_target_pairs={{0,1},{1,0},{2,3},{3,2},{4,5},{5,4},{6,7},{7,6},{8,9},{9,8},{10,11... | collective-permute-start | bytes 1179656 | tf_op jit(solution)/shard_map/ppermute | solution.py:42
  81.9 5.9 %collective-permute-start.14 = (bf16[384,512]{1,0:T(8,128)(2,1)S(1)}, bf16[384,512]{1,0:T(8,128)(2,1)S(1)}, u32[]{:S(2)}, u32[]{:S(2)}) collective-permute-start(bf16[384,512]{1,0:T(8,128)(2,1)S(1)} %collective-permute-done.13), channel_id=1, source_target_pairs={{0,1},{1,0},{2,3},{3,2},{4,5},{5,4},{6,7},{7,6},{8,9},{9,8},{10,11... | collective-permute-start | bytes 1179656 | tf_op jit(solution)/shard_map/ppermute | solution.py:42
  127.6 18.7 %copy-start.2 = (s32[32]{0:T(128)S(1)}, s32[32]{0:T(128)}, u32[]{:S(2)}) copy-start(s32[32]{0:T(128)} %param.15) | copy-start | bytes 388
  131.7 97.2 %all-to-all-start = ((f32[512,1,1656]{2,1,0:T(1,128)}), f32[512,1,1656]{2,1,0:T(1,128)S(1)}, u32[]{:S(2)}, u32[]{:S(2)}) async-start(f32[512,1,1656]{2,1,0:T(1,128)} %broadcast_in_dim.8), calls=%async_computation | async-start | bytes 6815744 | tf_op jit(solution)/shard_map/all_to_all | solution.py:96
  238.5 9.3 %copy-start.1 = (f32[32,1,384]{2,0,1:T(8,128)S(1)}, f32[32,1,384]{2,0,1:T(8,128)}, u32[]{:S(2)}) copy-start(f32[32,1,384]{2,0,1:T(8,128)} %get-tuple-element.24) | copy-start | bytes 147460
  238.5 9.7 %copy-start.3 = (s32[32]{0:T(128)S(1)}, s32[32]{0:T(128)}, u32[]{:S(2)}) copy-start(s32[32]{0:T(128)} %param.15) | copy-start | bytes 388
Sparse Core Ops, SparseCore 0:
  11.2 108.3 all-gather.1

commit v10 on v5

--- a/solution.py
+++ b/solution.py
@@ -74,32 +74,29 @@
     return buf
 
 
+def spread_gather(block, axis):
+    n = lax.axis_size(axis)
+    return lax.all_to_all(jnp.broadcast_to(block[None], (n,) + block.shape), axis, 0, 0, tiled=True)
+
+
 def gather_head(head):
     depth, cols = head.shape
     nx = lax.axis_size("x")
     ny = lax.axis_size("y")
     half = (cols // 2) // 128 * 128
 
-    def put_x(buf, piece, index):
-        return lax.dynamic_update_slice(buf, piece, (index * depth, 0))
-
     def put_y(buf, piece, index):
         return lax.dynamic_update_slice(buf, piece, (index * depth * nx, 0))
 
-    first = head[:, :half]
-    strip = ring_gather(first, "x", put_x, jnp.zeros((depth * nx, half), head.dtype))
+    strip = spread_gather(head[:, :half], "x").reshape(nx * depth, half)
     first_full = ring_gather(strip, "y", put_y, jnp.zeros((depth * nx * ny, half), head.dtype))
 
-    second = head[:, half:]
     width = cols - half
 
     def put_col(buf, piece, index):
         return lax.dynamic_update_slice(buf, piece[:, None], (0, index, 0, 0))
 
-    def put_row(buf, piece, index):
-        return lax.dynamic_update_slice(buf, piece[None], (index, 0, 0))
-
-    column = ring_gather(second, "y", put_row, jnp.zeros((ny, depth, width), head.dtype))
+    column = spread_gather(head[:, half:], "y")
     second_full = ring_gather(column, "x", put_col, jnp.zeros((ny, nx, depth, width), head.dtype))
     return first_full, second_full.reshape(ny * nx * depth, width)
 
@@ -129,7 +126,8 @@
     picked = jnp.sum(jnp.where(columns == column[:, None], logits, jnp.zeros_like(logits)), axis=1)
 
     stats = jnp.stack([row_peak, row_mass, moment, picked])
-    every = lax.all_gather(stats, VOCAB_AXES, axis=0, tiled=False)
+    copies = jnp.broadcast_to(stats[None], (spread,) + stats.shape)
+    every = lax.all_to_all(copies, VOCAB_AXES, 0, 0, tiled=True)
     peaks = every[:, 0]
     highest = jnp.max(peaks, axis=0)
     factor = jnp.exp(peaks - highest[None, :])
@@ -151,7 +149,9 @@
     member = jnp.sum((global_rows[:, None] >= endings[None, :]).astype(jnp.int32), axis=1)
     onehot = (member[:, None] == jnp.arange(SEQS, dtype=jnp.int32)[None, :]).astype(jnp.float32)
     partial_sums = jnp.sum(onehot * logprob[:, None], axis=0)
-    sums = lax.psum(lax.psum(partial_sums, "x"), "y")
+    peers = lax.axis_size(ROW_AXES)
+    spread_sums = jnp.broadcast_to(partial_sums[None], (peers, SEQS))
+    sums = jnp.sum(lax.all_to_all(spread_sums, ROW_AXES, 0, 0, tiled=True), axis=0)
     seq_mean = sums / seq_lengths.astype(jnp.float32)
     grouped = seq_mean.reshape(SEQS // GSIZE, GSIZE)
     seq_score = (grouped - jnp.mean(grouped, axis=1, keepdims=True)).reshape(SEQS)

time: 189 us -> 182 us (0.963)
  the two profiles are of different devices: /device:TPU:26 before, /device:TPU:1 now
where the time goes in v10:
time: 182 us; the launch traced here: 181 us
  waiting for transfers between devices  70.2 us (39%)
  starting transfers between devices  59.2 us (33%)
  local copies, waits for them, and re-layouts  14.9 us (8%)
  between operations  14.6 us (8%)
  blocking collectives  11.6 us (6%)
  matrix products  8.99 us (5%)
    ppermute x6, waiting for transfers between devices, ring_gather(): fwd = lax.ppermute(fwd, axis, ahead)  49.6 us
    ppermute x4, starting transfers between devices, ring_gather(): bwd = lax.ppermute(bwd, axis, behind)  16.2 us
    all_to_all x1, starting transfers between devices, local(): every = lax.all_to_all(copies, VOCAB_AXES, 0, 0, tiled=True)  14.6 us
    ppermute x6, starting transfers between devices, ring_gather(): fwd = lax.ppermute(fwd, axis, ahead)  13.5 us
    all_to_all x1, blocking collectives, spread_gather(): lax.all_to_all(jnp.broadcast_to(block[None], (n,) + block.shape), axis, 0...  11.6 us
    all_to_all x1, starting transfers between devices, spread_gather(): lax.all_to_all(jnp.broadcast_to(block[None], (n,) + block.shape), axis, 0...  8.45 us
    all_to_all x1, waiting for transfers between devices, local(): every = lax.all_to_all(copies, VOCAB_AXES, 0, 0, tiled=True)  8.39 us
    all_to_all x1, waiting for transfers between devices, local(): lax.all_to_all(spread_sums, ROW_AXES, 0, 0, tiled=True)  7.43 us
  transfers between devices with their start and end apart: 14, of which 8 were waited for; matrix products, arithmetic and copies ran while one was open for 7% of the time, Pallas kernels for 0%

profile of v10, /device:TPU:1, one launch (start us, length us, event | category | flops | bytes accessed | tf_op | source)
XLA Modules:
  0.0 181.0 jit_solution(14353222592078157027)
XLA Ops:
  7.2 0.7 all-gather.2.cloned.1.call-update
  7.9 1.0 fusion.6
  9.0 11.6 %all_to_all.21 = bf16[4,256,256]{2,1,0:T(8,128)(2,1)S(1)} all-to-all(bf16[4,256,256]{2,1,0:T(8,128)(2,1)S(1)} %broadcast_in_dim.23), channel_id=1, replica_groups=mesh['y'=8,'x'=4,'z'=8,'c'=2] {'x'}, dimensions={0} | all-to-all | bytes 1048576 | tf_op jit(solution)/shard_map/all_to_all | solution.py:79
  20.5 1.1 broadcast_in_dim.25
  21.6 8.5 %all-to-all-start.1 = ((bf16[8,256,256]{2,1,0:T(8,128)(2,1)}), bf16[8,256,256]{2,1,0:T(8,128)(2,1)S(1)}, u32[]{:S(2)}, u32[]{:S(2)}) async-start(bf16[8,256,256]{2,1,0:T(8,128)(2,1)} %broadcast_in_dim.25), calls=%async_computation.1 | async-start | bytes 2097152 | tf_op jit(solution)/shard_map/all_to_all | solution.py:79
  30.1 3.4 %collective-permute-start = (bf16[1024,256]{1,0:T(8,128)(2,1)S(1)}, bf16[1024,256]{1,0:T(8,128)(2,1)}, u32[]{:S(2)}, u32[]{:S(2)}) collective-permute-start(bf16[1024,256]{1,0:T(8,128)(2,1)S(1)} %bitcast.44), channel_id=1, source_target_pairs={{0,64},{64,128},{128,192},{192,256},{256,320},{320,384},{384,448},... | collective-permute-start | bytes 1572872 | tf_op jit(solution)/shard_map/ppermute | solution.py:68
  33.4 3.1 %collective-permute-start.1 = (bf16[1024,256]{1,0:T(8,128)(2,1)S(1)}, bf16[1024,256]{1,0:T(8,128)(2,1)}, u32[]{:S(2)}, u32[]{:S(2)}) collective-permute-start(bf16[1024,256]{1,0:T(8,128)(2,1)S(1)} %bitcast.45), channel_id=1, source_target_pairs={{0,448},{64,0},{128,64},{192,128},{256,192},{320,256},{384,320},{4... | collective-permute-start | bytes 1572872 | tf_op jit(solution)/shard_map/ppermute | solution.py:70
  36.6 30.4 %collective-permute-done = bf16[1024,256]{1,0:T(8,128)(2,1)} collective-permute-done((bf16[1024,256]{1,0:T(8,128)(2,1)S(1)}, bf16[1024,256]{1,0:T(8,128)(2,1)}, u32[]{:S(2)}, u32[]{:S(2)}) %collective-permute-start) | collective-permute-done | bytes 524320 | tf_op jit(solution)/shard_map/ppermute | solution.py:68
  66.9 1.9 %collective-permute-start.2 = (bf16[1024,256]{1,0:T(8,128)(2,1)}, bf16[1024,256]{1,0:T(8,128)(2,1)S(1)}, u32[]{:S(2)}, u32[]{:S(2)}) collective-permute-start(bf16[1024,256]{1,0:T(8,128)(2,1)} %collective-permute-done), channel_id=1, source_target_pairs={{0,64},{64,128},{128,192},{192,256},{256,320},{320,384},{384,448},... | collective-permute-start | bytes 1572872 | tf_op jit(solution)/shard_map/ppermute | solution.py:68
  68.9 2.2 %collective-permute-start.7 = (bf16[8,256,256]{2,1,0:T(8,128)(2,1)S(1)}, bf16[8,256,256]{2,1,0:T(8,128)(2,1)S(1)}, u32[]{:S(2)}, u32[]{:S(2)}) collective-permute-start(bf16[8,256,256]{2,1,0:T(8,128)(2,1)S(1)} %all-to-all-done.1), channel_id=1, source_target_pairs={{0,16},{16,32},{32,48},{48,0},{1,17},{17,33},{33,49},{49,1},{2,18}... | collective-permute-start | bytes 3145736 | tf_op jit(solution)/shard_map/ppermute | solution.py:68
  71.2 0.1 copy.33
  71.4 0.1 reduce.7
  71.6 4.6 %collective-permute-start.3 = (bf16[1024,256]{1,0:T(8,128)(2,1)}, bf16[1024,256]{1,0:T(8,128)(2,1)S(1)}, u32[]{:S(2)}, u32[]{:S(2)}) collective-permute-start(bf16[1024,256]{1,0:T(8,128)(2,1)} %collective-permute-done.1), channel_id=1, source_target_pairs={{0,448},{64,0},{128,64},{192,128},{256,192},{320,256},{384,320},{4... | collective-permute-start | bytes 1572872 | tf_op jit(solution)/shard_map/ppermute | solution.py:70
  76.2 6.0 %collective-permute-done.2 = bf16[1024,256]{1,0:T(8,128)(2,1)S(1)} collective-permute-done((bf16[1024,256]{1,0:T(8,128)(2,1)}, bf16[1024,256]{1,0:T(8,128)(2,1)S(1)}, u32[]{:S(2)}, u32[]{:S(2)}) %collective-permute-start.2) | collective-permute-done | bytes 524320 | tf_op jit(solution)/shard_map/ppermute | solution.py:68
  82.2 1.9 %collective-permute-start.4 = (bf16[1024,256]{1,0:T(8,128)(2,1)S(1)}, bf16[1024,256]{1,0:T(8,128)(2,1)S(1)}, u32[]{:S(2)}, u32[]{:S(2)}) collective-permute-start(bf16[1024,256]{1,0:T(8,128)(2,1)S(1)} %collective-permute-done.2), channel_id=1, source_target_pairs={{0,64},{64,128},{128,192},{192,256},{256,320},{320,384},{384,448},... | collective-permute-start | bytes 1572872 | tf_op jit(solution)/shard_map/ppermute | solution.py:68
  84.1 0.3 broadcast_in_dim.22
  84.4 1.1 constant_dynamic-update-slice_fusion.6
  85.5 1.1 constant_dynamic-update-slice_fusion.5
  86.6 4.6 %collective-permute-start.5 = (bf16[1024,256]{1,0:T(8,128)(2,1)S(1)}, bf16[1024,256]{1,0:T(8,128)(2,1)S(1)}, u32[]{:S(2)}, u32[]{:S(2)}) collective-permute-start(bf16[1024,256]{1,0:T(8,128)(2,1)S(1)} %collective-permute-done.3), channel_id=1, source_target_pairs={{0,448},{64,0},{128,64},{192,128},{256,192},{320,256},{384,320},{4... | collective-permute-start | bytes 1572872 | tf_op jit(solution)/shard_map/ppermute | solution.py:70
  91.3 4.0 %collective-permute-start.8 = (bf16[8,256,256]{2,1,0:T(8,128)(2,1)S(1)}, bf16[8,256,256]{2,1,0:T(8,128)(2,1)S(1)}, u32[]{:S(2)}, u32[]{:S(2)}) collective-permute-start(bf16[8,256,256]{2,1,0:T(8,128)(2,1)S(1)} %all-to-all-done.1), channel_id=1, source_target_pairs={{0,48},{16,0},{32,16},{48,32},{1,49},{17,1},{33,17},{49,33},{2,50}... | collective-permute-start | bytes 3145736 | tf_op jit(solution)/shard_map/ppermute | solution.py:70
  95.3 1.1 collective-permute-done.4
  96.3 1.9 %collective-permute-start.6 = (bf16[1024,256]{1,0:T(8,128)(2,1)S(1)}, bf16[1024,256]{1,0:T(8,128)(2,1)S(1)}, u32[]{:S(2)}, u32[]{:S(2)}) collective-permute-start(bf16[1024,256]{1,0:T(8,128)(2,1)S(1)} %collective-permute-done.4), channel_id=1, source_target_pairs={{0,64},{64,128},{128,192},{192,256},{256,320},{320,384},{384,448},... | collective-permute-start | bytes 1572872 | tf_op jit(solution)/shard_map/ppermute | solution.py:68
  98.2 2.2 %collective-permute-start.9 = (bf16[8,256,256]{2,1,0:T(8,128)(2,1)S(1)}, bf16[8,256,256]{2,1,0:T(8,128)(2,1)S(1)}, u32[]{:S(2)}, u32[]{:S(2)}) collective-permute-start(bf16[8,256,256]{2,1,0:T(8,128)(2,1)S(1)} %collective-permute-done.7), channel_id=1, source_target_pairs={{0,16},{16,32},{32,48},{48,0},{1,17},{17,33},{33,49},{49,1},{2,18}... | collective-permute-start | bytes 3145736 | tf_op jit(solution)/shard_map/ppermute | solution.py:68
  100.5 2.6 %broadcast_in_dim.24 = bf16[8,4,256,256]{3,2,1,0:T(8,128)(2,1)} broadcast(bf16[]{:T(256)} %constant.100.clone.1), dimensions={} | broadcast | bytes 4194306 | tf_op jit(solution)/shard_map/broadcast_in_dim | solution.py:100
  103.0 1.1 bitcast_dynamic-update-slice_fusion.2
  104.2 5.4 %collective-permute-done.6 = bf16[1024,256]{1,0:T(8,128)(2,1)S(1)} collective-permute-done((bf16[1024,256]{1,0:T(8,128)(2,1)S(1)}, bf16[1024,256]{1,0:T(8,128)(2,1)S(1)}, u32[]{:S(2)}, u32[]{:S(2)}) %collective-permute-start.6) | collective-permute-done | bytes 524320 | tf_op jit(solution)/shard_map/ppermute | solution.py:68
  109.6 1.1 bitcast_dynamic-update-slice_fusion.1
  110.7 4.1 %collective-permute-done.8 = bf16[8,256,256]{2,1,0:T(8,128)(2,1)S(1)} collective-permute-done((bf16[8,256,256]{2,1,0:T(8,128)(2,1)S(1)}, bf16[8,256,256]{2,1,0:T(8,128)(2,1)S(1)}, u32[]{:S(2)}, u32[]{:S(2)}) %collective-permute-start.8) | collective-permute-done | bytes 1048608 | tf_op jit(solution)/shard_map/ppermute | solution.py:70
  114.9 1.1 bitcast_dynamic-update-slice_fusion
  115.9 6.8 %collective-permute-done.9 = bf16[8,256,256]{2,1,0:T(8,128)(2,1)S(1)} collective-permute-done((bf16[8,256,256]{2,1,0:T(8,128)(2,1)S(1)}, bf16[8,256,256]{2,1,0:T(8,128)(2,1)S(1)}, u32[]{:S(2)}, u32[]{:S(2)}) %collective-permute-start.9) | collective-permute-done | bytes 1048608 | tf_op jit(solution)/shard_map/ppermute | solution.py:68
  122.7 1.0 bitcast_dynamic-update-slice_fusion.3
  123.7 6.6 %fusion.9 = (f32[384]{0:T(512)S(1)}, f32[256,384]{1,0:T(8,128)S(1)}) fusion(bf16[8192,256]{1,0:T(8,128)(2,1)} %bitcast.8, bf16[384,8192]{1,0:T(8,128)(2,1)} %all-gather.2.cloned.1.call-done), kind=kOutput, calls=%fused_computation.45 | convolution fusion | flops 1610710656 | bytes 10880512 | tf_op jit(solution)/shard_map/dot_general | solution.py:116
  130.4 0.5 copy-done.8
  130.9 2.4 %fusion.8 = (f32[384]{0:T(512)S(1)}, f32[256,384]{1,0:T(8,128)S(1)}) fusion(bf16[8192,256]{1,0:T(8,128)(2,1)S(1)} %copy-done.1, bf16[384,8192]{1,0:T(8,128)(2,1)S(1)} %copy-done.8), kind=kOutput, calls=%fused_computation.44 | convolution fusion | flops 1610710656 | bytes 10880512 | tf_op jit(solution)/shard_map/dot_general | solution.py:115
  133.3 0.3 fusion
  133.6 0.6 broadcast_in_dim.31
  134.2 14.6 %all-to-all-start.2 = ((f32[16,4,384]{2,1,0:T(4,128)}), f32[16,4,384]{2,1,0:T(4,128)S(1)}, u32[]{:S(2)}, u32[]{:S(2)}) async-start(f32[16,4,384]{2,1,0:T(4,128)} %broadcast_in_dim.31), calls=%async_computation.2 | async-start | bytes 196608 | tf_op jit(solution)/shard_map/all_to_all | solution.py:130
  148.8 0.1 convert_reduce_fusion
  148.9 8.4 %all-to-all-done.2 = f32[16,4,384]{2,1,0:T(4,128)S(1)} async-done(((f32[16,4,384]{2,1,0:T(4,128)}), f32[16,4,384]{2,1,0:T(4,128)S(1)}, u32[]{:S(2)}, u32[]{:S(2)}) %all-to-all-start.2) | async-done | bytes 98336 | tf_op jit(solution)/shard_map/all_to_all | solution.py:130
  157.3 0.1 fusion.7
  157.5 0.1 select_reduce_fusion.1
  157.6 0.6 broadcast_in_dim.64
  158.2 6.4 %all-to-all-start.3 = ((f32[32,1,32]{2,1,0:T(1,128)}), f32[32,1,32]{2,1,0:T(1,128)S(1)}, u32[]{:S(2)}, u32[]{:S(2)}) async-start(f32[32,1,32]{2,1,0:T(1,128)} %broadcast_in_dim.64), calls=%async_computation.3 | async-start | bytes 32768 | tf_op jit(solution)/shard_map/all_to_all | solution.py:154
  164.7 0.6 dynamic_slice.6
  165.3 0.6 dynamic_slice.7
  165.8 7.4 %all-to-all-done.3 = f32[32,1,32]{2,1,0:T(1,128)S(1)} async-done(((f32[32,1,32]{2,1,0:T(1,128)}), f32[32,1,32]{2,1,0:T(1,128)S(1)}, u32[]{:S(2)}, u32[]{:S(2)}) %all-to-all-start.3) | async-done | bytes 4128 | tf_op jit(solution)/shard_map/all_to_all | solution.py:154
  173.4 0.1 reduce_sum.99
  173.7 0.5 sub.81
  (48 shorter events, 0.8 us)
Async XLA Ops:
  7.2 64.1 %copy-start.7 = (s32[32]{0:T(128)S(1)}, s32[32]{0:T(128)}, u32[]{:S(2)}) copy-start(s32[32]{0:T(128)} %param.15) | copy-start | bytes 388
  7.2 69.0 %copy-start.2 = (s32[384]{0:T(512)S(1)}, s32[384]{0:T(512)}, u32[]{:S(2)}) copy-start(s32[384]{0:T(512)} %param.10) | copy-start | bytes 4612
  7.2 116.6 %all-gather.2.cloned.1.call-start = ((), (), s32[]{:S(2)}) async-start(), calls=%async_computation.4 | async-start | bytes 6684672 | tf_op jit(solution)/shard_map/all_gather | solution.py:111
  21.6 47.2 %all-to-all-start.1 = ((bf16[8,256,256]{2,1,0:T(8,128)(2,1)}), bf16[8,256,256]{2,1,0:T(8,128)(2,1)S(1)}, u32[]{:S(2)}, u32[]{:S(2)}) async-start(bf16[8,256,256]{2,1,0:T(8,128)(2,1)} %broadcast_in_dim.25), calls=%async_computation.1 | async-start | bytes 2097152 | tf_op jit(solution)/shard_map/all_to_all | solution.py:79
  30.1 36.9 %collective-permute-start = (bf16[1024,256]{1,0:T(8,128)(2,1)S(1)}, bf16[1024,256]{1,0:T(8,128)(2,1)}, u32[]{:S(2)}, u32[]{:S(2)}) collective-permute-start(bf16[1024,256]{1,0:T(8,128)(2,1)S(1)} %bitcast.44), channel_id=1, source_target_pairs={{0,64},{64,128},{128,192},{192,256},{256,320},{320,384},{384,448},... | collective-permute-start | bytes 1572872 | tf_op jit(solution)/shard_map/ppermute | solution.py:68
  33.4 38.1 %collective-permute-start.1 = (bf16[1024,256]{1,0:T(8,128)(2,1)S(1)}, bf16[1024,256]{1,0:T(8,128)(2,1)}, u32[]{:S(2)}, u32[]{:S(2)}) collective-permute-start(bf16[1024,256]{1,0:T(8,128)(2,1)S(1)} %bitcast.45), channel_id=1, source_target_pairs={{0,448},{64,0},{128,64},{192,128},{256,192},{320,256},{384,320},{4... | collective-permute-start | bytes 1572872 | tf_op jit(solution)/shard_map/ppermute | solution.py:70
  66.9 15.3 %collective-permute-start.2 = (bf16[1024,256]{1,0:T(8,128)(2,1)}, bf16[1024,256]{1,0:T(8,128)(2,1)S(1)}, u32[]{:S(2)}, u32[]{:S(2)}) collective-permute-start(bf16[1024,256]{1,0:T(8,128)(2,1)} %collective-permute-done), channel_id=1, source_target_pairs={{0,64},{64,128},{128,192},{192,256},{256,320},{320,384},{384,448},... | collective-permute-start | bytes 1572872 | tf_op jit(solution)/shard_map/ppermute | solution.py:68
  68.9 29.4 %collective-permute-start.7 = (bf16[8,256,256]{2,1,0:T(8,128)(2,1)S(1)}, bf16[8,256,256]{2,1,0:T(8,128)(2,1)S(1)}, u32[]{:S(2)}, u32[]{:S(2)}) collective-permute-start(bf16[8,256,256]{2,1,0:T(8,128)(2,1)S(1)} %all-to-all-done.1), channel_id=1, source_target_pairs={{0,16},{16,32},{32,48},{48,0},{1,17},{17,33},{33,49},{49,1},{2,18}... | collective-permute-start | bytes 3145736 | tf_op jit(solution)/shard_map/ppermute | solution.py:68
  71.6 15.0 %collective-permute-start.3 = (bf16[1024,256]{1,0:T(8,128)(2,1)}, bf16[1024,256]{1,0:T(8,128)(2,1)S(1)}, u32[]{:S(2)}, u32[]{:S(2)}) collective-permute-start(bf16[1024,256]{1,0:T(8,128)(2,1)} %collective-permute-done.1), channel_id=1, source_target_pairs={{0,448},{64,0},{128,64},{192,128},{256,192},{320,256},{384,320},{4... | collective-permute-start | bytes 1572872 | tf_op jit(solution)/shard_map/ppermute | solution.py:70
  82.2 14.1 %collective-permute-start.4 = (bf16[1024,256]{1,0:T(8,128)(2,1)S(1)}, bf16[1024,256]{1,0:T(8,128)(2,1)S(1)}, u32[]{:S(2)}, u32[]{:S(2)}) collective-permute-start(bf16[1024,256]{1,0:T(8,128)(2,1)S(1)} %collective-permute-done.2), channel_id=1, source_target_pairs={{0,64},{64,128},{128,192},{192,256},{256,320},{320,384},{384,448},... | collective-permute-start | bytes 1572872 | tf_op jit(solution)/shard_map/ppermute | solution.py:68
  86.6 17.5 %collective-permute-start.5 = (bf16[1024,256]{1,0:T(8,128)(2,1)S(1)}, bf16[1024,256]{1,0:T(8,128)(2,1)S(1)}, u32[]{:S(2)}, u32[]{:S(2)}) collective-permute-start(bf16[1024,256]{1,0:T(8,128)(2,1)S(1)} %collective-permute-done.3), channel_id=1, source_target_pairs={{0,448},{64,0},{128,64},{192,128},{256,192},{320,256},{384,320},{4... | collective-permute-start | bytes 1572872 | tf_op jit(solution)/shard_map/ppermute | solution.py:70
  91.3 23.6 %collective-permute-start.8 = (bf16[8,256,256]{2,1,0:T(8,128)(2,1)S(1)}, bf16[8,256,256]{2,1,0:T(8,128)(2,1)S(1)}, u32[]{:S(2)}, u32[]{:S(2)}) collective-permute-start(bf16[8,256,256]{2,1,0:T(8,128)(2,1)S(1)} %all-to-all-done.1), channel_id=1, source_target_pairs={{0,48},{16,0},{32,16},{48,32},{1,49},{17,1},{33,17},{49,33},{2,50}... | collective-permute-start | bytes 3145736 | tf_op jit(solution)/shard_map/ppermute | solution.py:70
  96.3 13.2 %collective-permute-start.6 = (bf16[1024,256]{1,0:T(8,128)(2,1)S(1)}, bf16[1024,256]{1,0:T(8,128)(2,1)S(1)}, u32[]{:S(2)}, u32[]{:S(2)}) collective-permute-start(bf16[1024,256]{1,0:T(8,128)(2,1)S(1)} %collective-permute-done.4), channel_id=1, source_target_pairs={{0,64},{64,128},{128,192},{192,256},{256,320},{320,384},{384,448},... | collective-permute-start | bytes 1572872 | tf_op jit(solution)/shard_map/ppermute | solution.py:68
  98.2 24.5 %collective-permute-start.9 = (bf16[8,256,256]{2,1,0:T(8,128)(2,1)S(1)}, bf16[8,256,256]{2,1,0:T(8,128)(2,1)S(1)}, u32[]{:S(2)}, u32[]{:S(2)}) collective-permute-start(bf16[8,256,256]{2,1,0:T(8,128)(2,1)S(1)} %collective-permute-done.7), channel_id=1, source_target_pairs={{0,16},{16,32},{32,48},{48,0},{1,17},{17,33},{33,49},{49,1},{2,18}... | collective-permute-start | bytes 3145736 | tf_op jit(solution)/shard_map/ppermute | solution.py:68
  109.6 5.3 %copy-start = (bf16[8192,256]{1,0:T(8,128)(2,1)}, bf16[8192,256]{1,0:T(8,128)(2,1)S(1)}, u32[]{:S(2)}) copy-start(bf16[8192,256]{1,0:T(8,128)(2,1)S(1)} %constant_dynamic-update-slice_fusion) | copy-start | bytes 12582916
  123.7 6.6 %copy-start.1 = (bf16[8192,256]{1,0:T(8,128)(2,1)S(1)}, bf16[8192,256]{1,0:T(8,128)(2,1)}, u32[]{:S(2)}) copy-start(bf16[8192,256]{1,0:T(8,128)(2,1)} %copy-done) | copy-start | bytes 12582916
  123.7 7.1 %copy-start.8 = (bf16[384,8192]{1,0:T(8,128)(2,1)S(1)}, bf16[384,8192]{1,0:T(8,128)(2,1)}, u32[]{:S(2)}) copy-start(bf16[384,8192]{1,0:T(8,128)(2,1)} %all-gather.2.cloned.1.call-done) | copy-start | bytes 18874372
  130.9 26.6 %copy-start.3 = (f32[384]{0:T(512)S(1)}, f32[384]{0:T(512)}, u32[]{:S(2)}) copy-start(f32[384]{0:T(512)} %param.13) | copy-start | bytes 4612
  130.9 26.6 %copy-start.4 = (s32[384]{0:T(512)S(1)}, s32[384]{0:T(512)}, u32[]{:S(2)}) copy-start(s32[384]{0:T(512)} %param.11) | copy-start | bytes 4612
  130.9 26.6 %copy-start.5 = (f32[384]{0:T(512)S(1)}, f32[384]{0:T(512)}, u32[]{:S(2)}) copy-start(f32[384]{0:T(512)} %param.12) | copy-start | bytes 4612
  130.9 26.6 %copy-start.6 = (f32[384]{0:T(512)S(1)}, f32[384]{0:T(512)}, u32[]{:S(2)}) copy-start(f32[384]{0:T(512)} %param.14) | copy-start | bytes 4612
  134.2 23.0 %all-to-all-start.2 = ((f32[16,4,384]{2,1,0:T(4,128)}), f32[16,4,384]{2,1,0:T(4,128)S(1)}, u32[]{:S(2)}, u32[]{:S(2)}) async-start(f32[16,4,384]{2,1,0:T(4,128)} %broadcast_in_dim.31), calls=%async_computation.2 | async-start | bytes 196608 | tf_op jit(solution)/shard_map/all_to_all | solution.py:130
  158.2 15.0 %all-to-all-start.3 = ((f32[32,1,32]{2,1,0:T(1,128)}), f32[32,1,32]{2,1,0:T(1,128)S(1)}, u32[]{:S(2)}, u32[]{:S(2)}) async-start(f32[32,1,32]{2,1,0:T(1,128)} %broadcast_in_dim.64), calls=%async_computation.3 | async-start | bytes 32768 | tf_op jit(solution)/shard_map/all_to_all | solution.py:154
Sparse Core Ops, SparseCore 0:
  10.2 55.3 all-gather.1

commit v11 on v8

--- a/solution.py
+++ b/solution.py
@@ -1,6 +1,8 @@
 import jax
 import jax.numpy as jnp
 from jax import lax
+from jax.experimental import pallas as pl
+from jax.experimental.pallas import tpu as pltpu
 from jax.sharding import PartitionSpec as P
 
 VOCAB = 128256
@@ -56,6 +58,39 @@
     return full
 
 
+def logits_kernel(h_ref, w_ref, o_ref, acc_ref):
+    @pl.when(pl.program_id(0) == 0)
+    def _():
+        acc_ref[...] = jnp.zeros_like(acc_ref)
+
+    acc_ref[...] += jnp.dot(h_ref[...], w_ref[...], preferred_element_type=jnp.float32)
+
+    @pl.when(pl.program_id(0) == pl.num_programs(0) - 1)
+    def _():
+        o_ref[...] = acc_ref[...]
+
+
+def logits_of(rows, head_full):
+    m, k = rows.shape
+    n = head_full.shape[1]
+    depth = 2048 if k % 2048 == 0 else k
+    return pl.pallas_call(
+        logits_kernel,
+        out_shape=jax.ShapeDtypeStruct((m, n), jnp.float32),
+        grid=(k // depth,),
+        in_specs=[
+            pl.BlockSpec((m, depth), lambda i: (0, i)),
+            pl.BlockSpec((depth, n), lambda i: (i, 0)),
+        ],
+        out_specs=pl.BlockSpec((m, n), lambda i: (0, 0)),
+        scratch_shapes=[pltpu.VMEM((m, n), jnp.float32)],
+        compiler_params=pltpu.CompilerParams(dimension_semantics=("arbitrary",)),
+        cost_estimate=pl.CostEstimate(
+            flops=2 * m * k * n, transcendentals=0, bytes_accessed=2 * (m * k + k * n) + 4 * m * n
+        ),
+    )(rows, head_full)
+
+
 def local(hidden, head, targets, live, prior_lse, prior_mean, prior_target, seq_lengths):
     rows_here = hidden.shape[0]
     cols_here = head.shape[1]
@@ -64,11 +99,7 @@
     block_first = VOCAB - cols_here * spread
     first_col = block_first + which * cols_here
     gathered = gather_hidden(hidden)
-    logits = jnp.dot(
-        gathered,
-        lax.all_gather(head, ROW_AXES, axis=0, tiled=True),
-        preferred_element_type=jnp.float32,
-    )
+    logits = logits_of(gathered, lax.all_gather(head, ROW_AXES, axis=0, tiled=True))
     row_peak = jnp.max(logits, axis=1)
     weights = jnp.exp(logits - row_peak[:, None])
     row_mass = jnp.sum(weights, axis=1)

time: 169 us -> 172 us (1.018)
  Pallas kernels: 0 us -> 8.4 us
  matrix products: 8 us -> 0 us
  other arithmetic: 2.39 us -> 4.77 us
    pallas_call x0 -> x1, Pallas kernels: none -> 8.4 us  [logits_of(): pl.pallas_call(logits_kernel, out_shape=jax.ShapeDtypeStruct((m, n), jnp....]
    dot_general x1 -> x0, matrix products: 8 us -> none  [local(): jnp.dot(gathered, lax.all_gather(head, ROW_AXES, axis=0, tiled=True), pre...]
  transfers between devices with their start and end apart: 18 -> 18, of which waited for: 6 -> 6; matrix products, arithmetic and copies ran while one was open for 12% -> 11% of each run, Pallas kernels for 0% -> 0%
where the time goes in v11:
time: 172 us; the launch traced here: 171 us
  starting transfers between devices  63.2 us (37%)
  waiting for transfers between devices  60.7 us (35%)
  local copies, waits for them, and re-layouts  20 us (12%)
  between operations  14.4 us (8%)
  Pallas kernels  8.4 us (5%)
  other arithmetic  4.77 us (3%)
    all_gather x1, waiting for transfers between devices, local(): lax.all_gather(head, ROW_AXES, axis=0, tiled=True)  32.4 us
    ppermute x8, starting transfers between devices, share(): other = lax.ppermute(piece, 'c', across)  20.6 us
    ppermute x3, starting transfers between devices, gather_hidden(): bwd = lax.ppermute(bwd, 'z', behind)  18 us
    dynamic_update_slice x16, local copies, waits for them, and re-layouts, place(): return lax.dynamic_update_slice(buf, piece, (0, slot))  13.1 us
    ppermute x4, waiting for transfers between devices, gather_hidden(): fwd = lax.ppermute(fwd, 'z', ahead)  11.8 us
    ppermute x4, starting transfers between devices, gather_hidden(): fwd = lax.ppermute(fwd, 'z', ahead)  10.6 us
    all_to_all x1, starting transfers between devices, local(): every = lax.all_to_all(copies, VOCAB_AXES, 0, 0, tiled=True)  8.48 us
    pallas_call x1, Pallas kernels, logits_of(): pl.pallas_call(logits_kernel, out_shape=jax.ShapeDtypeStruct((m, n), jnp....  8.4 us
  transfers between devices with their start and end apart: 18, of which 6 were waited for; matrix products, arithmetic and copies ran while one was open for 11% of the time, Pallas kernels for 0%

profile of v11, /device:TPU:1, one launch (start us, length us, event | category | flops | bytes accessed | tf_op | source)
XLA Modules:
  0.0 171.4 jit_solution(967046157605163425)
XLA Ops:
  7.2 0.7 all-gather.2.cloned.1.call-update
  7.9 4.8 %collective-permute-start.1 = (bf16[384,512]{1,0:T(8,128)(2,1)}, bf16[384,512]{1,0:T(8,128)(2,1)S(1)}, u32[]{:S(2)}, u32[]{:S(2)}) collective-permute-start(bf16[384,512]{1,0:T(8,128)(2,1)} %param.8), channel_id=1, source_target_pairs={{0,2},{2,4},{4,6},{6,8},{8,10},{10,12},{12,14},{14,0},{1,3},{3,5},... | collective-permute-start | bytes 1179656 | tf_op jit(solution)/shard_map/ppermute | solution.py:52
  12.7 8.6 %collective-permute-start.3 = (bf16[384,512]{1,0:T(8,128)(2,1)}, bf16[384,512]{1,0:T(8,128)(2,1)S(1)}, u32[]{:S(2)}, u32[]{:S(2)}) collective-permute-start(bf16[384,512]{1,0:T(8,128)(2,1)} %param.8), channel_id=1, source_target_pairs={{0,14},{2,0},{4,2},{6,4},{8,6},{10,8},{12,10},{14,12},{1,15},{3,1}... | collective-permute-start | bytes 1179656 | tf_op jit(solution)/shard_map/ppermute | solution.py:54
  21.3 2.9 %collective-permute-start = (bf16[384,512]{1,0:T(8,128)(2,1)}, bf16[384,512]{1,0:T(8,128)(2,1)S(1)}, u32[]{:S(2)}, u32[]{:S(2)}) collective-permute-start(bf16[384,512]{1,0:T(8,128)(2,1)} %param.8), channel_id=1, source_target_pairs={{0,1},{1,0},{2,3},{3,2},{4,5},{5,4},{6,7},{7,6},{8,9},{9,8},{10,11... | collective-permute-start | bytes 1179656 | tf_op jit(solution)/shard_map/ppermute | solution.py:44
  24.2 4.2 %collective-permute-done.1 = bf16[384,512]{1,0:T(8,128)(2,1)S(1)} collective-permute-done((bf16[384,512]{1,0:T(8,128)(2,1)}, bf16[384,512]{1,0:T(8,128)(2,1)S(1)}, u32[]{:S(2)}, u32[]{:S(2)}) %collective-permute-start.1) | collective-permute-done | bytes 393248 | tf_op jit(solution)/shard_map/ppermute | solution.py:52
  28.4 3.1 %collective-permute-start.2 = (bf16[384,512]{1,0:T(8,128)(2,1)S(1)}, bf16[384,512]{1,0:T(8,128)(2,1)S(1)}, u32[]{:S(2)}, u32[]{:S(2)}) collective-permute-start(bf16[384,512]{1,0:T(8,128)(2,1)S(1)} %collective-permute-done.1), channel_id=1, source_target_pairs={{0,1},{1,0},{2,3},{3,2},{4,5},{5,4},{6,7},{7,6},{8,9},{9,8},{10,11... | collective-permute-start | bytes 1179656 | tf_op jit(solution)/shard_map/ppermute | solution.py:44
  31.6 1.9 %collective-permute-start.5 = (bf16[384,512]{1,0:T(8,128)(2,1)S(1)}, bf16[384,512]{1,0:T(8,128)(2,1)S(1)}, u32[]{:S(2)}, u32[]{:S(2)}) collective-permute-start(bf16[384,512]{1,0:T(8,128)(2,1)S(1)} %collective-permute-done.1), channel_id=1, source_target_pairs={{0,2},{2,4},{4,6},{6,8},{8,10},{10,12},{12,14},{14,0},{1,3},{3,5},... | collective-permute-start | bytes 1179656 | tf_op jit(solution)/shard_map/ppermute | solution.py:52
  33.5 4.6 %collective-permute-start.7 = (bf16[384,512]{1,0:T(8,128)(2,1)S(1)}, bf16[384,512]{1,0:T(8,128)(2,1)S(1)}, u32[]{:S(2)}, u32[]{:S(2)}) collective-permute-start(bf16[384,512]{1,0:T(8,128)(2,1)S(1)} %collective-permute-done.3), channel_id=1, source_target_pairs={{0,14},{2,0},{4,2},{6,4},{8,6},{10,8},{12,10},{14,12},{1,15},{3,1}... | collective-permute-start | bytes 1179656 | tf_op jit(solution)/shard_map/ppermute | solution.py:54
  38.1 0.7 broadcast_subtract_fusion
  38.8 0.7 copy.21
  39.8 3.5 %broadcast_in_dim.8 = bf16[384,8192]{1,0:T(8,128)(2,1)} broadcast(bf16[]{:T(256)} %constant.94.clone.1), dimensions={} | broadcast | bytes 6291458 | tf_op jit(solution)/shard_map/broadcast_in_dim | solution.py:35
  43.2 0.9 constant_dynamic-update-slice_fusion.15
  44.1 2.5 %collective-permute-start.4 = (bf16[384,512]{1,0:T(8,128)(2,1)S(1)}, bf16[384,512]{1,0:T(8,128)(2,1)S(1)}, u32[]{:S(2)}, u32[]{:S(2)}) collective-permute-start(bf16[384,512]{1,0:T(8,128)(2,1)S(1)} %collective-permute-done.3), channel_id=1, source_target_pairs={{0,1},{1,0},{2,3},{3,2},{4,5},{5,4},{6,7},{7,6},{8,9},{9,8},{10,11... | collective-permute-start | bytes 1179656 | tf_op jit(solution)/shard_map/ppermute | solution.py:44
  46.6 0.9 constant_dynamic-update-slice_fusion.14
  47.5 0.8 constant_dynamic-update-slice_fusion.13
  48.3 1.9 %collective-permute-start.6 = (bf16[384,512]{1,0:T(8,128)(2,1)S(1)}, bf16[384,512]{1,0:T(8,128)(2,1)S(1)}, u32[]{:S(2)}, u32[]{:S(2)}) collective-permute-start(bf16[384,512]{1,0:T(8,128)(2,1)S(1)} %collective-permute-done.5), channel_id=1, source_target_pairs={{0,1},{1,0},{2,3},{3,2},{4,5},{5,4},{6,7},{7,6},{8,9},{9,8},{10,11... | collective-permute-start | bytes 1179656 | tf_op jit(solution)/shard_map/ppermute | solution.py:44
  50.2 1.9 %collective-permute-start.9 = (bf16[384,512]{1,0:T(8,128)(2,1)S(1)}, bf16[384,512]{1,0:T(8,128)(2,1)S(1)}, u32[]{:S(2)}, u32[]{:S(2)}) collective-permute-start(bf16[384,512]{1,0:T(8,128)(2,1)S(1)} %collective-permute-done.5), channel_id=1, source_target_pairs={{0,2},{2,4},{4,6},{6,8},{8,10},{10,12},{12,14},{14,0},{1,3},{3,5},... | collective-permute-start | bytes 1179656 | tf_op jit(solution)/shard_map/ppermute | solution.py:52
  52.1 2.4 %collective-permute-start.8 = (bf16[384,512]{1,0:T(8,128)(2,1)S(1)}, bf16[384,512]{1,0:T(8,128)(2,1)S(1)}, u32[]{:S(2)}, u32[]{:S(2)}) collective-permute-start(bf16[384,512]{1,0:T(8,128)(2,1)S(1)} %collective-permute-done.7), channel_id=1, source_target_pairs={{0,1},{1,0},{2,3},{3,2},{4,5},{5,4},{6,7},{7,6},{8,9},{9,8},{10,11... | collective-permute-start | bytes 1179656 | tf_op jit(solution)/shard_map/ppermute | solution.py:44
  54.6 4.9 %collective-permute-start.11 = (bf16[384,512]{1,0:T(8,128)(2,1)S(1)}, bf16[384,512]{1,0:T(8,128)(2,1)S(1)}, u32[]{:S(2)}, u32[]{:S(2)}) collective-permute-start(bf16[384,512]{1,0:T(8,128)(2,1)S(1)} %collective-permute-done.7), channel_id=1, source_target_pairs={{0,14},{2,0},{4,2},{6,4},{8,6},{10,8},{12,10},{14,12},{1,15},{3,1}... | collective-permute-start | bytes 1179656 | tf_op jit(solution)/shard_map/ppermute | solution.py:54
  59.4 0.8 constant_dynamic-update-slice_fusion.12
  60.2 0.8 constant_dynamic-update-slice_fusion.11
  61.1 0.8 constant_dynamic-update-slice_fusion.10
  61.9 0.8 constant_dynamic-update-slice_fusion.9
  62.7 0.8 collective-permute-done.9
  63.5 3.2 %collective-permute-start.10 = (bf16[384,512]{1,0:T(8,128)(2,1)S(1)}, bf16[384,512]{1,0:T(8,128)(2,1)S(1)}, u32[]{:S(2)}, u32[]{:S(2)}) collective-permute-start(bf16[384,512]{1,0:T(8,128)(2,1)S(1)} %collective-permute-done.9), channel_id=1, source_target_pairs={{0,1},{1,0},{2,3},{3,2},{4,5},{5,4},{6,7},{7,6},{8,9},{9,8},{10,11... | collective-permute-start | bytes 1179656 | tf_op jit(solution)/shard_map/ppermute | solution.py:44
  66.7 1.9 %collective-permute-start.13 = (bf16[384,512]{1,0:T(8,128)(2,1)S(1)}, bf16[384,512]{1,0:T(8,128)(2,1)S(1)}, u32[]{:S(2)}, u32[]{:S(2)}) collective-permute-start(bf16[384,512]{1,0:T(8,128)(2,1)S(1)} %collective-permute-done.9), channel_id=1, source_target_pairs={{0,2},{2,4},{4,6},{6,8},{8,10},{10,12},{12,14},{14,0},{1,3},{3,5},... | collective-permute-start | bytes 1179656 | tf_op jit(solution)/shard_map/ppermute | solution.py:52
  68.7 1.9 %collective-permute-start.12 = (bf16[384,512]{1,0:T(8,128)(2,1)S(1)}, bf16[384,512]{1,0:T(8,128)(2,1)S(1)}, u32[]{:S(2)}, u32[]{:S(2)}) collective-permute-start(bf16[384,512]{1,0:T(8,128)(2,1)S(1)} %collective-permute-done.11), channel_id=1, source_target_pairs={{0,1},{1,0},{2,3},{3,2},{4,5},{5,4},{6,7},{7,6},{8,9},{9,8},{10,11... | collective-permute-start | bytes 1179656 | tf_op jit(solution)/shard_map/ppermute | solution.py:44
  70.6 0.8 constant_dynamic-update-slice_fusion.8
  71.4 0.8 constant_dynamic-update-slice_fusion.7
  72.3 0.8 constant_dynamic-update-slice_fusion.6
  73.1 0.8 constant_dynamic-update-slice_fusion.5
  73.9 6.8 %collective-permute-done.13 = bf16[384,512]{1,0:T(8,128)(2,1)S(1)} collective-permute-done((bf16[384,512]{1,0:T(8,128)(2,1)S(1)}, bf16[384,512]{1,0:T(8,128)(2,1)S(1)}, u32[]{:S(2)}, u32[]{:S(2)}) %collective-permute-start.13) | collective-permute-done | bytes 393248 | tf_op jit(solution)/shard_map/ppermute | solution.py:52
  80.7 2.6 %collective-permute-start.14 = (bf16[384,512]{1,0:T(8,128)(2,1)S(1)}, bf16[384,512]{1,0:T(8,128)(2,1)S(1)}, u32[]{:S(2)}, u32[]{:S(2)}) collective-permute-start(bf16[384,512]{1,0:T(8,128)(2,1)S(1)} %collective-permute-done.13), channel_id=1, source_target_pairs={{0,1},{1,0},{2,3},{3,2},{4,5},{5,4},{6,7},{7,6},{8,9},{9,8},{10,11... | collective-permute-start | bytes 1179656 | tf_op jit(solution)/shard_map/ppermute | solution.py:44
  83.3 0.8 constant_dynamic-update-slice_fusion.4
  84.1 0.8 constant_dynamic-update-slice_fusion.3
  84.9 0.8 constant_dynamic-update-slice_fusion.2
  85.7 0.8 constant_dynamic-update-slice_fusion.1
  86.5 0.8 constant_dynamic-update-slice_fusion.h_ref
  87.4 32.4 %all-gather.2.cloned.1.call-done.w_ref = bf16[8192,512]{1,0:T(8,128)(2,1)} async-done(((bf16[256,512]{1,0:T(8,128)(2,1)}), bf16[8192,512]{1,0:T(8,128)(2,1)}) %all-gather.2.cloned.1.call-update) | async-done | bytes 8388624 | tf_op jit(solution)/shard_map/all_gather | solution.py:102
  119.7 8.4 %shard_map.103 = f32[384,512]{1,0:T(8,128)} custom-call(bf16[384,8192]{1,0:T(8,128)(2,1)} %constant_dynamic-update-slice_fusion.h_ref, bf16[8192,512]{1,0:T(8,128)(2,1)} %all-gather.2.cloned.1.call-done.w_ref), custom_call_target="tpu_custom_call" | custom-call | flops 3221225472 | bytes 15466496 | tf_op jit(solution)/shard_map/pallas_call | solution.py:77
  128.1 1.3 reduce_max.18
  129.4 1.6 fusion
  131.0 0.6 broadcast_in_dim.10
  131.7 8.5 %all-to-all-start = ((f32[16,4,384]{2,1,0:T(4,128)}), f32[16,4,384]{2,1,0:T(4,128)S(1)}, u32[]{:S(2)}, u32[]{:S(2)}) async-start(f32[16,4,384]{2,1,0:T(4,128)} %broadcast_in_dim.10), calls=%async_computation | async-start | bytes 196608 | tf_op jit(solution)/shard_map/all_to_all | solution.py:113
  140.3 8.4 %all-to-all-done = f32[16,4,384]{2,1,0:T(4,128)S(1)} async-done(((f32[16,4,384]{2,1,0:T(4,128)}), f32[16,4,384]{2,1,0:T(4,128)S(1)}, u32[]{:S(2)}, u32[]{:S(2)}) %all-to-all-start) | async-done | bytes 98336 | tf_op jit(solution)/shard_map/all_to_all | solution.py:113
  149.0 0.6 broadcast_in_dim.11
  149.6 5.5 %all-to-all-start.1 = ((f32[32,1,32]{2,1,0:T(1,128)}), f32[32,1,32]{2,1,0:T(1,128)S(1)}, u32[]{:S(2)}, u32[]{:S(2)}) async-start(f32[32,1,32]{2,1,0:T(1,128)} %broadcast_in_dim.11), calls=%async_computation.1 | async-start | bytes 32768 | tf_op jit(solution)/shard_map/all_to_all | solution.py:137
  156.2 7.4 %all-to-all-done.1 = f32[32,1,32]{2,1,0:T(1,128)S(1)} async-done(((f32[32,1,32]{2,1,0:T(1,128)}), f32[32,1,32]{2,1,0:T(1,128)S(1)}, u32[]{:S(2)}, u32[]{:S(2)}) %all-to-all-start.1) | async-done | bytes 4128 | tf_op jit(solution)/shard_map/all_to_all | solution.py:137
  (50 shorter events, 2.7 us)
Async XLA Ops:
  7.2 36.1 %copy-start = (bf16[384,512]{1,0:T(8,128)(2,1)S(1)}, bf16[384,512]{1,0:T(8,128)(2,1)}, u32[]{:S(2)}) copy-start(bf16[384,512]{1,0:T(8,128)(2,1)} %param.8) | copy-start | bytes 1179652
  7.2 112.5 %all-gather.2.cloned.1.call-start = ((), (), s32[]{:S(2)}) async-start(), calls=%async_computation.2 | async-start | bytes 8650752 | tf_op jit(solution)/shard_map/all_gather | solution.py:102
  7.9 20.5 %collective-permute-start.1 = (bf16[384,512]{1,0:T(8,128)(2,1)}, bf16[384,512]{1,0:T(8,128)(2,1)S(1)}, u32[]{:S(2)}, u32[]{:S(2)}) collective-permute-start(bf16[384,512]{1,0:T(8,128)(2,1)} %param.8), channel_id=1, source_target_pairs={{0,2},{2,4},{4,6},{6,8},{8,10},{10,12},{12,14},{14,0},{1,3},{3,5},... | collective-permute-start | bytes 1179656 | tf_op jit(solution)/shard_map/ppermute | solution.py:52
  12.7 20.8 %collective-permute-start.3 = (bf16[384,512]{1,0:T(8,128)(2,1)}, bf16[384,512]{1,0:T(8,128)(2,1)S(1)}, u32[]{:S(2)}, u32[]{:S(2)}) collective-permute-start(bf16[384,512]{1,0:T(8,128)(2,1)} %param.8), channel_id=1, source_target_pairs={{0,14},{2,0},{4,2},{6,4},{8,6},{10,8},{12,10},{14,12},{1,15},{3,1}... | collective-permute-start | bytes 1179656 | tf_op jit(solution)/shard_map/ppermute | solution.py:54
  21.3 25.2 %collective-permute-start = (bf16[384,512]{1,0:T(8,128)(2,1)}, bf16[384,512]{1,0:T(8,128)(2,1)S(1)}, u32[]{:S(2)}, u32[]{:S(2)}) collective-permute-start(bf16[384,512]{1,0:T(8,128)(2,1)} %param.8), channel_id=1, source_target_pairs={{0,1},{1,0},{2,3},{3,2},{4,5},{5,4},{6,7},{7,6},{8,9},{9,8},{10,11... | collective-permute-start | bytes 1179656 | tf_op jit(solution)/shard_map/ppermute | solution.py:44
  28.4 26.1 %collective-permute-start.2 = (bf16[384,512]{1,0:T(8,128)(2,1)S(1)}, bf16[384,512]{1,0:T(8,128)(2,1)S(1)}, u32[]{:S(2)}, u32[]{:S(2)}) collective-permute-start(bf16[384,512]{1,0:T(8,128)(2,1)S(1)} %collective-permute-done.1), channel_id=1, source_target_pairs={{0,1},{1,0},{2,3},{3,2},{4,5},{5,4},{6,7},{7,6},{8,9},{9,8},{10,11... | collective-permute-start | bytes 1179656 | tf_op jit(solution)/shard_map/ppermute | solution.py:44
  31.6 16.7 %collective-permute-start.5 = (bf16[384,512]{1,0:T(8,128)(2,1)S(1)}, bf16[384,512]{1,0:T(8,128)(2,1)S(1)}, u32[]{:S(2)}, u32[]{:S(2)}) collective-permute-start(bf16[384,512]{1,0:T(8,128)(2,1)S(1)} %collective-permute-done.1), channel_id=1, source_target_pairs={{0,2},{2,4},{4,6},{6,8},{8,10},{10,12},{12,14},{14,0},{1,3},{3,5},... | collective-permute-start | bytes 1179656 | tf_op jit(solution)/shard_map/ppermute | solution.py:52
  33.5 18.6 %collective-permute-start.7 = (bf16[384,512]{1,0:T(8,128)(2,1)S(1)}, bf16[384,512]{1,0:T(8,128)(2,1)S(1)}, u32[]{:S(2)}, u32[]{:S(2)}) collective-permute-start(bf16[384,512]{1,0:T(8,128)(2,1)S(1)} %collective-permute-done.3), channel_id=1, source_target_pairs={{0,14},{2,0},{4,2},{6,4},{8,6},{10,8},{12,10},{14,12},{1,15},{3,1}... | collective-permute-start | bytes 1179656 | tf_op jit(solution)/shard_map/ppermute | solution.py:54
  44.1 16.9 %collective-permute-start.4 = (bf16[384,512]{1,0:T(8,128)(2,1)S(1)}, bf16[384,512]{1,0:T(8,128)(2,1)S(1)}, u32[]{:S(2)}, u32[]{:S(2)}) collective-permute-start(bf16[384,512]{1,0:T(8,128)(2,1)S(1)} %collective-permute-done.3), channel_id=1, source_target_pairs={{0,1},{1,0},{2,3},{3,2},{4,5},{5,4},{6,7},{7,6},{8,9},{9,8},{10,11... | collective-permute-start | bytes 1179656 | tf_op jit(solution)/shard_map/ppermute | solution.py:44
  48.3 22.4 %collective-permute-start.6 = (bf16[384,512]{1,0:T(8,128)(2,1)S(1)}, bf16[384,512]{1,0:T(8,128)(2,1)S(1)}, u32[]{:S(2)}, u32[]{:S(2)}) collective-permute-start(bf16[384,512]{1,0:T(8,128)(2,1)S(1)} %collective-permute-done.5), channel_id=1, source_target_pairs={{0,1},{1,0},{2,3},{3,2},{4,5},{5,4},{6,7},{7,6},{8,9},{9,8},{10,11... | collective-permute-start | bytes 1179656 | tf_op jit(solution)/shard_map/ppermute | solution.py:44
  50.2 13.3 %collective-permute-start.9 = (bf16[384,512]{1,0:T(8,128)(2,1)S(1)}, bf16[384,512]{1,0:T(8,128)(2,1)S(1)}, u32[]{:S(2)}, u32[]{:S(2)}) collective-permute-start(bf16[384,512]{1,0:T(8,128)(2,1)S(1)} %collective-permute-done.5), channel_id=1, source_target_pairs={{0,2},{2,4},{4,6},{6,8},{8,10},{10,12},{12,14},{14,0},{1,3},{3,5},... | collective-permute-start | bytes 1179656 | tf_op jit(solution)/shard_map/ppermute | solution.py:52
  52.1 20.1 %collective-permute-start.8 = (bf16[384,512]{1,0:T(8,128)(2,1)S(1)}, bf16[384,512]{1,0:T(8,128)(2,1)S(1)}, u32[]{:S(2)}, u32[]{:S(2)}) collective-permute-start(bf16[384,512]{1,0:T(8,128)(2,1)S(1)} %collective-permute-done.7), channel_id=1, source_target_pairs={{0,1},{1,0},{2,3},{3,2},{4,5},{5,4},{6,7},{7,6},{8,9},{9,8},{10,11... | collective-permute-start | bytes 1179656 | tf_op jit(solution)/shard_map/ppermute | solution.py:44
  54.6 14.1 %collective-permute-start.11 = (bf16[384,512]{1,0:T(8,128)(2,1)S(1)}, bf16[384,512]{1,0:T(8,128)(2,1)S(1)}, u32[]{:S(2)}, u32[]{:S(2)}) collective-permute-start(bf16[384,512]{1,0:T(8,128)(2,1)S(1)} %collective-permute-done.7), channel_id=1, source_target_pairs={{0,14},{2,0},{4,2},{6,4},{8,6},{10,8},{12,10},{14,12},{1,15},{3,1}... | collective-permute-start | bytes 1179656 | tf_op jit(solution)/shard_map/ppermute | solution.py:54
  63.5 19.8 %collective-permute-start.10 = (bf16[384,512]{1,0:T(8,128)(2,1)S(1)}, bf16[384,512]{1,0:T(8,128)(2,1)S(1)}, u32[]{:S(2)}, u32[]{:S(2)}) collective-permute-start(bf16[384,512]{1,0:T(8,128)(2,1)S(1)} %collective-permute-done.9), channel_id=1, source_target_pairs={{0,1},{1,0},{2,3},{3,2},{4,5},{5,4},{6,7},{7,6},{8,9},{9,8},{10,11... | collective-permute-start | bytes 1179656 | tf_op jit(solution)/shard_map/ppermute | solution.py:44
  66.7 13.9 %collective-permute-start.13 = (bf16[384,512]{1,0:T(8,128)(2,1)S(1)}, bf16[384,512]{1,0:T(8,128)(2,1)S(1)}, u32[]{:S(2)}, u32[]{:S(2)}) collective-permute-start(bf16[384,512]{1,0:T(8,128)(2,1)S(1)} %collective-permute-done.9), channel_id=1, source_target_pairs={{0,2},{2,4},{4,6},{6,8},{8,10},{10,12},{12,14},{14,0},{1,3},{3,5},... | collective-permute-start | bytes 1179656 | tf_op jit(solution)/shard_map/ppermute | solution.py:52
  68.7 16.2 %collective-permute-start.12 = (bf16[384,512]{1,0:T(8,128)(2,1)S(1)}, bf16[384,512]{1,0:T(8,128)(2,1)S(1)}, u32[]{:S(2)}, u32[]{:S(2)}) collective-permute-start(bf16[384,512]{1,0:T(8,128)(2,1)S(1)} %collective-permute-done.11), channel_id=1, source_target_pairs={{0,1},{1,0},{2,3},{3,2},{4,5},{5,4},{6,7},{7,6},{8,9},{9,8},{10,11... | collective-permute-start | bytes 1179656 | tf_op jit(solution)/shard_map/ppermute | solution.py:44
  80.7 5.9 %collective-permute-start.14 = (bf16[384,512]{1,0:T(8,128)(2,1)S(1)}, bf16[384,512]{1,0:T(8,128)(2,1)S(1)}, u32[]{:S(2)}, u32[]{:S(2)}) collective-permute-start(bf16[384,512]{1,0:T(8,128)(2,1)S(1)} %collective-permute-done.13), channel_id=1, source_target_pairs={{0,1},{1,0},{2,3},{3,2},{4,5},{5,4},{6,7},{7,6},{8,9},{9,8},{10,11... | collective-permute-start | bytes 1179656 | tf_op jit(solution)/shard_map/ppermute | solution.py:44
  87.3 61.5 %copy-start.1 = (s32[384]{0:T(512)S(1)}, s32[384]{0:T(512)}, u32[]{:S(2)}) copy-start(s32[384]{0:T(512)} %param.10) | copy-start | bytes 4612
  87.3 61.5 %copy-start.2 = (f32[384]{0:T(512)S(1)}, f32[384]{0:T(512)}, u32[]{:S(2)}) copy-start(f32[384]{0:T(512)} %param.13) | copy-start | bytes 4612
  87.3 61.5 %copy-start.3 = (s32[384]{0:T(512)S(1)}, s32[384]{0:T(512)}, u32[]{:S(2)}) copy-start(s32[384]{0:T(512)} %param.11) | copy-start | bytes 4612
  87.3 61.5 %copy-start.4 = (f32[384]{0:T(512)S(1)}, f32[384]{0:T(512)}, u32[]{:S(2)}) copy-start(f32[384]{0:T(512)} %param.12) | copy-start | bytes 4612
  87.3 61.5 %copy-start.5 = (f32[384]{0:T(512)S(1)}, f32[384]{0:T(512)}, u32[]{:S(2)}) copy-start(f32[384]{0:T(512)} %param.14) | copy-start | bytes 4612
  87.3 76.4 %copy-start.6 = (s32[32]{0:T(128)S(1)}, s32[32]{0:T(128)}, u32[]{:S(2)}) copy-start(s32[32]{0:T(128)} %param.15) | copy-start | bytes 388
  131.7 17.0 %all-to-all-start = ((f32[16,4,384]{2,1,0:T(4,128)}), f32[16,4,384]{2,1,0:T(4,128)S(1)}, u32[]{:S(2)}, u32[]{:S(2)}) async-start(f32[16,4,384]{2,1,0:T(4,128)} %broadcast_in_dim.10), calls=%async_computation | async-start | bytes 196608 | tf_op jit(solution)/shard_map/all_to_all | solution.py:113
  149.6 14.1 %all-to-all-start.1 = ((f32[32,1,32]{2,1,0:T(1,128)}), f32[32,1,32]{2,1,0:T(1,128)S(1)}, u32[]{:S(2)}, u32[]{:S(2)}) async-start(f32[32,1,32]{2,1,0:T(1,128)} %broadcast_in_dim.11), calls=%async_computation.1 | async-start | bytes 32768 | tf_op jit(solution)/shard_map/all_to_all | solution.py:137
Sparse Core Ops, SparseCore 0:
  11.2 108.4 all-gather.1

commit v12 on v10

--- a/solution.py
+++ b/solution.py
@@ -84,12 +84,8 @@
     nx = lax.axis_size("x")
     ny = lax.axis_size("y")
     half = (cols // 2) // 128 * 128
-
-    def put_y(buf, piece, index):
-        return lax.dynamic_update_slice(buf, piece, (index * depth * nx, 0))
-
     strip = spread_gather(head[:, :half], "x").reshape(nx * depth, half)
-    first_full = ring_gather(strip, "y", put_y, jnp.zeros((depth * nx * ny, half), head.dtype))
+    first_full = lax.all_gather(strip, "y", axis=0, tiled=True)
 
     width = cols - half
 
@@ -108,7 +104,7 @@
     which = lax.axis_index(VOCAB_AXES)
     block_first = VOCAB - cols_here * spread
     first_col = block_first + which * cols_here
-    gathered = lax.all_gather(hidden, VOCAB_AXES, axis=1, tiled=True)
+    gathered = gather_hidden(hidden)
     head_first, head_second = gather_head(head)
     logits = jnp.concatenate(
         [

time: 182 us -> 192 us (1.055)
  waiting for transfers between devices: 70.2 us -> 45.1 us
  starting transfers between devices: 59.2 us -> 79.8 us
  local copies, waits for them, and re-layouts: 14.9 us -> 26.4 us
  matrix products: 8.99 us -> 11.6 us
    ppermute x0 -> x15, starting transfers between devices: none -> 50.5 us  [the longest x8 22.7 us: share(): other = lax.ppermute(piece, 'c', across)]
    ppermute x6 -> x2, waiting for transfers between devices: 49.6 us -> 7.41 us  [ring_gather(): fwd = lax.ppermute(fwd, axis, ahead)]
    dynamic_update_slice x8 -> x16, local copies, waits for them, and re-layouts: 2.41 us -> 17.3 us  [place(): return lax.dynamic_update_slice(buf, piece, (0, slot))]
    ppermute x4 -> x1, starting transfers between devices: 16.2 us -> 4.3 us  [ring_gather(): bwd = lax.ppermute(bwd, axis, behind)]
    ppermute x4 -> x1, waiting for transfers between devices: 4.14 us -> 15.8 us  [ring_gather(): bwd = lax.ppermute(bwd, axis, behind)]
    ppermute x6 -> x2, starting transfers between devices: 13.5 us -> 4.1 us  [ring_gather(): fwd = lax.ppermute(fwd, axis, ahead)]
    all_to_all x1, starting transfers between devices: 14.6 us -> 5.35 us  [local(): every = lax.all_to_all(copies, VOCAB_AXES, 0, 0, tiled=True)]
    ppermute x0 -> x15, waiting for transfers between devices: none -> 5.99 us  [the longest x4 5.96 us: gather_hidden(): fwd = lax.ppermute(fwd, 'z', ahead)]
  transfers between devices with their start and end apart: 14 -> 22, of which waited for: 8 -> 6; matrix products, arithmetic and copies ran while one was open for 7% -> 16% of each run, Pallas kernels for 0% -> 0%
where the time goes in v12:
time: 192 us; the launch traced here: 191 us
  starting transfers between devices  79.8 us (42%)
  waiting for transfers between devices  45.1 us (23%)
  local copies, waits for them, and re-layouts  26.4 us (14%)
  between operations  14.6 us (8%)
  blocking collectives  11.8 us (6%)
  matrix products  11.6 us (6%)
  other arithmetic  2.17 us (1%)
    ppermute x8, starting transfers between devices, share(): other = lax.ppermute(piece, 'c', across)  22.7 us
    ppermute x3, starting transfers between devices, gather_hidden(): bwd = lax.ppermute(bwd, 'z', behind)  18 us
    dynamic_update_slice x16, local copies, waits for them, and re-layouts, place(): return lax.dynamic_update_slice(buf, piece, (0, slot))  17.3 us
    ppermute x1, waiting for transfers between devices, ring_gather(): bwd = lax.ppermute(bwd, axis, behind)  15.8 us
    all_to_all x1, blocking collectives, spread_gather(): lax.all_to_all(jnp.broadcast_to(block[None], (n,) + block.shape), axis, 0...  11.8 us
    ppermute x4, starting transfers between devices, gather_hidden(): fwd = lax.ppermute(fwd, 'z', ahead)  9.75 us
    all_to_all x1, starting transfers between devices, spread_gather(): lax.all_to_all(jnp.broadcast_to(block[None], (n,) + block.shape), axis, 0...  8.45 us
    all_to_all x1, waiting for transfers between devices, local(): every = lax.all_to_all(copies, VOCAB_AXES, 0, 0, tiled=True)  8.39 us
  transfers between devices with their start and end apart: 22, of which 6 were waited for; matrix products, arithmetic and copies ran while one was open for 16% of the time, Pallas kernels for 0%

profile of v12, /device:TPU:1, one launch (start us, length us, event | category | flops | bytes accessed | tf_op | source)
XLA Modules:
  0.0 191.4 jit_solution(12840601398005161815)
XLA Ops:
  7.2 1.0 fusion.6
  8.3 11.8 %all_to_all.21 = bf16[4,256,256]{2,1,0:T(8,128)(2,1)} all-to-all(bf16[4,256,256]{2,1,0:T(8,128)(2,1)S(1)} %broadcast_in_dim.23), channel_id=1, replica_groups=mesh['y'=8,'x'=4,'z'=8,'c'=2] {'x'}, dimensions={0} | all-to-all | bytes 1048576 | tf_op jit(solution)/shard_map/all_to_all | solution.py:79
  20.1 1.0 broadcast_in_dim.25
  21.2 8.5 %all-to-all-start.1 = ((bf16[8,256,256]{2,1,0:T(8,128)(2,1)}), bf16[8,256,256]{2,1,0:T(8,128)(2,1)S(1)}, u32[]{:S(2)}, u32[]{:S(2)}) async-start(bf16[8,256,256]{2,1,0:T(8,128)(2,1)} %broadcast_in_dim.25), calls=%async_computation.1 | async-start | bytes 2097152 | tf_op jit(solution)/shard_map/all_to_all | solution.py:79
  29.6 4.0 %collective-permute-start.1 = (bf16[384,512]{1,0:T(8,128)(2,1)}, bf16[384,512]{1,0:T(8,128)(2,1)S(1)}, u32[]{:S(2)}, u32[]{:S(2)}) collective-permute-start(bf16[384,512]{1,0:T(8,128)(2,1)} %param.8), channel_id=1, source_target_pairs={{0,2},{2,4},{4,6},{6,8},{8,10},{10,12},{12,14},{14,0},{1,3},{3,5},... | collective-permute-start | bytes 1179656 | tf_op jit(solution)/shard_map/ppermute | solution.py:50
  33.6 8.6 %collective-permute-start.3 = (bf16[384,512]{1,0:T(8,128)(2,1)}, bf16[384,512]{1,0:T(8,128)(2,1)S(1)}, u32[]{:S(2)}, u32[]{:S(2)}) collective-permute-start(bf16[384,512]{1,0:T(8,128)(2,1)} %param.8), channel_id=1, source_target_pairs={{0,14},{2,0},{4,2},{6,4},{8,6},{10,8},{12,10},{14,12},{1,15},{3,1}... | collective-permute-start | bytes 1179656 | tf_op jit(solution)/shard_map/ppermute | solution.py:52
  42.2 4.3 %collective-permute-start = (bf16[384,512]{1,0:T(8,128)(2,1)}, bf16[384,512]{1,0:T(8,128)(2,1)}, u32[]{:S(2)}, u32[]{:S(2)}) collective-permute-start(bf16[384,512]{1,0:T(8,128)(2,1)} %param.8), channel_id=1, source_target_pairs={{0,1},{1,0},{2,3},{3,2},{4,5},{5,4},{6,7},{7,6},{8,9},{9,8},{10,11... | collective-permute-start | bytes 1179656 | tf_op jit(solution)/shard_map/ppermute | solution.py:42
  46.6 1.3 collective-permute-done.1
  47.9 4.6 %collective-permute-start.2 = (bf16[384,512]{1,0:T(8,128)(2,1)S(1)}, bf16[384,512]{1,0:T(8,128)(2,1)S(1)}, u32[]{:S(2)}, u32[]{:S(2)}) collective-permute-start(bf16[384,512]{1,0:T(8,128)(2,1)S(1)} %collective-permute-done.1), channel_id=1, source_target_pairs={{0,1},{1,0},{2,3},{3,2},{4,5},{5,4},{6,7},{7,6},{8,9},{9,8},{10,11... | collective-permute-start | bytes 1179656 | tf_op jit(solution)/shard_map/ppermute | solution.py:42
  52.4 1.9 %collective-permute-start.5 = (bf16[384,512]{1,0:T(8,128)(2,1)S(1)}, bf16[384,512]{1,0:T(8,128)(2,1)S(1)}, u32[]{:S(2)}, u32[]{:S(2)}) collective-permute-start(bf16[384,512]{1,0:T(8,128)(2,1)S(1)} %collective-permute-done.1), channel_id=1, source_target_pairs={{0,2},{2,4},{4,6},{6,8},{8,10},{10,12},{12,14},{14,0},{1,3},{3,5},... | collective-permute-start | bytes 1179656 | tf_op jit(solution)/shard_map/ppermute | solution.py:50
  54.4 4.6 %collective-permute-start.7 = (bf16[384,512]{1,0:T(8,128)(2,1)S(1)}, bf16[384,512]{1,0:T(8,128)(2,1)S(1)}, u32[]{:S(2)}, u32[]{:S(2)}) collective-permute-start(bf16[384,512]{1,0:T(8,128)(2,1)S(1)} %collective-permute-done.3), channel_id=1, source_target_pairs={{0,14},{2,0},{4,2},{6,4},{8,6},{10,8},{12,10},{14,12},{1,15},{3,1}... | collective-permute-start | bytes 1179656 | tf_op jit(solution)/shard_map/ppermute | solution.py:52
  60.0 3.4 %broadcast_in_dim.22 = bf16[384,8192]{1,0:T(8,128)(2,1)} broadcast(bf16[]{:T(256)} %constant.112.clone.1), dimensions={} | broadcast | bytes 6291458 | tf_op jit(solution)/shard_map/broadcast_in_dim | solution.py:33
  63.4 0.9 constant_dynamic-update-slice_fusion.15
  64.3 2.4 %collective-permute-start.4 = (bf16[384,512]{1,0:T(8,128)(2,1)S(1)}, bf16[384,512]{1,0:T(8,128)(2,1)}, u32[]{:S(2)}, u32[]{:S(2)}) collective-permute-start(bf16[384,512]{1,0:T(8,128)(2,1)S(1)} %collective-permute-done.3), channel_id=1, source_target_pairs={{0,1},{1,0},{2,3},{3,2},{4,5},{5,4},{6,7},{7,6},{8,9},{9,8},{10,11... | collective-permute-start | bytes 1179656 | tf_op jit(solution)/shard_map/ppermute | solution.py:42
  66.7 1.8 constant_dynamic-update-slice_fusion.14
  69.4 1.9 %collective-permute-start.6 = (bf16[384,512]{1,0:T(8,128)(2,1)S(1)}, bf16[384,512]{1,0:T(8,128)(2,1)}, u32[]{:S(2)}, u32[]{:S(2)}) collective-permute-start(bf16[384,512]{1,0:T(8,128)(2,1)S(1)} %collective-permute-done.5), channel_id=1, source_target_pairs={{0,1},{1,0},{2,3},{3,2},{4,5},{5,4},{6,7},{7,6},{8,9},{9,8},{10,11... | collective-permute-start | bytes 1179656 | tf_op jit(solution)/shard_map/ppermute | solution.py:42
  71.3 1.9 %collective-permute-start.9 = (bf16[384,512]{1,0:T(8,128)(2,1)S(1)}, bf16[384,512]{1,0:T(8,128)(2,1)S(1)}, u32[]{:S(2)}, u32[]{:S(2)}) collective-permute-start(bf16[384,512]{1,0:T(8,128)(2,1)S(1)} %collective-permute-done.5), channel_id=1, source_target_pairs={{0,2},{2,4},{4,6},{6,8},{8,10},{10,12},{12,14},{14,0},{1,3},{3,5},... | collective-permute-start | bytes 1179656 | tf_op jit(solution)/shard_map/ppermute | solution.py:50
  73.3 2.4 %collective-permute-start.8 = (bf16[384,512]{1,0:T(8,128)(2,1)S(1)}, bf16[384,512]{1,0:T(8,128)(2,1)}, u32[]{:S(2)}, u32[]{:S(2)}) collective-permute-start(bf16[384,512]{1,0:T(8,128)(2,1)S(1)} %collective-permute-done.7), channel_id=1, source_target_pairs={{0,1},{1,0},{2,3},{3,2},{4,5},{5,4},{6,7},{7,6},{8,9},{9,8},{10,11... | collective-permute-start | bytes 1179656 | tf_op jit(solution)/shard_map/ppermute | solution.py:42
  75.7 4.9 %collective-permute-start.11 = (bf16[384,512]{1,0:T(8,128)(2,1)S(1)}, bf16[384,512]{1,0:T(8,128)(2,1)S(1)}, u32[]{:S(2)}, u32[]{:S(2)}) collective-permute-start(bf16[384,512]{1,0:T(8,128)(2,1)S(1)} %collective-permute-done.7), channel_id=1, source_target_pairs={{0,14},{2,0},{4,2},{6,4},{8,6},{10,8},{12,10},{14,12},{1,15},{3,1}... | collective-permute-start | bytes 1179656 | tf_op jit(solution)/shard_map/ppermute | solution.py:52
  80.5 0.8 constant_dynamic-update-slice_fusion.12
  81.4 0.9 constant_dynamic-update-slice_fusion.11
  82.2 2.2 %collective-permute-start.15 = (bf16[8,256,256]{2,1,0:T(8,128)(2,1)S(1)}, bf16[8,256,256]{2,1,0:T(8,128)(2,1)S(1)}, u32[]{:S(2)}, u32[]{:S(2)}) collective-permute-start(bf16[8,256,256]{2,1,0:T(8,128)(2,1)S(1)} %all-to-all-done.1), channel_id=1, source_target_pairs={{0,16},{16,32},{32,48},{48,0},{1,17},{17,33},{33,49},{49,1},{2,18}... | collective-permute-start | bytes 3145736 | tf_op jit(solution)/shard_map/ppermute | solution.py:68
  84.4 1.9 constant_dynamic-update-slice_fusion.10
  86.3 0.8 constant_dynamic-update-slice_fusion.9
  87.1 2.5 %collective-permute-start.10 = (bf16[384,512]{1,0:T(8,128)(2,1)S(1)}, bf16[384,512]{1,0:T(8,128)(2,1)S(1)}, u32[]{:S(2)}, u32[]{:S(2)}) collective-permute-start(bf16[384,512]{1,0:T(8,128)(2,1)S(1)} %collective-permute-done.9), channel_id=1, source_target_pairs={{0,1},{1,0},{2,3},{3,2},{4,5},{5,4},{6,7},{7,6},{8,9},{9,8},{10,11... | collective-permute-start | bytes 1179656 | tf_op jit(solution)/shard_map/ppermute | solution.py:42
  89.6 1.9 %collective-permute-start.13 = (bf16[384,512]{1,0:T(8,128)(2,1)S(1)}, bf16[384,512]{1,0:T(8,128)(2,1)S(1)}, u32[]{:S(2)}, u32[]{:S(2)}) collective-permute-start(bf16[384,512]{1,0:T(8,128)(2,1)S(1)} %collective-permute-done.9), channel_id=1, source_target_pairs={{0,2},{2,4},{4,6},{6,8},{8,10},{10,12},{12,14},{14,0},{1,3},{3,5},... | collective-permute-start | bytes 1179656 | tf_op jit(solution)/shard_map/ppermute | solution.py:50
  91.5 1.9 %collective-permute-start.12 = (bf16[384,512]{1,0:T(8,128)(2,1)S(1)}, bf16[384,512]{1,0:T(8,128)(2,1)S(1)}, u32[]{:S(2)}, u32[]{:S(2)}) collective-permute-start(bf16[384,512]{1,0:T(8,128)(2,1)S(1)} %collective-permute-done.11), channel_id=1, source_target_pairs={{0,1},{1,0},{2,3},{3,2},{4,5},{5,4},{6,7},{7,6},{8,9},{9,8},{10,11... | collective-permute-start | bytes 1179656 | tf_op jit(solution)/shard_map/ppermute | solution.py:42
  93.4 1.8 constant_dynamic-update-slice_fusion.8
  95.3 0.8 constant_dynamic-update-slice_fusion.7
  96.1 1.9 constant_dynamic-update-slice_fusion.6
  98.0 0.8 constant_dynamic-update-slice_fusion.5
  98.8 4.7 %collective-permute-done.13 = bf16[384,512]{1,0:T(8,128)(2,1)S(1)} collective-permute-done((bf16[384,512]{1,0:T(8,128)(2,1)S(1)}, bf16[384,512]{1,0:T(8,128)(2,1)S(1)}, u32[]{:S(2)}, u32[]{:S(2)}) %collective-permute-start.13) | collective-permute-done | bytes 393248 | tf_op jit(solution)/shard_map/ppermute | solution.py:50
  103.4 2.7 %collective-permute-start.14 = (bf16[384,512]{1,0:T(8,128)(2,1)S(1)}, bf16[384,512]{1,0:T(8,128)(2,1)S(1)}, u32[]{:S(2)}, u32[]{:S(2)}) collective-permute-start(bf16[384,512]{1,0:T(8,128)(2,1)S(1)} %collective-permute-done.13), channel_id=1, source_target_pairs={{0,1},{1,0},{2,3},{3,2},{4,5},{5,4},{6,7},{7,6},{8,9},{9,8},{10,11... | collective-permute-start | bytes 1179656 | tf_op jit(solution)/shard_map/ppermute | solution.py:42
  106.1 4.3 %collective-permute-start.16 = (bf16[8,256,256]{2,1,0:T(8,128)(2,1)S(1)}, bf16[8,256,256]{2,1,0:T(8,128)(2,1)S(1)}, u32[]{:S(2)}, u32[]{:S(2)}) collective-permute-start(bf16[8,256,256]{2,1,0:T(8,128)(2,1)S(1)} %all-to-all-done.1), channel_id=1, source_target_pairs={{0,48},{16,0},{32,16},{48,32},{1,49},{17,1},{33,17},{49,33},{2,50}... | collective-permute-start | bytes 3145736 | tf_op jit(solution)/shard_map/ppermute | solution.py:70
  110.4 0.8 constant_dynamic-update-slice_fusion.4
  111.2 0.9 constant_dynamic-update-slice_fusion.3
  112.1 0.8 constant_dynamic-update-slice_fusion.2
  112.9 1.9 collective-permute-start.17
  114.9 0.8 constant_dynamic-update-slice_fusion.1
  116.2 0.8 constant_dynamic-update-slice_fusion
  117.2 15.8 %collective-permute-done.16 = bf16[8,256,256]{2,1,0:T(8,128)(2,1)S(1)} collective-permute-done((bf16[8,256,256]{2,1,0:T(8,128)(2,1)S(1)}, bf16[8,256,256]{2,1,0:T(8,128)(2,1)S(1)}, u32[]{:S(2)}, u32[]{:S(2)}) %collective-permute-start.16) | collective-permute-done | bytes 1048608 | tf_op jit(solution)/shard_map/ppermute | solution.py:70
  133.1 7.4 %collective-permute-done.17 = bf16[8,256,256]{2,1,0:T(8,128)(2,1)S(1)} collective-permute-done((bf16[8,256,256]{2,1,0:T(8,128)(2,1)S(1)}, bf16[8,256,256]{2,1,0:T(8,128)(2,1)S(1)}, u32[]{:S(2)}, u32[]{:S(2)}) %collective-permute-start.17) | collective-permute-done | bytes 1048608 | tf_op jit(solution)/shard_map/ppermute | solution.py:68
  140.6 5.2 %fusion.9 = (f32[384]{0:T(512)S(1)}, f32[384,256]{0,1:T(8,128)S(1)}) fusion(bf16[384,8192]{1,0:T(8,128)(2,1)} %constant_dynamic-update-slice_fusion, bf16[8192,256]{1,0:T(8,128)(2,1)S(1)} %bitcast.42), kind=kOutput, calls=%fused_computation.53 | convolution fusion | flops 1610710656 | bytes 10880512 | tf_op jit(solution)/shard_map/dot_general | solution.py:112
  145.9 6.4 %fusion.8 = (f32[384]{0:T(512)S(1)}, f32[384,256]{0,1:T(8,128)S(1)}) fusion(bf16[384,8192]{1,0:T(8,128)(2,1)} %constant_dynamic-update-slice_fusion, bf16[8192,256]{1,0:T(8,128)(2,1)} %all-gather.2.cloned.1.call-done), kind=kOutput, calls=%fused_computation.52 | convolution fusion | flops 1610710656 | bytes 10880512 | tf_op jit(solution)/shard_map/dot_general | solution.py:111
  153.3 5.3 %all-to-all-start.2 = ((f32[16,4,384]{2,1,0:T(4,128)}), f32[16,4,384]{2,1,0:T(4,128)S(1)}, u32[]{:S(2)}, u32[]{:S(2)}) async-start(f32[16,4,384]{2,1,0:T(4,128)} %broadcast_in_dim.31), calls=%async_computation.2 | async-start | bytes 196608 | tf_op jit(solution)/shard_map/all_to_all | solution.py:126
  158.7 8.4 %all-to-all-done.2 = f32[16,4,384]{2,1,0:T(4,128)S(1)} async-done(((f32[16,4,384]{2,1,0:T(4,128)}), f32[16,4,384]{2,1,0:T(4,128)S(1)}, u32[]{:S(2)}, u32[]{:S(2)}) %all-to-all-start.2) | async-done | bytes 98336 | tf_op jit(solution)/shard_map/all_to_all | solution.py:126
  168.0 7.0 %all-to-all-start.3 = ((f32[32,1,32]{2,1,0:T(1,128)}), f32[32,1,32]{2,1,0:T(1,128)S(1)}, u32[]{:S(2)}, u32[]{:S(2)}) async-start(f32[32,1,32]{2,1,0:T(1,128)} %broadcast_in_dim.64), calls=%async_computation.3 | async-start | bytes 32768 | tf_op jit(solution)/shard_map/all_to_all | solution.py:150
  176.2 7.4 %all-to-all-done.3 = f32[32,1,32]{2,1,0:T(1,128)S(1)} async-done(((f32[32,1,32]{2,1,0:T(1,128)}), f32[32,1,32]{2,1,0:T(1,128)S(1)}, u32[]{:S(2)}, u32[]{:S(2)}) %all-to-all-start.3) | async-done | bytes 4128 | tf_op jit(solution)/shard_map/all_to_all | solution.py:150
  (68 shorter events, 6.7 us)
Async XLA Ops:
  7.2 52.5 %copy-start.6 = (s32[32]{0:T(128)S(1)}, s32[32]{0:T(128)}, u32[]{:S(2)}) copy-start(s32[32]{0:T(128)} %param.15) | copy-start | bytes 388
  7.2 138.7 %all-gather.2.cloned.1.call-start = ((), (), s32[]{:S(2)}) async-start(), calls=%async_computation.4 | async-start | bytes 4718592 | tf_op jit(solution)/shard_map/all_gather | solution.py:88
  8.2 55.2 %copy-start = (bf16[384,512]{1,0:T(8,128)(2,1)S(1)}, bf16[384,512]{1,0:T(8,128)(2,1)}, u32[]{:S(2)}) copy-start(bf16[384,512]{1,0:T(8,128)(2,1)} %param.8) | copy-start | bytes 1179652
  21.2 61.1 %all-to-all-start.1 = ((bf16[8,256,256]{2,1,0:T(8,128)(2,1)}), bf16[8,256,256]{2,1,0:T(8,128)(2,1)S(1)}, u32[]{:S(2)}, u32[]{:S(2)}) async-start(bf16[8,256,256]{2,1,0:T(8,128)(2,1)} %broadcast_in_dim.25), calls=%async_computation.1 | async-start | bytes 2097152 | tf_op jit(solution)/shard_map/all_to_all | solution.py:79
  29.6 18.2 %collective-permute-start.1 = (bf16[384,512]{1,0:T(8,128)(2,1)}, bf16[384,512]{1,0:T(8,128)(2,1)S(1)}, u32[]{:S(2)}, u32[]{:S(2)}) collective-permute-start(bf16[384,512]{1,0:T(8,128)(2,1)} %param.8), channel_id=1, source_target_pairs={{0,2},{2,4},{4,6},{6,8},{8,10},{10,12},{12,14},{14,0},{1,3},{3,5},... | collective-permute-start | bytes 1179656 | tf_op jit(solution)/shard_map/ppermute | solution.py:50
  33.6 20.8 %collective-permute-start.3 = (bf16[384,512]{1,0:T(8,128)(2,1)}, bf16[384,512]{1,0:T(8,128)(2,1)S(1)}, u32[]{:S(2)}, u32[]{:S(2)}) collective-permute-start(bf16[384,512]{1,0:T(8,128)(2,1)} %param.8), channel_id=1, source_target_pairs={{0,14},{2,0},{4,2},{6,4},{8,6},{10,8},{12,10},{14,12},{1,15},{3,1}... | collective-permute-start | bytes 1179656 | tf_op jit(solution)/shard_map/ppermute | solution.py:52
  42.2 24.5 %collective-permute-start = (bf16[384,512]{1,0:T(8,128)(2,1)}, bf16[384,512]{1,0:T(8,128)(2,1)}, u32[]{:S(2)}, u32[]{:S(2)}) collective-permute-start(bf16[384,512]{1,0:T(8,128)(2,1)} %param.8), channel_id=1, source_target_pairs={{0,1},{1,0},{2,3},{3,2},{4,5},{5,4},{6,7},{7,6},{8,9},{9,8},{10,11... | collective-permute-start | bytes 1179656 | tf_op jit(solution)/shard_map/ppermute | solution.py:42
  47.9 27.8 %collective-permute-start.2 = (bf16[384,512]{1,0:T(8,128)(2,1)S(1)}, bf16[384,512]{1,0:T(8,128)(2,1)S(1)}, u32[]{:S(2)}, u32[]{:S(2)}) collective-permute-start(bf16[384,512]{1,0:T(8,128)(2,1)S(1)} %collective-permute-done.1), channel_id=1, source_target_pairs={{0,1},{1,0},{2,3},{3,2},{4,5},{5,4},{6,7},{7,6},{8,9},{9,8},{10,11... | collective-permute-start | bytes 1179656 | tf_op jit(solution)/shard_map/ppermute | solution.py:42
  52.4 17.0 %collective-permute-start.5 = (bf16[384,512]{1,0:T(8,128)(2,1)S(1)}, bf16[384,512]{1,0:T(8,128)(2,1)S(1)}, u32[]{:S(2)}, u32[]{:S(2)}) collective-permute-start(bf16[384,512]{1,0:T(8,128)(2,1)S(1)} %collective-permute-done.1), channel_id=1, source_target_pairs={{0,2},{2,4},{4,6},{6,8},{8,10},{10,12},{12,14},{14,0},{1,3},{3,5},... | collective-permute-start | bytes 1179656 | tf_op jit(solution)/shard_map/ppermute | solution.py:50
  54.4 18.9 %collective-permute-start.7 = (bf16[384,512]{1,0:T(8,128)(2,1)S(1)}, bf16[384,512]{1,0:T(8,128)(2,1)S(1)}, u32[]{:S(2)}, u32[]{:S(2)}) collective-permute-start(bf16[384,512]{1,0:T(8,128)(2,1)S(1)} %collective-permute-done.3), channel_id=1, source_target_pairs={{0,14},{2,0},{4,2},{6,4},{8,6},{10,8},{12,10},{14,12},{1,15},{3,1}... | collective-permute-start | bytes 1179656 | tf_op jit(solution)/shard_map/ppermute | solution.py:52
  64.3 17.9 %collective-permute-start.4 = (bf16[384,512]{1,0:T(8,128)(2,1)S(1)}, bf16[384,512]{1,0:T(8,128)(2,1)}, u32[]{:S(2)}, u32[]{:S(2)}) collective-permute-start(bf16[384,512]{1,0:T(8,128)(2,1)S(1)} %collective-permute-done.3), channel_id=1, source_target_pairs={{0,1},{1,0},{2,3},{3,2},{4,5},{5,4},{6,7},{7,6},{8,9},{9,8},{10,11... | collective-permute-start | bytes 1179656 | tf_op jit(solution)/shard_map/ppermute | solution.py:42
  69.4 20.2 %collective-permute-start.6 = (bf16[384,512]{1,0:T(8,128)(2,1)S(1)}, bf16[384,512]{1,0:T(8,128)(2,1)}, u32[]{:S(2)}, u32[]{:S(2)}) collective-permute-start(bf16[384,512]{1,0:T(8,128)(2,1)S(1)} %collective-permute-done.5), channel_id=1, source_target_pairs={{0,1},{1,0},{2,3},{3,2},{4,5},{5,4},{6,7},{7,6},{8,9},{9,8},{10,11... | collective-permute-start | bytes 1179656 | tf_op jit(solution)/shard_map/ppermute | solution.py:42
  71.3 15.8 %collective-permute-start.9 = (bf16[384,512]{1,0:T(8,128)(2,1)S(1)}, bf16[384,512]{1,0:T(8,128)(2,1)S(1)}, u32[]{:S(2)}, u32[]{:S(2)}) collective-permute-start(bf16[384,512]{1,0:T(8,128)(2,1)S(1)} %collective-permute-done.5), channel_id=1, source_target_pairs={{0,2},{2,4},{4,6},{6,8},{8,10},{10,12},{12,14},{14,0},{1,3},{3,5},... | collective-permute-start | bytes 1179656 | tf_op jit(solution)/shard_map/ppermute | solution.py:50
  73.3 22.8 %collective-permute-start.8 = (bf16[384,512]{1,0:T(8,128)(2,1)S(1)}, bf16[384,512]{1,0:T(8,128)(2,1)}, u32[]{:S(2)}, u32[]{:S(2)}) collective-permute-start(bf16[384,512]{1,0:T(8,128)(2,1)S(1)} %collective-permute-done.7), channel_id=1, source_target_pairs={{0,1},{1,0},{2,3},{3,2},{4,5},{5,4},{6,7},{7,6},{8,9},{9,8},{10,11... | collective-permute-start | bytes 1179656 | tf_op jit(solution)/shard_map/ppermute | solution.py:42
  75.7 15.8 %collective-permute-start.11 = (bf16[384,512]{1,0:T(8,128)(2,1)S(1)}, bf16[384,512]{1,0:T(8,128)(2,1)S(1)}, u32[]{:S(2)}, u32[]{:S(2)}) collective-permute-start(bf16[384,512]{1,0:T(8,128)(2,1)S(1)} %collective-permute-done.7), channel_id=1, source_target_pairs={{0,14},{2,0},{4,2},{6,4},{8,6},{10,8},{12,10},{14,12},{1,15},{3,1}... | collective-permute-start | bytes 1179656 | tf_op jit(solution)/shard_map/ppermute | solution.py:52
  82.2 30.7 %collective-permute-start.15 = (bf16[8,256,256]{2,1,0:T(8,128)(2,1)S(1)}, bf16[8,256,256]{2,1,0:T(8,128)(2,1)S(1)}, u32[]{:S(2)}, u32[]{:S(2)}) collective-permute-start(bf16[8,256,256]{2,1,0:T(8,128)(2,1)S(1)} %all-to-all-done.1), channel_id=1, source_target_pairs={{0,16},{16,32},{32,48},{48,0},{1,17},{17,33},{33,49},{49,1},{2,18}... | collective-permute-start | bytes 3145736 | tf_op jit(solution)/shard_map/ppermute | solution.py:68
  87.1 23.3 %collective-permute-start.10 = (bf16[384,512]{1,0:T(8,128)(2,1)S(1)}, bf16[384,512]{1,0:T(8,128)(2,1)S(1)}, u32[]{:S(2)}, u32[]{:S(2)}) collective-permute-start(bf16[384,512]{1,0:T(8,128)(2,1)S(1)} %collective-permute-done.9), channel_id=1, source_target_pairs={{0,1},{1,0},{2,3},{3,2},{4,5},{5,4},{6,7},{7,6},{8,9},{9,8},{10,11... | collective-permute-start | bytes 1179656 | tf_op jit(solution)/shard_map/ppermute | solution.py:42
  89.6 13.8 %collective-permute-start.13 = (bf16[384,512]{1,0:T(8,128)(2,1)S(1)}, bf16[384,512]{1,0:T(8,128)(2,1)S(1)}, u32[]{:S(2)}, u32[]{:S(2)}) collective-permute-start(bf16[384,512]{1,0:T(8,128)(2,1)S(1)} %collective-permute-done.9), channel_id=1, source_target_pairs={{0,2},{2,4},{4,6},{6,8},{8,10},{10,12},{12,14},{14,0},{1,3},{3,5},... | collective-permute-start | bytes 1179656 | tf_op jit(solution)/shard_map/ppermute | solution.py:50
  91.5 20.6 %collective-permute-start.12 = (bf16[384,512]{1,0:T(8,128)(2,1)S(1)}, bf16[384,512]{1,0:T(8,128)(2,1)S(1)}, u32[]{:S(2)}, u32[]{:S(2)}) collective-permute-start(bf16[384,512]{1,0:T(8,128)(2,1)S(1)} %collective-permute-done.11), channel_id=1, source_target_pairs={{0,1},{1,0},{2,3},{3,2},{4,5},{5,4},{6,7},{7,6},{8,9},{9,8},{10,11... | collective-permute-start | bytes 1179656 | tf_op jit(solution)/shard_map/ppermute | solution.py:42
  103.4 12.8 %collective-permute-start.14 = (bf16[384,512]{1,0:T(8,128)(2,1)S(1)}, bf16[384,512]{1,0:T(8,128)(2,1)S(1)}, u32[]{:S(2)}, u32[]{:S(2)}) collective-permute-start(bf16[384,512]{1,0:T(8,128)(2,1)S(1)} %collective-permute-done.13), channel_id=1, source_target_pairs={{0,1},{1,0},{2,3},{3,2},{4,5},{5,4},{6,7},{7,6},{8,9},{9,8},{10,11... | collective-permute-start | bytes 1179656 | tf_op jit(solution)/shard_map/ppermute | solution.py:42
  106.1 26.9 %collective-permute-start.16 = (bf16[8,256,256]{2,1,0:T(8,128)(2,1)S(1)}, bf16[8,256,256]{2,1,0:T(8,128)(2,1)S(1)}, u32[]{:S(2)}, u32[]{:S(2)}) collective-permute-start(bf16[8,256,256]{2,1,0:T(8,128)(2,1)S(1)} %all-to-all-done.1), channel_id=1, source_target_pairs={{0,48},{16,0},{32,16},{48,32},{1,49},{17,1},{33,17},{49,33},{2,50}... | collective-permute-start | bytes 3145736 | tf_op jit(solution)/shard_map/ppermute | solution.py:70
  112.9 27.5 %collective-permute-start.17 = (bf16[8,256,256]{2,1,0:T(8,128)(2,1)S(1)}, bf16[8,256,256]{2,1,0:T(8,128)(2,1)S(1)}, u32[]{:S(2)}, u32[]{:S(2)}) collective-permute-start(bf16[8,256,256]{2,1,0:T(8,128)(2,1)S(1)} %collective-permute-done.15), channel_id=1, source_target_pairs={{0,16},{16,32},{32,48},{48,0},{1,17},{17,33},{33,49},{49,1},{2,18}... | collective-permute-start | bytes 3145736 | tf_op jit(solution)/shard_map/ppermute | solution.py:68
  145.8 21.4 %copy-start.1 = (s32[384]{0:T(512)S(1)}, s32[384]{0:T(512)}, u32[]{:S(2)}) copy-start(s32[384]{0:T(512)} %param.10) | copy-start | bytes 4612
  145.8 21.4 %copy-start.2 = (f32[384]{0:T(512)S(1)}, f32[384]{0:T(512)}, u32[]{:S(2)}) copy-start(f32[384]{0:T(512)} %param.13) | copy-start | bytes 4612
  145.8 21.4 %copy-start.3 = (s32[384]{0:T(512)S(1)}, s32[384]{0:T(512)}, u32[]{:S(2)}) copy-start(s32[384]{0:T(512)} %param.11) | copy-start | bytes 4612
  145.8 21.4 %copy-start.4 = (f32[384]{0:T(512)S(1)}, f32[384]{0:T(512)}, u32[]{:S(2)}) copy-start(f32[384]{0:T(512)} %param.12) | copy-start | bytes 4612
  145.8 21.4 %copy-start.5 = (f32[384]{0:T(512)S(1)}, f32[384]{0:T(512)}, u32[]{:S(2)}) copy-start(f32[384]{0:T(512)} %param.14) | copy-start | bytes 4612
  153.3 13.8 %all-to-all-start.2 = ((f32[16,4,384]{2,1,0:T(4,128)}), f32[16,4,384]{2,1,0:T(4,128)S(1)}, u32[]{:S(2)}, u32[]{:S(2)}) async-start(f32[16,4,384]{2,1,0:T(4,128)} %broadcast_in_dim.31), calls=%async_computation.2 | async-start | bytes 196608 | tf_op jit(solution)/shard_map/all_to_all | solution.py:126
  168.0 15.6 %all-to-all-start.3 = ((f32[32,1,32]{2,1,0:T(1,128)}), f32[32,1,32]{2,1,0:T(1,128)S(1)}, u32[]{:S(2)}, u32[]{:S(2)}) async-start(f32[32,1,32]{2,1,0:T(1,128)} %broadcast_in_dim.64), calls=%async_computation.3 | async-start | bytes 32768 | tf_op jit(solution)/shard_map/all_to_all | solution.py:150
Sparse Core Ops, SparseCore 0:
  20.2 75.8 all-gather.1

commit v13 on v12

--- a/solution.py
+++ b/solution.py
@@ -22,38 +22,23 @@
 
 
 def gather_hidden(hidden):
+    rows, width = hidden.shape
     nz = lax.axis_size("z")
-    z = lax.axis_index("z")
+    nc = lax.axis_size("c")
     c = lax.axis_index("c")
-    nc = lax.axis_size("c")
-    width = hidden.shape[1]
-    ahead = [(i, (i + 1) % nz) for i in range(nz)]
-    behind = [(i, (i - 1) % nz) for i in range(nz)]
-    across = [(i, (i + 1) % nc) for i in range(nc)]
-    full = jnp.zeros((hidden.shape[0], width * nz * nc), hidden.dtype)
 
-    def place(buf, piece, chip, core):
-        slot = (chip * nc + core) * width
-        return lax.dynamic_update_slice(buf, piece, (0, slot))
+    def put(buf, piece, index):
+        return lax.dynamic_update_slice(buf, piece, (0, index * width))
 
-    def share(buf, piece, chip):
-        buf = place(buf, piece, chip, c)
-        if nc > 1:
-            other = lax.ppermute(piece, "c", across)
-            buf = place(buf, other, chip, (c + 1) % nc)
-        return buf
-
-    full = share(full, hidden, z)
-    fwd = hidden
-    bwd = hidden
-    for step in range(1, nz // 2 + 1):
-        fwd = lax.ppermute(fwd, "z", ahead)
-        if step <= (nz - 1) // 2:
-            bwd = lax.ppermute(bwd, "z", behind)
-        full = share(full, fwd, (z - step) % nz)
-        if step <= (nz - 1) // 2:
-            full = share(full, bwd, (z + step) % nz)
-    return full
+    own = ring_gather(hidden, "z", put, jnp.zeros((rows, nz * width), hidden.dtype))
+    if nc == 1:
+        return own
+    other = lax.ppermute(own, "c", [(i, (i + 1) % nc) for i in range(nc)])
+    own = own.reshape(rows, nz, 1, width)
+    other = other.reshape(rows, nz, 1, width)
+    first = jnp.where(c == 0, own, other)
+    second = jnp.where(c == 0, other, own)
+    return jnp.concatenate([first, second], axis=2).reshape(rows, nz * nc * width)
 
 
 def ring_gather(block, axis, place, buf):
@@ -83,7 +68,7 @@
     depth, cols = head.shape
     nx = lax.axis_size("x")
     ny = lax.axis_size("y")
-    half = (cols // 2) // 128 * 128
+    half = (cols * 3 // 4) // 128 * 128
     strip = spread_gather(head[:, :half], "x").reshape(nx * depth, half)
     first_full = lax.all_gather(strip, "y", axis=0, tiled=True)
 

time: 192 us -> 199 us (1.036)
  blocking collectives: 11.8 us -> 43.2 us
  starting transfers between devices: 79.8 us -> 56.3 us
  local copies, waits for them, and re-layouts: 26.4 us -> 22.5 us
  other arithmetic: 2.17 us -> 4.66 us
  matrix products: 11.6 us -> 9.38 us
    ppermute x15 -> x1, starting transfers between devices: 50.5 us -> 6.74 us  [gather_hidden(): other = lax.ppermute(own, 'c', [(i, (i + 1) % nc) for i in range(nc)])]
    all_to_all x1 -> x2, blocking collectives: 11.8 us -> 43.2 us  [spread_gather(): lax.all_to_all(jnp.broadcast_to(block[None], (n,) + block.shape), axis, 0...]
    ppermute x2 -> x6, waiting for transfers between devices: 7.41 us -> 31.1 us  [ring_gather(): fwd = lax.ppermute(fwd, axis, ahead)]
    ppermute x1 -> x4, starting transfers between devices: 4.3 us -> 22.1 us  [ring_gather(): bwd = lax.ppermute(bwd, axis, behind)]
    ppermute x1 -> x4, waiting for transfers between devices: 15.8 us -> 0.01 us  [ring_gather(): bwd = lax.ppermute(bwd, axis, behind)]
    dynamic_update_slice x16 -> x8, local copies, waits for them, and re-layouts: 17.3 us -> 1.55 us  [put(): return lax.dynamic_update_slice(buf, piece, (0, index * width))]
    ppermute x2 -> x6, starting transfers between devices: 4.1 us -> 16.9 us  [ring_gather(): fwd = lax.ppermute(fwd, axis, ahead)]
    ppermute x0 -> x7, local copies, waits for them, and re-layouts: none -> 9.19 us  [the longest x4 4.85 us: ring_gather(): fwd = lax.ppermute(fwd, axis, ahead)]
  transfers between devices with their start and end apart: 22 -> 14, of which waited for: 6 -> 7; matrix products, arithmetic and copies ran while one was open for 16% -> 11% of each run, Pallas kernels for 0% -> 0%
where the time goes in v13:
time: 199 us; the launch traced here: 198 us
  starting transfers between devices  56.3 us (28%)
  waiting for transfers between devices  46.9 us (24%)
  blocking collectives  43.2 us (22%)
  local copies, waits for them, and re-layouts  22.5 us (11%)
  between operations  14.8 us (7%)
  matrix products  9.38 us (5%)
  other arithmetic  4.66 us (2%)
    all_to_all x2, blocking collectives, spread_gather(): lax.all_to_all(jnp.broadcast_to(block[None], (n,) + block.shape), axis, 0...  43.2 us
    ppermute x6, waiting for transfers between devices, ring_gather(): fwd = lax.ppermute(fwd, axis, ahead)  31.1 us
    ppermute x4, starting transfers between devices, ring_gather(): bwd = lax.ppermute(bwd, axis, behind)  22.1 us
    ppermute x6, starting transfers between devices, ring_gather(): fwd = lax.ppermute(fwd, axis, ahead)  16.9 us
    all_to_all x1, waiting for transfers between devices, local(): every = lax.all_to_all(copies, VOCAB_AXES, 0, 0, tiled=True)  8.39 us
    dot_general x1, matrix products, local(): jnp.dot(gathered, head_first, preferred_element_type=jnp.float32)  8.07 us
    all_to_all x1, waiting for transfers between devices, local(): lax.all_to_all(spread_sums, ROW_AXES, 0, 0, tiled=True)  7.42 us
    all_to_all x1, starting transfers between devices, local(): every = lax.all_to_all(copies, VOCAB_AXES, 0, 0, tiled=True)  6.78 us
  transfers between devices with their start and end apart: 14, of which 7 were waited for; matrix products, arithmetic and copies ran while one was open for 11% of the time, Pallas kernels for 0%

profile of v13, /device:TPU:1, one launch (start us, length us, event | category | flops | bytes accessed | tf_op | source)
XLA Modules:
  0.0 197.8 jit_solution(9371299753365037173)
XLA Ops:
  7.2 1.0 slice.18
  8.3 13.1 %all_to_all.21 = bf16[4,256,384]{2,1,0:T(8,128)(2,1)} all-to-all(bf16[4,256,384]{2,1,0:T(8,128)(2,1)S(1)} %broadcast_in_dim.23), channel_id=1, replica_groups=mesh['y'=8,'x'=4,'z'=8,'c'=2] {'x'}, dimensions={0} | all-to-all | bytes 1572864 | tf_op jit(solution)/shard_map/all_to_all | solution.py:64
  21.4 7.0 %collective-permute-start = (bf16[384,512]{1,0:T(8,128)(2,1)S(1)}, bf16[384,512]{1,0:T(8,128)(2,1)S(1)}, u32[]{:S(2)}, u32[]{:S(2)}) collective-permute-start(bf16[384,512]{1,0:T(8,128)(2,1)S(1)} %copy-done.1), channel_id=1, source_target_pairs={{0,2},{2,4},{4,6},{6,8},{8,10},{10,12},{12,14},{14,0},{1,3},{3,5},... | collective-permute-start | bytes 1179656 | tf_op jit(solution)/shard_map/ppermute | solution.py:53
  28.5 8.6 %collective-permute-start.1 = (bf16[384,512]{1,0:T(8,128)(2,1)S(1)}, bf16[384,512]{1,0:T(8,128)(2,1)}, u32[]{:S(2)}, u32[]{:S(2)}) collective-permute-start(bf16[384,512]{1,0:T(8,128)(2,1)S(1)} %copy-done.1), channel_id=1, source_target_pairs={{0,14},{2,0},{4,2},{6,4},{8,6},{10,8},{12,10},{14,12},{1,15},{3,1}... | collective-permute-start | bytes 1179656 | tf_op jit(solution)/shard_map/ppermute | solution.py:55
  37.1 5.6 %collective-permute-done = bf16[384,512]{1,0:T(8,128)(2,1)S(1)} collective-permute-done((bf16[384,512]{1,0:T(8,128)(2,1)S(1)}, bf16[384,512]{1,0:T(8,128)(2,1)S(1)}, u32[]{:S(2)}, u32[]{:S(2)}) %collective-permute-start) | collective-permute-done | bytes 393248 | tf_op jit(solution)/shard_map/ppermute | solution.py:53
  42.7 1.9 collective-permute-start.2
  44.6 4.6 %collective-permute-start.3 = (bf16[384,512]{1,0:T(8,128)(2,1)}, bf16[384,512]{1,0:T(8,128)(2,1)}, u32[]{:S(2)}, u32[]{:S(2)}) collective-permute-start(bf16[384,512]{1,0:T(8,128)(2,1)} %collective-permute-done.1), channel_id=1, source_target_pairs={{0,14},{2,0},{4,2},{6,4},{8,6},{10,8},{12,10},{14,12},{1,15},{3,1}... | collective-permute-start | bytes 1179656 | tf_op jit(solution)/shard_map/ppermute | solution.py:55
  49.2 4.8 %collective-permute-done.2 = bf16[384,512]{1,0:T(8,128)(2,1)} collective-permute-done((bf16[384,512]{1,0:T(8,128)(2,1)S(1)}, bf16[384,512]{1,0:T(8,128)(2,1)}, u32[]{:S(2)}, u32[]{:S(2)}) %collective-permute-start.2) | collective-permute-done | bytes 393248 | tf_op jit(solution)/shard_map/ppermute | solution.py:53
  54.0 1.9 collective-permute-start.4
  56.3 0.3 broadcast_in_dim.22
  56.6 1.2 copy.44
  57.8 4.6 %collective-permute-start.5 = (bf16[384,512]{1,0:T(8,128)(2,1)}, bf16[384,512]{1,0:T(8,128)(2,1)}, u32[]{:S(2)}, u32[]{:S(2)}) collective-permute-start(bf16[384,512]{1,0:T(8,128)(2,1)} %collective-permute-done.3), channel_id=1, source_target_pairs={{0,14},{2,0},{4,2},{6,4},{8,6},{10,8},{12,10},{14,12},{1,15},{3,1}... | collective-permute-start | bytes 1179656 | tf_op jit(solution)/shard_map/ppermute | solution.py:55
  62.5 1.2 copy.45
  63.8 1.2 copy.46
  65.0 1.9 collective-permute-start.6
  67.0 1.2 copy.47
  68.3 1.2 copy.48
  69.6 1.9 copy.49
  71.6 1.1 constant_dynamic-update-slice_fusion.1
  72.6 2.7 %collective-permute-done.6 = bf16[384,512]{1,0:T(8,128)(2,1)} collective-permute-done((bf16[384,512]{1,0:T(8,128)(2,1)}, bf16[384,512]{1,0:T(8,128)(2,1)}, u32[]{:S(2)}, u32[]{:S(2)}) %collective-permute-start.6) | collective-permute-done | bytes 393248 | tf_op jit(solution)/shard_map/ppermute | solution.py:53
  75.4 1.2 copy.50
  76.7 6.7 %collective-permute-start.7 = (bf16[384,4096]{0,1:T(8,128)(2,1)S(1)}, bf16[384,4096]{0,1:T(8,128)(2,1)}, u32[]{:S(2)}, u32[]{:S(2)}) collective-permute-start(bf16[384,4096]{0,1:T(8,128)(2,1)S(1)} %constant_dynamic-update-slice_fusion), channel_id=1, source_target_pairs={{0,1},{1,0},{2,3},{3,2},{4,5},{5,4},{6,7},{7,6},{8,9},{9,8},{10,11... | collective-permute-start | bytes 9437192 | tf_op jit(solution)/shard_map/ppermute | solution.py:36
  83.4 0.8 slice.19
  84.3 30.1 %all_to_all.22 = bf16[8,256,128]{2,1,0:T(8,128)(2,1)} all-to-all(bf16[8,256,128]{2,1,0:T(8,128)(2,1)S(1)} %broadcast_in_dim.25), channel_id=1, replica_groups=mesh['y'=8,'x'=4,'z'=8,'c'=2] {'y'}, dimensions={0} | all-to-all | bytes 1048576 | tf_op jit(solution)/shard_map/all_to_all | solution.py:64
  114.4 2.2 %collective-permute-start.8 = (bf16[8,256,128]{2,1,0:T(8,128)(2,1)}, bf16[8,256,128]{2,1,0:T(8,128)(2,1)}, u32[]{:S(2)}, u32[]{:S(2)}) collective-permute-start(bf16[8,256,128]{2,1,0:T(8,128)(2,1)} %all_to_all.22), channel_id=1, source_target_pairs={{0,16},{16,32},{32,48},{48,0},{1,17},{17,33},{33,49},{49,1},{2,18}... | collective-permute-start | bytes 1572872 | tf_op jit(solution)/shard_map/ppermute | solution.py:53
  116.6 4.3 %collective-permute-start.9 = (bf16[8,256,128]{2,1,0:T(8,128)(2,1)}, bf16[8,256,128]{2,1,0:T(8,128)(2,1)}, u32[]{:S(2)}, u32[]{:S(2)}) collective-permute-start(bf16[8,256,128]{2,1,0:T(8,128)(2,1)} %all_to_all.22), channel_id=1, source_target_pairs={{0,48},{16,0},{32,16},{48,32},{1,49},{17,1},{33,17},{49,33},{2,50}... | collective-permute-start | bytes 1572872 | tf_op jit(solution)/shard_map/ppermute | solution.py:55
  121.3 8.9 %collective-permute-done.8 = bf16[8,256,128]{2,1,0:T(8,128)(2,1)} collective-permute-done((bf16[8,256,128]{2,1,0:T(8,128)(2,1)}, bf16[8,256,128]{2,1,0:T(8,128)(2,1)}, u32[]{:S(2)}, u32[]{:S(2)}) %collective-permute-start.8) | collective-permute-done | bytes 524320 | tf_op jit(solution)/shard_map/ppermute | solution.py:53
  130.2 1.9 collective-permute-start.10
  132.1 0.5 broadcast_in_dim.24
  132.6 1.1 bitcast_dynamic-update-slice_fusion.2
  133.7 1.1 bitcast_dynamic-update-slice_fusion.1
  134.9 1.1 bitcast_dynamic-update-slice_fusion
  136.0 9.0 %collective-permute-done.10 = bf16[8,256,128]{2,1,0:T(8,128)(2,1)S(1)} collective-permute-done((bf16[8,256,128]{2,1,0:T(8,128)(2,1)}, bf16[8,256,128]{2,1,0:T(8,128)(2,1)S(1)}, u32[]{:S(2)}, u32[]{:S(2)}) %collective-permute-start.10) | collective-permute-done | bytes 524320 | tf_op jit(solution)/shard_map/ppermute | solution.py:53
  145.1 2.5 %broadcast_select_fusion.1 = (bf16[384,4096]{0,1:T(8,128)(2,1)S(1)}, bf16[384,4096]{0,1:T(8,128)(2,1)S(1)}) fusion(bf16[384,4096]{0,1:T(8,128)(2,1)S(1)} %constant_dynamic-update-slice_fusion, bf16[384,4096]{0,1:T(8,128)(2,1)} %collective-permute-done.7, pred[]{:T(512)S(6)} %eq.36), kind=kLoop, calls=%fused_computation.2 | loop fusion | flops 3145728 | bytes 12582913 | tf_op jit(solution)/shard_map/jit(_where)/select_n | solution.py:39
  147.6 0.7 pad_maximum_fusion
  148.3 2.6 %copy-done = bf16[384,8,2,512]{0,3,2,1:T(8,128)(2,1)} copy-done((bf16[384,8,2,512]{0,3,2,1:T(8,128)(2,1)}, bf16[384,8,2,512]{0,3,2,1:T(8,128)(2,1)S(1)}, u32[]{:S(2)}) %copy-start) | copy-done | bytes 6291480
  150.9 1.3 fusion.8
  152.3 8.1 %fusion.7 = (f32[384]{0:T(512)S(1)}, f32[384,384]{0,1:T(8,128)S(1)}) fusion(bf16[384,8192]{0,1:T(8,128)(2,1)} %bitcast.48, bf16[8192,384]{1,0:T(8,128)(2,1)} %all-gather.2.cloned.1.call-done), kind=kOutput, calls=%fused_computation.46 | convolution fusion | flops 2416066048 | bytes 13174272 | tf_op jit(solution)/shard_map/dot_general | solution.py:96
  160.4 0.3 fusion
  160.7 0.6 broadcast_in_dim.31
  161.4 6.8 %all-to-all-start.2 = ((f32[16,4,384]{2,1,0:T(4,128)}), f32[16,4,384]{2,1,0:T(4,128)S(1)}, u32[]{:S(2)}, u32[]{:S(2)}) async-start(f32[16,4,384]{2,1,0:T(4,128)} %broadcast_in_dim.31), calls=%async_computation.2 | async-start | bytes 196608 | tf_op jit(solution)/shard_map/all_to_all | solution.py:111
  168.2 8.4 %all-to-all-done.2 = f32[16,4,384]{2,1,0:T(4,128)S(1)} async-done(((f32[16,4,384]{2,1,0:T(4,128)}), f32[16,4,384]{2,1,0:T(4,128)S(1)}, u32[]{:S(2)}, u32[]{:S(2)}) %all-to-all-start.2) | async-done | bytes 98336 | tf_op jit(solution)/shard_map/all_to_all | solution.py:111
  176.9 0.6 broadcast_in_dim.64
  177.6 3.8 %all-to-all-start.3 = ((f32[32,1,32]{2,1,0:T(1,128)}), f32[32,1,32]{2,1,0:T(1,128)S(1)}, u32[]{:S(2)}, u32[]{:S(2)}) async-start(f32[32,1,32]{2,1,0:T(1,128)} %broadcast_in_dim.64), calls=%async_computation.3 | async-start | bytes 32768 | tf_op jit(solution)/shard_map/all_to_all | solution.py:135
  181.4 0.6 dynamic_slice.6
  182.0 0.6 dynamic_slice.7
  182.6 7.4 %all-to-all-done.3 = f32[32,1,32]{2,1,0:T(1,128)S(1)} async-done(((f32[32,1,32]{2,1,0:T(1,128)}), f32[32,1,32]{2,1,0:T(1,128)S(1)}, u32[]{:S(2)}, u32[]{:S(2)}) %all-to-all-start.3) | async-done | bytes 4128 | tf_op jit(solution)/shard_map/all_to_all | solution.py:135
  190.4 0.5 sub.81
  (60 shorter events, 2.1 us)
Async XLA Ops:
  7.2 14.2 %copy-start.1 = (bf16[384,512]{1,0:T(8,128)(2,1)S(1)}, bf16[384,512]{1,0:T(8,128)(2,1)}, u32[]{:S(2)}) copy-start(bf16[384,512]{1,0:T(8,128)(2,1)} %param.8) | copy-start | bytes 1179652
  7.2 145.1 %all-gather.2.cloned.1.call-start = ((), (), s32[]{:S(2)}) async-start(), calls=%async_computation.4 | async-start | bytes 7077888 | tf_op jit(solution)/shard_map/all_gather | solution.py:73
  21.4 21.3 %collective-permute-start = (bf16[384,512]{1,0:T(8,128)(2,1)S(1)}, bf16[384,512]{1,0:T(8,128)(2,1)S(1)}, u32[]{:S(2)}, u32[]{:S(2)}) collective-permute-start(bf16[384,512]{1,0:T(8,128)(2,1)S(1)} %copy-done.1), channel_id=1, source_target_pairs={{0,2},{2,4},{4,6},{6,8},{8,10},{10,12},{12,14},{14,0},{1,3},{3,5},... | collective-permute-start | bytes 1179656 | tf_op jit(solution)/shard_map/ppermute | solution.py:53
  28.5 16.1 %collective-permute-start.1 = (bf16[384,512]{1,0:T(8,128)(2,1)S(1)}, bf16[384,512]{1,0:T(8,128)(2,1)}, u32[]{:S(2)}, u32[]{:S(2)}) collective-permute-start(bf16[384,512]{1,0:T(8,128)(2,1)S(1)} %copy-done.1), channel_id=1, source_target_pairs={{0,14},{2,0},{4,2},{6,4},{8,6},{10,8},{12,10},{14,12},{1,15},{3,1}... | collective-permute-start | bytes 1179656 | tf_op jit(solution)/shard_map/ppermute | solution.py:55
  42.7 1.9 copy-start.2
  42.7 11.3 %collective-permute-start.2 = (bf16[384,512]{1,0:T(8,128)(2,1)S(1)}, bf16[384,512]{1,0:T(8,128)(2,1)}, u32[]{:S(2)}, u32[]{:S(2)}) collective-permute-start(bf16[384,512]{1,0:T(8,128)(2,1)S(1)} %collective-permute-done), channel_id=1, source_target_pairs={{0,2},{2,4},{4,6},{6,8},{8,10},{10,12},{12,14},{14,0},{1,3},{3,5},... | collective-permute-start | bytes 1179656 | tf_op jit(solution)/shard_map/ppermute | solution.py:53
  44.6 13.2 %collective-permute-start.3 = (bf16[384,512]{1,0:T(8,128)(2,1)}, bf16[384,512]{1,0:T(8,128)(2,1)}, u32[]{:S(2)}, u32[]{:S(2)}) collective-permute-start(bf16[384,512]{1,0:T(8,128)(2,1)} %collective-permute-done.1), channel_id=1, source_target_pairs={{0,14},{2,0},{4,2},{6,4},{8,6},{10,8},{12,10},{14,12},{1,15},{3,1}... | collective-permute-start | bytes 1179656 | tf_op jit(solution)/shard_map/ppermute | solution.py:55
  54.0 11.0 %collective-permute-start.4 = (bf16[384,512]{1,0:T(8,128)(2,1)}, bf16[384,512]{1,0:T(8,128)(2,1)}, u32[]{:S(2)}, u32[]{:S(2)}) collective-permute-start(bf16[384,512]{1,0:T(8,128)(2,1)} %collective-permute-done.2), channel_id=1, source_target_pairs={{0,2},{2,4},{4,6},{6,8},{8,10},{10,12},{12,14},{14,0},{1,3},{3,5},... | collective-permute-start | bytes 1179656 | tf_op jit(solution)/shard_map/ppermute | solution.py:53
  57.8 11.7 %collective-permute-start.5 = (bf16[384,512]{1,0:T(8,128)(2,1)}, bf16[384,512]{1,0:T(8,128)(2,1)}, u32[]{:S(2)}, u32[]{:S(2)}) collective-permute-start(bf16[384,512]{1,0:T(8,128)(2,1)} %collective-permute-done.3), channel_id=1, source_target_pairs={{0,14},{2,0},{4,2},{6,4},{8,6},{10,8},{12,10},{14,12},{1,15},{3,1}... | collective-permute-start | bytes 1179656 | tf_op jit(solution)/shard_map/ppermute | solution.py:55
  65.0 10.3 %collective-permute-start.6 = (bf16[384,512]{1,0:T(8,128)(2,1)}, bf16[384,512]{1,0:T(8,128)(2,1)}, u32[]{:S(2)}, u32[]{:S(2)}) collective-permute-start(bf16[384,512]{1,0:T(8,128)(2,1)} %collective-permute-done.4), channel_id=1, source_target_pairs={{0,2},{2,4},{4,6},{6,8},{8,10},{10,12},{12,14},{14,0},{1,3},{3,5},... | collective-permute-start | bytes 1179656 | tf_op jit(solution)/shard_map/ppermute | solution.py:53
  68.3 52.6 %copy-start.3 = (s32[384]{0:T(512)S(1)}, s32[384]{0:T(512)}, u32[]{:S(2)}) copy-start(s32[384]{0:T(512)} %param.10) | copy-start | bytes 4612
  68.3 52.7 %copy-start.8 = (s32[32]{0:T(128)S(1)}, s32[32]{0:T(128)}, u32[]{:S(2)}) copy-start(s32[32]{0:T(128)} %param.15) | copy-start | bytes 388
  76.7 68.4 %collective-permute-start.7 = (bf16[384,4096]{0,1:T(8,128)(2,1)S(1)}, bf16[384,4096]{0,1:T(8,128)(2,1)}, u32[]{:S(2)}, u32[]{:S(2)}) collective-permute-start(bf16[384,4096]{0,1:T(8,128)(2,1)S(1)} %constant_dynamic-update-slice_fusion), channel_id=1, source_target_pairs={{0,1},{1,0},{2,3},{3,2},{4,5},{5,4},{6,7},{7,6},{8,9},{9,8},{10,11... | collective-permute-start | bytes 9437192 | tf_op jit(solution)/shard_map/ppermute | solution.py:36
  114.4 15.8 %collective-permute-start.8 = (bf16[8,256,128]{2,1,0:T(8,128)(2,1)}, bf16[8,256,128]{2,1,0:T(8,128)(2,1)}, u32[]{:S(2)}, u32[]{:S(2)}) collective-permute-start(bf16[8,256,128]{2,1,0:T(8,128)(2,1)} %all_to_all.22), channel_id=1, source_target_pairs={{0,16},{16,32},{32,48},{48,0},{1,17},{17,33},{33,49},{49,1},{2,18}... | collective-permute-start | bytes 1572872 | tf_op jit(solution)/shard_map/ppermute | solution.py:53
  116.6 18.3 %collective-permute-start.9 = (bf16[8,256,128]{2,1,0:T(8,128)(2,1)}, bf16[8,256,128]{2,1,0:T(8,128)(2,1)}, u32[]{:S(2)}, u32[]{:S(2)}) collective-permute-start(bf16[8,256,128]{2,1,0:T(8,128)(2,1)} %all_to_all.22), channel_id=1, source_target_pairs={{0,48},{16,0},{32,16},{48,32},{1,49},{17,1},{33,17},{49,33},{2,50}... | collective-permute-start | bytes 1572872 | tf_op jit(solution)/shard_map/ppermute | solution.py:55
  130.2 14.8 %collective-permute-start.10 = (bf16[8,256,128]{2,1,0:T(8,128)(2,1)}, bf16[8,256,128]{2,1,0:T(8,128)(2,1)S(1)}, u32[]{:S(2)}, u32[]{:S(2)}) collective-permute-start(bf16[8,256,128]{2,1,0:T(8,128)(2,1)} %collective-permute-done.8), channel_id=1, source_target_pairs={{0,16},{16,32},{32,48},{48,0},{1,17},{17,33},{33,49},{49,1},{2,18}... | collective-permute-start | bytes 1572872 | tf_op jit(solution)/shard_map/ppermute | solution.py:53
  148.3 2.7 %copy-start = (bf16[384,8,2,512]{0,3,2,1:T(8,128)(2,1)}, bf16[384,8,2,512]{0,3,2,1:T(8,128)(2,1)S(1)}, u32[]{:S(2)}) copy-start(bf16[384,8,2,512]{0,3,2,1:T(8,128)(2,1)S(1)} %pad_maximum_fusion) | copy-start | bytes 18874372
  152.2 24.5 %copy-start.4 = (f32[384]{0:T(512)S(1)}, f32[384]{0:T(512)}, u32[]{:S(2)}) copy-start(f32[384]{0:T(512)} %param.13) | copy-start | bytes 4612
  152.2 24.5 %copy-start.5 = (s32[384]{0:T(512)S(1)}, s32[384]{0:T(512)}, u32[]{:S(2)}) copy-start(s32[384]{0:T(512)} %param.11) | copy-start | bytes 4612
  152.3 24.5 %copy-start.6 = (f32[384]{0:T(512)S(1)}, f32[384]{0:T(512)}, u32[]{:S(2)}) copy-start(f32[384]{0:T(512)} %param.12) | copy-start | bytes 4612
  152.3 24.5 %copy-start.7 = (f32[384]{0:T(512)S(1)}, f32[384]{0:T(512)}, u32[]{:S(2)}) copy-start(f32[384]{0:T(512)} %param.14) | copy-start | bytes 4612
  161.4 15.3 %all-to-all-start.2 = ((f32[16,4,384]{2,1,0:T(4,128)}), f32[16,4,384]{2,1,0:T(4,128)S(1)}, u32[]{:S(2)}, u32[]{:S(2)}) async-start(f32[16,4,384]{2,1,0:T(4,128)} %broadcast_in_dim.31), calls=%async_computation.2 | async-start | bytes 196608 | tf_op jit(solution)/shard_map/all_to_all | solution.py:111
  177.6 12.4 %all-to-all-start.3 = ((f32[32,1,32]{2,1,0:T(1,128)}), f32[32,1,32]{2,1,0:T(1,128)S(1)}, u32[]{:S(2)}, u32[]{:S(2)}) async-start(f32[32,1,32]{2,1,0:T(1,128)} %broadcast_in_dim.64), calls=%async_computation.3 | async-start | bytes 32768 | tf_op jit(solution)/shard_map/all_to_all | solution.py:135
Sparse Core Ops, SparseCore 0:
  21.5 95.0 all-gather.1

commit v14 on v8

--- a/solution.py
+++ b/solution.py
@@ -6,7 +6,7 @@
 VOCAB = 128256
 SEQS = 32
 GSIZE = 8
-ROW_AXES = ("y", "x")
+ROW_AXES = ("y", "x_hi", "x_lo")
 VOCAB_AXES = ("z", "c")
 
 
@@ -56,6 +56,18 @@
     return full
 
 
+def gather_head(head):
+    n = lax.axis_size("x_lo")
+    lo = lax.axis_index("x_lo")
+    other = lax.ppermute(head, "x_lo", [(i, i ^ 1) for i in range(n)])
+    pair = jnp.where(
+        lo % 2 == 0,
+        jnp.concatenate([head, other], axis=0),
+        jnp.concatenate([other, head], axis=0),
+    )
+    return lax.all_gather(pair, ("y", "x_hi"), axis=0, tiled=True)
+
+
 def local(hidden, head, targets, live, prior_lse, prior_mean, prior_target, seq_lengths):
     rows_here = hidden.shape[0]
     cols_here = head.shape[1]
@@ -66,7 +78,7 @@
     gathered = gather_hidden(hidden)
     logits = jnp.dot(
         gathered,
-        lax.all_gather(head, ROW_AXES, axis=0, tiled=True),
+        gather_head(head),
         preferred_element_type=jnp.float32,
     )
     row_peak = jnp.max(logits, axis=1)
@@ -114,9 +126,9 @@
     rows_y = 8 if mesh.shape["rows"] % 8 == 0 else 1
     vocab_c = 2 if mesh.shape["vocab"] % 2 == 0 else 1
     devices = mesh.devices.reshape(
-        rows_y, mesh.shape["rows"] // rows_y, mesh.shape["vocab"] // vocab_c, vocab_c
+        rows_y, mesh.shape["rows"] // rows_y // 2, 2, mesh.shape["vocab"] // vocab_c, vocab_c
     )
-    fine = jax.sharding.Mesh(devices, ("y", "x", "z", "c"))
+    fine = jax.sharding.Mesh(devices, ("y", "x_hi", "x_lo", "z", "c"))
     rows, vocab = ROW_AXES, VOCAB_AXES
     return jax.shard_map(
         local,

time: 169 us -> 215 us (1.27)
  waiting for transfers between devices: 60.7 us -> 97.3 us
  starting transfers between devices: 63.2 us -> 70.1 us
    all_gather x1, waiting for transfers between devices: 32.4 us -> 67.5 us  [gather_head(): return lax.all_gather(pair, ('y', 'x_hi'), axis=0, tiled=True)]
    ppermute x0 -> x1, starting transfers between devices: none -> 4.08 us  [gather_head(): other = lax.ppermute(head, 'x_lo', [(i, i ^ 1) for i in range(n)])]
    ppermute x0 -> x1, waiting for transfers between devices: none -> 3.94 us  [gather_head(): other = lax.ppermute(head, 'x_lo', [(i, i ^ 1) for i in range(n)])]
  transfers between devices with their start and end apart: 18 -> 19, of which waited for: 6 -> 7; matrix products, arithmetic and copies ran while one was open for 12% -> 9% of each run, Pallas kernels for 0% -> 0%
where the time goes in v14:
time: 215 us; the launch traced here: 214 us
  waiting for transfers between devices  97.3 us (45%)
  starting transfers between devices  70.1 us (33%)
  local copies, waits for them, and re-layouts  20 us (9%)
  between operations  14.5 us (7%)
  matrix products  8 us (4%)
  other arithmetic  4.4 us (2%)
    all_gather x1, waiting for transfers between devices, gather_head(): return lax.all_gather(pair, ('y', 'x_hi'), axis=0, tiled=True)  67.5 us
    ppermute x8, starting transfers between devices, share(): other = lax.ppermute(piece, 'c', across)  22.4 us
    ppermute x3, starting transfers between devices, gather_hidden(): bwd = lax.ppermute(bwd, 'z', behind)  18 us
    dynamic_update_slice x16, local copies, waits for them, and re-layouts, place(): return lax.dynamic_update_slice(buf, piece, (0, slot))  13.1 us
    ppermute x4, starting transfers between devices, gather_hidden(): fwd = lax.ppermute(fwd, 'z', ahead)  12 us
    ppermute x4, waiting for transfers between devices, gather_hidden(): fwd = lax.ppermute(fwd, 'z', ahead)  9.97 us
    all_to_all x1, starting transfers between devices, local(): every = lax.all_to_all(copies, VOCAB_AXES, 0, 0, tiled=True)  8.47 us
    all_to_all x1, waiting for transfers between devices, local(): every = lax.all_to_all(copies, VOCAB_AXES, 0, 0, tiled=True)  8.39 us
  transfers between devices with their start and end apart: 19, of which 7 were waited for; matrix products, arithmetic and copies ran while one was open for 9% of the time, Pallas kernels for 0%

profile of v14, /device:TPU:1, one launch (start us, length us, event | category | flops | bytes accessed | tf_op | source)
XLA Modules:
  0.0 214.3 jit_solution(890705470140365044)
XLA Ops:
  7.2 4.1 %collective-permute-start.15 = (bf16[256,512]{1,0:T(8,128)(2,1)}, bf16[256,512]{1,0:T(8,128)(2,1)S(1)}, u32[]{:S(2)}, u32[]{:S(2)}) collective-permute-start(bf16[256,512]{1,0:T(8,128)(2,1)} %param.9), channel_id=1, source_target_pairs={{0,16},{16,0},{1,17},{17,1},{2,18},{18,2},{3,19},{19,3},{4,20},{20... | collective-permute-start | bytes 786440 | tf_op jit(solution)/shard_map/ppermute | solution.py:62
  11.3 3.9 %collective-permute-done.15 = bf16[256,512]{1,0:T(8,128)(2,1)S(1)} collective-permute-done((bf16[256,512]{1,0:T(8,128)(2,1)}, bf16[256,512]{1,0:T(8,128)(2,1)S(1)}, u32[]{:S(2)}, u32[]{:S(2)}) %collective-permute-start.15) | collective-permute-done | bytes 262176 | tf_op jit(solution)/shard_map/ppermute | solution.py:62
  15.3 2.0 maximum_select_fusion
  17.3 6.2 %collective-permute-start.1 = (bf16[384,512]{1,0:T(8,128)(2,1)}, bf16[384,512]{1,0:T(8,128)(2,1)S(1)}, u32[]{:S(2)}, u32[]{:S(2)}) collective-permute-start(bf16[384,512]{1,0:T(8,128)(2,1)} %param.8), channel_id=1, source_target_pairs={{0,2},{2,4},{4,6},{6,8},{8,10},{10,12},{12,14},{14,0},{1,3},{3,5},... | collective-permute-start | bytes 1179656 | tf_op jit(solution)/shard_map/ppermute | solution.py:50
  23.5 8.6 %collective-permute-start.3 = (bf16[384,512]{1,0:T(8,128)(2,1)}, bf16[384,512]{1,0:T(8,128)(2,1)S(1)}, u32[]{:S(2)}, u32[]{:S(2)}) collective-permute-start(bf16[384,512]{1,0:T(8,128)(2,1)} %param.8), channel_id=1, source_target_pairs={{0,14},{2,0},{4,2},{6,4},{8,6},{10,8},{12,10},{14,12},{1,15},{3,1}... | collective-permute-start | bytes 1179656 | tf_op jit(solution)/shard_map/ppermute | solution.py:52
  32.1 3.7 %collective-permute-start = (bf16[384,512]{1,0:T(8,128)(2,1)}, bf16[384,512]{1,0:T(8,128)(2,1)S(1)}, u32[]{:S(2)}, u32[]{:S(2)}) collective-permute-start(bf16[384,512]{1,0:T(8,128)(2,1)} %param.8), channel_id=1, source_target_pairs={{0,1},{1,0},{2,3},{3,2},{4,5},{5,4},{6,7},{7,6},{8,9},{9,8},{10,11... | collective-permute-start | bytes 1179656 | tf_op jit(solution)/shard_map/ppermute | solution.py:42
  35.9 2.4 %collective-permute-done.1 = bf16[384,512]{1,0:T(8,128)(2,1)S(1)} collective-permute-done((bf16[384,512]{1,0:T(8,128)(2,1)}, bf16[384,512]{1,0:T(8,128)(2,1)S(1)}, u32[]{:S(2)}, u32[]{:S(2)}) %collective-permute-start.1) | collective-permute-done | bytes 393248 | tf_op jit(solution)/shard_map/ppermute | solution.py:50
  38.3 4.1 %collective-permute-start.2 = (bf16[384,512]{1,0:T(8,128)(2,1)S(1)}, bf16[384,512]{1,0:T(8,128)(2,1)S(1)}, u32[]{:S(2)}, u32[]{:S(2)}) collective-permute-start(bf16[384,512]{1,0:T(8,128)(2,1)S(1)} %collective-permute-done.1), channel_id=1, source_target_pairs={{0,1},{1,0},{2,3},{3,2},{4,5},{5,4},{6,7},{7,6},{8,9},{9,8},{10,11... | collective-permute-start | bytes 1179656 | tf_op jit(solution)/shard_map/ppermute | solution.py:42
  42.3 1.9 collective-permute-start.5
  44.3 4.6 %collective-permute-start.7 = (bf16[384,512]{1,0:T(8,128)(2,1)S(1)}, bf16[384,512]{1,0:T(8,128)(2,1)S(1)}, u32[]{:S(2)}, u32[]{:S(2)}) collective-permute-start(bf16[384,512]{1,0:T(8,128)(2,1)S(1)} %collective-permute-done.3), channel_id=1, source_target_pairs={{0,14},{2,0},{4,2},{6,4},{8,6},{10,8},{12,10},{14,12},{1,15},{3,1}... | collective-permute-start | bytes 1179656 | tf_op jit(solution)/shard_map/ppermute | solution.py:52
  48.9 0.7 broadcast_subtract_fusion
  49.6 0.7 copy.21
  50.6 3.5 %broadcast_in_dim.8 = bf16[384,8192]{1,0:T(8,128)(2,1)} broadcast(bf16[]{:T(256)} %constant.100.clone.1), dimensions={} | broadcast | bytes 6291458 | tf_op jit(solution)/shard_map/broadcast_in_dim | solution.py:33
  54.0 0.9 constant_dynamic-update-slice_fusion.15
  54.9 2.5 %collective-permute-start.4 = (bf16[384,512]{1,0:T(8,128)(2,1)S(1)}, bf16[384,512]{1,0:T(8,128)(2,1)S(1)}, u32[]{:S(2)}, u32[]{:S(2)}) collective-permute-start(bf16[384,512]{1,0:T(8,128)(2,1)S(1)} %collective-permute-done.3), channel_id=1, source_target_pairs={{0,1},{1,0},{2,3},{3,2},{4,5},{5,4},{6,7},{7,6},{8,9},{9,8},{10,11... | collective-permute-start | bytes 1179656 | tf_op jit(solution)/shard_map/ppermute | solution.py:42
  57.4 0.9 constant_dynamic-update-slice_fusion.14
  58.2 0.8 constant_dynamic-update-slice_fusion.13
  59.0 1.9 collective-permute-start.6
  61.0 1.9 collective-permute-start.9
  62.9 2.4 %collective-permute-start.8 = (bf16[384,512]{1,0:T(8,128)(2,1)S(1)}, bf16[384,512]{1,0:T(8,128)(2,1)S(1)}, u32[]{:S(2)}, u32[]{:S(2)}) collective-permute-start(bf16[384,512]{1,0:T(8,128)(2,1)S(1)} %collective-permute-done.7), channel_id=1, source_target_pairs={{0,1},{1,0},{2,3},{3,2},{4,5},{5,4},{6,7},{7,6},{8,9},{9,8},{10,11... | collective-permute-start | bytes 1179656 | tf_op jit(solution)/shard_map/ppermute | solution.py:42
  65.3 4.9 %collective-permute-start.11 = (bf16[384,512]{1,0:T(8,128)(2,1)S(1)}, bf16[384,512]{1,0:T(8,128)(2,1)S(1)}, u32[]{:S(2)}, u32[]{:S(2)}) collective-permute-start(bf16[384,512]{1,0:T(8,128)(2,1)S(1)} %collective-permute-done.7), channel_id=1, source_target_pairs={{0,14},{2,0},{4,2},{6,4},{8,6},{10,8},{12,10},{14,12},{1,15},{3,1}... | collective-permute-start | bytes 1179656 | tf_op jit(solution)/shard_map/ppermute | solution.py:52
  70.2 0.8 constant_dynamic-update-slice_fusion.12
  71.0 0.8 constant_dynamic-update-slice_fusion.11
  71.8 0.8 constant_dynamic-update-slice_fusion.10
  72.7 0.8 constant_dynamic-update-slice_fusion.9
  73.5 0.8 collective-permute-done.9
  74.2 3.2 %collective-permute-start.10 = (bf16[384,512]{1,0:T(8,128)(2,1)S(1)}, bf16[384,512]{1,0:T(8,128)(2,1)S(1)}, u32[]{:S(2)}, u32[]{:S(2)}) collective-permute-start(bf16[384,512]{1,0:T(8,128)(2,1)S(1)} %collective-permute-done.9), channel_id=1, source_target_pairs={{0,1},{1,0},{2,3},{3,2},{4,5},{5,4},{6,7},{7,6},{8,9},{9,8},{10,11... | collective-permute-start | bytes 1179656 | tf_op jit(solution)/shard_map/ppermute | solution.py:42
  77.5 1.9 collective-permute-start.13
  79.4 1.9 collective-permute-start.12
  81.4 0.8 constant_dynamic-update-slice_fusion.8
  82.2 0.8 constant_dynamic-update-slice_fusion.7
  83.0 0.8 constant_dynamic-update-slice_fusion.6
  83.9 0.8 constant_dynamic-update-slice_fusion.5
  84.6 6.8 %collective-permute-done.13 = bf16[384,512]{1,0:T(8,128)(2,1)S(1)} collective-permute-done((bf16[384,512]{1,0:T(8,128)(2,1)S(1)}, bf16[384,512]{1,0:T(8,128)(2,1)S(1)}, u32[]{:S(2)}, u32[]{:S(2)}) %collective-permute-start.13) | collective-permute-done | bytes 393248 | tf_op jit(solution)/shard_map/ppermute | solution.py:50
  91.4 2.6 %collective-permute-start.14 = (bf16[384,512]{1,0:T(8,128)(2,1)S(1)}, bf16[384,512]{1,0:T(8,128)(2,1)S(1)}, u32[]{:S(2)}, u32[]{:S(2)}) collective-permute-start(bf16[384,512]{1,0:T(8,128)(2,1)S(1)} %collective-permute-done.13), channel_id=1, source_target_pairs={{0,1},{1,0},{2,3},{3,2},{4,5},{5,4},{6,7},{7,6},{8,9},{9,8},{10,11... | collective-permute-start | bytes 1179656 | tf_op jit(solution)/shard_map/ppermute | solution.py:42
  94.0 0.8 constant_dynamic-update-slice_fusion.4
  94.9 0.8 constant_dynamic-update-slice_fusion.3
  95.7 0.8 constant_dynamic-update-slice_fusion.2
  96.5 0.8 constant_dynamic-update-slice_fusion.1
  97.3 0.8 constant_dynamic-update-slice_fusion
  98.1 67.5 %all-gather.2.cloned.1.call-done = bf16[8192,512]{1,0:T(8,128)(2,1)} async-done(((bf16[512,512]{1,0:T(8,128)(2,1)}), bf16[8192,512]{1,0:T(8,128)(2,1)}) %all-gather.2.cloned.1.call-update) | async-done | bytes 8388624 | tf_op jit(solution)/shard_map/all_gather | solution.py:68
  165.6 8.0 %fusion.7 = (f32[384]{0:T(512)S(1)}, f32[384,512]{1,0:T(8,128)S(1)}) fusion(bf16[384,8192]{1,0:T(8,128)(2,1)} %constant_dynamic-update-slice_fusion, bf16[8192,512]{1,0:T(8,128)(2,1)} %all-gather.2.cloned.1.call-done), kind=kOutput, calls=%fused_computation.47 | convolution fusion | flops 3221421568 | bytes 15468032 | tf_op jit(solution)/shard_map/dot_general | solution.py:79
  174.2 0.6 broadcast_in_dim.10
  174.8 8.5 %all-to-all-start = ((f32[16,4,384]{2,1,0:T(4,128)}), f32[16,4,384]{2,1,0:T(4,128)S(1)}, u32[]{:S(2)}, u32[]{:S(2)}) async-start(f32[16,4,384]{2,1,0:T(4,128)} %broadcast_in_dim.10), calls=%async_computation | async-start | bytes 196608 | tf_op jit(solution)/shard_map/all_to_all | solution.py:94
  183.4 8.4 %all-to-all-done = f32[16,4,384]{2,1,0:T(4,128)S(1)} async-done(((f32[16,4,384]{2,1,0:T(4,128)}), f32[16,4,384]{2,1,0:T(4,128)S(1)}, u32[]{:S(2)}, u32[]{:S(2)}) %all-to-all-start) | async-done | bytes 98336 | tf_op jit(solution)/shard_map/all_to_all | solution.py:94
  192.1 0.6 broadcast_in_dim.11
  192.7 5.2 %all-to-all-start.1 = ((f32[32,1,32]{2,1,0:T(1,128)}), f32[32,1,32]{2,1,0:T(1,128)S(1)}, u32[]{:S(2)}, u32[]{:S(2)}) async-start(f32[32,1,32]{2,1,0:T(1,128)} %broadcast_in_dim.11), calls=%async_computation.1 | async-start | bytes 32768 | tf_op jit(solution)/shard_map/all_to_all | solution.py:118
  199.1 7.4 %all-to-all-done.1 = f32[32,1,32]{2,1,0:T(1,128)S(1)} async-done(((f32[32,1,32]{2,1,0:T(1,128)}), f32[32,1,32]{2,1,0:T(1,128)S(1)}, u32[]{:S(2)}, u32[]{:S(2)}) %all-to-all-start.1) | async-done | bytes 4128 | tf_op jit(solution)/shard_map/all_to_all | solution.py:118
  (52 shorter events, 3.2 us)
Async XLA Ops:
  7.2 46.8 %copy-start = (bf16[384,512]{1,0:T(8,128)(2,1)S(1)}, bf16[384,512]{1,0:T(8,128)(2,1)}, u32[]{:S(2)}) copy-start(bf16[384,512]{1,0:T(8,128)(2,1)} %param.8) | copy-start | bytes 1179652
  7.2 158.4 %all-gather.2.cloned.1.call-start = ((), (), s32[]{:S(2)}) async-start(), calls=%async_computation.2 | async-start | bytes 8912896 | tf_op jit(solution)/shard_map/all_gather | solution.py:68
  7.2 8.0 %collective-permute-start.15 = (bf16[256,512]{1,0:T(8,128)(2,1)}, bf16[256,512]{1,0:T(8,128)(2,1)S(1)}, u32[]{:S(2)}, u32[]{:S(2)}) collective-permute-start(bf16[256,512]{1,0:T(8,128)(2,1)} %param.9), channel_id=1, source_target_pairs={{0,16},{16,0},{1,17},{17,1},{2,18},{18,2},{3,19},{19,3},{4,20},{20... | collective-permute-start | bytes 786440 | tf_op jit(solution)/shard_map/ppermute | solution.py:62
  17.3 20.9 %collective-permute-start.1 = (bf16[384,512]{1,0:T(8,128)(2,1)}, bf16[384,512]{1,0:T(8,128)(2,1)S(1)}, u32[]{:S(2)}, u32[]{:S(2)}) collective-permute-start(bf16[384,512]{1,0:T(8,128)(2,1)} %param.8), channel_id=1, source_target_pairs={{0,2},{2,4},{4,6},{6,8},{8,10},{10,12},{12,14},{14,0},{1,3},{3,5},... | collective-permute-start | bytes 1179656 | tf_op jit(solution)/shard_map/ppermute | solution.py:50
  23.5 20.8 %collective-permute-start.3 = (bf16[384,512]{1,0:T(8,128)(2,1)}, bf16[384,512]{1,0:T(8,128)(2,1)S(1)}, u32[]{:S(2)}, u32[]{:S(2)}) collective-permute-start(bf16[384,512]{1,0:T(8,128)(2,1)} %param.8), channel_id=1, source_target_pairs={{0,14},{2,0},{4,2},{6,4},{8,6},{10,8},{12,10},{14,12},{1,15},{3,1}... | collective-permute-start | bytes 1179656 | tf_op jit(solution)/shard_map/ppermute | solution.py:52
  32.1 25.2 %collective-permute-start = (bf16[384,512]{1,0:T(8,128)(2,1)}, bf16[384,512]{1,0:T(8,128)(2,1)S(1)}, u32[]{:S(2)}, u32[]{:S(2)}) collective-permute-start(bf16[384,512]{1,0:T(8,128)(2,1)} %param.8), channel_id=1, source_target_pairs={{0,1},{1,0},{2,3},{3,2},{4,5},{5,4},{6,7},{7,6},{8,9},{9,8},{10,11... | collective-permute-start | bytes 1179656 | tf_op jit(solution)/shard_map/ppermute | solution.py:42
  38.3 27.1 %collective-permute-start.2 = (bf16[384,512]{1,0:T(8,128)(2,1)S(1)}, bf16[384,512]{1,0:T(8,128)(2,1)S(1)}, u32[]{:S(2)}, u32[]{:S(2)}) collective-permute-start(bf16[384,512]{1,0:T(8,128)(2,1)S(1)} %collective-permute-done.1), channel_id=1, source_target_pairs={{0,1},{1,0},{2,3},{3,2},{4,5},{5,4},{6,7},{7,6},{8,9},{9,8},{10,11... | collective-permute-start | bytes 1179656 | tf_op jit(solution)/shard_map/ppermute | solution.py:42
  42.3 16.7 %collective-permute-start.5 = (bf16[384,512]{1,0:T(8,128)(2,1)S(1)}, bf16[384,512]{1,0:T(8,128)(2,1)S(1)}, u32[]{:S(2)}, u32[]{:S(2)}) collective-permute-start(bf16[384,512]{1,0:T(8,128)(2,1)S(1)} %collective-permute-done.1), channel_id=1, source_target_pairs={{0,2},{2,4},{4,6},{6,8},{8,10},{10,12},{12,14},{14,0},{1,3},{3,5},... | collective-permute-start | bytes 1179656 | tf_op jit(solution)/shard_map/ppermute | solution.py:50
  44.3 18.6 %collective-permute-start.7 = (bf16[384,512]{1,0:T(8,128)(2,1)S(1)}, bf16[384,512]{1,0:T(8,128)(2,1)S(1)}, u32[]{:S(2)}, u32[]{:S(2)}) collective-permute-start(bf16[384,512]{1,0:T(8,128)(2,1)S(1)} %collective-permute-done.3), channel_id=1, source_target_pairs={{0,14},{2,0},{4,2},{6,4},{8,6},{10,8},{12,10},{14,12},{1,15},{3,1}... | collective-permute-start | bytes 1179656 | tf_op jit(solution)/shard_map/ppermute | solution.py:52
  54.9 16.9 %collective-permute-start.4 = (bf16[384,512]{1,0:T(8,128)(2,1)S(1)}, bf16[384,512]{1,0:T(8,128)(2,1)S(1)}, u32[]{:S(2)}, u32[]{:S(2)}) collective-permute-start(bf16[384,512]{1,0:T(8,128)(2,1)S(1)} %collective-permute-done.3), channel_id=1, source_target_pairs={{0,1},{1,0},{2,3},{3,2},{4,5},{5,4},{6,7},{7,6},{8,9},{9,8},{10,11... | collective-permute-start | bytes 1179656 | tf_op jit(solution)/shard_map/ppermute | solution.py:42
  59.0 22.4 %collective-permute-start.6 = (bf16[384,512]{1,0:T(8,128)(2,1)S(1)}, bf16[384,512]{1,0:T(8,128)(2,1)S(1)}, u32[]{:S(2)}, u32[]{:S(2)}) collective-permute-start(bf16[384,512]{1,0:T(8,128)(2,1)S(1)} %collective-permute-done.5), channel_id=1, source_target_pairs={{0,1},{1,0},{2,3},{3,2},{4,5},{5,4},{6,7},{7,6},{8,9},{9,8},{10,11... | collective-permute-start | bytes 1179656 | tf_op jit(solution)/shard_map/ppermute | solution.py:42
  61.0 13.3 %collective-permute-start.9 = (bf16[384,512]{1,0:T(8,128)(2,1)S(1)}, bf16[384,512]{1,0:T(8,128)(2,1)S(1)}, u32[]{:S(2)}, u32[]{:S(2)}) collective-permute-start(bf16[384,512]{1,0:T(8,128)(2,1)S(1)} %collective-permute-done.5), channel_id=1, source_target_pairs={{0,2},{2,4},{4,6},{6,8},{8,10},{10,12},{12,14},{14,0},{1,3},{3,5},... | collective-permute-start | bytes 1179656 | tf_op jit(solution)/shard_map/ppermute | solution.py:50
  62.9 20.1 %collective-permute-start.8 = (bf16[384,512]{1,0:T(8,128)(2,1)S(1)}, bf16[384,512]{1,0:T(8,128)(2,1)S(1)}, u32[]{:S(2)}, u32[]{:S(2)}) collective-permute-start(bf16[384,512]{1,0:T(8,128)(2,1)S(1)} %collective-permute-done.7), channel_id=1, source_target_pairs={{0,1},{1,0},{2,3},{3,2},{4,5},{5,4},{6,7},{7,6},{8,9},{9,8},{10,11... | collective-permute-start | bytes 1179656 | tf_op jit(solution)/shard_map/ppermute | solution.py:42
  65.3 14.1 %collective-permute-start.11 = (bf16[384,512]{1,0:T(8,128)(2,1)S(1)}, bf16[384,512]{1,0:T(8,128)(2,1)S(1)}, u32[]{:S(2)}, u32[]{:S(2)}) collective-permute-start(bf16[384,512]{1,0:T(8,128)(2,1)S(1)} %collective-permute-done.7), channel_id=1, source_target_pairs={{0,14},{2,0},{4,2},{6,4},{8,6},{10,8},{12,10},{14,12},{1,15},{3,1}... | collective-permute-start | bytes 1179656 | tf_op jit(solution)/shard_map/ppermute | solution.py:52
  74.2 19.8 %collective-permute-start.10 = (bf16[384,512]{1,0:T(8,128)(2,1)S(1)}, bf16[384,512]{1,0:T(8,128)(2,1)S(1)}, u32[]{:S(2)}, u32[]{:S(2)}) collective-permute-start(bf16[384,512]{1,0:T(8,128)(2,1)S(1)} %collective-permute-done.9), channel_id=1, source_target_pairs={{0,1},{1,0},{2,3},{3,2},{4,5},{5,4},{6,7},{7,6},{8,9},{9,8},{10,11... | collective-permute-start | bytes 1179656 | tf_op jit(solution)/shard_map/ppermute | solution.py:42
  77.5 13.9 %collective-permute-start.13 = (bf16[384,512]{1,0:T(8,128)(2,1)S(1)}, bf16[384,512]{1,0:T(8,128)(2,1)S(1)}, u32[]{:S(2)}, u32[]{:S(2)}) collective-permute-start(bf16[384,512]{1,0:T(8,128)(2,1)S(1)} %collective-permute-done.9), channel_id=1, source_target_pairs={{0,2},{2,4},{4,6},{6,8},{8,10},{10,12},{12,14},{14,0},{1,3},{3,5},... | collective-permute-start | bytes 1179656 | tf_op jit(solution)/shard_map/ppermute | solution.py:50
  79.4 16.2 %collective-permute-start.12 = (bf16[384,512]{1,0:T(8,128)(2,1)S(1)}, bf16[384,512]{1,0:T(8,128)(2,1)S(1)}, u32[]{:S(2)}, u32[]{:S(2)}) collective-permute-start(bf16[384,512]{1,0:T(8,128)(2,1)S(1)} %collective-permute-done.11), channel_id=1, source_target_pairs={{0,1},{1,0},{2,3},{3,2},{4,5},{5,4},{6,7},{7,6},{8,9},{9,8},{10,11... | collective-permute-start | bytes 1179656 | tf_op jit(solution)/shard_map/ppermute | solution.py:42
  91.4 5.9 %collective-permute-start.14 = (bf16[384,512]{1,0:T(8,128)(2,1)S(1)}, bf16[384,512]{1,0:T(8,128)(2,1)S(1)}, u32[]{:S(2)}, u32[]{:S(2)}) collective-permute-start(bf16[384,512]{1,0:T(8,128)(2,1)S(1)} %collective-permute-done.13), channel_id=1, source_target_pairs={{0,1},{1,0},{2,3},{3,2},{4,5},{5,4},{6,7},{7,6},{8,9},{9,8},{10,11... | collective-permute-start | bytes 1179656 | tf_op jit(solution)/shard_map/ppermute | solution.py:42
  98.1 93.8 %copy-start.1 = (s32[384]{0:T(512)S(1)}, s32[384]{0:T(512)}, u32[]{:S(2)}) copy-start(s32[384]{0:T(512)} %param.10) | copy-start | bytes 4612
  98.1 93.8 %copy-start.2 = (f32[384]{0:T(512)S(1)}, f32[384]{0:T(512)}, u32[]{:S(2)}) copy-start(f32[384]{0:T(512)} %param.13) | copy-start | bytes 4612
  98.1 93.8 %copy-start.3 = (s32[384]{0:T(512)S(1)}, s32[384]{0:T(512)}, u32[]{:S(2)}) copy-start(s32[384]{0:T(512)} %param.11) | copy-start | bytes 4612
  98.1 93.8 %copy-start.4 = (f32[384]{0:T(512)S(1)}, f32[384]{0:T(512)}, u32[]{:S(2)}) copy-start(f32[384]{0:T(512)} %param.12) | copy-start | bytes 4612
  98.1 93.8 %copy-start.5 = (f32[384]{0:T(512)S(1)}, f32[384]{0:T(512)}, u32[]{:S(2)}) copy-start(f32[384]{0:T(512)} %param.14) | copy-start | bytes 4612
  98.1 108.4 %copy-start.6 = (s32[32]{0:T(128)S(1)}, s32[32]{0:T(128)}, u32[]{:S(2)}) copy-start(s32[32]{0:T(128)} %param.15) | copy-start | bytes 388
  174.8 17.0 %all-to-all-start = ((f32[16,4,384]{2,1,0:T(4,128)}), f32[16,4,384]{2,1,0:T(4,128)S(1)}, u32[]{:S(2)}, u32[]{:S(2)}) async-start(f32[16,4,384]{2,1,0:T(4,128)} %broadcast_in_dim.10), calls=%async_computation | async-start | bytes 196608 | tf_op jit(solution)/shard_map/all_to_all | solution.py:94
  192.7 13.8 %all-to-all-start.1 = ((f32[32,1,32]{2,1,0:T(1,128)}), f32[32,1,32]{2,1,0:T(1,128)S(1)}, u32[]{:S(2)}, u32[]{:S(2)}) async-start(f32[32,1,32]{2,1,0:T(1,128)} %broadcast_in_dim.11), calls=%async_computation.1 | async-start | bytes 32768 | tf_op jit(solution)/shard_map/all_to_all | solution.py:118
Sparse Core Ops, SparseCore 0:
  17.4 148.1 all-gather.1
